TPU v7x, 128 devices: a whole 4x4x4 slice. The times are simulated.
128 devices in a mesh: dom: 32 (over x, z, core), feat: 4 (over y).
Axes of the slice: x: 4, y: 4, z: 4, core: 2. Of those that a mesh axis runs over, the one named last changes fastest.
Arguments:
- features: bfloat16 [128, 131072], P('feat', 'dom'), may hold values from -6 to 6
- neighbours: int32 [8, 131072], P(None, 'dom'), may hold values from 0 to 27647, as said below
- hub_rows: int32 [20480], P('dom'), may hold values from 0 to 4095, as said below
- send_rows: int32 [96, 1024], P('dom'), may hold values from 0 to 4095
- labels: int32 [131072], P('dom'), may hold values from 0 to 171
- inner_self: bfloat16 [256, 128], P('feat'), may hold values from -0.375 to 0.375
- inner_neighbour: bfloat16 [256, 128], P('feat'), may hold values from -0.375 to 0.375
- outer_self: bfloat16 [172, 256], replicated, may hold values from -1.796875 to 1.796875
- outer_neighbour: bfloat16 [172, 256], replicated, may hold values from -1.796875 to 1.796875
Outputs:
- grad_inner_self: float32 [256, 128], P('feat')
- grad_inner_neighbour: float32 [256, 128], P('feat')
- grad_outer_self: float32 [172, 256], P(None, 'feat')
- grad_outer_neighbour: float32 [172, 256], P(None, 'feat')
Inputs may be any that keep to these rules, and one draw needn't show every extreme that they name: `hub_rows`: within each owner's block of 640 entries the rows are distinct; each block holds rows 0 and 4095. `neighbours`: entries below 4096 are own rows, the next 20480 are hubs, the rest are rows received in rounds.
All inputs are finite; a program needn't handle non-finite values.
Results may differ from a plain program's by a relative error of at most 0.004.
The roundings to bfloat16 on the way count: a program that leaves them out, or rounds other values in their place, can miss the bound.
Values may be sent and summed in bfloat16 or wider, within the bound.
No kernel may reach another device: no remote copies, remote signals or barrier semaphores. Data moves between devices by JAX's collectives and lax.ppermute only.
A program may use at most 128 MiB of HBM per device.

v0:
```python
import jax
import jax.numpy as jnp
from jax import lax
from jax.sharding import PartitionSpec as P

loss_scale = 4096.0


def partner(value, axis, stride):
    mask = 2**stride
    pairs = [(source, source ^ mask) for source in range(lax.axis_size(axis))]
    return lax.ppermute(value, axis, pairs)


def trade(piece, bit_index):
    return partner(piece, "dom", bit_index)


def widen(first_rows, second_rows):
    return (
        lax.all_gather(first_rows, "feat", axis=0, tiled=True),
        lax.all_gather(second_rows, "feat", axis=0, tiled=True),
    )


def average(table_rows, neighbours):
    picked = jnp.take(table_rows, neighbours, axis=0)
    summed = jnp.sum(picked.astype(jnp.float32), axis=0) / neighbours.shape[0]
    return summed.T.astype(jnp.bfloat16)


def source_table(local, hub_rows, send_rows):
    local_rows = local.T
    hub_local = jnp.take(local_rows, hub_rows, axis=0)
    hub_all = lax.all_gather(hub_local, "dom", axis=0, tiled=True)
    received = [
        trade(jnp.take(local_rows, send_rows[bit_index], axis=0), bit_index)
        for bit_index in range(send_rows.shape[0])
    ]
    return jnp.concatenate([local_rows, hub_all] + received, axis=0)


def contract(left, right):
    return lax.dot_general(
        left, right, (((1,), (1,)), ((), ())), preferred_element_type=jnp.float32
    )


def transpose_times(left, right):
    return lax.dot_general(
        left, right, (((0,), (0,)), ((), ())), preferred_element_type=jnp.float32
    )


def class_gradient(logits, labels, nodes_all):
    expd = jnp.exp(logits)
    probs = expd / jnp.sum(expd, axis=0, keepdims=True)
    classes = lax.broadcasted_iota(jnp.int32, logits.shape, 0)
    onehot = (classes == labels[None, :]).astype(jnp.float32)
    return ((probs - onehot) * (loss_scale / nodes_all)).astype(jnp.bfloat16)


def body(
    features,
    neighbours,
    hub_rows,
    send_rows,
    labels,
    inner_self,
    inner_neighbour,
    outer_self,
    outer_neighbour,
):
    rows = features.shape[1]
    nodes_all = rows * lax.axis_size("dom")
    mean_one = average(source_table(features, hub_rows, send_rows), neighbours)
    full_input, full_mean = widen(features, mean_one)
    pre_act = jnp.dot(inner_self, full_input, preferred_element_type=jnp.float32)
    pre_act = pre_act + jnp.dot(inner_neighbour, full_mean, preferred_element_type=jnp.float32)
    hidden = jnp.maximum(pre_act, 0.0).astype(jnp.bfloat16)
    mean_two = average(source_table(hidden, hub_rows, send_rows), neighbours)
    width = hidden.shape[0]
    offset = lax.axis_index("feat") * width
    self_cols = lax.dynamic_slice_in_dim(outer_self, offset, width, 1)
    neigh_cols = lax.dynamic_slice_in_dim(outer_neighbour, offset, width, 1)
    full_hidden, full_two = widen(hidden, mean_two)
    logits = jnp.dot(outer_self, full_hidden, preferred_element_type=jnp.float32)
    logits = logits + jnp.dot(outer_neighbour, full_two, preferred_element_type=jnp.float32)
    logit_grad = class_gradient(logits, labels, nodes_all)
    grad_outer_self = contract(logit_grad, hidden)
    grad_outer_neighbour = contract(logit_grad, mean_two)
    direct = transpose_times(self_cols, logit_grad)
    back_mean = transpose_times(neigh_cols, logit_grad).astype(jnp.bfloat16)
    degree = neighbours.shape[0]
    hub_count = lax.axis_size("dom") * hub_rows.shape[0]
    band = send_rows.shape[1]
    span = rows + hub_count + send_rows.shape[0] * band
    back_rows = back_mean.T.astype(jnp.float32)
    updates = jnp.broadcast_to(back_rows[None, :, :], (degree, rows, width)).reshape(
        degree * rows, width
    )
    spread = jnp.zeros((span, width), jnp.float32).at[neighbours.reshape(-1)].add(updates) * (
        1.0 / degree
    )
    grad_rows = direct.T + spread[:rows]
    hub_back = lax.psum_scatter(
        spread[rows : rows + hub_count], "dom", scatter_dimension=0, tiled=True
    )
    grad_rows = grad_rows.at[hub_rows].add(hub_back)
    base = rows + hub_count
    for bit_index in range(send_rows.shape[0]):
        outgoing = spread[base + bit_index * band : base + (bit_index + 1) * band].astype(
            jnp.bfloat16
        )
        returned = trade(outgoing, bit_index)
        grad_rows = grad_rows.at[send_rows[bit_index]].add(returned.astype(jnp.float32))
    grad_hidden = grad_rows.T
    grad_pre = jnp.where(hidden > 0, grad_hidden, 0.0).astype(jnp.bfloat16)
    grad_inner_self = contract(grad_pre, full_input)
    grad_inner_neighbour = contract(grad_pre, full_mean)
    summed = lax.psum(
        (grad_inner_self, grad_inner_neighbour, grad_outer_self, grad_outer_neighbour), "dom"
    )
    return (summed[0], summed[1], summed[2], summed[3])


def solution(mesh):
    return jax.shard_map(
        body,
        mesh=mesh,
        in_specs=(
            P("feat", "dom"),
            P(None, "dom"),
            P("dom"),
            P("dom", None),
            P("dom"),
            P("feat", None),
            P("feat", None),
            P(),
            P(),
        ),
        out_specs=(P("feat", None), P("feat", None), P(None, "feat"), P(None, "feat")),
        check_vma=False,
    )
```

profile of v0, /device:TPU:1, one launch (start us, length us, event | category | flops | bytes accessed | tf_op | source)
XLA Modules:
  0.0 951.2 jit_solution(6668150730996641724)
XLA Ops:
  10.2 3.2 gather_fusion.4
  15.1 2.0 gather_fusion
  18.1 3.2 gather_fusion.5
  21.5 1.8 collective-permute-start.1
  23.3 3.2 gather_fusion.6
  26.7 3.4 collective-permute-start.2
  31.4 38.8 %all-gather.9.cloned.1.call-done = bf16[20480,32]{1,0:T(8,128)(2,1)} async-done(((bf16[640,32]{1,0:T(8,128)(2,1)}), bf16[20480,32]{1,0:T(8,128)(2,1)}) %all-gather.9.cloned.1.call-update) | async-done | bytes 1310736 | tf_op jit(solution)/shard_map/all_gather | solution.py:35
  70.2 5.4 constant_dynamic-update-slice_fusion.3
  77.8 114.0 %gather_fusion.1 = bf16[32768,32]{1,0:T(8,128)(2,1)} fusion(bf16[27648,32]{1,0:T(8,128)(2,1)} %constant_dynamic-update-slice_fusion, s32[32768]{0:T(1024)S(1)} %broadcast_clamp_fusion), kind=kCustom, calls=%fused_computation.7 | custom fusion | bytes 4325376 | tf_op jit(solution)/shard_map/jit(_take)/gather | solution.py:27
  191.8 24.2 %convert_reduce_fusion.1 = f32[4096,32]{1,0:T(8,128)S(1)} fusion(bf16[8,4096,32]{2,1,0:T(8,128)(2,1)} %bitcast.73, pred[8,4096]{1,0:T(8,128)(4,1)S(1)} %compare_and_fusion), kind=kLoop, calls=%fused_computation.16 | loop fusion | flops 3014656 | bytes 2654208 | tf_op jit(solution)/shard_map/reduce_sum | solution.py:28
  218.1 20.1 %all-gather.11.cloned.1.call-done = bf16[128,4096]{1,0:T(8,128)(2,1)} async-done(((bf16[32,4096]{1,0:T(8,128)(2,1)}), bf16[128,4096]{1,0:T(8,128)(2,1)}) %all-gather.11.cloned.1.call-update) | async-done | bytes 1048592 | tf_op jit(solution)/shard_map/all_gather | solution.py:22
  238.2 1.5 fusion.33
  239.7 24.6 %all-gather.7.cloned.1.call-done = bf16[128,4096]{1,0:T(8,128)(2,1)} async-done(((bf16[32,4096]{1,0:T(8,128)(2,1)}), bf16[128,4096]{1,0:T(8,128)(2,1)}) %all-gather.7.cloned.1.call-update) | async-done | bytes 1048592 | tf_op jit(solution)/shard_map/all_gather | solution.py:21
  264.3 2.3 fusion.11
  267.3 2.0 gather_fusion.2
  270.3 3.2 gather_fusion.7
  273.5 3.2 gather_fusion.8
  276.7 3.2 gather_fusion.9
  280.1 2.8 collective-permute-start.3
  284.7 2.7 collective-permute-start.5
  288.8 34.4 %all-gather.15.cloned.1.call-done = bf16[20480,64]{1,0:T(8,128)(2,1)} async-done(((bf16[640,64]{1,0:T(8,128)(2,1)}), bf16[20480,64]{1,0:T(8,128)(2,1)}) %all-gather.15.cloned.1.call-update) | async-done | bytes 2621456 | tf_op jit(solution)/shard_map/all_gather | solution.py:35
  323.2 5.4 constant_dynamic-update-slice_fusion.8
  330.8 114.4 %gather_fusion.3 = bf16[32768,64]{1,0:T(8,128)(2,1)} fusion(bf16[27648,64]{1,0:T(8,128)(2,1)} %constant_dynamic-update-slice_fusion.5, s32[32768]{0:T(1024)S(1)} %broadcast_clamp_fusion), kind=kCustom, calls=%fused_computation.9 | custom fusion | bytes 8519680 | tf_op jit(solution)/shard_map/jit(_take)/gather | solution.py:27
  445.1 24.2 %convert_reduce_fusion = f32[4096,64]{1,0:T(8,128)S(1)} fusion(bf16[8,4096,64]{2,1,0:T(8,128)(2,1)} %bitcast.72, pred[8,4096]{1,0:T(8,128)(4,1)S(1)} %compare_and_fusion), kind=kLoop, calls=%fused_computation.15 | loop fusion | flops 6029312 | bytes 5275648 | tf_op jit(solution)/shard_map/reduce_sum | solution.py:28
  472.2 2.1 fusion.31
  474.4 26.7 %all-gather.17.cloned.1.call-done = bf16[256,4096]{1,0:T(8,128)(2,1)} async-done(((bf16[64,4096]{1,0:T(8,128)(2,1)}), bf16[256,4096]{1,0:T(8,128)(2,1)}) %all-gather.17.cloned.1.call-update) | async-done | bytes 2097168 | tf_op jit(solution)/shard_map/all_gather | solution.py:22
  501.1 2.4 fusion.30
  504.6 1.9 copy.83
  506.5 8.4 broadcast_in_dim.91
  514.9 180.2 %scatter_custom_fusion = f32[27648,64]{1,0:T(8,128)} fusion(s32[32768]{0:T(1024)S(1)} %bitcast.78, f32[32768,64]{1,0:T(8,128)} %bitcast.74, f32[]{:T(128)} %constant.59.clone.1), kind=kCustom, calls=%fused_computation.17 | custom fusion | flops 2097152 | bytes 7078400 | tf_op jit(solution)/shard_map/scatter-add | solution.py:102
  695.1 11.8 %copy.84 = f32[27648,64]{0,1:T(8,128)} copy(f32[27648,64]{1,0:T(8,128)} %scatter_custom_fusion) | data formatting | bytes 14155776 | tf_op jit(solution)/shard_map/scatter-add | solution.py:102
  706.9 5.7 fusion.27
  712.6 2.9 copy-done.1
  715.5 2.7 slice.62
  718.9 1.9 fusion.28
  722.9 2.6 collective-permute-start.8
  725.5 2.8 convolution_add_fusion.1
  730.7 1.9 copy.85
  735.6 66.0 %reduce-scatter.2.cloned.1.call-done = f32[640,64]{0,1:T(8,128)} async-done(((f32[20480,64]{0,1:T(8,128)}), f32[640,64]{0,1:T(8,128)}) %reduce-scatter.2.cloned.1.call-update) | async-done | bytes 163856 | tf_op jit(solution)/shard_map/reduce_scatter | solution.py:106
  801.6 1.8 copy.86
  803.4 7.2 scatter_fusion
  810.7 6.8 scatter_fusion.1
  817.5 7.2 scatter_fusion.2
  824.7 6.8 scatter_fusion.3
  831.8 2.4 fusion.23
  834.2 2.4 fusion.25
  836.5 102.1 %all-reduce.3.cloned.1.call-done = (f32[64,128]{1,0:T(8,128)}, f32[64,128]{1,0:T(8,128)}, f32[172,64]{0,1:T(8,128)}, f32[172,64]{0,1:T(8,128)}) async-done(((f32[64,128]{1,0:T(8,128)}, f32[64,128]{1,0:T(8,128)}, f32[172,64]{0,1:T(8,128)}, f32[172,64]{0,1:T(8,128)}), (f32[64,128]{1,0:T(8,128)}, f32[64,128]{1,0:T(8,128)}, f32[172,64]{0,1:T(8,128)}, f32[172,64]{0,1:T(8,128)})) %all-reduce.3.cloned.1.call-update) | async-done | bytes 153616 | tf_op jit(solution)/shard_map/psum | solution.py:121
  941.4 1.5 copy.111
  (104 shorter events, 35.3 us)
Async XLA Ops:
  7.2 494.0 %copy-start = (bf16[172,256]{1,0:T(8,128)(2,1)S(1)}, bf16[172,256]{1,0:T(8,128)(2,1)}, u32[]{:S(2)}) copy-start(bf16[172,256]{1,0:T(8,128)(2,1)} %param.21) | copy-start | bytes 264196
  7.2 7.9 copy-start.12
  7.2 63.1 %all-gather.9.cloned.1.call-start = ((), (), s32[]{:S(2)}) async-start(), calls=%async_computation.2 | async-start | bytes 5406720 | tf_op jit(solution)/shard_map/all_gather | solution.py:35
  13.4 16.7 %copy-start.6 = (s32[8,4096]{1,0:T(8,128)S(1)}, s32[8,4096]{1,0:T(8,128)}, u32[]{:S(2)}) copy-start(s32[8,4096]{1,0:T(8,128)} %param.14) | copy-start | bytes 393220
  13.7 61.9 %collective-permute-start = (bf16[1024,32]{1,0:T(8,128)(2,1)S(1)}, bf16[1024,32]{1,0:T(8,128)(2,1)S(1)}, u32[]{:S(2)}, u32[]{:S(2)}) collective-permute-start(bf16[1024,32]{1,0:T(8,128)(2,1)S(1)} %broadcast_select_fusion.5), channel_id=1, source_target_pairs={{0,4},{4,0},{8,12},{12,8},{16,20},{20,16},{24,28},{28,24},{32,36},... | collective-permute-start | bytes 196616 | tf_op jit(solution)/shard_map/ppermute | solution.py:12
  18.0 220.2 %all-gather.11.cloned.1.call-start = ((), (), s32[]{:S(2)}) async-start(), calls=%async_computation.3 | async-start | bytes 1310720 | tf_op jit(solution)/shard_map/all_gather | solution.py:22
  21.5 54.8 %collective-permute-start.1 = (bf16[1024,32]{1,0:T(8,128)(2,1)S(1)}, bf16[1024,32]{1,0:T(8,128)(2,1)S(1)}, u32[]{:S(2)}, u32[]{:S(2)}) collective-permute-start(bf16[1024,32]{1,0:T(8,128)(2,1)S(1)} %broadcast_select_fusion.4), channel_id=1, source_target_pairs={{0,8},{4,12},{8,0},{12,4},{16,24},{20,28},{24,16},{28,20},{32,40},... | collective-permute-start | bytes 196616 | tf_op jit(solution)/shard_map/ppermute | solution.py:12
  26.7 50.3 %collective-permute-start.2 = (bf16[1024,32]{1,0:T(8,128)(2,1)S(1)}, bf16[1024,32]{1,0:T(8,128)(2,1)S(1)}, u32[]{:S(2)}, u32[]{:S(2)}) collective-permute-start(bf16[1024,32]{1,0:T(8,128)(2,1)S(1)} %broadcast_select_fusion.3), channel_id=1, source_target_pairs={{0,16},{4,20},{8,24},{12,28},{16,0},{20,4},{24,8},{28,12},{32,48},... | collective-permute-start | bytes 196616 | tf_op jit(solution)/shard_map/ppermute | solution.py:12
  216.1 22.1 %copy-start.9 = (bf16[64,128]{1,0:T(8,128)(2,1)S(1)}, bf16[64,128]{1,0:T(8,128)(2,1)}, u32[]{:S(2)}) copy-start(bf16[64,128]{1,0:T(8,128)(2,1)} %param.19) | copy-start | bytes 49156
  216.1 48.2 %copy-start.10 = (bf16[64,128]{1,0:T(8,128)(2,1)S(1)}, bf16[64,128]{1,0:T(8,128)(2,1)}, u32[]{:S(2)}) copy-start(bf16[64,128]{1,0:T(8,128)(2,1)} %param.18) | copy-start | bytes 49156
  217.3 47.0 %all-gather.7.cloned.1.call-start = ((), (), s32[]{:S(2)}) async-start(), calls=%async_computation.1 | async-start | bytes 1310720 | tf_op jit(solution)/shard_map/all_gather | solution.py:21
  218.0 105.2 %all-gather.15.cloned.1.call-start = ((), (), s32[]{:S(2)}) async-start(), calls=%async_computation.5 | async-start | bytes 5406720 | tf_op jit(solution)/shard_map/all_gather | solution.py:35
  270.1 202.1 %all-gather.13.cloned.1.call-start = ((), (), s32[]{:S(2)}) async-start(), calls=%async_computation.4 | async-start | bytes 2621440 | tf_op jit(solution)/shard_map/all_gather | solution.py:21
  280.1 48.4 %collective-permute-start.3 = (bf16[1024,64]{1,0:T(8,128)(2,1)S(1)}, bf16[1024,64]{1,0:T(8,128)(2,1)S(1)}, u32[]{:S(2)}, u32[]{:S(2)}) collective-permute-start(bf16[1024,64]{1,0:T(8,128)(2,1)S(1)} %broadcast_select_fusion.2), channel_id=1, source_target_pairs={{0,4},{4,0},{8,12},{12,8},{16,20},{20,16},{24,28},{28,24},{32,36},... | collective-permute-start | bytes 393224 | tf_op jit(solution)/shard_map/ppermute | solution.py:12
  283.2 46.1 %collective-permute-start.4 = (bf16[1024,64]{1,0:T(8,128)(2,1)S(1)}, bf16[1024,64]{1,0:T(8,128)(2,1)S(1)}, u32[]{:S(2)}, u32[]{:S(2)}) collective-permute-start(bf16[1024,64]{1,0:T(8,128)(2,1)S(1)} %broadcast_select_fusion.1), channel_id=1, source_target_pairs={{0,8},{4,12},{8,0},{12,4},{16,24},{20,28},{24,16},{28,20},{32,40},... | collective-permute-start | bytes 393224 | tf_op jit(solution)/shard_map/ppermute | solution.py:12
  284.7 45.3 %collective-permute-start.5 = (bf16[1024,64]{1,0:T(8,128)(2,1)S(1)}, bf16[1024,64]{1,0:T(8,128)(2,1)S(1)}, u32[]{:S(2)}, u32[]{:S(2)}) collective-permute-start(bf16[1024,64]{1,0:T(8,128)(2,1)S(1)} %broadcast_select_fusion), channel_id=1, source_target_pairs={{0,16},{4,20},{8,24},{12,28},{16,0},{20,4},{24,8},{28,12},{32,48},... | collective-permute-start | bytes 393224 | tf_op jit(solution)/shard_map/ppermute | solution.py:12
  288.6 212.6 %all-gather.17.cloned.1.call-start = ((), (), s32[]{:S(2)}) async-start(), calls=%async_computation.6 | async-start | bytes 2621440 | tf_op jit(solution)/shard_map/all_gather | solution.py:22
  469.4 1.3 copy-start.2
  470.7 1.5 copy-start.7
  472.0 329.6 %reduce-scatter.2.cloned.1.call-start = ((), (), s32[]{:S(2)}) async-start(), calls=%async_computation.7 | async-start | bytes 5406720 | tf_op jit(solution)/shard_map/reduce_scatter | solution.py:106
  474.4 29.1 %copy-start.11 = (s32[4096]{0:T(1024)S(1)}, s32[4096]{0:T(1024)}, u32[]{:S(2)}) copy-start(s32[4096]{0:T(1024)} %param.17) | copy-start | bytes 49156
  712.6 2.9 copy-start.1
  718.1 0.7 copy-start.8
  718.1 11.4 %copy-start.4 = (bf16[64,4096]{1,0:T(8,128)(2,1)S(1)}, bf16[64,4096]{1,0:T(8,128)(2,1)}, u32[]{:S(2)}) copy-start(bf16[64,4096]{1,0:T(8,128)(2,1)} %get-tuple-element.21) | copy-start | bytes 1572868
  718.1 220.5 %all-reduce.3.cloned.1.call-start = ((), (), s32[]{:S(2)}) async-start(), calls=%async_computation.8 | async-start | bytes 393216 | tf_op jit(solution)/shard_map/psum | solution.py:121
  718.8 9.4 copy-start.3
  720.8 11.9 %collective-permute-start.6 = (bf16[1024,64]{0,1:T(8,128)(2,1)S(1)}, bf16[1024,64]{0,1:T(8,128)(2,1)}, u32[]{:S(2)}, u32[]{:S(2)}) collective-permute-start(bf16[1024,64]{0,1:T(8,128)(2,1)S(1)} %get-tuple-element.14), channel_id=1, source_target_pairs={{0,4},{4,0},{8,12},{12,8},{16,20},{20,16},{24,28},{28,24},{32,36},... | collective-permute-start | bytes 393224 | tf_op jit(solution)/shard_map/ppermute | solution.py:12
  721.6 12.1 %collective-permute-start.7 = (bf16[1024,64]{0,1:T(8,128)(2,1)}, bf16[1024,64]{0,1:T(8,128)(2,1)S(1)}, u32[]{:S(2)}, u32[]{:S(2)}) collective-permute-start(bf16[1024,64]{0,1:T(8,128)(2,1)} %get-tuple-element.13), channel_id=1, source_target_pairs={{0,8},{4,12},{8,0},{12,4},{16,24},{20,28},{24,16},{28,20},{32,40},... | collective-permute-start | bytes 393224 | tf_op jit(solution)/shard_map/ppermute | solution.py:12
  722.9 11.7 %collective-permute-start.8 = (bf16[1024,64]{0,1:T(8,128)(2,1)}, bf16[1024,64]{0,1:T(8,128)(2,1)S(1)}, u32[]{:S(2)}, u32[]{:S(2)}) collective-permute-start(bf16[1024,64]{0,1:T(8,128)(2,1)} %get-tuple-element.12), channel_id=1, source_target_pairs={{0,16},{4,20},{8,24},{12,28},{16,0},{20,4},{24,8},{28,12},{32,48},... | collective-permute-start | bytes 393224 | tf_op jit(solution)/shard_map/ppermute | solution.py:12
  817.5 7.2 copy-start.5
Sparse Core Ops, SparseCore 0:
  18.1 52.0 all-gather.8
  217.4 20.7 all-gather.10
  239.8 24.4 all-gather.6
  270.2 52.9 all-gather.14
  324.7 29.2 all-gather.12
  472.1 28.9 all-gather.16
  718.3 83.3 reduce-scatter.1
  836.7 101.9 all-reduce.2
where the time goes:
time: 953 us; the launch traced here: 951 us
  local copies, waits for them, and re-layouts  318 us (33%)
  waiting for transfers between devices  314 us (33%)
  other arithmetic  267 us (28%)
  starting transfers between devices  18.9 us (2%)
  matrix products  18.8 us (2%)
  between operations  14.6 us (2%)
    gather x2, local copies, waits for them, and re-layouts, average(): picked = jnp.take(table_rows, neighbours, axis=0)  228 us
    scatter-add x1, other arithmetic, body(): jnp.zeros((span, width), jnp.float32).at[neighbours.reshape(-1)]  180 us
    psum x1, waiting for transfers between devices, body(): lax.psum((grad_inner_self, grad_inner_neighbour, grad_outer_self, grad_ou...  102 us
    all_gather x2, waiting for transfers between devices, source_table(): hub_all = lax.all_gather(hub_local, 'dom', axis=0, tiled=True)  73.3 us
    reduce_scatter x1, waiting for transfers between devices, body(): lax.psum_scatter(spread[rows:rows + hub_count], 'dom', scatter_dimension=...  66 us
    reduce_sum x2, other arithmetic, average(): summed = jnp.sum(picked.astype(jnp.float32), axis=0) / neighbours.shape[0]  48.4 us
    all_gather x2, waiting for transfers between devices, widen(): lax.all_gather(second_rows, 'feat', axis=0, tiled=True)  46.8 us
    unnamed x41, local copies, waits for them, and re-layouts  27.8 us
  transfers between devices with their start and end apart: 17, of which 7 were waited for; matrix products, arithmetic and copies ran while one was open for 20% of the time, Pallas kernels for 0%

commit v1 on v0

--- a/solution.py
+++ b/solution.py
@@ -3,7 +3,83 @@
 from jax import lax
 from jax.sharding import PartitionSpec as P
 
+from jax.experimental import pallas as pl
+from jax.experimental.pallas import tpu as pltpu
+
 loss_scale = 4096.0
+
+
+def gather_mean(table, neighbours, block=512):
+    size, width = table.shape
+    degree, nodes = neighbours.shape
+
+    def kernel(nb_ref, tab_ref, out_ref):
+        base = pl.program_id(0) * block
+
+        def group(g, carry):
+            picked = []
+            for r in range(8):
+                n = base + g * 8 + r
+                acc = tab_ref[pl.ds(nb_ref[0, n], 1), :]
+                for k in range(1, degree):
+                    acc = acc + tab_ref[pl.ds(nb_ref[k, n], 1), :]
+                picked.append(acc)
+            start = pl.multiple_of(g * 8, 8)
+            out_ref[pl.ds(start, 8), :] = jnp.concatenate(picked, axis=0) / degree
+            return carry
+
+        lax.fori_loop(0, block // 8, group, 0, unroll=2)
+
+    return pl.pallas_call(
+        kernel,
+        grid_spec=pltpu.PrefetchScalarGridSpec(
+            num_scalar_prefetch=1,
+            grid=(nodes // block,),
+            in_specs=[pl.BlockSpec((size, width), lambda j, nb: (0, 0))],
+            out_specs=pl.BlockSpec((block, width), lambda j, nb: (j, 0)),
+        ),
+        out_shape=jax.ShapeDtypeStruct((nodes, width), jnp.float32),
+    )(neighbours, table)
+
+
+def scatter_mean(rows, neighbours, size, block=512):
+    nodes, width = rows.shape
+    degree = neighbours.shape[0]
+
+    def kernel(nb_ref, rows_ref, out_ref):
+        j = pl.program_id(0)
+
+        @pl.when(j == 0)
+        def _():
+            out_ref[...] = jnp.zeros_like(out_ref)
+
+        base = j * block
+
+        def step(i, carry):
+            n = base + i
+            x = rows_ref[pl.ds(i, 1), :]
+            for k in range(degree):
+                s = nb_ref[k, n]
+                out_ref[pl.ds(s, 1), :] = out_ref[pl.ds(s, 1), :] + x
+            return carry
+
+        lax.fori_loop(0, block, step, 0, unroll=8)
+
+        @pl.when(j == pl.num_programs(0) - 1)
+        def _():
+            out_ref[...] = out_ref[...] * (1.0 / degree)
+
+    return pl.pallas_call(
+        kernel,
+        grid_spec=pltpu.PrefetchScalarGridSpec(
+            num_scalar_prefetch=1,
+            grid=(nodes // block,),
+            in_specs=[pl.BlockSpec((block, width), lambda j, nb: (j, 0))],
+            out_specs=pl.BlockSpec((size, width), lambda j, nb: (0, 0)),
+        ),
+        out_shape=jax.ShapeDtypeStruct((size, width), jnp.float32),
+        compiler_params=pltpu.CompilerParams(dimension_semantics=("arbitrary",)),
+    )(neighbours, rows)
 
 
 def partner(value, axis, stride):
@@ -24,8 +100,7 @@
 
 
 def average(table_rows, neighbours):
-    picked = jnp.take(table_rows, neighbours, axis=0)
-    summed = jnp.sum(picked.astype(jnp.float32), axis=0) / neighbours.shape[0]
+    summed = gather_mean(table_rows.astype(jnp.float32), neighbours)
     return summed.T.astype(jnp.bfloat16)
 
 
@@ -89,6 +164,7 @@
     logit_grad = class_gradient(logits, labels, nodes_all)
     grad_outer_self = contract(logit_grad, hidden)
     grad_outer_neighbour = contract(logit_grad, mean_two)
+    grad_outer_self, grad_outer_neighbour = lax.psum((grad_outer_self, grad_outer_neighbour), "dom")
     direct = transpose_times(self_cols, logit_grad)
     back_mean = transpose_times(neigh_cols, logit_grad).astype(jnp.bfloat16)
     degree = neighbours.shape[0]
@@ -96,12 +172,7 @@
     band = send_rows.shape[1]
     span = rows + hub_count + send_rows.shape[0] * band
     back_rows = back_mean.T.astype(jnp.float32)
-    updates = jnp.broadcast_to(back_rows[None, :, :], (degree, rows, width)).reshape(
-        degree * rows, width
-    )
-    spread = jnp.zeros((span, width), jnp.float32).at[neighbours.reshape(-1)].add(updates) * (
-        1.0 / degree
-    )
+    spread = scatter_mean(back_rows, neighbours, span)
     grad_rows = direct.T + spread[:rows]
     hub_back = lax.psum_scatter(
         spread[rows : rows + hub_count], "dom", scatter_dimension=0, tiled=True
@@ -118,10 +189,8 @@
     grad_pre = jnp.where(hidden > 0, grad_hidden, 0.0).astype(jnp.bfloat16)
     grad_inner_self = contract(grad_pre, full_input)
     grad_inner_neighbour = contract(grad_pre, full_mean)
-    summed = lax.psum(
-        (grad_inner_self, grad_inner_neighbour, grad_outer_self, grad_outer_neighbour), "dom"
-    )
-    return (summed[0], summed[1], summed[2], summed[3])
+    summed = lax.psum((grad_inner_self, grad_inner_neighbour), "dom")
+    return (summed[0], summed[1], grad_outer_self, grad_outer_neighbour)
 
 
 def solution(mesh):

time: 953 us -> 764 us (0.80)
  Pallas kernels: 0 us -> 262 us
  local copies, waits for them, and re-layouts: 318 us -> 61.5 us
  other arithmetic: 267 us -> 64.7 us
  waiting for transfers between devices: 314 us -> 324 us
    pallas_call x0 -> x3, Pallas kernels: none -> 262 us  [the longest x1 145 us: scatter_mean(): pl.pallas_call(kernel, grid_spec=pltpu.PrefetchScalarGridSpec(num_scalar_...]
    gather x2 -> x0, local copies, waits for them, and re-layouts: 228 us -> none  [average(): picked = jnp.take(table_rows, neighbours, axis=0)]
    scatter-add x1 -> x0, other arithmetic: 180 us -> none  [body(): jnp.zeros((span, width), jnp.float32).at[neighbours.reshape(-1)]]
    reduce_sum x2 -> x0, other arithmetic: 48.4 us -> none  [average(): summed = jnp.sum(picked.astype(jnp.float32), axis=0) / neighbours.shape[0]]
    convert_element_type x1 -> x3, other arithmetic: 0.1 us -> 18.6 us  [the longest x2 17.2 us: average(): summed = gather_mean(table_rows.astype(jnp.float32), neighbours)]
    reduce_scatter x1, waiting for transfers between devices: 66 us -> 78.9 us  [body(): lax.psum_scatter(spread[rows:rows + hub_count], 'dom', scatter_dimension=...]
    scatter-add x2 -> x0, local copies, waits for them, and re-layouts: 12.1 us -> none  [the longest x1 11.8 us: body(): jnp.zeros((span, width), jnp.float32).at[neighbours.reshape(-1)]]
    unnamed x41 -> x40, local copies, waits for them, and re-layouts: 27.8 us -> 22.4 us
  transfers between devices with their start and end apart: 17 -> 17, of which waited for: 7 -> 7; matrix products, arithmetic and copies ran while one was open for 20% -> 11% of each run, Pallas kernels for 0% -> 8%
where the time goes in v1:
time: 764 us; the launch traced here: 763 us
  waiting for transfers between devices  324 us (42%)
  Pallas kernels  262 us (34%)
  other arithmetic  64.7 us (8%)
  local copies, waits for them, and re-layouts  61.5 us (8%)
  starting transfers between devices  18.7 us (2%)
  matrix products  17.7 us (2%)
  between operations  14.5 us (2%)
    pallas_call x1, Pallas kernels, scatter_mean(): pl.pallas_call(kernel, grid_spec=pltpu.PrefetchScalarGridSpec(num_scalar_...  145 us
    pallas_call x2, Pallas kernels, gather_mean(): pl.pallas_call(kernel, grid_spec=pltpu.PrefetchScalarGridSpec(num_scalar_...  117 us
    psum x1, waiting for transfers between devices, body(): summed = lax.psum((grad_inner_self, grad_inner_neighbour), 'dom')  102 us
    reduce_scatter x1, waiting for transfers between devices, body(): lax.psum_scatter(spread[rows:rows + hub_count], 'dom', scatter_dimension=...  78.9 us
    all_gather x2, waiting for transfers between devices, source_table(): hub_all = lax.all_gather(hub_local, 'dom', axis=0, tiled=True)  70 us
    all_gather x2, waiting for transfers between devices, widen(): lax.all_gather(second_rows, 'feat', axis=0, tiled=True)  47.2 us
    all_gather x2, waiting for transfers between devices, widen(): lax.all_gather(first_rows, 'feat', axis=0, tiled=True)  24.5 us
    unnamed x40, local copies, waits for them, and re-layouts  22.4 us
  transfers between devices with their start and end apart: 17, of which 7 were waited for; matrix products, arithmetic and copies ran while one was open for 11% of the time, Pallas kernels for 8%

profile of v1, /device:TPU:1, one launch (start us, length us, event | category | flops | bytes accessed | tf_op | source)
XLA Modules:
  0.0 762.9 jit_solution(16955448225057995119)
XLA Ops:
  9.5 1.4 copy.53
  10.9 2.0 gather_fusion
  13.8 3.2 gather_fusion.2
  17.2 1.5 collective-permute-start
  18.7 3.2 gather_fusion.3
  22.1 1.8 collective-permute-start.1
  24.0 3.2 gather_fusion.4
  27.4 3.4 collective-permute-start.2
  31.8 35.4 %all-gather.9.cloned.1.call-done = bf16[20480,32]{1,0:T(8,128)(2,1)} async-done(((bf16[640,32]{1,0:T(8,128)(2,1)}), bf16[20480,32]{1,0:T(8,128)(2,1)}) %all-gather.9.cloned.1.call-update) | async-done | bytes 1310736 | tf_op jit(solution)/shard_map/all_gather | solution.py:110
  67.2 5.3 constant_dynamic-update-slice_fusion.3
  74.7 8.6 %convert_element_type.52.tab_ref = f32[27648,32]{1,0:T(8,128)} convert(bf16[27648,32]{1,0:T(8,128)(2,1)} %constant_dynamic-update-slice_fusion) | non-fusion elementwise | flops 884736 | bytes 5308416 | tf_op jit(solution)/shard_map/convert_element_type | solution.py:103
  83.3 58.5 %shard_map.120 = f32[4096,32]{1,0:T(8,128)} custom-call(s32[8,4096]{1,0:T(8,128)} %nb_ref.5, f32[27648,32]{1,0:T(8,128)} %convert_element_type.52.tab_ref), custom_call_target="tpu_custom_call" | custom-call | tf_op jit(solution)/shard_map/pallas_call | solution.py:33
  141.7 1.7 convert_bitcast_fusion
  145.3 20.1 %all-gather.11.cloned.1.call-done = bf16[128,4096]{1,0:T(8,128)(2,1)} async-done(((bf16[32,4096]{1,0:T(8,128)(2,1)}), bf16[128,4096]{1,0:T(8,128)(2,1)}) %all-gather.11.cloned.1.call-update) | async-done | bytes 1048592 | tf_op jit(solution)/shard_map/all_gather | solution.py:98
  165.4 1.7 fusion.31
  167.1 24.4 %all-gather.7.cloned.1.call-done = bf16[128,4096]{1,0:T(8,128)(2,1)} async-done(((bf16[32,4096]{1,0:T(8,128)(2,1)}), bf16[128,4096]{1,0:T(8,128)(2,1)}) %all-gather.7.cloned.1.call-update) | async-done | bytes 1048592 | tf_op jit(solution)/shard_map/all_gather | solution.py:97
  191.6 1.8 fusion.7
  193.4 3.3 constant_dynamic-update-slice_fusion.9
  196.7 2.0 gather_fusion.1
  199.5 3.2 gather_fusion.5
  202.8 3.2 gather_fusion.6
  206.0 3.2 gather_fusion.7
  209.4 2.8 collective-permute-start.3
  214.0 2.7 collective-permute-start.5
  217.9 34.6 %all-gather.15.cloned.1.call-done = bf16[20480,64]{1,0:T(8,128)(2,1)} async-done(((bf16[640,64]{1,0:T(8,128)(2,1)}), bf16[20480,64]{1,0:T(8,128)(2,1)}) %all-gather.15.cloned.1.call-update) | async-done | bytes 2621456 | tf_op jit(solution)/shard_map/all_gather | solution.py:110
  252.5 5.3 constant_dynamic-update-slice_fusion.8
  260.0 8.6 %convert_element_type.57.tab_ref = f32[27648,64]{1,0:T(8,128)} convert(bf16[27648,64]{1,0:T(8,128)(2,1)} %constant_dynamic-update-slice_fusion.5) | non-fusion elementwise | flops 1769472 | bytes 10616832 | tf_op jit(solution)/shard_map/convert_element_type | solution.py:103
  268.7 58.6 %shard_map.121 = f32[4096,64]{1,0:T(8,128)} custom-call(s32[8,4096]{1,0:T(8,128)} %nb_ref.5, f32[27648,64]{1,0:T(8,128)} %convert_element_type.57.tab_ref), custom_call_target="tpu_custom_call" | custom-call | tf_op jit(solution)/shard_map/pallas_call | solution.py:33
  327.2 1.7 convert_bitcast_fusion.1
  330.4 2.1 fusion.32
  332.6 27.1 %all-gather.17.cloned.1.call-done = bf16[256,4096]{1,0:T(8,128)(2,1)} async-done(((bf16[64,4096]{1,0:T(8,128)(2,1)}), bf16[256,4096]{1,0:T(8,128)(2,1)}) %all-gather.17.cloned.1.call-update) | async-done | bytes 2097168 | tf_op jit(solution)/shard_map/all_gather | solution.py:98
  359.7 2.3 fusion.30
  363.6 1.4 convert_element_type.63.rows_ref
  365.1 145.0 %shard_map.122 = f32[27648,64]{1,0:T(8,128)} custom-call(s32[8,4096]{1,0:T(8,128)} %nb_ref.5, f32[4096,64]{1,0:T(8,128)} %convert_element_type.63.rows_ref), custom_call_target="tpu_custom_call" | custom-call | tf_op jit(solution)/shard_map/pallas_call | solution.py:72
  510.1 8.9 %slice.58 = f32[20480,64]{1,0:T(8,128)} slice(f32[27648,64]{1,0:T(8,128)} %shard_map.122), slice={[4096:24576], [0:64]} | slice | bytes 10485760 | tf_op jit(solution)/shard_map/slice | solution.py:178
  519.8 5.8 convert.5
  528.6 2.6 collective-permute-start.8
  532.4 3.2 convolution_add_fusion.1
  536.9 78.9 %reduce-scatter.2.cloned.1.call-done = f32[640,64]{1,0:T(8,128)} async-done(((f32[20480,64]{1,0:T(8,128)}), f32[640,64]{1,0:T(8,128)}) %reduce-scatter.2.cloned.1.call-update) | async-done | bytes 163856 | tf_op jit(solution)/shard_map/reduce_scatter | solution.py:177
  615.9 7.2 scatter_fusion
  623.1 7.4 scatter_custom_fusion.1
  630.5 7.2 scatter_custom_fusion.2
  637.7 6.8 scatter_custom_fusion.3
  644.6 2.4 fusion.23
  648.2 102.2 %all-reduce.3.cloned.1.call-done = (f32[64,128]{1,0:T(8,128)}, f32[64,128]{1,0:T(8,128)}, f32[172,64]{0,1:T(8,128)}, f32[172,64]{0,1:T(8,128)}) async-done(((f32[64,128]{1,0:T(8,128)}, f32[64,128]{1,0:T(8,128)}, f32[172,64]{0,1:T(8,128)}, f32[172,64]{0,1:T(8,128)}), (f32[64,128]{1,0:T(8,128)}, f32[64,128]{1,0:T(8,128)}, f32[172,64]{0,1:T(8,128)}, f32[172,64]{0,1:T(8,128)})) %all-reduce.3.cloned.1.call-update) | async-done | bytes 153616 | tf_op jit(solution)/shard_map/psum | solution.py:192
  750.4 1.4 copy.82
  753.1 1.5 copy.84
  754.6 1.5 copy.85
  (92 shorter events, 27.0 us)
Async XLA Ops:
  7.2 352.5 %copy-start = (bf16[172,256]{1,0:T(8,128)(2,1)S(1)}, bf16[172,256]{1,0:T(8,128)(2,1)}, u32[]{:S(2)}) copy-start(bf16[172,256]{1,0:T(8,128)(2,1)} %param.21) | copy-start | bytes 264196
  7.2 60.1 %all-gather.9.cloned.1.call-start = ((), (), s32[]{:S(2)}) async-start(), calls=%async_computation.2 | async-start | bytes 5406720 | tf_op jit(solution)/shard_map/all_gather | solution.py:110
  13.8 151.7 %all-gather.11.cloned.1.call-start = ((), (), s32[]{:S(2)}) async-start(), calls=%async_computation.3 | async-start | bytes 1310720 | tf_op jit(solution)/shard_map/all_gather | solution.py:98
  17.2 55.3 %collective-permute-start = (bf16[1024,32]{1,0:T(8,128)(2,1)S(1)}, bf16[1024,32]{1,0:T(8,128)(2,1)S(1)}, u32[]{:S(2)}, u32[]{:S(2)}) collective-permute-start(bf16[1024,32]{1,0:T(8,128)(2,1)S(1)} %broadcast_select_fusion.5), channel_id=1, source_target_pairs={{0,4},{4,0},{8,12},{12,8},{16,20},{20,16},{24,28},{28,24},{32,36},... | collective-permute-start | bytes 196616 | tf_op jit(solution)/shard_map/ppermute | solution.py:88
  22.1 51.1 %collective-permute-start.1 = (bf16[1024,32]{1,0:T(8,128)(2,1)S(1)}, bf16[1024,32]{1,0:T(8,128)(2,1)S(1)}, u32[]{:S(2)}, u32[]{:S(2)}) collective-permute-start(bf16[1024,32]{1,0:T(8,128)(2,1)S(1)} %broadcast_select_fusion.4), channel_id=1, source_target_pairs={{0,8},{4,12},{8,0},{12,4},{16,24},{20,28},{24,16},{28,20},{32,40},... | collective-permute-start | bytes 196616 | tf_op jit(solution)/shard_map/ppermute | solution.py:88
  27.4 46.6 %collective-permute-start.2 = (bf16[1024,32]{1,0:T(8,128)(2,1)S(1)}, bf16[1024,32]{1,0:T(8,128)(2,1)S(1)}, u32[]{:S(2)}, u32[]{:S(2)}) collective-permute-start(bf16[1024,32]{1,0:T(8,128)(2,1)S(1)} %broadcast_select_fusion.3), channel_id=1, source_target_pairs={{0,16},{4,20},{8,24},{12,28},{16,0},{20,4},{24,8},{28,12},{32,48},... | collective-permute-start | bytes 196616 | tf_op jit(solution)/shard_map/ppermute | solution.py:88
  141.7 23.7 %copy-start.11 = (bf16[64,128]{1,0:T(8,128)(2,1)S(1)}, bf16[64,128]{1,0:T(8,128)(2,1)}, u32[]{:S(2)}) copy-start(bf16[64,128]{1,0:T(8,128)(2,1)} %param.19) | copy-start | bytes 49156
  144.5 47.1 %copy-start.12 = (bf16[64,128]{1,0:T(8,128)(2,1)S(1)}, bf16[64,128]{1,0:T(8,128)(2,1)}, u32[]{:S(2)}) copy-start(bf16[64,128]{1,0:T(8,128)(2,1)} %param.18) | copy-start | bytes 49156
  144.5 47.0 %all-gather.7.cloned.1.call-start = ((), (), s32[]{:S(2)}) async-start(), calls=%async_computation.1 | async-start | bytes 1310720 | tf_op jit(solution)/shard_map/all_gather | solution.py:97
  145.3 107.3 %all-gather.15.cloned.1.call-start = ((), (), s32[]{:S(2)}) async-start(), calls=%async_computation.5 | async-start | bytes 5406720 | tf_op jit(solution)/shard_map/all_gather | solution.py:110
  167.1 26.3 %copy-start.5 = (f32[4096,64]{1,0:T(8,128)}, f32[4096,64]{1,0:T(8,128)S(1)}, u32[]{:S(2)}) copy-start(f32[4096,64]{1,0:T(8,128)S(1)} %fusion.31) | copy-start | bytes 3145732
  193.4 23.3 %copy-start.3 = (bf16[64,4096]{0,1:T(8,128)(2,1)}, bf16[64,4096]{0,1:T(8,128)(2,1)S(1)}, u32[]{:S(2)}) copy-start(bf16[64,4096]{0,1:T(8,128)(2,1)S(1)} %get-tuple-element.21) | copy-start | bytes 1572868
  199.5 130.9 %all-gather.13.cloned.1.call-start = ((), (), s32[]{:S(2)}) async-start(), calls=%async_computation.4 | async-start | bytes 2621440 | tf_op jit(solution)/shard_map/all_gather | solution.py:97
  209.4 48.4 %collective-permute-start.3 = (bf16[1024,64]{1,0:T(8,128)(2,1)S(1)}, bf16[1024,64]{1,0:T(8,128)(2,1)S(1)}, u32[]{:S(2)}, u32[]{:S(2)}) collective-permute-start(bf16[1024,64]{1,0:T(8,128)(2,1)S(1)} %broadcast_select_fusion.2), channel_id=1, source_target_pairs={{0,4},{4,0},{8,12},{12,8},{16,20},{20,16},{24,28},{28,24},{32,36},... | collective-permute-start | bytes 393224 | tf_op jit(solution)/shard_map/ppermute | solution.py:88
  212.4 46.1 %collective-permute-start.4 = (bf16[1024,64]{1,0:T(8,128)(2,1)S(1)}, bf16[1024,64]{1,0:T(8,128)(2,1)S(1)}, u32[]{:S(2)}, u32[]{:S(2)}) collective-permute-start(bf16[1024,64]{1,0:T(8,128)(2,1)S(1)} %broadcast_select_fusion.1), channel_id=1, source_target_pairs={{0,8},{4,12},{8,0},{12,4},{16,24},{20,28},{24,16},{28,20},{32,40},... | collective-permute-start | bytes 393224 | tf_op jit(solution)/shard_map/ppermute | solution.py:88
  214.0 45.3 %collective-permute-start.5 = (bf16[1024,64]{1,0:T(8,128)(2,1)S(1)}, bf16[1024,64]{1,0:T(8,128)(2,1)S(1)}, u32[]{:S(2)}, u32[]{:S(2)}) collective-permute-start(bf16[1024,64]{1,0:T(8,128)(2,1)S(1)} %broadcast_select_fusion), channel_id=1, source_target_pairs={{0,16},{4,20},{8,24},{12,28},{16,0},{20,4},{24,8},{28,12},{32,48},... | collective-permute-start | bytes 393224 | tf_op jit(solution)/shard_map/ppermute | solution.py:88
  217.9 141.8 %all-gather.17.cloned.1.call-start = ((), (), s32[]{:S(2)}) async-start(), calls=%async_computation.6 | async-start | bytes 2621440 | tf_op jit(solution)/shard_map/all_gather | solution.py:98
  327.2 3.2 copy-start.8
  330.2 285.7 %reduce-scatter.2.cloned.1.call-start = ((), (), s32[]{:S(2)}) async-start(), calls=%async_computation.7 | async-start | bytes 10813440 | tf_op jit(solution)/shard_map/reduce_scatter | solution.py:177
  332.6 29.5 %copy-start.13 = (s32[4096]{0:T(1024)S(1)}, s32[4096]{0:T(1024)}, u32[]{:S(2)}) copy-start(s32[4096]{0:T(1024)} %param.17) | copy-start | bytes 49156
  362.6 168.5 %copy-start.1 = (bf16[172,4096]{1,0:T(8,128)(2,1)}, bf16[172,4096]{1,0:T(8,128)(2,1)S(1)}, u32[]{:S(2)}) copy-start(bf16[172,4096]{1,0:T(8,128)(2,1)S(1)} %fusion.2) | copy-start | bytes 4227076
  519.0 0.7 copy-start.10
  519.0 231.3 %all-reduce.3.cloned.1.call-start = ((), (), s32[]{:S(2)}) async-start(), calls=%async_computation.8 | async-start | bytes 393216 | tf_op jit(solution)/shard_map/psum | solution.py:192
  519.8 11.4 %copy-start.6 = (f32[4096,64]{1,0:T(8,128)S(1)}, f32[4096,64]{1,0:T(8,128)}, u32[]{:S(2)}) copy-start(f32[4096,64]{1,0:T(8,128)} %shard_map.121) | copy-start | bytes 3145732
  526.5 6.0 copy-start.9
  526.5 96.6 %collective-permute-start.6 = (bf16[1024,64]{1,0:T(8,128)(2,1)}, bf16[1024,64]{1,0:T(8,128)(2,1)}, u32[]{:S(2)}, u32[]{:S(2)}) collective-permute-start(bf16[1024,64]{1,0:T(8,128)(2,1)} %get-tuple-element.14), channel_id=1, source_target_pairs={{0,4},{4,0},{8,12},{12,8},{16,20},{20,16},{24,28},{28,24},{32,36},... | collective-permute-start | bytes 393224 | tf_op jit(solution)/shard_map/ppermute | solution.py:88
  527.3 103.2 %collective-permute-start.7 = (bf16[1024,64]{1,0:T(8,128)(2,1)}, bf16[1024,64]{1,0:T(8,128)(2,1)}, u32[]{:S(2)}, u32[]{:S(2)}) collective-permute-start(bf16[1024,64]{1,0:T(8,128)(2,1)} %get-tuple-element.13), channel_id=1, source_target_pairs={{0,8},{4,12},{8,0},{12,4},{16,24},{20,28},{24,16},{28,20},{32,40},... | collective-permute-start | bytes 393224 | tf_op jit(solution)/shard_map/ppermute | solution.py:88
  528.6 109.1 %collective-permute-start.8 = (bf16[1024,64]{1,0:T(8,128)(2,1)}, bf16[1024,64]{1,0:T(8,128)(2,1)S(1)}, u32[]{:S(2)}, u32[]{:S(2)}) collective-permute-start(bf16[1024,64]{1,0:T(8,128)(2,1)} %get-tuple-element.12), channel_id=1, source_target_pairs={{0,16},{4,20},{8,24},{12,28},{16,0},{20,4},{24,8},{28,12},{32,48},... | collective-permute-start | bytes 393224 | tf_op jit(solution)/shard_map/ppermute | solution.py:88
  532.4 3.2 copy-start.2
  532.4 3.2 copy-start.4
  644.6 2.4 copy-start.7
Sparse Core Ops, SparseCore 0:
  13.9 53.3 all-gather.8
  144.7 20.7 all-gather.10
  167.1 24.4 all-gather.6
  199.6 52.8 all-gather.14
  254.0 29.2 all-gather.12
  330.3 29.3 all-gather.16
  519.2 96.6 reduce-scatter.1
  648.3 102.0 all-reduce.2

commit v2 on v1

--- a/solution.py
+++ b/solution.py
@@ -42,44 +42,52 @@
     )(neighbours, table)
 
 
-def scatter_mean(rows, neighbours, size, block=512):
+def scatter_mean(rows, neighbours, size):
     nodes, width = rows.shape
     degree = neighbours.shape[0]
-
-    def kernel(nb_ref, rows_ref, out_ref):
-        j = pl.program_id(0)
-
-        @pl.when(j == 0)
-        def _():
-            out_ref[...] = jnp.zeros_like(out_ref)
-
-        base = j * block
-
-        def step(i, carry):
-            n = base + i
-            x = rows_ref[pl.ds(i, 1), :]
-            for k in range(degree):
+    half = degree // 2
+
+    def kernel(nb_ref, rows_ref, first_ref, second_ref):
+        first_ref[...] = jnp.zeros_like(first_ref)
+        second_ref[...] = jnp.zeros_like(second_ref)
+
+        def step(n, carry):
+            x = rows_ref[pl.ds(n, 1), :]
+            for k in range(half):
                 s = nb_ref[k, n]
-                out_ref[pl.ds(s, 1), :] = out_ref[pl.ds(s, 1), :] + x
+                t = nb_ref[k + half, n]
+                first_ref[pl.ds(s, 1), :] = first_ref[pl.ds(s, 1), :] + x
+                second_ref[pl.ds(t, 1), :] = second_ref[pl.ds(t, 1), :] + x
             return carry
 
-        lax.fori_loop(0, block, step, 0, unroll=8)
-
-        @pl.when(j == pl.num_programs(0) - 1)
-        def _():
-            out_ref[...] = out_ref[...] * (1.0 / degree)
-
-    return pl.pallas_call(
+        lax.fori_loop(0, nodes, step, 0, unroll=4)
+
+    first, second = pl.pallas_call(
         kernel,
-        grid_spec=pltpu.PrefetchScalarGridSpec(
-            num_scalar_prefetch=1,
-            grid=(nodes // block,),
-            in_specs=[pl.BlockSpec((block, width), lambda j, nb: (j, 0))],
-            out_specs=pl.BlockSpec((size, width), lambda j, nb: (0, 0)),
-        ),
-        out_shape=jax.ShapeDtypeStruct((size, width), jnp.float32),
-        compiler_params=pltpu.CompilerParams(dimension_semantics=("arbitrary",)),
+        in_specs=[
+            pl.BlockSpec(memory_space=pltpu.SMEM),
+            pl.BlockSpec(memory_space=pltpu.VMEM),
+        ],
+        out_specs=(
+            pl.BlockSpec(memory_space=pltpu.VMEM),
+            pl.BlockSpec(memory_space=pltpu.VMEM),
+        ),
+        out_shape=(
+            jax.ShapeDtypeStruct((size, width), jnp.float32),
+            jax.ShapeDtypeStruct((size, width), jnp.float32),
+        ),
     )(neighbours, rows)
+    return (first + second) * (1.0 / degree)
+
+
+def tree_sum(value, axis):
+    count = lax.axis_size(axis)
+    stride = 1
+    while stride < count:
+        pairs = [(source, source ^ stride) for source in range(count)]
+        value = value + lax.ppermute(value, axis, pairs)
+        stride *= 2
+    return value
 
 
 def partner(value, axis, stride):
@@ -164,7 +172,7 @@
     logit_grad = class_gradient(logits, labels, nodes_all)
     grad_outer_self = contract(logit_grad, hidden)
     grad_outer_neighbour = contract(logit_grad, mean_two)
-    grad_outer_self, grad_outer_neighbour = lax.psum((grad_outer_self, grad_outer_neighbour), "dom")
+    outer_both = tree_sum(jnp.concatenate([grad_outer_self, grad_outer_neighbour], axis=0), "dom")
     direct = transpose_times(self_cols, logit_grad)
     back_mean = transpose_times(neigh_cols, logit_grad).astype(jnp.bfloat16)
     degree = neighbours.shape[0]
@@ -189,8 +197,9 @@
     grad_pre = jnp.where(hidden > 0, grad_hidden, 0.0).astype(jnp.bfloat16)
     grad_inner_self = contract(grad_pre, full_input)
     grad_inner_neighbour = contract(grad_pre, full_mean)
-    summed = lax.psum((grad_inner_self, grad_inner_neighbour), "dom")
-    return (summed[0], summed[1], grad_outer_self, grad_outer_neighbour)
+    inner_both = tree_sum(jnp.concatenate([grad_inner_self, grad_inner_neighbour], axis=0), "dom")
+    classes = outer_self.shape[0]
+    return (inner_both[:width], inner_both[width:], outer_both[:classes], outer_both[classes:])
 
 
 def solution(mesh):

time: 764 us -> 640 us (0.84)
  waiting for transfers between devices: 324 us -> 235 us
  Pallas kernels: 262 us -> 207 us
  starting transfers between devices: 18.7 us -> 32.1 us
  other arithmetic: 64.7 us -> 72.4 us
    psum x1 -> x0, waiting for transfers between devices: 102 us -> none  [body(): summed = lax.psum((grad_inner_self, grad_inner_neighbour), 'dom')]
    pallas_call x1, Pallas kernels: 145 us -> 89.9 us  [scatter_mean(): pl.pallas_call(kernel, in_specs=[pl.BlockSpec(memory_space=pltpu.SMEM), p...]
    ppermute x0 -> x10, starting transfers between devices: none -> 14.3 us  [tree_sum(): value = value + lax.ppermute(value, axis, pairs)]
    ppermute x0 -> x10, waiting for transfers between devices: none -> 8.65 us  [tree_sum(): value = value + lax.ppermute(value, axis, pairs)]
    unnamed x40 -> x36, local copies, waits for them, and re-layouts: 22.4 us -> 22.8 us
  transfers between devices with their start and end apart: 17 -> 26, of which waited for: 7 -> 12; matrix products, arithmetic and copies ran while one was open for 11% -> 14% of each run, Pallas kernels for 8% -> 9%
where the time goes in v2:
time: 640 us; the launch traced here: 636 us
  waiting for transfers between devices  235 us (37%)
  Pallas kernels  207 us (32%)
  other arithmetic  72.4 us (11%)
  local copies, waits for them, and re-layouts  59.7 us (9%)
  starting transfers between devices  32.1 us (5%)
  matrix products  14.8 us (2%)
  between operations  14.6 us (2%)
    pallas_call x2, Pallas kernels, gather_mean(): pl.pallas_call(kernel, grid_spec=pltpu.PrefetchScalarGridSpec(num_scalar_...  117 us
    pallas_call x1, Pallas kernels, scatter_mean(): pl.pallas_call(kernel, in_specs=[pl.BlockSpec(memory_space=pltpu.SMEM), p...  89.9 us
    reduce_scatter x1, waiting for transfers between devices, body(): lax.psum_scatter(spread[rows:rows + hub_count], 'dom', scatter_dimension=...  84 us
    all_gather x2, waiting for transfers between devices, source_table(): hub_all = lax.all_gather(hub_local, 'dom', axis=0, tiled=True)  70 us
    all_gather x2, waiting for transfers between devices, widen(): lax.all_gather(second_rows, 'feat', axis=0, tiled=True)  47.2 us
    all_gather x2, waiting for transfers between devices, widen(): lax.all_gather(first_rows, 'feat', axis=0, tiled=True)  24.5 us
    unnamed x36, local copies, waits for them, and re-layouts  22.8 us
    scatter-add x3, other arithmetic, body(): grad_rows.at[send_rows[bit_index]].add(returned.astype(jnp.float32))  21.8 us
  transfers between devices with their start and end apart: 26, of which 12 were waited for; matrix products, arithmetic and copies ran while one was open for 14% of the time, Pallas kernels for 9%

profile of v2, /device:TPU:1, one launch (start us, length us, event | category | flops | bytes accessed | tf_op | source)
XLA Modules:
  0.0 635.6 jit_solution(1815538385241602462)
XLA Ops:
  10.9 2.0 gather_fusion
  13.8 3.2 gather_fusion.2
  18.7 3.2 gather_fusion.3
  22.2 1.8 collective-permute-start.1
  24.0 3.2 gather_fusion.4
  27.4 3.4 collective-permute-start.2
  31.8 35.4 %all-gather.9.cloned.1.call-done = bf16[20480,32]{1,0:T(8,128)(2,1)} async-done(((bf16[640,32]{1,0:T(8,128)(2,1)}), bf16[20480,32]{1,0:T(8,128)(2,1)}) %all-gather.9.cloned.1.call-update) | async-done | bytes 1310736 | tf_op jit(solution)/shard_map/all_gather | solution.py:118
  67.3 5.3 constant_dynamic-update-slice_fusion.3
  74.8 8.5 %convert_element_type.52.tab_ref = f32[27648,32]{1,0:T(8,128)} convert(bf16[27648,32]{1,0:T(8,128)(2,1)} %constant_dynamic-update-slice_fusion) | non-fusion elementwise | flops 884736 | bytes 5308416 | tf_op jit(solution)/shard_map/convert_element_type | solution.py:111
  83.3 58.4 %shard_map.120 = f32[4096,32]{1,0:T(8,128)} custom-call(s32[8,4096]{1,0:T(8,128)} %nb_ref.5, f32[27648,32]{1,0:T(8,128)} %convert_element_type.52.tab_ref), custom_call_target="tpu_custom_call" | custom-call | tf_op jit(solution)/shard_map/pallas_call | solution.py:33
  145.3 20.1 %all-gather.11.cloned.1.call-done = bf16[128,4096]{1,0:T(8,128)(2,1)} async-done(((bf16[32,4096]{1,0:T(8,128)(2,1)}), bf16[128,4096]{1,0:T(8,128)(2,1)}) %all-gather.11.cloned.1.call-update) | async-done | bytes 1048592 | tf_op jit(solution)/shard_map/all_gather | solution.py:106
  167.1 24.4 %all-gather.7.cloned.1.call-done = bf16[128,4096]{1,0:T(8,128)(2,1)} async-done(((bf16[32,4096]{1,0:T(8,128)(2,1)}), bf16[128,4096]{1,0:T(8,128)(2,1)}) %all-gather.7.cloned.1.call-update) | async-done | bytes 1048592 | tf_op jit(solution)/shard_map/all_gather | solution.py:105
  191.6 1.8 fusion.7
  193.4 3.3 constant_dynamic-update-slice_fusion.9
  196.7 2.0 gather_fusion.1
  199.5 3.2 gather_fusion.5
  202.7 3.2 gather_fusion.6
  206.0 3.2 gather_fusion.7
  209.4 2.8 collective-permute-start.3
  214.0 2.7 collective-permute-start.5
  217.9 34.6 %all-gather.15.cloned.1.call-done = bf16[20480,64]{1,0:T(8,128)(2,1)} async-done(((bf16[640,64]{1,0:T(8,128)(2,1)}), bf16[20480,64]{1,0:T(8,128)(2,1)}) %all-gather.15.cloned.1.call-update) | async-done | bytes 2621456 | tf_op jit(solution)/shard_map/all_gather | solution.py:118
  252.5 5.3 constant_dynamic-update-slice_fusion.8
  260.0 8.6 %convert_element_type.57.tab_ref = f32[27648,64]{1,0:T(8,128)} convert(bf16[27648,64]{1,0:T(8,128)(2,1)} %constant_dynamic-update-slice_fusion.5) | non-fusion elementwise | flops 1769472 | bytes 10616832 | tf_op jit(solution)/shard_map/convert_element_type | solution.py:111
  268.6 58.6 %shard_map.121 = f32[4096,64]{1,0:T(8,128)} custom-call(s32[8,4096]{1,0:T(8,128)} %nb_ref.5, f32[27648,64]{1,0:T(8,128)} %convert_element_type.57.tab_ref), custom_call_target="tpu_custom_call" | custom-call | tf_op jit(solution)/shard_map/pallas_call | solution.py:33
  330.4 2.1 fusion.36
  332.6 27.1 %all-gather.17.cloned.1.call-done = bf16[256,4096]{1,0:T(8,128)(2,1)} async-done(((bf16[64,4096]{1,0:T(8,128)(2,1)}), bf16[256,4096]{1,0:T(8,128)(2,1)}) %all-gather.17.cloned.1.call-update) | async-done | bytes 2097168 | tf_op jit(solution)/shard_map/all_gather | solution.py:106
  359.6 2.3 fusion.34
  365.1 89.9 %shard_map.122 = (f32[27648,64]{1,0:T(8,128)}, f32[27648,64]{1,0:T(8,128)}) custom-call(s32[8,4096]{1,0:T(8,128)} %nb_ref.5, f32[4096,64]{1,0:T(8,128)} %convert_element_type.63.rows_ref), custom_call_target="tpu_custom_call" | custom-call | tf_op jit(solution)/shard_map/pallas_call | solution.py:65
  455.0 12.9 %fusion.28 = (bf16[27648,64]{1,0:T(8,128)(2,1)}, f32[27648,64]{1,0:T(8,128)S(1)}) fusion(f32[27648,64]{1,0:T(8,128)} %get-tuple-element.8, f32[27648,64]{1,0:T(8,128)} %get-tuple-element.9), kind=kLoop, calls=%fused_computation.81 | loop fusion | flops 5308416 | bytes 24772608 | tf_op jit(solution)/shard_map/convert.2
  467.9 5.0 copy-done.2
  472.9 4.1 slice.74
  481.0 2.8 convolution_add_fusion.1
  483.9 2.1 fusion.30
  487.2 2.6 collective-permute-start.8
  490.0 84.0 %reduce-scatter.2.cloned.1.call-done = f32[640,64]{1,0:T(8,128)} async-done(((f32[20480,64]{1,0:T(8,128)}), f32[640,64]{1,0:T(8,128)}) %reduce-scatter.2.cloned.1.call-update) | async-done | bytes 163856 | tf_op jit(solution)/shard_map/reduce_scatter | solution.py:185
  574.0 7.2 %scatter_fusion = f32[4096,64]{1,0:T(8,128)S(1)} fusion(f32[4096,64]{1,0:T(8,128)S(1)} %convolution_add_fusion.1, s32[640]{0:T(1024)S(1)} %compare_select_fusion.6, f32[640,64]{1,0:T(8,128)} %reduce-scatter.2.cloned.1.call-done), kind=kCustom, calls=%fused_computation.8 | custom fusion | flops 40960 | bytes 494080 | tf_op jit(solution)/shard_map/scatter-add | solution.py:188
  581.2 7.4 %scatter_custom_fusion.1 = f32[4096,64]{1,0:T(8,128)S(1)} fusion(f32[4096,64]{1,0:T(8,128)S(1)} %scatter_fusion, s32[1024]{0:T(1024)S(1)} %bitcast.70, bf16[1024,64]{1,0:T(8,128)(2,1)} %collective-permute-done.6), kind=kCustom, calls=%fused_computation.34 | custom fusion | flops 131072 | bytes 1179648 | tf_op jit(solution)/shard_map/scatter-add | solution.py:195
  588.6 7.2 %scatter_custom_fusion.2 = f32[4096,64]{1,0:T(8,128)S(1)} fusion(f32[4096,64]{1,0:T(8,128)S(1)} %scatter_custom_fusion.1, s32[1024]{0:T(1024)S(1)} %bitcast.69, bf16[1024,64]{1,0:T(8,128)(2,1)} %collective-permute-done.7), kind=kCustom, calls=%fused_computation.32 | custom fusion | flops 131072 | bytes 1179648 | tf_op jit(solution)/shard_map/scatter-add | solution.py:195
  595.8 7.2 %scatter_custom_fusion.3 = f32[4096,64]{1,0:T(8,128)S(1)} fusion(f32[4096,64]{1,0:T(8,128)S(1)} %scatter_custom_fusion.2, s32[1024]{0:T(1024)S(1)} %bitcast.68, bf16[1024,64]{1,0:T(8,128)(2,1)} %collective-permute-done.8), kind=kCustom, calls=%fused_computation.30 | custom fusion | flops 131072 | bytes 1179648 | tf_op jit(solution)/shard_map/scatter-add | solution.py:195
  603.0 1.8 fusion.26
  605.4 2.5 collective-permute-start.9
  607.9 2.4 collective-permute-start.16
  610.8 3.0 collective-permute-done.16
  615.0 1.9 collective-permute-start.11
  617.4 2.4 collective-permute-start.18
  620.3 2.2 collective-permute-done.18
  623.1 2.2 collective-permute-start.13
  626.0 2.2 collective-permute-done.13
  (119 shorter events, 38.3 us)
Async XLA Ops:
  7.2 352.5 %copy-start = (bf16[172,256]{1,0:T(8,128)(2,1)S(1)}, bf16[172,256]{1,0:T(8,128)(2,1)}, u32[]{:S(2)}) copy-start(bf16[172,256]{1,0:T(8,128)(2,1)} %param.21) | copy-start | bytes 264196
  7.2 60.1 %all-gather.9.cloned.1.call-start = ((), (), s32[]{:S(2)}) async-start(), calls=%async_computation.2 | async-start | bytes 5406720 | tf_op jit(solution)/shard_map/all_gather | solution.py:118
  13.8 151.7 %all-gather.11.cloned.1.call-start = ((), (), s32[]{:S(2)}) async-start(), calls=%async_computation.3 | async-start | bytes 1310720 | tf_op jit(solution)/shard_map/all_gather | solution.py:106
  17.3 55.3 %collective-permute-start = (bf16[1024,32]{1,0:T(8,128)(2,1)S(1)}, bf16[1024,32]{1,0:T(8,128)(2,1)S(1)}, u32[]{:S(2)}, u32[]{:S(2)}) collective-permute-start(bf16[1024,32]{1,0:T(8,128)(2,1)S(1)} %broadcast_select_fusion.5), channel_id=1, source_target_pairs={{0,4},{4,0},{8,12},{12,8},{16,20},{20,16},{24,28},{28,24},{32,36},... | collective-permute-start | bytes 196616 | tf_op jit(solution)/shard_map/ppermute | solution.py:96
  22.2 51.1 %collective-permute-start.1 = (bf16[1024,32]{1,0:T(8,128)(2,1)S(1)}, bf16[1024,32]{1,0:T(8,128)(2,1)S(1)}, u32[]{:S(2)}, u32[]{:S(2)}) collective-permute-start(bf16[1024,32]{1,0:T(8,128)(2,1)S(1)} %broadcast_select_fusion.4), channel_id=1, source_target_pairs={{0,8},{4,12},{8,0},{12,4},{16,24},{20,28},{24,16},{28,20},{32,40},... | collective-permute-start | bytes 196616 | tf_op jit(solution)/shard_map/ppermute | solution.py:96
  27.4 46.6 %collective-permute-start.2 = (bf16[1024,32]{1,0:T(8,128)(2,1)S(1)}, bf16[1024,32]{1,0:T(8,128)(2,1)S(1)}, u32[]{:S(2)}, u32[]{:S(2)}) collective-permute-start(bf16[1024,32]{1,0:T(8,128)(2,1)S(1)} %broadcast_select_fusion.3), channel_id=1, source_target_pairs={{0,16},{4,20},{8,24},{12,28},{16,0},{20,4},{24,8},{28,12},{32,48},... | collective-permute-start | bytes 196616 | tf_op jit(solution)/shard_map/ppermute | solution.py:96
  141.7 23.7 %copy-start.11 = (bf16[64,128]{1,0:T(8,128)(2,1)S(1)}, bf16[64,128]{1,0:T(8,128)(2,1)}, u32[]{:S(2)}) copy-start(bf16[64,128]{1,0:T(8,128)(2,1)} %param.19) | copy-start | bytes 49156
  144.5 47.1 %copy-start.12 = (bf16[64,128]{1,0:T(8,128)(2,1)S(1)}, bf16[64,128]{1,0:T(8,128)(2,1)}, u32[]{:S(2)}) copy-start(bf16[64,128]{1,0:T(8,128)(2,1)} %param.18) | copy-start | bytes 49156
  144.5 47.0 %all-gather.7.cloned.1.call-start = ((), (), s32[]{:S(2)}) async-start(), calls=%async_computation.1 | async-start | bytes 1310720 | tf_op jit(solution)/shard_map/all_gather | solution.py:105
  145.3 107.3 %all-gather.15.cloned.1.call-start = ((), (), s32[]{:S(2)}) async-start(), calls=%async_computation.5 | async-start | bytes 5406720 | tf_op jit(solution)/shard_map/all_gather | solution.py:118
  167.1 26.2 %copy-start.6 = (f32[4096,64]{1,0:T(8,128)}, f32[4096,64]{1,0:T(8,128)S(1)}, u32[]{:S(2)}) copy-start(f32[4096,64]{1,0:T(8,128)S(1)} %fusion.35) | copy-start | bytes 3145732
  193.4 23.3 %copy-start.4 = (bf16[64,4096]{0,1:T(8,128)(2,1)}, bf16[64,4096]{0,1:T(8,128)(2,1)S(1)}, u32[]{:S(2)}) copy-start(bf16[64,4096]{0,1:T(8,128)(2,1)S(1)} %get-tuple-element.27) | copy-start | bytes 1572868
  199.5 130.9 %all-gather.13.cloned.1.call-start = ((), (), s32[]{:S(2)}) async-start(), calls=%async_computation.4 | async-start | bytes 2621440 | tf_op jit(solution)/shard_map/all_gather | solution.py:105
  209.4 48.5 %collective-permute-start.3 = (bf16[1024,64]{1,0:T(8,128)(2,1)S(1)}, bf16[1024,64]{1,0:T(8,128)(2,1)S(1)}, u32[]{:S(2)}, u32[]{:S(2)}) collective-permute-start(bf16[1024,64]{1,0:T(8,128)(2,1)S(1)} %broadcast_select_fusion.2), channel_id=1, source_target_pairs={{0,4},{4,0},{8,12},{12,8},{16,20},{20,16},{24,28},{28,24},{32,36},... | collective-permute-start | bytes 393224 | tf_op jit(solution)/shard_map/ppermute | solution.py:96
  212.4 46.1 %collective-permute-start.4 = (bf16[1024,64]{1,0:T(8,128)(2,1)S(1)}, bf16[1024,64]{1,0:T(8,128)(2,1)S(1)}, u32[]{:S(2)}, u32[]{:S(2)}) collective-permute-start(bf16[1024,64]{1,0:T(8,128)(2,1)S(1)} %broadcast_select_fusion.1), channel_id=1, source_target_pairs={{0,8},{4,12},{8,0},{12,4},{16,24},{20,28},{24,16},{28,20},{32,40},... | collective-permute-start | bytes 393224 | tf_op jit(solution)/shard_map/ppermute | solution.py:96
  214.0 45.3 %collective-permute-start.5 = (bf16[1024,64]{1,0:T(8,128)(2,1)S(1)}, bf16[1024,64]{1,0:T(8,128)(2,1)S(1)}, u32[]{:S(2)}, u32[]{:S(2)}) collective-permute-start(bf16[1024,64]{1,0:T(8,128)(2,1)S(1)} %broadcast_select_fusion), channel_id=1, source_target_pairs={{0,16},{4,20},{8,24},{12,28},{16,0},{20,4},{24,8},{28,12},{32,48},... | collective-permute-start | bytes 393224 | tf_op jit(solution)/shard_map/ppermute | solution.py:96
  217.8 141.8 %all-gather.17.cloned.1.call-start = ((), (), s32[]{:S(2)}) async-start(), calls=%async_computation.6 | async-start | bytes 2621440 | tf_op jit(solution)/shard_map/all_gather | solution.py:106
  327.2 3.2 copy-start.9
  330.1 243.8 %reduce-scatter.2.cloned.1.call-start = ((), (), s32[]{:S(2)}) async-start(), calls=%async_computation.7 | async-start | bytes 10813440 | tf_op jit(solution)/shard_map/reduce_scatter | solution.py:185
  332.5 29.5 %copy-start.13 = (s32[4096]{0:T(1024)S(1)}, s32[4096]{0:T(1024)}, u32[]{:S(2)}) copy-start(s32[4096]{0:T(1024)} %param.17) | copy-start | bytes 49156
  362.6 116.2 %copy-start.3 = (bf16[172,4096]{1,0:T(8,128)(2,1)}, bf16[172,4096]{1,0:T(8,128)(2,1)S(1)}, u32[]{:S(2)}) copy-start(bf16[172,4096]{1,0:T(8,128)(2,1)S(1)} %fusion.2) | copy-start | bytes 4227076
  467.9 5.0 copy-start.2
  477.0 0.7 copy-start.10
  477.0 1.2 copy-start.5
  477.7 1.7 copy-start.7
  480.1 9.7 %collective-permute-start.14 = (f32[344,64]{0,1:T(8,128)S(1)}, f32[344,64]{0,1:T(8,128)S(1)}, u32[]{:S(2)}, u32[]{:S(2)}) collective-permute-start(f32[344,64]{0,1:T(8,128)S(1)} %pad_maximum_fusion), channel_id=1, source_target_pairs={{0,4},{4,0},{8,12},{12,8},{16,20},{20,16},{24,28},{28,24},{32,36},... | collective-permute-start | bytes 264200 | tf_op jit(solution)/shard_map/ppermute | solution.py:88
  485.9 95.2 %collective-permute-start.6 = (bf16[1024,64]{1,0:T(8,128)(2,1)}, bf16[1024,64]{1,0:T(8,128)(2,1)}, u32[]{:S(2)}, u32[]{:S(2)}) collective-permute-start(bf16[1024,64]{1,0:T(8,128)(2,1)} %get-tuple-element.16), channel_id=1, source_target_pairs={{0,4},{4,0},{8,12},{12,8},{16,20},{20,16},{24,28},{28,24},{32,36},... | collective-permute-start | bytes 393224 | tf_op jit(solution)/shard_map/ppermute | solution.py:96
  486.0 102.6 %collective-permute-start.7 = (bf16[1024,64]{1,0:T(8,128)(2,1)}, bf16[1024,64]{1,0:T(8,128)(2,1)}, u32[]{:S(2)}, u32[]{:S(2)}) collective-permute-start(bf16[1024,64]{1,0:T(8,128)(2,1)} %get-tuple-element.15), channel_id=1, source_target_pairs={{0,8},{4,12},{8,0},{12,4},{16,24},{20,28},{24,16},{28,20},{32,40},... | collective-permute-start | bytes 393224 | tf_op jit(solution)/shard_map/ppermute | solution.py:96
  487.2 108.6 %collective-permute-start.8 = (bf16[1024,64]{1,0:T(8,128)(2,1)}, bf16[1024,64]{1,0:T(8,128)(2,1)}, u32[]{:S(2)}, u32[]{:S(2)}) collective-permute-start(bf16[1024,64]{1,0:T(8,128)(2,1)} %get-tuple-element.14), channel_id=1, source_target_pairs={{0,16},{4,20},{8,24},{12,28},{16,0},{20,4},{24,8},{28,12},{32,48},... | collective-permute-start | bytes 393224 | tf_op jit(solution)/shard_map/ppermute | solution.py:96
  489.9 118.0 %collective-permute-start.15 = (f32[344,64]{0,1:T(8,128)S(1)}, f32[344,64]{0,1:T(8,128)S(1)}, u32[]{:S(2)}, u32[]{:S(2)}) collective-permute-start(f32[344,64]{0,1:T(8,128)S(1)} %fusion.53), channel_id=1, source_target_pairs={{0,8},{4,12},{8,0},{12,4},{16,24},{20,28},{24,16},{28,20},{32,40},... | collective-permute-start | bytes 264200 | tf_op jit(solution)/shard_map/ppermute | solution.py:88
  603.0 1.8 copy-start.8
  604.8 23.9 %copy-start.1 = (bf16[172,256]{1,0:T(8,128)(2,1)S(1)}, bf16[172,256]{1,0:T(8,128)(2,1)}, u32[]{:S(2)}) copy-start(bf16[172,256]{1,0:T(8,128)(2,1)} %param.21) | copy-start | bytes 264196
  605.4 4.9 collective-permute-start.9
  607.9 5.9 collective-permute-start.16
  610.3 4.7 collective-permute-start.10
  613.8 3.5 collective-permute-start.17
  615.0 4.9 collective-permute-start.11
  617.4 5.1 collective-permute-start.18
  619.8 3.2 collective-permute-start.12
  623.1 5.1 collective-permute-start.13
Sparse Core Ops, SparseCore 0:
  13.9 53.3 all-gather.8
  144.7 20.7 all-gather.10
  167.1 24.4 all-gather.6
  199.6 52.8 all-gather.14
  254.0 29.2 all-gather.12
  330.2 29.3 all-gather.16
  477.1 96.7 reduce-scatter.1

commit v3 on v2

--- a/solution.py
+++ b/solution.py
@@ -88,6 +88,24 @@
         value = value + lax.ppermute(value, axis, pairs)
         stride *= 2
     return value
+
+
+def tree_scatter(value, axis):
+    count = lax.axis_size(axis)
+    index = lax.axis_index(axis)
+    width = value.shape[1]
+    parts = value.reshape(count, -1, width)
+    rows = parts.shape[1]
+    stride = 1
+    while stride < count:
+        bit = (index // stride) % 2
+        paired = parts.reshape(parts.shape[0] // 2, 2, rows, width)
+        keep = lax.dynamic_index_in_dim(paired, bit, axis=1, keepdims=False)
+        send = lax.dynamic_index_in_dim(paired, 1 - bit, axis=1, keepdims=False)
+        pairs = [(source, source ^ stride) for source in range(count)]
+        parts = keep + lax.ppermute(send, axis, pairs)
+        stride *= 2
+    return parts.reshape(rows, width)
 
 
 def partner(value, axis, stride):
@@ -182,9 +200,7 @@
     back_rows = back_mean.T.astype(jnp.float32)
     spread = scatter_mean(back_rows, neighbours, span)
     grad_rows = direct.T + spread[:rows]
-    hub_back = lax.psum_scatter(
-        spread[rows : rows + hub_count], "dom", scatter_dimension=0, tiled=True
-    )
+    hub_back = tree_scatter(spread[rows : rows + hub_count], "dom")
     grad_rows = grad_rows.at[hub_rows].add(hub_back)
     base = rows + hub_count
     for bit_index in range(send_rows.shape[0]):

time: 640 us -> 634 us (level)
  waiting for transfers between devices: 235 us -> 189 us
  starting transfers between devices: 32.1 us -> 46.3 us
  local copies, waits for them, and re-layouts: 59.7 us -> 73.1 us
  other arithmetic: 72.4 us -> 83.5 us
    reduce_scatter x1 -> x0, waiting for transfers between devices: 84 us -> none  [body(): lax.psum_scatter(spread[rows:rows + hub_count], 'dom', scatter_dimension=...]
    ppermute x0 -> x5, waiting for transfers between devices: none -> 40.3 us  [tree_scatter(): parts = keep + lax.ppermute(send, axis, pairs)]
    dynamic_slice x0 -> x5, local copies, waits for them, and re-layouts: none -> 16 us  [the longest x4 10.5 us: tree_scatter(): keep = lax.dynamic_index_in_dim(paired, bit, axis=1, keepdims=False)]
    ppermute x0 -> x5, starting transfers between devices: none -> 9.33 us  [tree_scatter(): parts = keep + lax.ppermute(send, axis, pairs)]
    ppermute x10, starting transfers between devices: 14.3 us -> 21 us  [tree_sum(): value = value + lax.ppermute(value, axis, pairs)]
    unnamed x36 -> x40, local copies, waits for them, and re-layouts: 22.8 us -> 22.1 us
  transfers between devices with their start and end apart: 26 -> 30, of which waited for: 12 -> 14; matrix products, arithmetic and copies ran while one was open for 14% -> 17% of each run, Pallas kernels for 9% -> 9%
where the time goes in v3:
time: 634 us; the launch traced here: 630 us
  Pallas kernels  207 us (33%)
  waiting for transfers between devices  189 us (30%)
  other arithmetic  83.5 us (13%)
  local copies, waits for them, and re-layouts  73.1 us (12%)
  starting transfers between devices  46.3 us (7%)
  matrix products  16.2 us (3%)
  between operations  14.7 us (2%)
    pallas_call x2, Pallas kernels, gather_mean(): pl.pallas_call(kernel, grid_spec=pltpu.PrefetchScalarGridSpec(num_scalar_...  117 us
    pallas_call x1, Pallas kernels, scatter_mean(): pl.pallas_call(kernel, in_specs=[pl.BlockSpec(memory_space=pltpu.SMEM), p...  89.9 us
    all_gather x2, waiting for transfers between devices, source_table(): hub_all = lax.all_gather(hub_local, 'dom', axis=0, tiled=True)  69.9 us
    all_gather x2, waiting for transfers between devices, widen(): lax.all_gather(second_rows, 'feat', axis=0, tiled=True)  47.4 us
    ppermute x5, waiting for transfers between devices, tree_scatter(): parts = keep + lax.ppermute(send, axis, pairs)  40.3 us
    scatter-add x3, other arithmetic, body(): grad_rows.at[send_rows[bit_index]].add(returned.astype(jnp.float32))  26.2 us
    all_gather x2, waiting for transfers between devices, widen(): lax.all_gather(first_rows, 'feat', axis=0, tiled=True)  24.5 us
    unnamed x40, local copies, waits for them, and re-layouts  22.1 us
  transfers between devices with their start and end apart: 30, of which 14 were waited for; matrix products, arithmetic and copies ran while one was open for 17% of the time, Pallas kernels for 9%

profile of v3, /device:TPU:1, one launch (start us, length us, event | category | flops | bytes accessed | tf_op | source)
XLA Modules:
  0.0 630.1 jit_solution(597263708551840567)
XLA Ops:
  13.0 3.2 gather_fusion.2
  17.9 3.2 gather_fusion.3
  23.2 3.2 gather_fusion.4
  26.6 3.4 collective-permute-start.2
  31.0 35.4 %all-gather.9.cloned.1.call-done = bf16[20480,32]{1,0:T(8,128)(2,1)} async-done(((bf16[640,32]{1,0:T(8,128)(2,1)}), bf16[20480,32]{1,0:T(8,128)(2,1)}) %all-gather.9.cloned.1.call-update) | async-done | bytes 1310736 | tf_op jit(solution)/shard_map/all_gather | solution.py:136
  66.4 5.3 constant_dynamic-update-slice_fusion.3
  73.9 8.5 %convert_element_type.52.tab_ref = f32[27648,32]{1,0:T(8,128)} convert(bf16[27648,32]{1,0:T(8,128)(2,1)} %constant_dynamic-update-slice_fusion) | non-fusion elementwise | flops 884736 | bytes 5308416 | tf_op jit(solution)/shard_map/convert_element_type | solution.py:129
  82.5 58.4 %shard_map.120 = f32[4096,32]{1,0:T(8,128)} custom-call(s32[8,4096]{1,0:T(8,128)} %nb_ref.5, f32[27648,32]{1,0:T(8,128)} %convert_element_type.52.tab_ref), custom_call_target="tpu_custom_call" | custom-call | tf_op jit(solution)/shard_map/pallas_call | solution.py:33
  144.5 20.1 %all-gather.11.cloned.1.call-done = bf16[128,4096]{1,0:T(8,128)(2,1)} async-done(((bf16[32,4096]{1,0:T(8,128)(2,1)}), bf16[128,4096]{1,0:T(8,128)(2,1)}) %all-gather.11.cloned.1.call-update) | async-done | bytes 1048592 | tf_op jit(solution)/shard_map/all_gather | solution.py:124
  166.3 24.4 %all-gather.7.cloned.1.call-done = bf16[128,4096]{1,0:T(8,128)(2,1)} async-done(((bf16[32,4096]{1,0:T(8,128)(2,1)}), bf16[128,4096]{1,0:T(8,128)(2,1)}) %all-gather.7.cloned.1.call-update) | async-done | bytes 1048592 | tf_op jit(solution)/shard_map/all_gather | solution.py:123
  192.5 3.3 constant_dynamic-update-slice_fusion.9
  198.7 3.2 gather_fusion.5
  201.9 3.2 gather_fusion.6
  205.1 3.2 gather_fusion.7
  208.6 2.8 collective-permute-start.3
  213.2 2.7 collective-permute-start.5
  217.2 34.5 %all-gather.15.cloned.1.call-done = bf16[20480,64]{1,0:T(8,128)(2,1)} async-done(((bf16[640,64]{1,0:T(8,128)(2,1)}), bf16[20480,64]{1,0:T(8,128)(2,1)}) %all-gather.15.cloned.1.call-update) | async-done | bytes 2621456 | tf_op jit(solution)/shard_map/all_gather | solution.py:136
  251.7 5.3 constant_dynamic-update-slice_fusion.8
  259.2 8.6 %convert_element_type.57.tab_ref = f32[27648,64]{1,0:T(8,128)} convert(bf16[27648,64]{1,0:T(8,128)(2,1)} %constant_dynamic-update-slice_fusion.5) | non-fusion elementwise | flops 1769472 | bytes 10616832 | tf_op jit(solution)/shard_map/convert_element_type | solution.py:129
  267.8 58.6 %shard_map.121 = f32[4096,64]{1,0:T(8,128)} custom-call(s32[8,4096]{1,0:T(8,128)} %nb_ref.5, f32[27648,64]{1,0:T(8,128)} %convert_element_type.57.tab_ref), custom_call_target="tpu_custom_call" | custom-call | tf_op jit(solution)/shard_map/pallas_call | solution.py:33
  329.3 2.1 fusion.40
  331.5 27.3 %all-gather.17.cloned.1.call-done = bf16[256,4096]{1,0:T(8,128)(2,1)} async-done(((bf16[64,4096]{1,0:T(8,128)(2,1)}), bf16[256,4096]{1,0:T(8,128)(2,1)}) %all-gather.17.cloned.1.call-update) | async-done | bytes 2097168 | tf_op jit(solution)/shard_map/all_gather | solution.py:124
  358.8 2.3 fusion.38
  364.2 89.9 %shard_map.122 = (f32[27648,64]{1,0:T(8,128)}, f32[27648,64]{1,0:T(8,128)}) custom-call(s32[8,4096]{1,0:T(8,128)} %nb_ref.5, f32[4096,64]{1,0:T(8,128)} %convert_element_type.63.rows_ref), custom_call_target="tpu_custom_call" | custom-call | tf_op jit(solution)/shard_map/pallas_call | solution.py:65
  454.1 12.9 %fusion.32 = (bf16[27648,64]{1,0:T(8,128)(2,1)}, f32[27648,64]{1,0:T(8,128)S(1)}) fusion(f32[27648,64]{1,0:T(8,128)} %get-tuple-element.8, f32[27648,64]{1,0:T(8,128)} %get-tuple-element.9), kind=kLoop, calls=%fused_computation.96 | loop fusion | flops 5308416 | bytes 24772608 | tf_op jit(solution)/shard_map/convert.2
  467.7 4.3 copy-done.2
  472.1 4.6 constant_dynamic-slice_fusion.3
  476.7 5.5 copy.94
  483.0 5.6 copy.93
  488.7 2.8 bitcast_add_fusion
  495.4 29.2 %collective-permute-done.7 = f32[8,640,64]{1,2,0:T(8,128)S(1)} collective-permute-done((f32[8,640,64]{1,2,0:T(8,128)}, f32[8,640,64]{1,2,0:T(8,128)S(1)}, u32[]{:S(2)}, u32[]{:S(2)}) %collective-permute-start.7) | collective-permute-done | bytes 1310752 | tf_op jit(solution)/shard_map/ppermute | solution.py:106
  526.3 2.9 collective-permute-start.8
  531.8 2.0 fusion.34
  535.9 7.4 %collective-permute-done.8 = f32[4,640,64]{1,2,0:T(8,128)S(1)} collective-permute-done((f32[4,640,64]{1,2,0:T(8,128)S(1)}, f32[4,640,64]{1,2,0:T(8,128)S(1)}, u32[]{:S(2)}, u32[]{:S(2)}) %collective-permute-start.8) | collective-permute-done | bytes 655392 | tf_op jit(solution)/shard_map/ppermute | solution.py:106
  544.9 3.7 convolution_add_fusion.1
  551.4 2.8 collective-permute-start.10
  556.5 2.4 collective-permute-done.10
  558.9 8.5 %scatter_custom_fusion = f32[4096,64]{1,0:T(8,128)} fusion(f32[4096,64]{1,0:T(8,128)} %convolution_add_fusion.1, s32[640]{0:T(1024)S(1)} %compare_select_fusion.6, f32[1,640,64]{2,1,0:T(8,128)S(1)} %collective-permute-done.10, f32[2,640,64]{2,1,0:T(8,128)S(1)} %bitcast_add_fusion.4, s32[]{:T(128)S(6)} %select_n.160, s32[]{:T(128)} %constant.169.clone.1), kind=kCustom, calls=%fused_computation.45 | custom fusion | flops 81920 | bytes 1704452 | tf_op jit(solution)/shard_map/scatter-add | solution.py:204
  567.4 8.7 %scatter_custom_fusion.1 = f32[4096,64]{1,0:T(8,128)} fusion(f32[4096,64]{1,0:T(8,128)} %scatter_custom_fusion, s32[1024]{0:T(1024)S(1)} %bitcast.99, bf16[1024,64]{1,0:T(8,128)(2,1)} %collective-permute-done.11), kind=kCustom, calls=%fused_computation.40 | custom fusion | flops 131072 | bytes 1310720 | tf_op jit(solution)/shard_map/scatter-add | solution.py:211
  576.1 8.8 %scatter_custom_fusion.2 = f32[4096,64]{1,0:T(8,128)} fusion(f32[4096,64]{1,0:T(8,128)} %scatter_custom_fusion.1, s32[1024]{0:T(1024)S(1)} %bitcast.98, bf16[1024,64]{1,0:T(8,128)(2,1)} %collective-permute-done.12), kind=kCustom, calls=%fused_computation.38 | custom fusion | flops 131072 | bytes 1310720 | tf_op jit(solution)/shard_map/scatter-add | solution.py:211
  584.9 8.7 %scatter_custom_fusion.3 = f32[4096,64]{1,0:T(8,128)} fusion(f32[4096,64]{1,0:T(8,128)} %scatter_custom_fusion.2, s32[1024]{0:T(1024)S(1)} %bitcast.97, bf16[1024,64]{1,0:T(8,128)(2,1)} %collective-permute-done.13), kind=kCustom, calls=%fused_computation.36 | custom fusion | flops 131072 | bytes 1310720 | tf_op jit(solution)/shard_map/scatter-add | solution.py:211
  593.6 2.3 fusion.30
  596.6 5.1 collective-permute-start.14
  601.8 2.9 collective-permute-start.21
  605.2 2.5 collective-permute-done.21
  609.4 2.6 collective-permute-start.16
  611.9 2.5 collective-permute-start.23
  617.6 2.7 collective-permute-start.18
  (143 shorter events, 61.6 us)
Async XLA Ops:
  7.2 351.6 %copy-start = (bf16[172,256]{1,0:T(8,128)(2,1)S(1)}, bf16[172,256]{1,0:T(8,128)(2,1)}, u32[]{:S(2)}) copy-start(bf16[172,256]{1,0:T(8,128)(2,1)} %param.21) | copy-start | bytes 264196
  7.2 5.8 copy-start.12
  7.2 59.3 %all-gather.9.cloned.1.call-start = ((), (), s32[]{:S(2)}) async-start(), calls=%async_computation.1 | async-start | bytes 5406720 | tf_op jit(solution)/shard_map/all_gather | solution.py:136
  12.9 151.7 %all-gather.11.cloned.1.call-start = ((), (), s32[]{:S(2)}) async-start(), calls=%async_computation.2 | async-start | bytes 1310720 | tf_op jit(solution)/shard_map/all_gather | solution.py:124
  16.4 55.3 %collective-permute-start = (bf16[1024,32]{1,0:T(8,128)(2,1)S(1)}, bf16[1024,32]{1,0:T(8,128)(2,1)S(1)}, u32[]{:S(2)}, u32[]{:S(2)}) collective-permute-start(bf16[1024,32]{1,0:T(8,128)(2,1)S(1)} %broadcast_select_fusion.5), channel_id=1, source_target_pairs={{0,4},{4,0},{8,12},{12,8},{16,20},{20,16},{24,28},{28,24},{32,36},... | collective-permute-start | bytes 196616 | tf_op jit(solution)/shard_map/ppermute | solution.py:114
  21.3 51.1 %collective-permute-start.1 = (bf16[1024,32]{1,0:T(8,128)(2,1)S(1)}, bf16[1024,32]{1,0:T(8,128)(2,1)S(1)}, u32[]{:S(2)}, u32[]{:S(2)}) collective-permute-start(bf16[1024,32]{1,0:T(8,128)(2,1)S(1)} %broadcast_select_fusion.4), channel_id=1, source_target_pairs={{0,8},{4,12},{8,0},{12,4},{16,24},{20,28},{24,16},{28,20},{32,40},... | collective-permute-start | bytes 196616 | tf_op jit(solution)/shard_map/ppermute | solution.py:114
  26.6 46.6 %collective-permute-start.2 = (bf16[1024,32]{1,0:T(8,128)(2,1)S(1)}, bf16[1024,32]{1,0:T(8,128)(2,1)S(1)}, u32[]{:S(2)}, u32[]{:S(2)}) collective-permute-start(bf16[1024,32]{1,0:T(8,128)(2,1)S(1)} %broadcast_select_fusion.3), channel_id=1, source_target_pairs={{0,16},{4,20},{8,24},{12,28},{16,0},{20,4},{24,8},{28,12},{32,48},... | collective-permute-start | bytes 196616 | tf_op jit(solution)/shard_map/ppermute | solution.py:114
  140.9 23.7 %copy-start.13 = (bf16[64,128]{1,0:T(8,128)(2,1)S(1)}, bf16[64,128]{1,0:T(8,128)(2,1)}, u32[]{:S(2)}) copy-start(bf16[64,128]{1,0:T(8,128)(2,1)} %param.19) | copy-start | bytes 49156
  143.7 47.1 %copy-start.14 = (bf16[64,128]{1,0:T(8,128)(2,1)S(1)}, bf16[64,128]{1,0:T(8,128)(2,1)}, u32[]{:S(2)}) copy-start(bf16[64,128]{1,0:T(8,128)(2,1)} %param.18) | copy-start | bytes 49156
  143.7 47.0 %all-gather.7.cloned.1.call-start = ((), (), s32[]{:S(2)}) async-start(), calls=%async_computation | async-start | bytes 1310720 | tf_op jit(solution)/shard_map/all_gather | solution.py:123
  144.4 107.3 %all-gather.15.cloned.1.call-start = ((), (), s32[]{:S(2)}) async-start(), calls=%async_computation.4 | async-start | bytes 5406720 | tf_op jit(solution)/shard_map/all_gather | solution.py:136
  166.3 26.2 %copy-start.5 = (f32[4096,64]{1,0:T(8,128)}, f32[4096,64]{1,0:T(8,128)S(1)}, u32[]{:S(2)}) copy-start(f32[4096,64]{1,0:T(8,128)S(1)} %fusion.39) | copy-start | bytes 3145732
  192.5 23.3 %copy-start.3 = (bf16[64,4096]{0,1:T(8,128)(2,1)}, bf16[64,4096]{0,1:T(8,128)(2,1)S(1)}, u32[]{:S(2)}) copy-start(bf16[64,4096]{0,1:T(8,128)(2,1)S(1)} %get-tuple-element.31) | copy-start | bytes 1572868
  198.7 130.7 %all-gather.13.cloned.1.call-start = ((), (), s32[]{:S(2)}) async-start(), calls=%async_computation.3 | async-start | bytes 2621440 | tf_op jit(solution)/shard_map/all_gather | solution.py:123
  208.6 48.4 %collective-permute-start.3 = (bf16[1024,64]{1,0:T(8,128)(2,1)S(1)}, bf16[1024,64]{1,0:T(8,128)(2,1)S(1)}, u32[]{:S(2)}, u32[]{:S(2)}) collective-permute-start(bf16[1024,64]{1,0:T(8,128)(2,1)S(1)} %broadcast_select_fusion.2), channel_id=1, source_target_pairs={{0,4},{4,0},{8,12},{12,8},{16,20},{20,16},{24,28},{28,24},{32,36},... | collective-permute-start | bytes 393224 | tf_op jit(solution)/shard_map/ppermute | solution.py:114
  211.6 46.1 %collective-permute-start.4 = (bf16[1024,64]{1,0:T(8,128)(2,1)S(1)}, bf16[1024,64]{1,0:T(8,128)(2,1)S(1)}, u32[]{:S(2)}, u32[]{:S(2)}) collective-permute-start(bf16[1024,64]{1,0:T(8,128)(2,1)S(1)} %broadcast_select_fusion.1), channel_id=1, source_target_pairs={{0,8},{4,12},{8,0},{12,4},{16,24},{20,28},{24,16},{28,20},{32,40},... | collective-permute-start | bytes 393224 | tf_op jit(solution)/shard_map/ppermute | solution.py:114
  213.2 45.3 %collective-permute-start.5 = (bf16[1024,64]{1,0:T(8,128)(2,1)S(1)}, bf16[1024,64]{1,0:T(8,128)(2,1)S(1)}, u32[]{:S(2)}, u32[]{:S(2)}) collective-permute-start(bf16[1024,64]{1,0:T(8,128)(2,1)S(1)} %broadcast_select_fusion), channel_id=1, source_target_pairs={{0,16},{4,20},{8,24},{12,28},{16,0},{20,4},{24,8},{28,12},{32,48},... | collective-permute-start | bytes 393224 | tf_op jit(solution)/shard_map/ppermute | solution.py:114
  217.0 141.8 %all-gather.17.cloned.1.call-start = ((), (), s32[]{:S(2)}) async-start(), calls=%async_computation.5 | async-start | bytes 2621440 | tf_op jit(solution)/shard_map/all_gather | solution.py:124
  326.4 3.0 copy-start.11
  331.5 29.7 %copy-start.15 = (s32[4096]{0:T(1024)S(1)}, s32[4096]{0:T(1024)}, u32[]{:S(2)}) copy-start(s32[4096]{0:T(1024)} %param.17) | copy-start | bytes 49156
  467.0 5.1 copy-start.2
  482.2 6.4 %collective-permute-start.6 = (f32[16,640,64]{1,2,0:T(8,128)}, f32[16,640,64]{1,2,0:T(8,128)}, u32[]{:S(2)}, u32[]{:S(2)}) collective-permute-start(f32[16,640,64]{1,2,0:T(8,128)} %bitcast.90), channel_id=1, source_target_pairs={{0,4},{4,0},{8,12},{12,8},{16,20},{20,16},{24,28},{28,24},{32,36},... | collective-permute-start | bytes 7864328 | tf_op jit(solution)/shard_map/ppermute | solution.py:106
  491.5 1.5 copy-start.8
  494.1 30.5 %collective-permute-start.7 = (f32[8,640,64]{1,2,0:T(8,128)}, f32[8,640,64]{1,2,0:T(8,128)S(1)}, u32[]{:S(2)}, u32[]{:S(2)}) collective-permute-start(f32[8,640,64]{1,2,0:T(8,128)} %dynamic-slice_bitcast_fusion), channel_id=1, source_target_pairs={{0,8},{4,12},{8,0},{12,4},{16,24},{20,28},{24,16},{28,20},{32,40},... | collective-permute-start | bytes 3932168 | tf_op jit(solution)/shard_map/ppermute | solution.py:106
  495.4 33.8 %copy-start.7 = (f32[4096,64]{1,0:T(8,128)S(1)}, f32[4096,64]{1,0:T(8,128)}, u32[]{:S(2)}) copy-start(f32[4096,64]{1,0:T(8,128)} %shard_map.121) | copy-start | bytes 3145732
  526.3 3.6 copy-start.4
  526.3 17.0 %collective-permute-start.8 = (f32[4,640,64]{1,2,0:T(8,128)S(1)}, f32[4,640,64]{1,2,0:T(8,128)S(1)}, u32[]{:S(2)}, u32[]{:S(2)}) collective-permute-start(f32[4,640,64]{1,2,0:T(8,128)S(1)} %dynamic-slice_bitcast_fusion.1), channel_id=1, source_target_pairs={{0,16},{4,20},{8,24},{12,28},{16,0},{20,4},{24,8},{28,12},{32,48},... | collective-permute-start | bytes 1966088 | tf_op jit(solution)/shard_map/ppermute | solution.py:106
  530.6 23.6 %collective-permute-start.19 = (f32[344,64]{0,1:T(8,128)S(1)}, f32[344,64]{0,1:T(8,128)}, u32[]{:S(2)}, u32[]{:S(2)}) collective-permute-start(f32[344,64]{0,1:T(8,128)S(1)} %pad_maximum_fusion), channel_id=1, source_target_pairs={{0,4},{4,0},{8,12},{12,8},{16,20},{20,16},{24,28},{28,24},{32,36},... | collective-permute-start | bytes 264200 | tf_op jit(solution)/shard_map/ppermute | solution.py:88
  533.9 33.5 %collective-permute-start.11 = (bf16[1024,64]{1,0:T(8,128)(2,1)}, bf16[1024,64]{1,0:T(8,128)(2,1)}, u32[]{:S(2)}, u32[]{:S(2)}) collective-permute-start(bf16[1024,64]{1,0:T(8,128)(2,1)} %get-tuple-element.18), channel_id=1, source_target_pairs={{0,4},{4,0},{8,12},{12,8},{16,20},{20,16},{24,28},{28,24},{32,36},... | collective-permute-start | bytes 393224 | tf_op jit(solution)/shard_map/ppermute | solution.py:114
  533.9 42.2 %collective-permute-start.12 = (bf16[1024,64]{1,0:T(8,128)(2,1)}, bf16[1024,64]{1,0:T(8,128)(2,1)}, u32[]{:S(2)}, u32[]{:S(2)}) collective-permute-start(bf16[1024,64]{1,0:T(8,128)(2,1)} %get-tuple-element.17), channel_id=1, source_target_pairs={{0,8},{4,12},{8,0},{12,4},{16,24},{20,28},{24,16},{28,20},{32,40},... | collective-permute-start | bytes 393224 | tf_op jit(solution)/shard_map/ppermute | solution.py:114
  534.3 50.7 %collective-permute-start.13 = (bf16[1024,64]{1,0:T(8,128)(2,1)}, bf16[1024,64]{1,0:T(8,128)(2,1)}, u32[]{:S(2)}, u32[]{:S(2)}) collective-permute-start(bf16[1024,64]{1,0:T(8,128)(2,1)} %get-tuple-element.16), channel_id=1, source_target_pairs={{0,16},{4,20},{8,24},{12,28},{16,0},{20,4},{24,8},{28,12},{32,48},... | collective-permute-start | bytes 393224 | tf_op jit(solution)/shard_map/ppermute | solution.py:114
  543.4 6.6 %collective-permute-start.9 = (f32[2,640,64]{1,2,0:T(8,128)S(1)}, f32[2,640,64]{1,2,0:T(8,128)}, u32[]{:S(2)}, u32[]{:S(2)}) collective-permute-start(f32[2,640,64]{1,2,0:T(8,128)S(1)} %get-tuple-element.20), channel_id=1, source_target_pairs={{0,32},{4,36},{8,40},{12,44},{16,48},{20,52},{24,56},{28,60},{32,0... | collective-permute-start | bytes 983048 | tf_op jit(solution)/shard_map/ppermute | solution.py:106
  551.4 7.5 %collective-permute-start.10 = (f32[1,640,64]{2,1,0:T(8,128)S(1)}, f32[1,640,64]{2,1,0:T(8,128)S(1)}, u32[]{:S(2)}, u32[]{:S(2)}) collective-permute-start(f32[1,640,64]{2,1,0:T(8,128)S(1)} %constant_dynamic-slice_fusion), channel_id=1, source_target_pairs={{0,64},{4,68},{8,72},{12,76},{16,80},{20,84},{24,88},{28,92},{32,9... | collective-permute-start | bytes 491528 | tf_op jit(solution)/shard_map/ppermute | solution.py:106
  555.2 46.6 %collective-permute-start.20 = (f32[344,64]{0,1:T(8,128)S(1)}, f32[344,64]{0,1:T(8,128)S(1)}, u32[]{:S(2)}, u32[]{:S(2)}) collective-permute-start(f32[344,64]{0,1:T(8,128)S(1)} %fusion.57), channel_id=1, source_target_pairs={{0,8},{4,12},{8,0},{12,4},{16,24},{20,28},{24,16},{28,20},{32,40},... | collective-permute-start | bytes 264200 | tf_op jit(solution)/shard_map/ppermute | solution.py:88
  576.1 17.5 %copy-start.10 = (bf16[128,4096]{1,0:T(8,128)(2,1)S(1)}, bf16[128,4096]{1,0:T(8,128)(2,1)}, u32[]{:S(2)}) copy-start(bf16[128,4096]{1,0:T(8,128)(2,1)} %all-gather.7.cloned.1.call-done) | copy-start | bytes 3145732
  593.6 2.3 copy-start.6
  593.6 2.5 copy-start.9
  596.1 27.1 %copy-start.1 = (bf16[172,256]{1,0:T(8,128)(2,1)S(1)}, bf16[172,256]{1,0:T(8,128)(2,1)}, u32[]{:S(2)}) copy-start(bf16[172,256]{1,0:T(8,128)(2,1)} %param.21) | copy-start | bytes 264196
  596.6 8.1 %collective-permute-start.14 = (f32[128,128]{1,0:T(8,128)S(1)}, f32[128,128]{1,0:T(8,128)S(1)}, u32[]{:S(2)}, u32[]{:S(2)}) collective-permute-start(f32[128,128]{1,0:T(8,128)S(1)} %pad_maximum_fusion.1), channel_id=1, source_target_pairs={{0,4},{4,0},{8,12},{12,8},{16,20},{20,16},{24,28},{28,24},{32,36},... | collective-permute-start | bytes 196616 | tf_op jit(solution)/shard_map/ppermute | solution.py:88
  601.8 5.9 collective-permute-start.21
  604.7 4.6 collective-permute-start.15
  607.7 4.2 collective-permute-start.22
  609.4 5.1 collective-permute-start.16
  611.9 5.1 collective-permute-start.23
  614.4 3.2 collective-permute-start.17
  617.6 4.9 collective-permute-start.18
Sparse Core Ops, SparseCore 0:
  13.0 53.3 all-gather.8
  143.8 20.7 all-gather.10
  166.2 24.4 all-gather.6
  198.8 52.8 all-gather.14
  253.2 29.2 all-gather.12
  329.4 29.3 all-gather.16

commit v4 on v3

--- a/solution.py
+++ b/solution.py
@@ -28,7 +28,7 @@
             out_ref[pl.ds(start, 8), :] = jnp.concatenate(picked, axis=0) / degree
             return carry
 
-        lax.fori_loop(0, block // 8, group, 0, unroll=2)
+        lax.fori_loop(0, block // 8, group, 0)
 
     return pl.pallas_call(
         kernel,
@@ -61,23 +61,18 @@
             return carry
 
         lax.fori_loop(0, nodes, step, 0, unroll=4)
-
-    first, second = pl.pallas_call(
+        first_ref[...] = (first_ref[...] + second_ref[...]) * (1.0 / degree)
+
+    return pl.pallas_call(
         kernel,
         in_specs=[
             pl.BlockSpec(memory_space=pltpu.SMEM),
             pl.BlockSpec(memory_space=pltpu.VMEM),
         ],
-        out_specs=(
-            pl.BlockSpec(memory_space=pltpu.VMEM),
-            pl.BlockSpec(memory_space=pltpu.VMEM),
-        ),
-        out_shape=(
-            jax.ShapeDtypeStruct((size, width), jnp.float32),
-            jax.ShapeDtypeStruct((size, width), jnp.float32),
-        ),
+        out_specs=pl.BlockSpec(memory_space=pltpu.VMEM),
+        out_shape=jax.ShapeDtypeStruct((size, width), jnp.float32),
+        scratch_shapes=[pltpu.VMEM((size, width), jnp.float32)],
     )(neighbours, rows)
-    return (first + second) * (1.0 / degree)
 
 
 def tree_sum(value, axis):
@@ -200,7 +195,11 @@
     back_rows = back_mean.T.astype(jnp.float32)
     spread = scatter_mean(back_rows, neighbours, span)
     grad_rows = direct.T + spread[:rows]
-    hub_back = tree_scatter(spread[rows : rows + hub_count], "dom")
+    owners = lax.axis_size("dom")
+    hub_parts = spread[rows : rows + hub_count].reshape(owners, hub_count // owners, width)
+    hub_back = jnp.sum(
+        lax.all_to_all(hub_parts, "dom", split_axis=0, concat_axis=0, tiled=True), axis=0
+    )
     grad_rows = grad_rows.at[hub_rows].add(hub_back)
     base = rows + hub_count
     for bit_index in range(send_rows.shape[0]):

time: 634 us -> 631 us (level)
  other arithmetic: 83.5 us -> 67.4 us
  waiting for transfers between devices: 189 us -> 202 us
  Pallas kernels: 207 us -> 216 us
    all_to_all x0 -> x1, waiting for transfers between devices: none -> 47.1 us  [body(): lax.all_to_all(hub_parts, 'dom', split_axis=0, concat_axis=0, tiled=True)]
    ppermute x5 -> x0, waiting for transfers between devices: 40.3 us -> none  [tree_scatter(): parts = keep + lax.ppermute(send, axis, pairs)]
    dynamic_slice x5 -> x0, local copies, waits for them, and re-layouts: 16 us -> none  [the longest x4 10.5 us: tree_scatter(): keep = lax.dynamic_index_in_dim(paired, bit, axis=1, keepdims=False)]
    ppermute x5 -> x0, starting transfers between devices: 9.33 us -> none  [tree_scatter(): parts = keep + lax.ppermute(send, axis, pairs)]
    reshape x0 -> x1, local copies, waits for them, and re-layouts: none -> 9.19 us  [body(): spread[rows:rows + hub_count].reshape(owners, hub_count // owners, width)]
    slice x1, local copies, waits for them, and re-layouts: 0.72 us -> 8.9 us  [body(): spread[rows:rows + hub_count].reshape(owners, hub_count // owners, width)]
    all_to_all x0 -> x1, starting transfers between devices: none -> 8.01 us  [body(): lax.all_to_all(hub_parts, 'dom', split_axis=0, concat_axis=0, tiled=True)]
    ppermute x10, starting transfers between devices: 21 us -> 13.9 us  [tree_sum(): value = value + lax.ppermute(value, axis, pairs)]
  transfers between devices with their start and end apart: 30 -> 26, of which waited for: 14 -> 11; matrix products, arithmetic and copies ran while one was open for 17% -> 16% of each run, Pallas kernels for 9% -> 10%
where the time goes in v4:
time: 631 us; the launch traced here: 626 us
  Pallas kernels  216 us (34%)
  waiting for transfers between devices  202 us (32%)
  local copies, waits for them, and re-layouts  68.8 us (11%)
  other arithmetic  67.4 us (11%)
  starting transfers between devices  40 us (6%)
  matrix products  17.7 us (3%)
  between operations  14.6 us (2%)
    pallas_call x2, Pallas kernels, gather_mean(): pl.pallas_call(kernel, grid_spec=pltpu.PrefetchScalarGridSpec(num_scalar_...  123 us
    pallas_call x1, Pallas kernels, scatter_mean(): pl.pallas_call(kernel, in_specs=[pl.BlockSpec(memory_space=pltpu.SMEM), p...  93 us
    all_gather x2, waiting for transfers between devices, source_table(): hub_all = lax.all_gather(hub_local, 'dom', axis=0, tiled=True)  70.5 us
    all_gather x2, waiting for transfers between devices, widen(): lax.all_gather(second_rows, 'feat', axis=0, tiled=True)  47.5 us
    all_to_all x1, waiting for transfers between devices, body(): lax.all_to_all(hub_parts, 'dom', split_axis=0, concat_axis=0, tiled=True)  47.1 us
    all_gather x2, waiting for transfers between devices, widen(): lax.all_gather(first_rows, 'feat', axis=0, tiled=True)  24 us
    scatter-add x3, other arithmetic, body(): grad_rows.at[send_rows[bit_index]].add(returned.astype(jnp.float32))  21.6 us
    gather x6, local copies, waits for them, and re-layouts, source_table(): jnp.take(local_rows, send_rows[bit_index], axis=0)  19.2 us
  transfers between devices with their start and end apart: 26, of which 11 were waited for; matrix products, arithmetic and copies ran while one was open for 16% of the time, Pallas kernels for 10%

profile of v4, /device:TPU:1, one launch (start us, length us, event | category | flops | bytes accessed | tf_op | source)
XLA Modules:
  0.0 625.9 jit_solution(17807414848764110410)
XLA Ops:
  10.9 2.0 gather_fusion
  13.8 3.2 gather_fusion.2
  18.7 3.2 gather_fusion.3
  22.1 1.8 collective-permute-start.1
  24.0 3.2 gather_fusion.4
  27.4 3.4 collective-permute-start.2
  31.8 35.4 %all-gather.9.cloned.1.call-done = bf16[20480,32]{1,0:T(8,128)(2,1)} async-done(((bf16[640,32]{1,0:T(8,128)(2,1)}), bf16[20480,32]{1,0:T(8,128)(2,1)}) %all-gather.9.cloned.1.call-update) | async-done | bytes 1310736 | tf_op jit(solution)/shard_map/all_gather | solution.py:131
  67.2 5.3 constant_dynamic-update-slice_fusion.3
  74.7 8.5 %convert_element_type.52.tab_ref = f32[27648,32]{1,0:T(8,128)} convert(bf16[27648,32]{1,0:T(8,128)(2,1)} %constant_dynamic-update-slice_fusion) | non-fusion elementwise | flops 884736 | bytes 5308416 | tf_op jit(solution)/shard_map/convert_element_type | solution.py:124
  83.3 61.3 %shard_map.120 = f32[4096,32]{1,0:T(8,128)} custom-call(s32[8,4096]{1,0:T(8,128)} %nb_ref.5, f32[27648,32]{1,0:T(8,128)} %convert_element_type.52.tab_ref), custom_call_target="tpu_custom_call" | custom-call | tf_op jit(solution)/shard_map/pallas_call | solution.py:33
  148.1 20.1 %all-gather.11.cloned.1.call-done = bf16[128,4096]{1,0:T(8,128)(2,1)} async-done(((bf16[32,4096]{1,0:T(8,128)(2,1)}), bf16[128,4096]{1,0:T(8,128)(2,1)}) %all-gather.11.cloned.1.call-update) | async-done | bytes 1048592 | tf_op jit(solution)/shard_map/all_gather | solution.py:119
  170.4 24.0 %all-gather.7.cloned.1.call-done = bf16[128,4096]{1,0:T(8,128)(2,1)} async-done(((bf16[32,4096]{1,0:T(8,128)(2,1)}), bf16[128,4096]{1,0:T(8,128)(2,1)}) %all-gather.7.cloned.1.call-update) | async-done | bytes 1048592 | tf_op jit(solution)/shard_map/all_gather | solution.py:118
  194.4 2.7 fusion.7
  197.1 3.2 copy.84
  200.3 3.0 constant_dynamic-update-slice_fusion.9
  203.2 2.0 gather_fusion.1
  206.1 3.2 gather_fusion.7
  209.3 3.2 gather_fusion.6
  212.5 3.2 gather_fusion.5
  217.5 3.1 collective-permute-start.3
  220.8 2.7 collective-permute-start.5
  223.8 35.1 %all-gather.15.cloned.1.call-done = bf16[20480,64]{1,0:T(8,128)(2,1)} async-done(((bf16[640,64]{1,0:T(8,128)(2,1)}), bf16[20480,64]{1,0:T(8,128)(2,1)}) %all-gather.15.cloned.1.call-update) | async-done | bytes 2621456 | tf_op jit(solution)/shard_map/all_gather | solution.py:131
  258.8 5.3 constant_dynamic-update-slice_fusion.8
  266.3 8.6 %convert_element_type.57.tab_ref = f32[27648,64]{1,0:T(8,128)} convert(bf16[27648,64]{1,0:T(8,128)(2,1)} %constant_dynamic-update-slice_fusion.5) | non-fusion elementwise | flops 1769472 | bytes 10616832 | tf_op jit(solution)/shard_map/convert_element_type | solution.py:124
  274.9 61.4 %shard_map.121 = f32[4096,64]{1,0:T(8,128)} custom-call(s32[8,4096]{1,0:T(8,128)} %nb_ref.5, f32[27648,64]{1,0:T(8,128)} %convert_element_type.57.tab_ref), custom_call_target="tpu_custom_call" | custom-call | tf_op jit(solution)/shard_map/pallas_call | solution.py:33
  339.3 2.1 fusion.34
  341.4 27.4 %all-gather.17.cloned.1.call-done = bf16[256,4096]{1,0:T(8,128)(2,1)} async-done(((bf16[64,4096]{1,0:T(8,128)(2,1)}), bf16[256,4096]{1,0:T(8,128)(2,1)}) %all-gather.17.cloned.1.call-update) | async-done | bytes 2097168 | tf_op jit(solution)/shard_map/all_gather | solution.py:119
  368.8 2.3 fusion.33
  374.2 93.0 %shard_map.122 = f32[27648,64]{1,0:T(8,128)} custom-call(s32[8,4096]{1,0:T(8,128)} %nb_ref.5, f32[4096,64]{1,0:T(8,128)} %convert_element_type.63.rows_ref), custom_call_target="tpu_custom_call" | custom-call | tf_op jit(solution)/shard_map/pallas_call | solution.py:66
  467.2 8.9 %slice.74 = f32[20480,64]{1,0:T(8,128)} slice(f32[27648,64]{1,0:T(8,128)} %shard_map.122), slice={[4096:24576], [0:64]} | slice | bytes 10485760 | tf_op jit(solution)/shard_map/slice | solution.py:199
  476.1 9.2 %copy.89 = f32[32,640,64]{1,2,0:T(8,128)} copy(f32[32,640,64]{2,1,0:T(8,128)} %bitcast.63) | data formatting | bytes 10485760 | tf_op jit(solution)/shard_map/reshape | solution.py:199
  485.3 8.0 %all-to-all-start = ((f32[32,640,64]{1,2,0:T(8,128)}), f32[32,640,64]{1,2,0:T(8,128)}, u32[]{:S(2)}, u32[]{:S(2)}) async-start(f32[32,640,64]{1,2,0:T(8,128)} %copy.89), calls=%async_computation | async-start | bytes 10485760 | tf_op jit(solution)/shard_map/all_to_all | solution.py:201
  493.4 6.1 convert.5
  501.2 3.8 convolution_add_fusion.1
  505.9 3.0 collective-permute-start.8
  511.4 47.1 %all-to-all-done = f32[32,640,64]{1,2,0:T(8,128)} async-done(((f32[32,640,64]{1,2,0:T(8,128)}), f32[32,640,64]{1,2,0:T(8,128)}, u32[]{:S(2)}, u32[]{:S(2)}) %all-to-all-start) | async-done | bytes 5242912 | tf_op jit(solution)/shard_map/all_to_all | solution.py:201
  558.5 2.8 reduce_sum.19
  561.4 6.8 %scatter_fusion = f32[4096,64]{1,0:T(8,128)S(1)} fusion(f32[4096,64]{1,0:T(8,128)S(1)} %copy-done.2, s32[640]{0:T(1024)S(1)} %compare_select_fusion.6, f32[640,64]{1,0:T(8,128)S(1)} %copy.90), kind=kCustom, calls=%fused_computation.8 | custom fusion | flops 40960 | bytes 494080 | tf_op jit(solution)/shard_map/scatter-add | solution.py:203
  568.2 7.2 %scatter_custom_fusion.1 = f32[4096,64]{1,0:T(8,128)S(1)} fusion(f32[4096,64]{1,0:T(8,128)S(1)} %scatter_fusion, s32[1024]{0:T(1024)S(1)} %bitcast.72, bf16[1024,64]{1,0:T(8,128)(2,1)} %collective-permute-done.6), kind=kCustom, calls=%fused_computation.33 | custom fusion | flops 131072 | bytes 1179648 | tf_op jit(solution)/shard_map/scatter-add | solution.py:210
  575.4 7.2 %scatter_custom_fusion.2 = f32[4096,64]{1,0:T(8,128)S(1)} fusion(f32[4096,64]{1,0:T(8,128)S(1)} %scatter_custom_fusion.1, s32[1024]{0:T(1024)S(1)} %bitcast.71, bf16[1024,64]{1,0:T(8,128)(2,1)} %collective-permute-done.7), kind=kCustom, calls=%fused_computation.31 | custom fusion | flops 131072 | bytes 1179648 | tf_op jit(solution)/shard_map/scatter-add | solution.py:210
  582.6 7.2 %scatter_custom_fusion.3 = f32[4096,64]{1,0:T(8,128)S(1)} fusion(f32[4096,64]{1,0:T(8,128)S(1)} %scatter_custom_fusion.2, s32[1024]{0:T(1024)S(1)} %bitcast.70, bf16[1024,64]{1,0:T(8,128)(2,1)} %collective-permute-done.8), kind=kCustom, calls=%fused_computation.29 | custom fusion | flops 131072 | bytes 1179648 | tf_op jit(solution)/shard_map/scatter-add | solution.py:210
  590.2 1.8 fusion.24
  592.0 1.7 fusion.26
  595.1 6.5 %collective-permute-start.10 = (f32[128,128]{1,0:T(8,128)S(1)}, f32[128,128]{1,0:T(8,128)S(1)}, u32[]{:S(2)}, u32[]{:S(2)}) collective-permute-start(f32[128,128]{1,0:T(8,128)S(1)} %fusion.23), channel_id=1, source_target_pairs={{0,8},{4,12},{8,0},{12,4},{16,24},{20,28},{24,16},{28,20},{32,40},... | collective-permute-start | bytes 196616 | tf_op jit(solution)/shard_map/ppermute | solution.py:83
  601.6 3.5 collective-permute-done.10
  605.2 3.4 collective-permute-start.11
  610.3 3.3 collective-permute-done.18
  615.9 2.4 collective-permute-done.13
  (115 shorter events, 38.6 us)
Async XLA Ops:
  7.2 361.6 %copy-start = (bf16[172,256]{1,0:T(8,128)(2,1)S(1)}, bf16[172,256]{1,0:T(8,128)(2,1)}, u32[]{:S(2)}) copy-start(bf16[172,256]{1,0:T(8,128)(2,1)} %param.21) | copy-start | bytes 264196
  7.2 60.1 %all-gather.9.cloned.1.call-start = ((), (), s32[]{:S(2)}) async-start(), calls=%async_computation.2 | async-start | bytes 5406720 | tf_op jit(solution)/shard_map/all_gather | solution.py:131
  13.7 154.5 %all-gather.11.cloned.1.call-start = ((), (), s32[]{:S(2)}) async-start(), calls=%async_computation.3 | async-start | bytes 1310720 | tf_op jit(solution)/shard_map/all_gather | solution.py:119
  17.2 55.3 %collective-permute-start = (bf16[1024,32]{1,0:T(8,128)(2,1)S(1)}, bf16[1024,32]{1,0:T(8,128)(2,1)S(1)}, u32[]{:S(2)}, u32[]{:S(2)}) collective-permute-start(bf16[1024,32]{1,0:T(8,128)(2,1)S(1)} %broadcast_select_fusion.5), channel_id=1, source_target_pairs={{0,4},{4,0},{8,12},{12,8},{16,20},{20,16},{24,28},{28,24},{32,36},... | collective-permute-start | bytes 196616 | tf_op jit(solution)/shard_map/ppermute | solution.py:109
  22.1 51.1 %collective-permute-start.1 = (bf16[1024,32]{1,0:T(8,128)(2,1)S(1)}, bf16[1024,32]{1,0:T(8,128)(2,1)S(1)}, u32[]{:S(2)}, u32[]{:S(2)}) collective-permute-start(bf16[1024,32]{1,0:T(8,128)(2,1)S(1)} %broadcast_select_fusion.4), channel_id=1, source_target_pairs={{0,8},{4,12},{8,0},{12,4},{16,24},{20,28},{24,16},{28,20},{32,40},... | collective-permute-start | bytes 196616 | tf_op jit(solution)/shard_map/ppermute | solution.py:109
  27.4 46.6 %collective-permute-start.2 = (bf16[1024,32]{1,0:T(8,128)(2,1)S(1)}, bf16[1024,32]{1,0:T(8,128)(2,1)S(1)}, u32[]{:S(2)}, u32[]{:S(2)}) collective-permute-start(bf16[1024,32]{1,0:T(8,128)(2,1)S(1)} %broadcast_select_fusion.3), channel_id=1, source_target_pairs={{0,16},{4,20},{8,24},{12,28},{16,0},{20,4},{24,8},{28,12},{32,48},... | collective-permute-start | bytes 196616 | tf_op jit(solution)/shard_map/ppermute | solution.py:109
  144.6 23.7 %copy-start.7 = (bf16[64,128]{1,0:T(8,128)(2,1)S(1)}, bf16[64,128]{1,0:T(8,128)(2,1)}, u32[]{:S(2)}) copy-start(bf16[64,128]{1,0:T(8,128)(2,1)} %param.19) | copy-start | bytes 49156
  147.3 47.1 %copy-start.8 = (bf16[64,128]{1,0:T(8,128)(2,1)S(1)}, bf16[64,128]{1,0:T(8,128)(2,1)}, u32[]{:S(2)}) copy-start(bf16[64,128]{1,0:T(8,128)(2,1)} %param.18) | copy-start | bytes 49156
  147.3 47.0 %all-gather.7.cloned.1.call-start = ((), (), s32[]{:S(2)}) async-start(), calls=%async_computation.1 | async-start | bytes 1310720 | tf_op jit(solution)/shard_map/all_gather | solution.py:118
  148.1 110.7 %all-gather.15.cloned.1.call-start = ((), (), s32[]{:S(2)}) async-start(), calls=%async_computation.5 | async-start | bytes 5406720 | tf_op jit(solution)/shard_map/all_gather | solution.py:131
  206.1 133.2 %all-gather.13.cloned.1.call-start = ((), (), s32[]{:S(2)}) async-start(), calls=%async_computation.4 | async-start | bytes 2621440 | tf_op jit(solution)/shard_map/all_gather | solution.py:118
  216.0 48.9 %collective-permute-start.4 = (bf16[1024,64]{1,0:T(8,128)(2,1)S(1)}, bf16[1024,64]{1,0:T(8,128)(2,1)S(1)}, u32[]{:S(2)}, u32[]{:S(2)}) collective-permute-start(bf16[1024,64]{1,0:T(8,128)(2,1)S(1)} %broadcast_select_fusion.1), channel_id=1, source_target_pairs={{0,8},{4,12},{8,0},{12,4},{16,24},{20,28},{24,16},{28,20},{32,40},... | collective-permute-start | bytes 393224 | tf_op jit(solution)/shard_map/ppermute | solution.py:109
  217.5 46.6 %collective-permute-start.3 = (bf16[1024,64]{1,0:T(8,128)(2,1)S(1)}, bf16[1024,64]{1,0:T(8,128)(2,1)S(1)}, u32[]{:S(2)}, u32[]{:S(2)}) collective-permute-start(bf16[1024,64]{1,0:T(8,128)(2,1)S(1)} %broadcast_select_fusion.2), channel_id=1, source_target_pairs={{0,4},{4,0},{8,12},{12,8},{16,20},{20,16},{24,28},{28,24},{32,36},... | collective-permute-start | bytes 393224 | tf_op jit(solution)/shard_map/ppermute | solution.py:109
  220.8 44.7 %collective-permute-start.5 = (bf16[1024,64]{1,0:T(8,128)(2,1)S(1)}, bf16[1024,64]{1,0:T(8,128)(2,1)S(1)}, u32[]{:S(2)}, u32[]{:S(2)}) collective-permute-start(bf16[1024,64]{1,0:T(8,128)(2,1)S(1)} %broadcast_select_fusion), channel_id=1, source_target_pairs={{0,16},{4,20},{8,24},{12,28},{16,0},{20,4},{24,8},{28,12},{32,48},... | collective-permute-start | bytes 393224 | tf_op jit(solution)/shard_map/ppermute | solution.py:109
  223.5 145.3 %all-gather.17.cloned.1.call-start = ((), (), s32[]{:S(2)}) async-start(), calls=%async_computation.6 | async-start | bytes 2621440 | tf_op jit(solution)/shard_map/all_gather | solution.py:119
  336.3 3.0 copy-start.5
  341.4 29.7 %copy-start.9 = (s32[4096]{0:T(1024)S(1)}, s32[4096]{0:T(1024)}, u32[]{:S(2)}) copy-start(s32[4096]{0:T(1024)} %param.17) | copy-start | bytes 49156
  485.3 8.0 %copy-start.6 = (s32[3,1024]{1,0:T(4,128)S(1)}, s32[3,1024]{1,0:T(4,128)}, u32[]{:S(2)}) copy-start(s32[3,1024]{1,0:T(4,128)} %param.16) | copy-start | bytes 36868
  485.3 73.2 %all-to-all-start = ((f32[32,640,64]{1,2,0:T(8,128)}), f32[32,640,64]{1,2,0:T(8,128)}, u32[]{:S(2)}, u32[]{:S(2)}) async-start(f32[32,640,64]{1,2,0:T(8,128)} %copy.89), calls=%async_computation | async-start | bytes 10485760 | tf_op jit(solution)/shard_map/all_to_all | solution.py:201
  493.4 6.1 copy-start.4
  493.4 6.7 %copy-start.3 = (f32[4096,64]{1,0:T(8,128)S(1)}, f32[4096,64]{1,0:T(8,128)}, u32[]{:S(2)}) copy-start(f32[4096,64]{1,0:T(8,128)} %shard_map.121) | copy-start | bytes 3145732
  500.8 8.9 %collective-permute-start.14 = (f32[344,64]{0,1:T(8,128)S(1)}, f32[344,64]{0,1:T(8,128)S(1)}, u32[]{:S(2)}, u32[]{:S(2)}) collective-permute-start(f32[344,64]{0,1:T(8,128)S(1)} %pad_maximum_fusion), channel_id=1, source_target_pairs={{0,4},{4,0},{8,12},{12,8},{16,20},{20,16},{24,28},{28,24},{32,36},... | collective-permute-start | bytes 264200 | tf_op jit(solution)/shard_map/ppermute | solution.py:83
  505.9 76.8 %collective-permute-start.8 = (bf16[1024,64]{1,0:T(8,128)(2,1)}, bf16[1024,64]{1,0:T(8,128)(2,1)}, u32[]{:S(2)}, u32[]{:S(2)}) collective-permute-start(bf16[1024,64]{1,0:T(8,128)(2,1)} %get-tuple-element.8), channel_id=1, source_target_pairs={{0,16},{4,20},{8,24},{12,28},{16,0},{20,4},{24,8},{28,12},{32,48},... | collective-permute-start | bytes 393224 | tf_op jit(solution)/shard_map/ppermute | solution.py:109
  508.8 66.6 %collective-permute-start.7 = (bf16[1024,64]{1,0:T(8,128)(2,1)}, bf16[1024,64]{1,0:T(8,128)(2,1)}, u32[]{:S(2)}, u32[]{:S(2)}) collective-permute-start(bf16[1024,64]{1,0:T(8,128)(2,1)} %get-tuple-element.9), channel_id=1, source_target_pairs={{0,8},{4,12},{8,0},{12,4},{16,24},{20,28},{24,16},{28,20},{32,40},... | collective-permute-start | bytes 393224 | tf_op jit(solution)/shard_map/ppermute | solution.py:109
  509.1 59.1 %collective-permute-start.6 = (bf16[1024,64]{1,0:T(8,128)(2,1)}, bf16[1024,64]{1,0:T(8,128)(2,1)}, u32[]{:S(2)}, u32[]{:S(2)}) collective-permute-start(bf16[1024,64]{1,0:T(8,128)(2,1)} %get-tuple-element.10), channel_id=1, source_target_pairs={{0,4},{4,0},{8,12},{12,8},{16,20},{20,16},{24,28},{28,24},{32,36},... | collective-permute-start | bytes 393224 | tf_op jit(solution)/shard_map/ppermute | solution.py:109
  509.9 51.5 %copy-start.2 = (f32[4096,64]{1,0:T(8,128)S(1)}, f32[4096,64]{1,0:T(8,128)}, u32[]{:S(2)}) copy-start(f32[4096,64]{1,0:T(8,128)} %convolution_add_fusion.1) | copy-start | bytes 3145732
  509.9 83.9 %collective-permute-start.15 = (f32[344,64]{0,1:T(8,128)S(1)}, f32[344,64]{0,1:T(8,128)S(1)}, u32[]{:S(2)}, u32[]{:S(2)}) collective-permute-start(f32[344,64]{0,1:T(8,128)S(1)} %fusion.52), channel_id=1, source_target_pairs={{0,8},{4,12},{8,0},{12,4},{16,24},{20,28},{24,16},{28,20},{32,40},... | collective-permute-start | bytes 264200 | tf_op jit(solution)/shard_map/ppermute | solution.py:83
  590.2 28.8 %copy-start.1 = (bf16[172,256]{1,0:T(8,128)(2,1)S(1)}, bf16[172,256]{1,0:T(8,128)(2,1)}, u32[]{:S(2)}) copy-start(bf16[172,256]{1,0:T(8,128)(2,1)} %param.21) | copy-start | bytes 264196
  593.7 1.3 collective-permute-start.9
  593.8 7.7 %collective-permute-start.16 = (f32[344,64]{0,1:T(8,128)S(1)}, f32[344,64]{0,1:T(8,128)S(1)}, u32[]{:S(2)}, u32[]{:S(2)}) collective-permute-start(f32[344,64]{0,1:T(8,128)S(1)} %add.127), channel_id=1, source_target_pairs={{0,16},{4,20},{8,24},{12,28},{16,0},{20,4},{24,8},{28,12},{32,48},... | collective-permute-start | bytes 264200 | tf_op jit(solution)/shard_map/ppermute | solution.py:83
  595.1 10.1 %collective-permute-start.10 = (f32[128,128]{1,0:T(8,128)S(1)}, f32[128,128]{1,0:T(8,128)S(1)}, u32[]{:S(2)}, u32[]{:S(2)}) collective-permute-start(f32[128,128]{1,0:T(8,128)S(1)} %fusion.23), channel_id=1, source_target_pairs={{0,8},{4,12},{8,0},{12,4},{16,24},{20,28},{24,16},{28,20},{32,40},... | collective-permute-start | bytes 196616 | tf_op jit(solution)/shard_map/ppermute | solution.py:83
  601.5 7.0 %collective-permute-start.17 = (f32[344,64]{0,1:T(8,128)S(1)}, f32[344,64]{0,1:T(8,128)S(1)}, u32[]{:S(2)}, u32[]{:S(2)}) collective-permute-start(f32[344,64]{0,1:T(8,128)S(1)} %add.128), channel_id=1, source_target_pairs={{0,32},{4,36},{8,40},{12,44},{16,48},{20,52},{24,56},{28,60},{32,0... | collective-permute-start | bytes 264200 | tf_op jit(solution)/shard_map/ppermute | solution.py:83
  605.2 5.0 collective-permute-start.11
  608.6 5.1 collective-permute-start.18
  610.2 3.4 collective-permute-start.12
  613.7 4.7 collective-permute-start.13
Sparse Core Ops, SparseCore 0:
  13.9 53.3 all-gather.8
  147.5 20.7 all-gather.10
  169.9 24.4 all-gather.6
  206.2 52.5 all-gather.14
  260.3 29.2 all-gather.12
  339.4 29.3 all-gather.16

commit v5 on v4

--- a/solution.py
+++ b/solution.py
@@ -185,7 +185,6 @@
     logit_grad = class_gradient(logits, labels, nodes_all)
     grad_outer_self = contract(logit_grad, hidden)
     grad_outer_neighbour = contract(logit_grad, mean_two)
-    outer_both = tree_sum(jnp.concatenate([grad_outer_self, grad_outer_neighbour], axis=0), "dom")
     direct = transpose_times(self_cols, logit_grad)
     back_mean = transpose_times(neigh_cols, logit_grad).astype(jnp.bfloat16)
     degree = neighbours.shape[0]
@@ -198,23 +197,32 @@
     owners = lax.axis_size("dom")
     hub_parts = spread[rows : rows + hub_count].reshape(owners, hub_count // owners, width)
     hub_back = jnp.sum(
-        lax.all_to_all(hub_parts, "dom", split_axis=0, concat_axis=0, tiled=True), axis=0
-    )
-    grad_rows = grad_rows.at[hub_rows].add(hub_back)
+        lax.all_to_all(
+            hub_parts.astype(jnp.bfloat16), "dom", split_axis=0, concat_axis=0, tiled=True
+        ).astype(jnp.float32),
+        axis=0,
+    )
     base = rows + hub_count
+    landed = [hub_back]
     for bit_index in range(send_rows.shape[0]):
         outgoing = spread[base + bit_index * band : base + (bit_index + 1) * band].astype(
             jnp.bfloat16
         )
-        returned = trade(outgoing, bit_index)
-        grad_rows = grad_rows.at[send_rows[bit_index]].add(returned.astype(jnp.float32))
+        landed.append(trade(outgoing, bit_index).astype(jnp.float32))
+    targets = jnp.concatenate([hub_rows, send_rows.reshape(-1)])
+    grad_rows = grad_rows.at[targets].add(jnp.concatenate(landed, axis=0))
     grad_hidden = grad_rows.T
     grad_pre = jnp.where(hidden > 0, grad_hidden, 0.0).astype(jnp.bfloat16)
     grad_inner_self = contract(grad_pre, full_input)
     grad_inner_neighbour = contract(grad_pre, full_mean)
-    inner_both = tree_sum(jnp.concatenate([grad_inner_self, grad_inner_neighbour], axis=0), "dom")
-    classes = outer_self.shape[0]
-    return (inner_both[:width], inner_both[width:], outer_both[:classes], outer_both[classes:])
+    pieces = (grad_inner_self, grad_inner_neighbour, grad_outer_self, grad_outer_neighbour)
+    summed = tree_sum(jnp.concatenate([piece.reshape(-1) for piece in pieces]), "dom")
+    results = []
+    offset = 0
+    for piece in pieces:
+        results.append(summed[offset : offset + piece.size].reshape(piece.shape))
+        offset += piece.size
+    return tuple(results)
 
 
 def solution(mesh):

time: 631 us -> 603 us (0.956)
  waiting for transfers between devices: 202 us -> 189 us
  local copies, waits for them, and re-layouts: 68.8 us -> 60.7 us
  starting transfers between devices: 40 us -> 32.8 us
    all_to_all x1, waiting for transfers between devices: 47.1 us -> 0.01 us  [body(): lax.all_to_all(hub_parts.astype(jnp.bfloat16), 'dom', split_axis=0, conca...]
    ppermute x9, waiting for transfers between devices: 0.02 us -> 28.2 us  [partner(): return lax.ppermute(value, axis, pairs)]
    reshape x1 -> x2, local copies, waits for them, and re-layouts: 9.19 us -> 0.16 us  [body(): piece.reshape(-1)]
    convert_element_type x0 -> x2, local copies, waits for them, and re-layouts: none -> 7.3 us  [the longest x1 6.14 us: body(): hub_parts.astype(jnp.bfloat16)]
    ppermute x10 -> x5, starting transfers between devices: 13.9 us -> 6.71 us  [tree_sum(): value = value + lax.ppermute(value, axis, pairs)]
    ppermute x10 -> x5, waiting for transfers between devices: 11.7 us -> 16.6 us  [tree_sum(): value = value + lax.ppermute(value, axis, pairs)]
    unnamed x28 -> x40, local copies, waits for them, and re-layouts: 16 us -> 18.9 us
    scatter-add x4 -> x1, other arithmetic: 28.4 us -> 25.7 us  [body(): grad_rows = grad_rows.at[targets].add(jnp.concatenate(landed, axis=0))]
  transfers between devices with their start and end apart: 26 -> 21, of which waited for: 11 -> 12; matrix products, arithmetic and copies ran while one was open for 16% -> 11% of each run, Pallas kernels for 10% -> 10%
where the time goes in v5:
time: 603 us; the launch traced here: 598 us
  Pallas kernels  216 us (36%)
  waiting for transfers between devices  189 us (31%)
  other arithmetic  67.4 us (11%)
  local copies, waits for them, and re-layouts  60.7 us (10%)
  starting transfers between devices  32.8 us (5%)
  matrix products  17.8 us (3%)
  between operations  14.6 us (2%)
    pallas_call x2, Pallas kernels, gather_mean(): pl.pallas_call(kernel, grid_spec=pltpu.PrefetchScalarGridSpec(num_scalar_...  123 us
    pallas_call x1, Pallas kernels, scatter_mean(): pl.pallas_call(kernel, in_specs=[pl.BlockSpec(memory_space=pltpu.SMEM), p...  93 us
    all_gather x2, waiting for transfers between devices, source_table(): hub_all = lax.all_gather(hub_local, 'dom', axis=0, tiled=True)  72 us
    all_gather x2, waiting for transfers between devices, widen(): lax.all_gather(second_rows, 'feat', axis=0, tiled=True)  47.4 us
    ppermute x9, waiting for transfers between devices, partner(): return lax.ppermute(value, axis, pairs)  28.2 us
    scatter-add x1, other arithmetic, body(): grad_rows = grad_rows.at[targets].add(jnp.concatenate(landed, axis=0))  25.7 us
    all_gather x2, waiting for transfers between devices, widen(): lax.all_gather(first_rows, 'feat', axis=0, tiled=True)  24.5 us
    gather x6, local copies, waits for them, and re-layouts, source_table(): jnp.take(local_rows, send_rows[bit_index], axis=0)  19.2 us
  transfers between devices with their start and end apart: 21, of which 12 were waited for; matrix products, arithmetic and copies ran while one was open for 11% of the time, Pallas kernels for 10%

profile of v5, /device:TPU:1, one launch (start us, length us, event | category | flops | bytes accessed | tf_op | source)
XLA Modules:
  0.0 598.4 jit_solution(797625571410847799)
XLA Ops:
  10.9 2.0 gather_fusion
  13.8 3.2 gather_fusion.2
  18.7 3.2 gather_fusion.3
  22.1 1.8 collective-permute-start.1
  24.0 3.2 gather_fusion.4
  27.4 3.4 collective-permute-start.2
  31.8 35.4 %all-gather.9.cloned.1.call-done = bf16[20480,32]{1,0:T(8,128)(2,1)} async-done(((bf16[640,32]{1,0:T(8,128)(2,1)}), bf16[20480,32]{1,0:T(8,128)(2,1)}) %all-gather.9.cloned.1.call-update) | async-done | bytes 1310736 | tf_op jit(solution)/shard_map/all_gather | solution.py:131
  67.2 5.3 constant_dynamic-update-slice_fusion.3
  74.7 8.5 %convert_element_type.59.tab_ref = f32[27648,32]{1,0:T(8,128)} convert(bf16[27648,32]{1,0:T(8,128)(2,1)} %constant_dynamic-update-slice_fusion) | non-fusion elementwise | flops 884736 | bytes 5308416 | tf_op jit(solution)/shard_map/convert_element_type | solution.py:124
  83.2 61.3 %shard_map.120 = f32[4096,32]{1,0:T(8,128)} custom-call(s32[8,4096]{1,0:T(8,128)} %nb_ref.5, f32[27648,32]{1,0:T(8,128)} %convert_element_type.59.tab_ref), custom_call_target="tpu_custom_call" | custom-call | tf_op jit(solution)/shard_map/pallas_call | solution.py:33
  148.1 20.1 %all-gather.11.cloned.1.call-done = bf16[128,4096]{1,0:T(8,128)(2,1)} async-done(((bf16[32,4096]{1,0:T(8,128)(2,1)}), bf16[128,4096]{1,0:T(8,128)(2,1)}) %all-gather.11.cloned.1.call-update) | async-done | bytes 1048592 | tf_op jit(solution)/shard_map/all_gather | solution.py:119
  169.9 24.4 %all-gather.7.cloned.1.call-done = bf16[128,4096]{1,0:T(8,128)(2,1)} async-done(((bf16[32,4096]{1,0:T(8,128)(2,1)}), bf16[128,4096]{1,0:T(8,128)(2,1)}) %all-gather.7.cloned.1.call-update) | async-done | bytes 1048592 | tf_op jit(solution)/shard_map/all_gather | solution.py:118
  194.3 1.8 fusion.7
  196.1 3.3 constant_dynamic-update-slice_fusion.9
  199.4 2.0 gather_fusion.1
  202.3 3.2 gather_fusion.5
  205.5 3.2 gather_fusion.6
  208.7 3.2 gather_fusion.7
  213.3 2.8 collective-permute-start.3
  217.9 2.7 collective-permute-start.5
  220.8 36.6 %all-gather.15.cloned.1.call-done = bf16[20480,64]{1,0:T(8,128)(2,1)} async-done(((bf16[640,64]{1,0:T(8,128)(2,1)}), bf16[20480,64]{1,0:T(8,128)(2,1)}) %all-gather.15.cloned.1.call-update) | async-done | bytes 2621456 | tf_op jit(solution)/shard_map/all_gather | solution.py:131
  257.4 5.3 constant_dynamic-update-slice_fusion.8
  264.9 8.6 %convert_element_type.64.tab_ref = f32[27648,64]{1,0:T(8,128)} convert(bf16[27648,64]{1,0:T(8,128)(2,1)} %constant_dynamic-update-slice_fusion.5) | non-fusion elementwise | flops 1769472 | bytes 10616832 | tf_op jit(solution)/shard_map/convert_element_type | solution.py:124
  273.5 61.4 %shard_map.121 = f32[4096,64]{1,0:T(8,128)} custom-call(s32[8,4096]{1,0:T(8,128)} %nb_ref.5, f32[27648,64]{1,0:T(8,128)} %convert_element_type.64.tab_ref), custom_call_target="tpu_custom_call" | custom-call | tf_op jit(solution)/shard_map/pallas_call | solution.py:33
  337.8 2.1 fusion.35
  340.0 27.3 %all-gather.17.cloned.1.call-done = bf16[256,4096]{1,0:T(8,128)(2,1)} async-done(((bf16[64,4096]{1,0:T(8,128)(2,1)}), bf16[256,4096]{1,0:T(8,128)(2,1)}) %all-gather.17.cloned.1.call-update) | async-done | bytes 2097168 | tf_op jit(solution)/shard_map/all_gather | solution.py:119
  367.3 2.3 fusion.33
  372.7 93.0 %shard_map.122 = f32[27648,64]{1,0:T(8,128)} custom-call(s32[8,4096]{1,0:T(8,128)} %nb_ref.5, f32[4096,64]{1,0:T(8,128)} %convert_element_type.70.rows_ref), custom_call_target="tpu_custom_call" | custom-call | tf_op jit(solution)/shard_map/pallas_call | solution.py:66
  465.7 5.7 convert.6
  471.4 3.3 slice.116
  475.9 6.1 %copy.100 = bf16[32,640,64]{1,2,0:T(8,128)(2,1)} copy(bf16[32,640,64]{2,1,0:T(8,128)(2,1)} %bitcast.66) | data formatting | bytes 5242880 | tf_op jit(solution)/shard_map/convert_element_type | solution.py:201
  482.1 8.0 %all-to-all-start = ((bf16[32,640,64]{1,2,0:T(8,128)(2,1)}), bf16[32,640,64]{1,2,0:T(8,128)(2,1)}, u32[]{:S(2)}, u32[]{:S(2)}) async-start(bf16[32,640,64]{1,2,0:T(8,128)(2,1)} %copy.100), calls=%async_computation | async-start | bytes 5242880 | tf_op jit(solution)/shard_map/all_to_all | solution.py:200
  490.2 2.0 fusion.30
  492.2 2.9 collective-permute-start.8
  496.3 2.1 fusion.16
  498.4 3.9 convolution_add_fusion.1
  503.0 25.8 %collective-permute-done.8 = bf16[1024,64]{1,0:T(8,128)(2,1)} collective-permute-done((bf16[1024,64]{1,0:T(8,128)(2,1)S(1)}, bf16[1024,64]{1,0:T(8,128)(2,1)}, u32[]{:S(2)}, u32[]{:S(2)}) %collective-permute-start.8) | collective-permute-done | bytes 131104 | tf_op jit(solution)/shard_map/ppermute | solution.py:109
  529.8 2.4 collective-permute-done.7
  532.3 1.8 convert_element_type.74
  534.9 2.1 convert_reduce_fusion
  537.2 25.7 %scatter_custom_fusion = f32[4096,64]{1,0:T(8,128)} fusion(f32[4096,64]{1,0:T(8,128)} %convolution_add_fusion.1, s32[3712]{0:T(1024)S(1)} %fusion.20, f32[1024,64]{1,0:T(8,128)S(1)} %convert_element_type.75, f32[]{:T(128)} %constant.51, f32[1024,64]{1,0:T(8,128)} %convert_element_type.74, f32[1024,64]{1,0:T(8,128)} %convert_element_type.73, ...), kind=kCustom, calls=%fused_computation.26 | custom fusion | flops 950272 | bytes 2949632 | tf_op jit(solution)/shard_map/scatter-add | solution.py:213
  562.9 2.3 convolution_bitcast_fusion
  568.1 5.2 collective-permute-done.10
  573.3 2.6 collective-permute-start.11
  575.9 3.1 collective-permute-done.11
  579.7 3.5 collective-permute-done.12
  583.2 2.4 collective-permute-start.13
  585.5 3.7 collective-permute-done.13
  (114 shorter events, 38.6 us)
Async XLA Ops:
  7.2 360.2 %copy-start = (bf16[172,256]{1,0:T(8,128)(2,1)S(1)}, bf16[172,256]{1,0:T(8,128)(2,1)}, u32[]{:S(2)}) copy-start(bf16[172,256]{1,0:T(8,128)(2,1)} %param.21) | copy-start | bytes 264196
  7.2 60.1 %all-gather.9.cloned.1.call-start = ((), (), s32[]{:S(2)}) async-start(), calls=%async_computation.2 | async-start | bytes 5406720 | tf_op jit(solution)/shard_map/all_gather | solution.py:131
  13.7 154.4 %all-gather.11.cloned.1.call-start = ((), (), s32[]{:S(2)}) async-start(), calls=%async_computation.3 | async-start | bytes 1310720 | tf_op jit(solution)/shard_map/all_gather | solution.py:119
  17.2 55.3 %collective-permute-start = (bf16[1024,32]{1,0:T(8,128)(2,1)S(1)}, bf16[1024,32]{1,0:T(8,128)(2,1)S(1)}, u32[]{:S(2)}, u32[]{:S(2)}) collective-permute-start(bf16[1024,32]{1,0:T(8,128)(2,1)S(1)} %broadcast_select_fusion.5), channel_id=1, source_target_pairs={{0,4},{4,0},{8,12},{12,8},{16,20},{20,16},{24,28},{28,24},{32,36},... | collective-permute-start | bytes 196616 | tf_op jit(solution)/shard_map/ppermute | solution.py:109
  22.1 51.1 %collective-permute-start.1 = (bf16[1024,32]{1,0:T(8,128)(2,1)S(1)}, bf16[1024,32]{1,0:T(8,128)(2,1)S(1)}, u32[]{:S(2)}, u32[]{:S(2)}) collective-permute-start(bf16[1024,32]{1,0:T(8,128)(2,1)S(1)} %broadcast_select_fusion.4), channel_id=1, source_target_pairs={{0,8},{4,12},{8,0},{12,4},{16,24},{20,28},{24,16},{28,20},{32,40},... | collective-permute-start | bytes 196616 | tf_op jit(solution)/shard_map/ppermute | solution.py:109
  27.4 46.6 %collective-permute-start.2 = (bf16[1024,32]{1,0:T(8,128)(2,1)S(1)}, bf16[1024,32]{1,0:T(8,128)(2,1)S(1)}, u32[]{:S(2)}, u32[]{:S(2)}) collective-permute-start(bf16[1024,32]{1,0:T(8,128)(2,1)S(1)} %broadcast_select_fusion.3), channel_id=1, source_target_pairs={{0,16},{4,20},{8,24},{12,28},{16,0},{20,4},{24,8},{28,12},{32,48},... | collective-permute-start | bytes 196616 | tf_op jit(solution)/shard_map/ppermute | solution.py:109
  144.5 23.7 %copy-start.11 = (bf16[64,128]{1,0:T(8,128)(2,1)S(1)}, bf16[64,128]{1,0:T(8,128)(2,1)}, u32[]{:S(2)}) copy-start(bf16[64,128]{1,0:T(8,128)(2,1)} %param.19) | copy-start | bytes 49156
  147.3 47.1 %copy-start.12 = (bf16[64,128]{1,0:T(8,128)(2,1)S(1)}, bf16[64,128]{1,0:T(8,128)(2,1)}, u32[]{:S(2)}) copy-start(bf16[64,128]{1,0:T(8,128)(2,1)} %param.18) | copy-start | bytes 49156
  147.3 47.0 %all-gather.7.cloned.1.call-start = ((), (), s32[]{:S(2)}) async-start(), calls=%async_computation.1 | async-start | bytes 1310720 | tf_op jit(solution)/shard_map/all_gather | solution.py:118
  148.0 109.4 %all-gather.15.cloned.1.call-start = ((), (), s32[]{:S(2)}) async-start(), calls=%async_computation.5 | async-start | bytes 5406720 | tf_op jit(solution)/shard_map/all_gather | solution.py:131
  169.9 26.3 %copy-start.4 = (f32[4096,64]{1,0:T(8,128)}, f32[4096,64]{1,0:T(8,128)S(1)}, u32[]{:S(2)}) copy-start(f32[4096,64]{1,0:T(8,128)S(1)} %fusion.34) | copy-start | bytes 3145732
  196.1 15.8 %copy-start.1 = (bf16[64,4096]{0,1:T(8,128)(2,1)}, bf16[64,4096]{0,1:T(8,128)(2,1)S(1)}, u32[]{:S(2)}) copy-start(bf16[64,4096]{0,1:T(8,128)(2,1)S(1)} %get-tuple-element.38) | copy-start | bytes 1572868
  202.2 135.6 %all-gather.13.cloned.1.call-start = ((), (), s32[]{:S(2)}) async-start(), calls=%async_computation.4 | async-start | bytes 2621440 | tf_op jit(solution)/shard_map/all_gather | solution.py:118
  213.3 49.4 %collective-permute-start.3 = (bf16[1024,64]{1,0:T(8,128)(2,1)S(1)}, bf16[1024,64]{1,0:T(8,128)(2,1)S(1)}, u32[]{:S(2)}, u32[]{:S(2)}) collective-permute-start(bf16[1024,64]{1,0:T(8,128)(2,1)S(1)} %broadcast_select_fusion.2), channel_id=1, source_target_pairs={{0,4},{4,0},{8,12},{12,8},{16,20},{20,16},{24,28},{28,24},{32,36},... | collective-permute-start | bytes 393224 | tf_op jit(solution)/shard_map/ppermute | solution.py:109
  216.4 47.1 %collective-permute-start.4 = (bf16[1024,64]{1,0:T(8,128)(2,1)S(1)}, bf16[1024,64]{1,0:T(8,128)(2,1)S(1)}, u32[]{:S(2)}, u32[]{:S(2)}) collective-permute-start(bf16[1024,64]{1,0:T(8,128)(2,1)S(1)} %broadcast_select_fusion.1), channel_id=1, source_target_pairs={{0,8},{4,12},{8,0},{12,4},{16,24},{20,28},{24,16},{28,20},{32,40},... | collective-permute-start | bytes 393224 | tf_op jit(solution)/shard_map/ppermute | solution.py:109
  217.9 46.2 %collective-permute-start.5 = (bf16[1024,64]{1,0:T(8,128)(2,1)S(1)}, bf16[1024,64]{1,0:T(8,128)(2,1)S(1)}, u32[]{:S(2)}, u32[]{:S(2)}) collective-permute-start(bf16[1024,64]{1,0:T(8,128)(2,1)S(1)} %broadcast_select_fusion), channel_id=1, source_target_pairs={{0,16},{4,20},{8,24},{12,28},{16,0},{20,4},{24,8},{28,12},{32,48},... | collective-permute-start | bytes 393224 | tf_op jit(solution)/shard_map/ppermute | solution.py:109
  220.6 146.7 %all-gather.17.cloned.1.call-start = ((), (), s32[]{:S(2)}) async-start(), calls=%async_computation.6 | async-start | bytes 2621440 | tf_op jit(solution)/shard_map/all_gather | solution.py:119
  334.9 2.9 copy-start.8
  340.0 29.7 %copy-start.13 = (s32[4096]{0:T(1024)S(1)}, s32[4096]{0:T(1024)}, u32[]{:S(2)}) copy-start(s32[4096]{0:T(1024)} %param.17) | copy-start | bytes 49156
  471.4 4.6 copy-start.3
  482.1 8.0 %copy-start.9 = (s32[3,1024]{1,0:T(4,128)S(1)}, s32[3,1024]{1,0:T(4,128)}, u32[]{:S(2)}) copy-start(s32[3,1024]{1,0:T(4,128)} %param.16) | copy-start | bytes 36868
  482.1 8.1 %copy-start.10 = (s32[640]{0:T(1024)S(1)}, s32[640]{0:T(1024)}, u32[]{:S(2)}) copy-start(s32[640]{0:T(1024)} %param.15) | copy-start | bytes 7684
  482.1 52.8 %all-to-all-start = ((bf16[32,640,64]{1,2,0:T(8,128)(2,1)}), bf16[32,640,64]{1,2,0:T(8,128)(2,1)}, u32[]{:S(2)}, u32[]{:S(2)}) async-start(bf16[32,640,64]{1,2,0:T(8,128)(2,1)} %copy.100), calls=%async_computation | async-start | bytes 5242880 | tf_op jit(solution)/shard_map/all_to_all | solution.py:200
  492.2 36.7 %collective-permute-start.8 = (bf16[1024,64]{1,0:T(8,128)(2,1)S(1)}, bf16[1024,64]{1,0:T(8,128)(2,1)}, u32[]{:S(2)}, u32[]{:S(2)}) collective-permute-start(bf16[1024,64]{1,0:T(8,128)(2,1)S(1)} %get-tuple-element.29), channel_id=1, source_target_pairs={{0,16},{4,20},{8,24},{12,28},{16,0},{20,4},{24,8},{28,12},{32,48},... | collective-permute-start | bytes 393224 | tf_op jit(solution)/shard_map/ppermute | solution.py:109
  495.0 37.2 %collective-permute-start.7 = (bf16[1024,64]{1,0:T(8,128)(2,1)}, bf16[1024,64]{1,0:T(8,128)(2,1)}, u32[]{:S(2)}, u32[]{:S(2)}) collective-permute-start(bf16[1024,64]{1,0:T(8,128)(2,1)} %get-tuple-element.30), channel_id=1, source_target_pairs={{0,8},{4,12},{8,0},{12,4},{16,24},{20,28},{24,16},{28,20},{32,40},... | collective-permute-start | bytes 393224 | tf_op jit(solution)/shard_map/ppermute | solution.py:109
  495.3 38.7 %collective-permute-start.6 = (bf16[1024,64]{1,0:T(8,128)(2,1)}, bf16[1024,64]{1,0:T(8,128)(2,1)S(1)}, u32[]{:S(2)}, u32[]{:S(2)}) collective-permute-start(bf16[1024,64]{1,0:T(8,128)(2,1)} %get-tuple-element.28), channel_id=1, source_target_pairs={{0,4},{4,0},{8,12},{12,8},{16,20},{20,16},{24,28},{28,24},{32,36},... | collective-permute-start | bytes 393224 | tf_op jit(solution)/shard_map/ppermute | solution.py:109
  498.4 3.9 copy-start.2
  537.2 25.7 %copy-start.6 = (bf16[128,4096]{1,0:T(8,128)(2,1)S(1)}, bf16[128,4096]{1,0:T(8,128)(2,1)}, u32[]{:S(2)}) copy-start(bf16[128,4096]{1,0:T(8,128)(2,1)} %all-gather.11.cloned.1.call-done) | copy-start | bytes 3145732
  562.9 2.3 copy-start.5
  562.9 2.5 copy-start.7
  565.9 2.1 collective-permute-start.9
  568.0 5.3 collective-permute-start.10
  573.3 5.7 collective-permute-start.11
  579.0 4.2 collective-permute-start.12
  583.2 6.1 %collective-permute-start.13 = (f32[38400]{0:T(1024)S(1)}, f32[38400]{0:T(1024)S(1)}, u32[]{:S(2)}, u32[]{:S(2)}) collective-permute-start(f32[38400]{0:T(1024)S(1)} %add.83), channel_id=1, source_target_pairs={{0,64},{4,68},{8,72},{12,76},{16,80},{20,84},{24,88},{28,92},{32,9... | collective-permute-start | bytes 460808 | tf_op jit(solution)/shard_map/ppermute | solution.py:83
Sparse Core Ops, SparseCore 0:
  13.9 53.3 all-gather.8
  147.4 20.7 all-gather.10
  169.8 24.4 all-gather.6
  202.4 54.9 all-gather.14
  258.9 29.2 all-gather.12
  337.9 29.3 all-gather.16

commit v6 on v5

--- a/solution.py
+++ b/solution.py
@@ -73,6 +73,56 @@
         out_shape=jax.ShapeDtypeStruct((size, width), jnp.float32),
         scratch_shapes=[pltpu.VMEM((size, width), jnp.float32)],
     )(neighbours, rows)
+
+
+def land_rows(base, targets, updates):
+    count, width = updates.shape
+    half = count // 2
+
+    def kernel(t_ref, base_ref, upd_ref, out_ref, extra_ref):
+        out_ref[...] = base_ref[...]
+        extra_ref[...] = jnp.zeros_like(extra_ref)
+
+        def step(i, carry):
+            s = t_ref[i]
+            t = t_ref[i + half]
+            out_ref[pl.ds(s, 1), :] = out_ref[pl.ds(s, 1), :] + upd_ref[pl.ds(i, 1), :]
+            extra_ref[pl.ds(t, 1), :] = extra_ref[pl.ds(t, 1), :] + upd_ref[pl.ds(i + half, 1), :]
+            return carry
+
+        lax.fori_loop(0, half, step, 0, unroll=4)
+        for i in range(2 * half, count):
+            s = t_ref[i]
+            out_ref[pl.ds(s, 1), :] = out_ref[pl.ds(s, 1), :] + upd_ref[pl.ds(i, 1), :]
+        out_ref[...] = out_ref[...] + extra_ref[...]
+
+    return pl.pallas_call(
+        kernel,
+        in_specs=[
+            pl.BlockSpec(memory_space=pltpu.SMEM),
+            pl.BlockSpec(memory_space=pltpu.VMEM),
+            pl.BlockSpec(memory_space=pltpu.VMEM),
+        ],
+        out_specs=pl.BlockSpec(memory_space=pltpu.VMEM),
+        out_shape=jax.ShapeDtypeStruct(base.shape, jnp.float32),
+        scratch_shapes=[pltpu.VMEM(base.shape, jnp.float32)],
+    )(targets, base, updates)
+
+
+def tree_gather(value, axis):
+    count = lax.axis_size(axis)
+    index = lax.axis_index(axis)
+    block = value
+    stride = 1
+    while stride < count:
+        pairs = [(source, source ^ stride) for source in range(count)]
+        other = lax.ppermute(block, axis, pairs)
+        low = (index // stride) % 2 == 0
+        block = jnp.where(
+            low, jnp.concatenate([block, other], axis=0), jnp.concatenate([other, block], axis=0)
+        )
+        stride *= 2
+    return block
 
 
 def tree_sum(value, axis):
@@ -128,7 +178,7 @@
 def source_table(local, hub_rows, send_rows):
     local_rows = local.T
     hub_local = jnp.take(local_rows, hub_rows, axis=0)
-    hub_all = lax.all_gather(hub_local, "dom", axis=0, tiled=True)
+    hub_all = tree_gather(hub_local, "dom")
     received = [
         trade(jnp.take(local_rows, send_rows[bit_index], axis=0), bit_index)
         for bit_index in range(send_rows.shape[0])
@@ -210,7 +260,7 @@
         )
         landed.append(trade(outgoing, bit_index).astype(jnp.float32))
     targets = jnp.concatenate([hub_rows, send_rows.reshape(-1)])
-    grad_rows = grad_rows.at[targets].add(jnp.concatenate(landed, axis=0))
+    grad_rows = land_rows(grad_rows, targets, jnp.concatenate(landed, axis=0))
     grad_hidden = grad_rows.T
     grad_pre = jnp.where(hidden > 0, grad_hidden, 0.0).astype(jnp.bfloat16)
     grad_inner_self = contract(grad_pre, full_input)

time: 603 us -> 659 us (1.093); the launches traced: 598 us -> 646 us
  starting transfers between devices: 32.8 us -> 51 us
  other arithmetic: 67.4 us -> 83.3 us
  local copies, waits for them, and re-layouts: 60.7 us -> 75.4 us
  waiting for transfers between devices: 189 us -> 176 us
  Pallas kernels: 216 us -> 228 us
    all_gather x2 -> x0, waiting for transfers between devices: 72 us -> none  [source_table(): hub_all = lax.all_gather(hub_local, 'dom', axis=0, tiled=True)]
    ppermute x0 -> x10, waiting for transfers between devices: none -> 49.9 us  [tree_gather(): other = lax.ppermute(block, axis, pairs)]
    unnamed x1 -> x3, other arithmetic: 3.27 us -> 29.8 us
    scatter-add x1 -> x0, other arithmetic: 25.7 us -> none  [body(): grad_rows = grad_rows.at[targets].add(jnp.concatenate(landed, axis=0))]
    ppermute x0 -> x10, starting transfers between devices: none -> 21.7 us  [tree_gather(): other = lax.ppermute(block, axis, pairs)]
    select_n x1 -> x8, other arithmetic: 0.05 us -> 14.4 us  [tree_gather(): jnp.where(low, jnp.concatenate([block, other], axis=0), jnp.concatenate([...]
    pallas_call x0 -> x1, Pallas kernels: none -> 12.1 us  [land_rows(): pl.pallas_call(kernel, in_specs=[pl.BlockSpec(memory_space=pltpu.SMEM), p...]
    all_gather x2, waiting for transfers between devices: 47.4 us -> 56.7 us  [widen(): lax.all_gather(second_rows, 'feat', axis=0, tiled=True)]
  transfers between devices with their start and end apart: 21 -> 29, of which waited for: 12 -> 17; matrix products, arithmetic and copies ran while one was open for 11% -> 15% of each run, Pallas kernels for 10% -> 9%
where the time goes in v6:
time: 659 us; the launch traced here: 646 us
  Pallas kernels  228 us (35%)
  waiting for transfers between devices  176 us (27%)
  other arithmetic  83.3 us (13%)
  local copies, waits for them, and re-layouts  75.4 us (11%)
  starting transfers between devices  51 us (8%)
  matrix products  17.8 us (3%)
  between operations  14.8 us (2%)
    pallas_call x2, Pallas kernels, gather_mean(): pl.pallas_call(kernel, grid_spec=pltpu.PrefetchScalarGridSpec(num_scalar_...  123 us
    pallas_call x1, Pallas kernels, scatter_mean(): pl.pallas_call(kernel, in_specs=[pl.BlockSpec(memory_space=pltpu.SMEM), p...  93.3 us
    all_gather x2, waiting for transfers between devices, widen(): lax.all_gather(second_rows, 'feat', axis=0, tiled=True)  56.7 us
    ppermute x10, waiting for transfers between devices, tree_gather(): other = lax.ppermute(block, axis, pairs)  49.9 us
    unnamed x3, other arithmetic  29.8 us
    ppermute x9, waiting for transfers between devices, partner(): return lax.ppermute(value, axis, pairs)  27.6 us
    all_gather x2, waiting for transfers between devices, widen(): lax.all_gather(first_rows, 'feat', axis=0, tiled=True)  24.4 us
    ppermute x10, starting transfers between devices, tree_gather(): other = lax.ppermute(block, axis, pairs)  21.7 us
  transfers between devices with their start and end apart: 29, of which 17 were waited for; matrix products, arithmetic and copies ran while one was open for 15% of the time, Pallas kernels for 9%

profile of v6, /device:TPU:1, one launch (start us, length us, event | category | flops | bytes accessed | tf_op | source)
XLA Modules:
  0.0 646.1 jit_solution(2081174187460423451)
XLA Ops:
  14.5 3.2 gather_fusion.2
  20.2 3.2 gather_fusion.3
  23.5 3.4 collective-permute-start.2
  27.2 3.5 collective-permute-done.2
  32.1 3.2 gather_fusion.4
  36.2 2.7 collective-permute-start.7
  42.6 10.9 %collective-permute-done.4 = bf16[10240,32]{0,1:T(8,128)(2,1)S(1)} collective-permute-done((bf16[10240,32]{0,1:T(8,128)(2,1)S(1)}, bf16[10240,32]{0,1:T(8,128)(2,1)S(1)}, u32[]{:S(2)}, u32[]{:S(2)}) %collective-permute-start.4) | collective-permute-done | bytes 655392 | tf_op jit(solution)/shard_map/ppermute | solution.py:119
  53.7 4.1 copy.134
  57.8 4.1 copy.135
  61.9 5.8 select_dynamic-update-slice_fusion
  71.8 8.5 %convert_element_type.59.tab_ref = f32[27648,32]{1,0:T(8,128)} convert(bf16[27648,32]{1,0:T(8,128)(2,1)} %constant_dynamic-update-slice_fusion) | non-fusion elementwise | flops 884736 | bytes 5308416 | tf_op jit(solution)/shard_map/convert_element_type | solution.py:174
  80.3 61.3 %shard_map.120 = f32[4096,32]{1,0:T(8,128)} custom-call(s32[8,4096]{1,0:T(8,128)} %nb_ref.5, f32[27648,32]{1,0:T(8,128)} %convert_element_type.59.tab_ref), custom_call_target="tpu_custom_call" | custom-call | tf_op jit(solution)/shard_map/pallas_call | solution.py:33
  145.2 24.7 %all-gather.7.cloned.1.call-done = bf16[128,4096]{1,0:T(8,128)(2,1)} async-done(((bf16[32,4096]{1,0:T(8,128)(2,1)}), bf16[128,4096]{1,0:T(8,128)(2,1)}) %all-gather.7.cloned.1.call-update) | async-done | bytes 1048592 | tf_op jit(solution)/shard_map/all_gather | solution.py:169
  171.6 24.4 %all-gather.5.cloned.1.call-done = bf16[128,4096]{1,0:T(8,128)(2,1)} async-done(((bf16[32,4096]{1,0:T(8,128)(2,1)}), bf16[128,4096]{1,0:T(8,128)(2,1)}) %all-gather.5.cloned.1.call-update) | async-done | bytes 1048592 | tf_op jit(solution)/shard_map/all_gather | solution.py:168
  197.8 3.3 constant_dynamic-update-slice_fusion.7
  203.3 2.8 collective-permute-start.8
  208.6 7.6 %collective-permute-done.9 = bf16[1280,64]{1,0:T(8,128)(2,1)S(1)} collective-permute-done((bf16[1280,64]{1,0:T(8,128)(2,1)S(1)}, bf16[1280,64]{1,0:T(8,128)(2,1)S(1)}, u32[]{:S(2)}, u32[]{:S(2)}) %collective-permute-start.9) | collective-permute-done | bytes 163872 | tf_op jit(solution)/shard_map/ppermute | solution.py:119
  216.8 3.0 collective-permute-start.10
  219.7 6.7 %collective-permute-done.10 = bf16[2560,64]{0,1:T(8,128)(2,1)S(1)} collective-permute-done((bf16[2560,64]{0,1:T(8,128)(2,1)S(1)}, bf16[2560,64]{0,1:T(8,128)(2,1)S(1)}, u32[]{:S(2)}, u32[]{:S(2)}) %collective-permute-start.10) | collective-permute-done | bytes 327712 | tf_op jit(solution)/shard_map/ppermute | solution.py:119
  232.4 13.3 %collective-permute-done.11 = bf16[5120,64]{0,1:T(8,128)(2,1)} collective-permute-done((bf16[5120,64]{0,1:T(8,128)(2,1)}, bf16[5120,64]{0,1:T(8,128)(2,1)}, u32[]{:S(2)}, u32[]{:S(2)}) %collective-permute-start.11) | collective-permute-done | bytes 655392 | tf_op jit(solution)/shard_map/ppermute | solution.py:119
  248.1 11.5 %maximum_select_fusion.1 = bf16[10240,64]{1,0:T(8,128)(2,1)} fusion(bf16[5120,64]{1,0:T(8,128)(2,1)} %copy.146, bf16[5120,64]{1,0:T(8,128)(2,1)S(1)} %maximum_select_fusion.2, pred[]{:T(512)S(6)} %eq.40), kind=kLoop, calls=%fused_computation.20 | loop fusion | flops 5898240 | bytes 2621441 | tf_op jit(solution)/shard_map/jit(_where)/select_n | solution.py:121
  259.6 4.0 copy.148
  263.6 2.7 collective-permute-start.12
  266.3 3.2 gather_fusion.5
  269.5 3.2 gather_fusion.6
  272.8 3.2 gather_fusion.7
  277.4 3.3 collective-permute-start.13
  283.1 2.9 collective-permute-start.15
  286.0 6.9 %collective-permute-done.12 = bf16[10240,64]{0,1:T(8,128)(2,1)} collective-permute-done((bf16[10240,64]{0,1:T(8,128)(2,1)}, bf16[10240,64]{0,1:T(8,128)(2,1)}, u32[]{:S(2)}, u32[]{:S(2)}) %collective-permute-start.12) | collective-permute-done | bytes 1310752 | tf_op jit(solution)/shard_map/ppermute | solution.py:119
  292.9 3.9 copy.149
  296.7 20.7 %fusion = bf16[27648,64]{1,0:T(8,128)(2,1)} fusion(bf16[27648,64]{1,0:T(8,128)(2,1)} %get-tuple-element.26, bf16[10240,64]{1,0:T(8,128)(2,1)} %copy.149, bf16[10240,64]{1,0:T(8,128)(2,1)S(1)} %copy-done.4, pred[]{:T(512)S(6)} %eq.39), kind=kLoop, calls=%fused_computation.9 | loop fusion | flops 11796480 | bytes 9175041
  321.6 8.5 %convert_element_type.64.tab_ref = f32[27648,64]{1,0:T(8,128)} convert(bf16[27648,64]{1,0:T(8,128)(2,1)} %constant_dynamic-update-slice_fusion.4) | non-fusion elementwise | flops 1769472 | bytes 10616832 | tf_op jit(solution)/shard_map/convert_element_type | solution.py:174
  330.1 61.3 %shard_map.121 = f32[4096,64]{1,0:T(8,128)} custom-call(s32[8,4096]{1,0:T(8,128)} %nb_ref.5, f32[27648,64]{1,0:T(8,128)} %convert_element_type.64.tab_ref), custom_call_target="tpu_custom_call" | custom-call | tf_op jit(solution)/shard_map/pallas_call | solution.py:33
  396.5 32.0 %all-gather.11.cloned.1.call-done = bf16[256,4096]{1,0:T(8,128)(2,1)} async-done(((bf16[64,4096]{1,0:T(8,128)(2,1)}), bf16[256,4096]{1,0:T(8,128)(2,1)}) %all-gather.11.cloned.1.call-update) | async-done | bytes 2097168 | tf_op jit(solution)/shard_map/all_gather | solution.py:169
  433.9 93.3 %shard_map.122 = f32[27648,64]{1,0:T(8,128)} custom-call(s32[8,4096]{1,0:T(8,128)} %nb_ref.5, f32[4096,64]{1,0:T(8,128)} %convert_element_type.70.rows_ref), custom_call_target="tpu_custom_call" | custom-call | tf_op jit(solution)/shard_map/pallas_call | solution.py:66
  527.2 5.7 convert.6
  532.9 3.3 slice.116
  537.4 6.1 copy.154
  543.5 8.0 %all-to-all-start = ((bf16[32,640,64]{1,2,0:T(8,128)(2,1)}), bf16[32,640,64]{1,2,0:T(8,128)(2,1)}, u32[]{:S(2)}, u32[]{:S(2)}) async-start(bf16[32,640,64]{1,2,0:T(8,128)(2,1)} %copy.154), calls=%async_computation | async-start | bytes 5242880 | tf_op jit(solution)/shard_map/all_to_all | solution.py:250
  554.2 2.9 collective-permute-start.18
  560.5 3.9 convolution_add_fusion.1.base_ref
  565.1 25.2 %collective-permute-done.18 = bf16[1024,64]{1,0:T(8,128)(2,1)} collective-permute-done((bf16[1024,64]{1,0:T(8,128)(2,1)}, bf16[1024,64]{1,0:T(8,128)(2,1)}, u32[]{:S(2)}, u32[]{:S(2)}) %collective-permute-start.18) | collective-permute-done | bytes 131104 | tf_op jit(solution)/shard_map/ppermute | solution.py:159
  598.3 12.1 %shard_map.123 = f32[4096,64]{1,0:T(8,128)} custom-call(s32[3712]{0:T(1024)} %pad_add_fusion.t_ref, f32[4096,64]{1,0:T(8,128)} %convolution_add_fusion.1.base_ref, f32[3712,64]{1,0:T(8,128)} %pad_maximum_fusion.upd_ref), custom_call_target="tpu_custom_call" | custom-call | tf_op jit(solution)/shard_map/pallas_call | solution.py:99
  615.7 5.2 collective-permute-done.20
  620.9 2.6 collective-permute-start.21
  623.5 3.1 collective-permute-done.21
  627.3 3.5 collective-permute-done.22
  633.1 3.7 collective-permute-done.23
  (150 shorter events, 85.7 us)
Async XLA Ops:
  7.2 421.4 %copy-start = (bf16[172,256]{1,0:T(8,128)(2,1)S(1)}, bf16[172,256]{1,0:T(8,128)(2,1)}, u32[]{:S(2)}) copy-start(bf16[172,256]{1,0:T(8,128)(2,1)} %param.21) | copy-start | bytes 264196
  7.2 162.7 %all-gather.7.cloned.1.call-start = ((), (), s32[]{:S(2)}) async-start(), calls=%async_computation.2 | async-start | bytes 1310720 | tf_op jit(solution)/shard_map/all_gather | solution.py:169
  13.1 5.1 collective-permute-start
  17.9 49.7 %collective-permute-start.5 = (bf16[1024,32]{1,0:T(8,128)(2,1)S(1)}, bf16[1024,32]{1,0:T(8,128)(2,1)S(1)}, u32[]{:S(2)}, u32[]{:S(2)}) collective-permute-start(bf16[1024,32]{1,0:T(8,128)(2,1)S(1)} %broadcast_select_fusion.5), channel_id=1, source_target_pairs={{0,4},{4,0},{8,12},{12,8},{16,20},{20,16},{24,28},{28,24},{32,36},... | collective-permute-start | bytes 196616 | tf_op jit(solution)/shard_map/ppermute | solution.py:159
  18.4 5.0 collective-permute-start.1
  23.5 7.2 %collective-permute-start.2 = (bf16[2560,32]{0,1:T(8,128)(2,1)S(1)}, bf16[2560,32]{0,1:T(8,128)(2,1)S(1)}, u32[]{:S(2)}, u32[]{:S(2)}) collective-permute-start(bf16[2560,32]{0,1:T(8,128)(2,1)S(1)} %maximum_select_fusion.7), channel_id=1, source_target_pairs={{0,16},{4,20},{8,24},{12,28},{16,0},{20,4},{24,8},{28,12},{32,48},... | collective-permute-start | bytes 491528 | tf_op jit(solution)/shard_map/ppermute | solution.py:119
  27.1 41.3 %collective-permute-start.6 = (bf16[1024,32]{1,0:T(8,128)(2,1)S(1)}, bf16[1024,32]{1,0:T(8,128)(2,1)}, u32[]{:S(2)}, u32[]{:S(2)}) collective-permute-start(bf16[1024,32]{1,0:T(8,128)(2,1)S(1)} %broadcast_select_fusion.4), channel_id=1, source_target_pairs={{0,8},{4,12},{8,0},{12,4},{16,24},{20,28},{24,16},{28,20},{32,40},... | collective-permute-start | bytes 196616 | tf_op jit(solution)/shard_map/ppermute | solution.py:159
  30.8 8.1 %collective-permute-start.3 = (bf16[5120,32]{0,1:T(8,128)(2,1)S(1)}, bf16[5120,32]{0,1:T(8,128)(2,1)S(1)}, u32[]{:S(2)}, u32[]{:S(2)}) collective-permute-start(bf16[5120,32]{0,1:T(8,128)(2,1)S(1)} %maximum_select_fusion.5), channel_id=1, source_target_pairs={{0,32},{4,36},{8,40},{12,44},{16,48},{20,52},{24,56},{28,60},{32,0... | collective-permute-start | bytes 983048 | tf_op jit(solution)/shard_map/ppermute | solution.py:119
  36.2 33.9 %collective-permute-start.7 = (bf16[1024,32]{1,0:T(8,128)(2,1)}, bf16[1024,32]{1,0:T(8,128)(2,1)}, u32[]{:S(2)}, u32[]{:S(2)}) collective-permute-start(bf16[1024,32]{1,0:T(8,128)(2,1)} %broadcast_select_fusion.3), channel_id=1, source_target_pairs={{0,16},{4,20},{8,24},{12,28},{16,0},{20,4},{24,8},{28,12},{32,48},... | collective-permute-start | bytes 196616 | tf_op jit(solution)/shard_map/ppermute | solution.py:159
  39.0 14.5 %collective-permute-start.4 = (bf16[10240,32]{0,1:T(8,128)(2,1)S(1)}, bf16[10240,32]{0,1:T(8,128)(2,1)S(1)}, u32[]{:S(2)}, u32[]{:S(2)}) collective-permute-start(bf16[10240,32]{0,1:T(8,128)(2,1)S(1)} %maximum_select_fusion.3), channel_id=1, source_target_pairs={{0,64},{4,68},{8,72},{12,76},{16,80},{20,84},{24,88},{28,92},{32,9... | collective-permute-start | bytes 1966088 | tf_op jit(solution)/shard_map/ppermute | solution.py:119
  141.6 28.3 %copy-start.13 = (bf16[64,128]{1,0:T(8,128)(2,1)S(1)}, bf16[64,128]{1,0:T(8,128)(2,1)}, u32[]{:S(2)}) copy-start(bf16[64,128]{1,0:T(8,128)(2,1)} %param.19) | copy-start | bytes 49156
  143.3 52.7 %copy-start.14 = (bf16[64,128]{1,0:T(8,128)(2,1)S(1)}, bf16[64,128]{1,0:T(8,128)(2,1)}, u32[]{:S(2)}) copy-start(bf16[64,128]{1,0:T(8,128)(2,1)} %param.18) | copy-start | bytes 49156
  144.4 51.6 %all-gather.5.cloned.1.call-start = ((), (), s32[]{:S(2)}) async-start(), calls=%async_computation.1 | async-start | bytes 1310720 | tf_op jit(solution)/shard_map/all_gather | solution.py:168
  145.1 249.2 %all-gather.9.cloned.1.call-start = ((), (), s32[]{:S(2)}) async-start(), calls=%async_computation.3 | async-start | bytes 2621440 | tf_op jit(solution)/shard_map/all_gather | solution.py:168
  171.6 26.2 %copy-start.5 = (f32[4096,64]{1,0:T(8,128)}, f32[4096,64]{1,0:T(8,128)S(1)}, u32[]{:S(2)}) copy-start(f32[4096,64]{1,0:T(8,128)S(1)} %fusion.26) | copy-start | bytes 3145732
  197.8 78.2 %copy-start.1 = (bf16[64,4096]{0,1:T(8,128)(2,1)}, bf16[64,4096]{0,1:T(8,128)(2,1)S(1)}, u32[]{:S(2)}) copy-start(bf16[64,4096]{0,1:T(8,128)(2,1)S(1)} %get-tuple-element.40) | copy-start | bytes 1572868
  203.3 3.9 collective-permute-start.8
  207.3 9.0 %collective-permute-start.9 = (bf16[1280,64]{1,0:T(8,128)(2,1)S(1)}, bf16[1280,64]{1,0:T(8,128)(2,1)S(1)}, u32[]{:S(2)}, u32[]{:S(2)}) collective-permute-start(bf16[1280,64]{1,0:T(8,128)(2,1)S(1)} %maximum_select_fusion.6), channel_id=1, source_target_pairs={{0,8},{4,12},{8,0},{12,4},{16,24},{20,28},{24,16},{28,20},{32,40},... | collective-permute-start | bytes 491528 | tf_op jit(solution)/shard_map/ppermute | solution.py:119
  216.5 9.9 %copy-start.7 = (bf16[2560,64]{1,0:T(8,128)(2,1)}, bf16[2560,64]{1,0:T(8,128)(2,1)S(1)}, u32[]{:S(2)}) copy-start(bf16[2560,64]{1,0:T(8,128)(2,1)S(1)} %maximum_select_fusion.4) | copy-start | bytes 983044
  216.8 9.6 %collective-permute-start.10 = (bf16[2560,64]{0,1:T(8,128)(2,1)S(1)}, bf16[2560,64]{0,1:T(8,128)(2,1)S(1)}, u32[]{:S(2)}, u32[]{:S(2)}) collective-permute-start(bf16[2560,64]{0,1:T(8,128)(2,1)S(1)} %copy.142), channel_id=1, source_target_pairs={{0,16},{4,20},{8,24},{12,28},{16,0},{20,4},{24,8},{28,12},{32,48},... | collective-permute-start | bytes 983048 | tf_op jit(solution)/shard_map/ppermute | solution.py:119
  231.1 14.7 %collective-permute-start.11 = (bf16[5120,64]{0,1:T(8,128)(2,1)}, bf16[5120,64]{0,1:T(8,128)(2,1)}, u32[]{:S(2)}, u32[]{:S(2)}) collective-permute-start(bf16[5120,64]{0,1:T(8,128)(2,1)} %copy.145), channel_id=1, source_target_pairs={{0,32},{4,36},{8,40},{12,44},{16,48},{20,52},{24,56},{28,60},{32,0... | collective-permute-start | bytes 1966088 | tf_op jit(solution)/shard_map/ppermute | solution.py:119
  263.6 29.2 %collective-permute-start.12 = (bf16[10240,64]{0,1:T(8,128)(2,1)}, bf16[10240,64]{0,1:T(8,128)(2,1)}, u32[]{:S(2)}, u32[]{:S(2)}) collective-permute-start(bf16[10240,64]{0,1:T(8,128)(2,1)} %copy.148), channel_id=1, source_target_pairs={{0,64},{4,68},{8,72},{12,76},{16,80},{20,84},{24,88},{28,92},{32,9... | collective-permute-start | bytes 3932168 | tf_op jit(solution)/shard_map/ppermute | solution.py:119
  277.2 151.4 %all-gather.11.cloned.1.call-start = ((), (), s32[]{:S(2)}) async-start(), calls=%async_computation.4 | async-start | bytes 2621440 | tf_op jit(solution)/shard_map/all_gather | solution.py:169
  277.4 19.3 %copy-start.4 = (bf16[10240,64]{1,0:T(8,128)(2,1)S(1)}, bf16[10240,64]{1,0:T(8,128)(2,1)}, u32[]{:S(2)}) copy-start(bf16[10240,64]{1,0:T(8,128)(2,1)} %maximum_select_fusion.1) | copy-start | bytes 3932164
  277.4 40.0 %collective-permute-start.13 = (bf16[1024,64]{1,0:T(8,128)(2,1)S(1)}, bf16[1024,64]{1,0:T(8,128)(2,1)}, u32[]{:S(2)}, u32[]{:S(2)}) collective-permute-start(bf16[1024,64]{1,0:T(8,128)(2,1)S(1)} %broadcast_select_fusion.2), channel_id=1, source_target_pairs={{0,4},{4,0},{8,12},{12,8},{16,20},{20,16},{24,28},{28,24},{32,36},... | collective-permute-start | bytes 393224 | tf_op jit(solution)/shard_map/ppermute | solution.py:159
  281.6 37.5 %collective-permute-start.14 = (bf16[1024,64]{1,0:T(8,128)(2,1)}, bf16[1024,64]{1,0:T(8,128)(2,1)}, u32[]{:S(2)}, u32[]{:S(2)}) collective-permute-start(bf16[1024,64]{1,0:T(8,128)(2,1)} %broadcast_select_fusion.1), channel_id=1, source_target_pairs={{0,8},{4,12},{8,0},{12,4},{16,24},{20,28},{24,16},{28,20},{32,40},... | collective-permute-start | bytes 393224 | tf_op jit(solution)/shard_map/ppermute | solution.py:159
  283.1 37.7 %collective-permute-start.15 = (bf16[1024,64]{1,0:T(8,128)(2,1)S(1)}, bf16[1024,64]{1,0:T(8,128)(2,1)S(1)}, u32[]{:S(2)}, u32[]{:S(2)}) collective-permute-start(bf16[1024,64]{1,0:T(8,128)(2,1)S(1)} %broadcast_select_fusion), channel_id=1, source_target_pairs={{0,16},{4,20},{8,24},{12,28},{16,0},{20,4},{24,8},{28,12},{32,48},... | collective-permute-start | bytes 393224 | tf_op jit(solution)/shard_map/ppermute | solution.py:159
  391.4 3.0 copy-start.10
  396.5 34.4 %copy-start.15 = (s32[4096]{0:T(1024)S(1)}, s32[4096]{0:T(1024)}, u32[]{:S(2)}) copy-start(s32[4096]{0:T(1024)} %param.17) | copy-start | bytes 49156
  532.9 4.5 copy-start.3
  543.5 8.0 %copy-start.11 = (s32[3,1024]{1,0:T(4,128)S(1)}, s32[3,1024]{1,0:T(4,128)}, u32[]{:S(2)}) copy-start(s32[3,1024]{1,0:T(4,128)} %param.16) | copy-start | bytes 36868
  543.5 8.1 %copy-start.12 = (s32[640]{0:T(1024)S(1)}, s32[640]{0:T(1024)}, u32[]{:S(2)}) copy-start(s32[640]{0:T(1024)} %param.15) | copy-start | bytes 7684
  543.5 51.1 %all-to-all-start = ((bf16[32,640,64]{1,2,0:T(8,128)(2,1)}), bf16[32,640,64]{1,2,0:T(8,128)(2,1)}, u32[]{:S(2)}, u32[]{:S(2)}) async-start(bf16[32,640,64]{1,2,0:T(8,128)(2,1)} %copy.154), calls=%async_computation | async-start | bytes 5242880 | tf_op jit(solution)/shard_map/all_to_all | solution.py:250
  554.2 36.1 %collective-permute-start.18 = (bf16[1024,64]{1,0:T(8,128)(2,1)}, bf16[1024,64]{1,0:T(8,128)(2,1)}, u32[]{:S(2)}, u32[]{:S(2)}) collective-permute-start(bf16[1024,64]{1,0:T(8,128)(2,1)} %get-tuple-element.29), channel_id=1, source_target_pairs={{0,16},{4,20},{8,24},{12,28},{16,0},{20,4},{24,8},{28,12},{32,48},... | collective-permute-start | bytes 393224 | tf_op jit(solution)/shard_map/ppermute | solution.py:159
  557.1 36.5 %collective-permute-start.17 = (bf16[1024,64]{1,0:T(8,128)(2,1)}, bf16[1024,64]{1,0:T(8,128)(2,1)S(1)}, u32[]{:S(2)}, u32[]{:S(2)}) collective-permute-start(bf16[1024,64]{1,0:T(8,128)(2,1)} %get-tuple-element.30), channel_id=1, source_target_pairs={{0,8},{4,12},{8,0},{12,4},{16,24},{20,28},{24,16},{28,20},{32,40},... | collective-permute-start | bytes 393224 | tf_op jit(solution)/shard_map/ppermute | solution.py:159
  557.4 36.3 %collective-permute-start.16 = (bf16[1024,64]{1,0:T(8,128)(2,1)}, bf16[1024,64]{1,0:T(8,128)(2,1)}, u32[]{:S(2)}, u32[]{:S(2)}) collective-permute-start(bf16[1024,64]{1,0:T(8,128)(2,1)} %get-tuple-element.28), channel_id=1, source_target_pairs={{0,4},{4,0},{8,12},{12,8},{16,20},{20,16},{24,28},{28,24},{32,36},... | collective-permute-start | bytes 393224 | tf_op jit(solution)/shard_map/ppermute | solution.py:159
  560.5 3.9 copy-start.2
  598.3 12.1 %copy-start.8 = (bf16[128,4096]{1,0:T(8,128)(2,1)S(1)}, bf16[128,4096]{1,0:T(8,128)(2,1)}, u32[]{:S(2)}) copy-start(bf16[128,4096]{1,0:T(8,128)(2,1)} %all-gather.7.cloned.1.call-done) | copy-start | bytes 3145732
  610.5 2.3 copy-start.6
  610.5 2.5 copy-start.9
  613.5 2.1 collective-permute-start.19
  615.6 5.3 collective-permute-start.20
  620.9 5.7 collective-permute-start.21
  626.6 4.2 collective-permute-start.22
  630.8 6.1 collective-permute-start.23
Sparse Core Ops, SparseCore 0:
  144.5 25.3 all-gather.6
  171.5 24.4 all-gather.4
  277.3 31.6 all-gather.8
  394.4 34.0 all-gather.10

commit v7 on v6

--- a/solution.py
+++ b/solution.py
@@ -9,11 +9,11 @@
 loss_scale = 4096.0
 
 
-def gather_mean(table, neighbours, block=512):
+def gather_mean(table, neighbours, after, block=512):
     size, width = table.shape
     degree, nodes = neighbours.shape
 
-    def kernel(nb_ref, tab_ref, out_ref):
+    def kernel(nb_ref, tab_ref, after_ref, out_ref):
         base = pl.program_id(0) * block
 
         def group(g, carry):
@@ -35,11 +35,14 @@
         grid_spec=pltpu.PrefetchScalarGridSpec(
             num_scalar_prefetch=1,
             grid=(nodes // block,),
-            in_specs=[pl.BlockSpec((size, width), lambda j, nb: (0, 0))],
+            in_specs=[
+                pl.BlockSpec((size, width), lambda j, nb: (0, 0)),
+                pl.BlockSpec(memory_space=pl.ANY),
+            ],
             out_specs=pl.BlockSpec((block, width), lambda j, nb: (j, 0)),
         ),
         out_shape=jax.ShapeDtypeStruct((nodes, width), jnp.float32),
-    )(neighbours, table)
+    )(neighbours, table, after)
 
 
 def scatter_mean(rows, neighbours, size):
@@ -170,15 +173,15 @@
     )
 
 
-def average(table_rows, neighbours):
-    summed = gather_mean(table_rows.astype(jnp.float32), neighbours)
+def average(table_rows, neighbours, after):
+    summed = gather_mean(table_rows.astype(jnp.float32), neighbours, after)
     return summed.T.astype(jnp.bfloat16)
 
 
 def source_table(local, hub_rows, send_rows):
     local_rows = local.T
     hub_local = jnp.take(local_rows, hub_rows, axis=0)
-    hub_all = tree_gather(hub_local, "dom")
+    hub_all = lax.all_gather(hub_local, "dom", axis=0, tiled=True)
     received = [
         trade(jnp.take(local_rows, send_rows[bit_index], axis=0), bit_index)
         for bit_index in range(send_rows.shape[0])
@@ -219,12 +222,13 @@
 ):
     rows = features.shape[1]
     nodes_all = rows * lax.axis_size("dom")
-    mean_one = average(source_table(features, hub_rows, send_rows), neighbours)
-    full_input, full_mean = widen(features, mean_one)
+    full_input = lax.all_gather(features, "feat", axis=0, tiled=True)
+    mean_one = average(source_table(features, hub_rows, send_rows), neighbours, full_input)
+    full_mean = lax.all_gather(mean_one, "feat", axis=0, tiled=True)
     pre_act = jnp.dot(inner_self, full_input, preferred_element_type=jnp.float32)
     pre_act = pre_act + jnp.dot(inner_neighbour, full_mean, preferred_element_type=jnp.float32)
     hidden = jnp.maximum(pre_act, 0.0).astype(jnp.bfloat16)
-    mean_two = average(source_table(hidden, hub_rows, send_rows), neighbours)
+    mean_two = average(source_table(hidden, hub_rows, send_rows), neighbours, hidden)
     width = hidden.shape[0]
     offset = lax.axis_index("feat") * width
     self_cols = lax.dynamic_slice_in_dim(outer_self, offset, width, 1)

time: 659 us -> 571 us (0.87); the launches traced: 646 us -> 567 us
  other arithmetic: 83.3 us -> 40.2 us
  starting transfers between devices: 51 us -> 32.8 us
  local copies, waits for them, and re-layouts: 75.4 us -> 60.8 us
    all_gather x0 -> x4, waiting for transfers between devices: none -> 103 us  [the longest x2 71.9 us: source_table(): hub_all = lax.all_gather(hub_local, 'dom', axis=0, tiled=True)]
    ppermute x10 -> x0, waiting for transfers between devices: 49.9 us -> none  [tree_gather(): other = lax.ppermute(block, axis, pairs)]
    all_gather x2 -> x1, waiting for transfers between devices: 56.7 us -> 27.4 us  [widen(): lax.all_gather(second_rows, 'feat', axis=0, tiled=True)]
    unnamed x3 -> x1, other arithmetic: 29.8 us -> 1.34 us
    all_gather x2 -> x1, waiting for transfers between devices: 24.4 us -> 0.02 us  [widen(): lax.all_gather(first_rows, 'feat', axis=0, tiled=True)]
    ppermute x10 -> x0, starting transfers between devices: 21.7 us -> none  [tree_gather(): other = lax.ppermute(block, axis, pairs)]
    select_n x8 -> x0, other arithmetic: 14.4 us -> none  [tree_gather(): jnp.where(low, jnp.concatenate([block, other], axis=0), jnp.concatenate([...]
    concatenate x2 -> x0, local copies, waits for them, and re-layouts: 8.21 us -> none  [the longest x1 4.11 us: tree_gather(): jnp.concatenate([block, other], axis=0)]
  transfers between devices with their start and end apart: 29 -> 21, of which waited for: 17 -> 12; matrix products, arithmetic and copies ran while one was open for 15% -> 13% of each run, Pallas kernels for 9% -> 11%
where the time goes in v7:
time: 571 us; the launch traced here: 567 us
  Pallas kernels  228 us (40%)
  waiting for transfers between devices  174 us (30%)
  local copies, waits for them, and re-layouts  60.8 us (11%)
  other arithmetic  40.2 us (7%)
  starting transfers between devices  32.8 us (6%)
  matrix products  16.6 us (3%)
  between operations  14.6 us (3%)
    pallas_call x2, Pallas kernels, gather_mean(): pl.pallas_call(kernel, grid_spec=pltpu.PrefetchScalarGridSpec(num_scalar_...  123 us
    pallas_call x1, Pallas kernels, scatter_mean(): pl.pallas_call(kernel, in_specs=[pl.BlockSpec(memory_space=pltpu.SMEM), p...  93 us
    all_gather x2, waiting for transfers between devices, source_table(): hub_all = lax.all_gather(hub_local, 'dom', axis=0, tiled=True)  71.9 us
    ppermute x9, waiting for transfers between devices, partner(): return lax.ppermute(value, axis, pairs)  27.6 us
    all_gather x1, waiting for transfers between devices, widen(): lax.all_gather(second_rows, 'feat', axis=0, tiled=True)  27.4 us
    all_gather x1, waiting for transfers between devices, body(): full_mean = lax.all_gather(mean_one, 'feat', axis=0, tiled=True)  24.6 us
    gather x6, local copies, waits for them, and re-layouts, source_table(): jnp.take(local_rows, send_rows[bit_index], axis=0)  19.2 us
    unnamed x38, local copies, waits for them, and re-layouts  18.9 us
  transfers between devices with their start and end apart: 21, of which 12 were waited for; matrix products, arithmetic and copies ran while one was open for 13% of the time, Pallas kernels for 11%

profile of v7, /device:TPU:1, one launch (start us, length us, event | category | flops | bytes accessed | tf_op | source)
XLA Modules:
  0.0 567.1 jit_solution(5267498098087515375)
XLA Ops:
  10.9 2.0 gather_fusion
  13.8 3.2 gather_fusion.2
  18.7 3.2 gather_fusion.3
  22.1 1.8 collective-permute-start.1
  24.0 3.2 gather_fusion.4
  27.4 3.4 collective-permute-start.2
  31.9 35.3 %all-gather.9.cloned.1.call-done = bf16[20480,32]{1,0:T(8,128)(2,1)} async-done(((bf16[640,32]{1,0:T(8,128)(2,1)}), bf16[20480,32]{1,0:T(8,128)(2,1)}) %all-gather.9.cloned.1.call-update) | async-done | bytes 1310736 | tf_op jit(solution)/shard_map/all_gather | solution.py:184
  67.2 5.3 constant_dynamic-update-slice_fusion.3
  74.7 8.6 %convert_element_type.58.tab_ref = f32[27648,32]{1,0:T(8,128)} convert(bf16[27648,32]{1,0:T(8,128)(2,1)} %constant_dynamic-update-slice_fusion) | non-fusion elementwise | flops 884736 | bytes 5308416 | tf_op jit(solution)/shard_map/convert_element_type | solution.py:177
  83.3 6.4 %all-gather.7.cloned.1.call-done.after_ref = bf16[128,4096]{1,0:T(8,128)(2,1)} async-done(((bf16[32,4096]{1,0:T(8,128)(2,1)}), bf16[128,4096]{1,0:T(8,128)(2,1)}) %all-gather.7.cloned.1.call-update) | async-done | bytes 1048592 | tf_op jit(solution)/shard_map/all_gather | solution.py:225
  89.7 61.3 %shard_map.120 = f32[4096,32]{1,0:T(8,128)} custom-call(s32[8,4096]{1,0:T(8,128)} %nb_ref.5, f32[27648,32]{1,0:T(8,128)} %convert_element_type.58.tab_ref, bf16[128,4096]{1,0:T(8,128)(2,1)} %all-gather.7.cloned.1.call-done.after_ref), custom_call_target="tpu_custom_call" | custom-call | tf_op jit(solution)/shard_map/pallas_call | solution.py:33
  150.9 1.7 convert_bitcast_fusion
  153.8 24.6 %all-gather.11.cloned.1.call-done = bf16[128,4096]{1,0:T(8,128)(2,1)} async-done(((bf16[32,4096]{1,0:T(8,128)(2,1)}), bf16[128,4096]{1,0:T(8,128)(2,1)}) %all-gather.11.cloned.1.call-update) | async-done | bytes 1048592 | tf_op jit(solution)/shard_map/all_gather | solution.py:227
  178.3 1.7 fusion.25
  182.0 2.0 gather_fusion.1
  184.9 3.2 gather_fusion.5
  188.1 3.2 gather_fusion.6
  191.3 3.2 gather_fusion.7
  195.9 2.8 collective-permute-start.3
  200.5 2.6 collective-permute-start.5
  203.4 36.6 %all-gather.15.cloned.1.call-done = bf16[20480,64]{1,0:T(8,128)(2,1)} async-done(((bf16[640,64]{1,0:T(8,128)(2,1)}), bf16[20480,64]{1,0:T(8,128)(2,1)}) %all-gather.15.cloned.1.call-update) | async-done | bytes 2621456 | tf_op jit(solution)/shard_map/all_gather | solution.py:184
  239.9 5.3 constant_dynamic-update-slice_fusion.8
  247.4 8.6 %convert_element_type.63.tab_ref = f32[27648,64]{1,0:T(8,128)} convert(bf16[27648,64]{1,0:T(8,128)(2,1)} %constant_dynamic-update-slice_fusion.5) | non-fusion elementwise | flops 1769472 | bytes 10616832 | tf_op jit(solution)/shard_map/convert_element_type | solution.py:177
  256.0 61.4 %shard_map.121 = f32[4096,64]{1,0:T(8,128)} custom-call(s32[8,4096]{1,0:T(8,128)} %nb_ref.5, f32[27648,64]{1,0:T(8,128)} %convert_element_type.63.tab_ref, bf16[64,4096]{1,0:T(8,128)(2,1)} %copy.99.after_ref), custom_call_target="tpu_custom_call" | custom-call | tf_op jit(solution)/shard_map/pallas_call | solution.py:33
  317.4 1.7 convert_bitcast_fusion.1
  320.4 2.1 fusion.26
  322.5 27.4 %all-gather.17.cloned.1.call-done = bf16[256,4096]{1,0:T(8,128)(2,1)} async-done(((bf16[64,4096]{1,0:T(8,128)(2,1)}), bf16[256,4096]{1,0:T(8,128)(2,1)}) %all-gather.17.cloned.1.call-update) | async-done | bytes 2097168 | tf_op jit(solution)/shard_map/all_gather | solution.py:172
  349.9 2.3 fusion.24
  355.3 93.0 %shard_map.122 = f32[27648,64]{1,0:T(8,128)} custom-call(s32[8,4096]{1,0:T(8,128)} %nb_ref.5, f32[4096,64]{1,0:T(8,128)} %convert_element_type.69.rows_ref), custom_call_target="tpu_custom_call" | custom-call | tf_op jit(solution)/shard_map/pallas_call | solution.py:69
  448.3 5.7 convert.6
  454.0 3.3 slice.116
  458.5 6.1 %copy.106 = bf16[32,640,64]{1,2,0:T(8,128)(2,1)} copy(bf16[32,640,64]{2,1,0:T(8,128)(2,1)} %bitcast.62) | data formatting | bytes 5242880 | tf_op jit(solution)/shard_map/convert_element_type | solution.py:255
  464.7 8.0 %all-to-all-start = ((bf16[32,640,64]{1,2,0:T(8,128)(2,1)}), bf16[32,640,64]{1,2,0:T(8,128)(2,1)}, u32[]{:S(2)}, u32[]{:S(2)}) async-start(bf16[32,640,64]{1,2,0:T(8,128)(2,1)} %copy.106), calls=%async_computation | async-start | bytes 5242880 | tf_op jit(solution)/shard_map/all_to_all | solution.py:254
  473.3 2.0 fusion.21
  475.3 2.9 collective-permute-start.8
  479.4 2.2 fusion.8
  481.6 3.9 convolution_add_fusion.1.base_ref
  486.2 25.2 %collective-permute-done.8 = bf16[1024,64]{1,0:T(8,128)(2,1)} collective-permute-done((bf16[1024,64]{1,0:T(8,128)(2,1)}, bf16[1024,64]{1,0:T(8,128)(2,1)}, u32[]{:S(2)}, u32[]{:S(2)}) %collective-permute-start.8) | collective-permute-done | bytes 131104 | tf_op jit(solution)/shard_map/ppermute | solution.py:162
  512.4 2.3 collective-permute-done.7
  515.8 2.1 convert_reduce_fusion
  519.5 12.1 %shard_map.123 = f32[4096,64]{1,0:T(8,128)} custom-call(s32[3712]{0:T(1024)} %pad_add_fusion.t_ref, f32[4096,64]{1,0:T(8,128)} %convolution_add_fusion.1.base_ref, f32[3712,64]{1,0:T(8,128)} %pad_maximum_fusion.upd_ref), custom_call_target="tpu_custom_call" | custom-call | tf_op jit(solution)/shard_map/pallas_call | solution.py:102
  531.6 2.3 convolution_bitcast_fusion
  536.8 5.2 collective-permute-done.10
  542.0 2.6 collective-permute-start.11
  544.6 3.1 collective-permute-done.11
  548.4 3.5 collective-permute-done.12
  551.9 2.4 collective-permute-start.13
  554.3 3.7 collective-permute-done.13
  (113 shorter events, 36.8 us)
Async XLA Ops:
  7.2 342.7 %copy-start = (bf16[172,256]{1,0:T(8,128)(2,1)S(1)}, bf16[172,256]{1,0:T(8,128)(2,1)}, u32[]{:S(2)}) copy-start(bf16[172,256]{1,0:T(8,128)(2,1)} %param.21) | copy-start | bytes 264196
  7.2 60.1 %all-gather.9.cloned.1.call-start = ((), (), s32[]{:S(2)}) async-start(), calls=%async_computation.2 | async-start | bytes 5406720 | tf_op jit(solution)/shard_map/all_gather | solution.py:184
  13.8 75.9 %all-gather.7.cloned.1.call-start = ((), (), s32[]{:S(2)}) async-start(), calls=%async_computation.1 | async-start | bytes 1310720 | tf_op jit(solution)/shard_map/all_gather | solution.py:225
  17.2 55.3 %collective-permute-start = (bf16[1024,32]{1,0:T(8,128)(2,1)S(1)}, bf16[1024,32]{1,0:T(8,128)(2,1)S(1)}, u32[]{:S(2)}, u32[]{:S(2)}) collective-permute-start(bf16[1024,32]{1,0:T(8,128)(2,1)S(1)} %broadcast_select_fusion.5), channel_id=1, source_target_pairs={{0,4},{4,0},{8,12},{12,8},{16,20},{20,16},{24,28},{28,24},{32,36},... | collective-permute-start | bytes 196616 | tf_op jit(solution)/shard_map/ppermute | solution.py:162
  22.1 51.1 %collective-permute-start.1 = (bf16[1024,32]{1,0:T(8,128)(2,1)S(1)}, bf16[1024,32]{1,0:T(8,128)(2,1)S(1)}, u32[]{:S(2)}, u32[]{:S(2)}) collective-permute-start(bf16[1024,32]{1,0:T(8,128)(2,1)S(1)} %broadcast_select_fusion.4), channel_id=1, source_target_pairs={{0,8},{4,12},{8,0},{12,4},{16,24},{20,28},{24,16},{28,20},{32,40},... | collective-permute-start | bytes 196616 | tf_op jit(solution)/shard_map/ppermute | solution.py:162
  27.4 46.6 %collective-permute-start.2 = (bf16[1024,32]{1,0:T(8,128)(2,1)S(1)}, bf16[1024,32]{1,0:T(8,128)(2,1)S(1)}, u32[]{:S(2)}, u32[]{:S(2)}) collective-permute-start(bf16[1024,32]{1,0:T(8,128)(2,1)S(1)} %broadcast_select_fusion.3), channel_id=1, source_target_pairs={{0,16},{4,20},{8,24},{12,28},{16,0},{20,4},{24,8},{28,12},{32,48},... | collective-permute-start | bytes 196616 | tf_op jit(solution)/shard_map/ppermute | solution.py:162
  30.8 147.5 %all-gather.11.cloned.1.call-start = ((), (), s32[]{:S(2)}) async-start(), calls=%async_computation.3 | async-start | bytes 1310720 | tf_op jit(solution)/shard_map/all_gather | solution.py:227
  150.9 27.4 %copy-start.11 = (bf16[64,128]{1,0:T(8,128)(2,1)S(1)}, bf16[64,128]{1,0:T(8,128)(2,1)}, u32[]{:S(2)}) copy-start(bf16[64,128]{1,0:T(8,128)(2,1)} %param.19) | copy-start | bytes 49156
  152.6 27.4 %copy-start.5 = (bf16[128,4096]{1,0:T(8,128)(2,1)S(1)}, bf16[128,4096]{1,0:T(8,128)(2,1)}, u32[]{:S(2)}) copy-start(bf16[128,4096]{1,0:T(8,128)(2,1)} %all-gather.7.cloned.1.call-done.after_ref) | copy-start | bytes 3145732
  152.7 27.4 %copy-start.12 = (bf16[64,128]{1,0:T(8,128)(2,1)S(1)}, bf16[64,128]{1,0:T(8,128)(2,1)}, u32[]{:S(2)}) copy-start(bf16[64,128]{1,0:T(8,128)(2,1)} %param.18) | copy-start | bytes 49156
  153.7 86.2 %all-gather.15.cloned.1.call-start = ((), (), s32[]{:S(2)}) async-start(), calls=%async_computation.5 | async-start | bytes 5406720 | tf_op jit(solution)/shard_map/all_gather | solution.py:184
  180.6 13.9 %copy-start.1 = (bf16[64,4096]{0,1:T(8,128)(2,1)}, bf16[64,4096]{0,1:T(8,128)(2,1)S(1)}, u32[]{:S(2)}) copy-start(bf16[64,4096]{0,1:T(8,128)(2,1)S(1)} %get-tuple-element.38) | copy-start | bytes 1572868
  184.8 135.6 %all-gather.13.cloned.1.call-start = ((), (), s32[]{:S(2)}) async-start(), calls=%async_computation.4 | async-start | bytes 2621440 | tf_op jit(solution)/shard_map/all_gather | solution.py:171
  195.9 49.4 %collective-permute-start.3 = (bf16[1024,64]{1,0:T(8,128)(2,1)S(1)}, bf16[1024,64]{1,0:T(8,128)(2,1)S(1)}, u32[]{:S(2)}, u32[]{:S(2)}) collective-permute-start(bf16[1024,64]{1,0:T(8,128)(2,1)S(1)} %broadcast_select_fusion.2), channel_id=1, source_target_pairs={{0,4},{4,0},{8,12},{12,8},{16,20},{20,16},{24,28},{28,24},{32,36},... | collective-permute-start | bytes 393224 | tf_op jit(solution)/shard_map/ppermute | solution.py:162
  198.9 47.1 %collective-permute-start.4 = (bf16[1024,64]{1,0:T(8,128)(2,1)S(1)}, bf16[1024,64]{1,0:T(8,128)(2,1)S(1)}, u32[]{:S(2)}, u32[]{:S(2)}) collective-permute-start(bf16[1024,64]{1,0:T(8,128)(2,1)S(1)} %broadcast_select_fusion.1), channel_id=1, source_target_pairs={{0,8},{4,12},{8,0},{12,4},{16,24},{20,28},{24,16},{28,20},{32,40},... | collective-permute-start | bytes 393224 | tf_op jit(solution)/shard_map/ppermute | solution.py:162
  200.5 46.2 %collective-permute-start.5 = (bf16[1024,64]{1,0:T(8,128)(2,1)S(1)}, bf16[1024,64]{1,0:T(8,128)(2,1)S(1)}, u32[]{:S(2)}, u32[]{:S(2)}) collective-permute-start(bf16[1024,64]{1,0:T(8,128)(2,1)S(1)} %broadcast_select_fusion), channel_id=1, source_target_pairs={{0,16},{4,20},{8,24},{12,28},{16,0},{20,4},{24,8},{28,12},{32,48},... | collective-permute-start | bytes 393224 | tf_op jit(solution)/shard_map/ppermute | solution.py:162
  203.1 146.7 %all-gather.17.cloned.1.call-start = ((), (), s32[]{:S(2)}) async-start(), calls=%async_computation.6 | async-start | bytes 2621440 | tf_op jit(solution)/shard_map/all_gather | solution.py:172
  317.4 2.9 copy-start.8
  322.5 29.7 %copy-start.13 = (s32[4096]{0:T(1024)S(1)}, s32[4096]{0:T(1024)}, u32[]{:S(2)}) copy-start(s32[4096]{0:T(1024)} %param.17) | copy-start | bytes 49156
  454.0 4.5 copy-start.3
  464.7 8.0 %copy-start.9 = (s32[3,1024]{1,0:T(4,128)S(1)}, s32[3,1024]{1,0:T(4,128)}, u32[]{:S(2)}) copy-start(s32[3,1024]{1,0:T(4,128)} %param.16) | copy-start | bytes 36868
  464.7 8.1 %copy-start.10 = (s32[640]{0:T(1024)S(1)}, s32[640]{0:T(1024)}, u32[]{:S(2)}) copy-start(s32[640]{0:T(1024)} %param.15) | copy-start | bytes 7684
  464.7 51.1 %all-to-all-start = ((bf16[32,640,64]{1,2,0:T(8,128)(2,1)}), bf16[32,640,64]{1,2,0:T(8,128)(2,1)}, u32[]{:S(2)}, u32[]{:S(2)}) async-start(bf16[32,640,64]{1,2,0:T(8,128)(2,1)} %copy.106), calls=%async_computation | async-start | bytes 5242880 | tf_op jit(solution)/shard_map/all_to_all | solution.py:254
  475.3 36.1 %collective-permute-start.8 = (bf16[1024,64]{1,0:T(8,128)(2,1)}, bf16[1024,64]{1,0:T(8,128)(2,1)}, u32[]{:S(2)}, u32[]{:S(2)}) collective-permute-start(bf16[1024,64]{1,0:T(8,128)(2,1)} %get-tuple-element.29), channel_id=1, source_target_pairs={{0,16},{4,20},{8,24},{12,28},{16,0},{20,4},{24,8},{28,12},{32,48},... | collective-permute-start | bytes 393224 | tf_op jit(solution)/shard_map/ppermute | solution.py:162
  478.2 36.6 %collective-permute-start.7 = (bf16[1024,64]{1,0:T(8,128)(2,1)}, bf16[1024,64]{1,0:T(8,128)(2,1)S(1)}, u32[]{:S(2)}, u32[]{:S(2)}) collective-permute-start(bf16[1024,64]{1,0:T(8,128)(2,1)} %get-tuple-element.30), channel_id=1, source_target_pairs={{0,8},{4,12},{8,0},{12,4},{16,24},{20,28},{24,16},{28,20},{32,40},... | collective-permute-start | bytes 393224 | tf_op jit(solution)/shard_map/ppermute | solution.py:162
  478.5 36.3 %collective-permute-start.6 = (bf16[1024,64]{1,0:T(8,128)(2,1)}, bf16[1024,64]{1,0:T(8,128)(2,1)}, u32[]{:S(2)}, u32[]{:S(2)}) collective-permute-start(bf16[1024,64]{1,0:T(8,128)(2,1)} %get-tuple-element.28), channel_id=1, source_target_pairs={{0,4},{4,0},{8,12},{12,8},{16,20},{20,16},{24,28},{28,24},{32,36},... | collective-permute-start | bytes 393224 | tf_op jit(solution)/shard_map/ppermute | solution.py:162
  481.6 3.9 copy-start.2
  519.5 12.1 %copy-start.7 = (bf16[128,4096]{1,0:T(8,128)(2,1)S(1)}, bf16[128,4096]{1,0:T(8,128)(2,1)}, u32[]{:S(2)}) copy-start(bf16[128,4096]{1,0:T(8,128)(2,1)} %all-gather.11.cloned.1.call-done) | copy-start | bytes 3145732
  531.6 2.3 copy-start.4
  531.6 2.5 copy-start.6
  534.6 2.1 collective-permute-start.9
  536.7 5.3 collective-permute-start.10
  542.0 5.7 collective-permute-start.11
  547.7 4.2 collective-permute-start.12
  551.9 6.1 %collective-permute-start.13 = (f32[38400]{0:T(1024)S(1)}, f32[38400]{0:T(1024)S(1)}, u32[]{:S(2)}, u32[]{:S(2)}) collective-permute-start(f32[38400]{0:T(1024)S(1)} %add.66), channel_id=1, source_target_pairs={{0,64},{4,68},{8,72},{12,76},{16,80},{20,84},{24,88},{28,92},{32,9... | collective-permute-start | bytes 460808 | tf_op jit(solution)/shard_map/ppermute | solution.py:136
Sparse Core Ops, SparseCore 0:
  13.9 53.3 all-gather.8
  68.9 20.7 all-gather.6
  153.9 24.4 all-gather.10
  184.9 54.9 all-gather.14
  241.4 29.2 all-gather.12
  320.5 29.3 all-gather.16

commit v8 on v7

--- a/solution.py
+++ b/solution.py
@@ -45,12 +45,13 @@
     )(neighbours, table, after)
 
 
-def scatter_mean(rows, neighbours, size):
+def scatter_mean(rows, neighbours, own, hubs, bands, chunk=512):
     nodes, width = rows.shape
     degree = neighbours.shape[0]
     half = degree // 2
-
-    def kernel(nb_ref, rows_ref, first_ref, second_ref):
+    size = own + hubs + bands
+
+    def kernel(nb_ref, rows_ref, own_ref, hub_ref, band_ref, first_ref, second_ref):
         first_ref[...] = jnp.zeros_like(first_ref)
         second_ref[...] = jnp.zeros_like(second_ref)
 
@@ -64,7 +65,16 @@
             return carry
 
         lax.fori_loop(0, nodes, step, 0, unroll=4)
-        first_ref[...] = (first_ref[...] + second_ref[...]) * (1.0 / degree)
+
+        for out_ref, start, count in ((own_ref, 0, own), (hub_ref, own, hubs), (band_ref, own + hubs, bands)):
+
+            def finish(c, carry, out_ref=out_ref, start=start):
+                r = pl.multiple_of(c * chunk, chunk)
+                total = first_ref[pl.ds(start + r, chunk), :] + second_ref[pl.ds(start + r, chunk), :]
+                out_ref[pl.ds(r, chunk), :] = (total * (1.0 / degree)).astype(out_ref.dtype)
+                return carry
+
+            lax.fori_loop(0, count // chunk, finish, 0)
 
     return pl.pallas_call(
         kernel,
@@ -72,10 +82,33 @@
             pl.BlockSpec(memory_space=pltpu.SMEM),
             pl.BlockSpec(memory_space=pltpu.VMEM),
         ],
-        out_specs=pl.BlockSpec(memory_space=pltpu.VMEM),
-        out_shape=jax.ShapeDtypeStruct((size, width), jnp.float32),
-        scratch_shapes=[pltpu.VMEM((size, width), jnp.float32)],
+        out_specs=(
+            pl.BlockSpec(memory_space=pltpu.VMEM),
+            pl.BlockSpec(memory_space=pltpu.VMEM),
+            pl.BlockSpec(memory_space=pltpu.VMEM),
+        ),
+        out_shape=(
+            jax.ShapeDtypeStruct((own, width), jnp.float32),
+            jax.ShapeDtypeStruct((hubs, width), jnp.bfloat16),
+            jax.ShapeDtypeStruct((bands, width), jnp.bfloat16),
+        ),
+        scratch_shapes=[
+            pltpu.VMEM((size, width), jnp.float32),
+            pltpu.VMEM((size, width), jnp.float32),
+        ],
     )(neighbours, rows)
+
+
+def feat_gather(value, axis):
+    count = lax.axis_size(axis)
+    index = lax.axis_index(axis)
+    got = [value] + [
+        lax.ppermute(value, axis, [(source, (source + shift) % count) for source in range(count)])
+        for shift in range(1, count)
+    ]
+    stacked = jnp.stack(got[::-1] * 2)
+    full = lax.dynamic_slice_in_dim(stacked, (count - 1 - index) % count, count, axis=0)
+    return full.reshape(count * value.shape[0], value.shape[1])
 
 
 def land_rows(base, targets, updates):
@@ -224,7 +257,7 @@
     nodes_all = rows * lax.axis_size("dom")
     full_input = lax.all_gather(features, "feat", axis=0, tiled=True)
     mean_one = average(source_table(features, hub_rows, send_rows), neighbours, full_input)
-    full_mean = lax.all_gather(mean_one, "feat", axis=0, tiled=True)
+    full_mean = feat_gather(mean_one, "feat")
     pre_act = jnp.dot(inner_self, full_input, preferred_element_type=jnp.float32)
     pre_act = pre_act + jnp.dot(inner_neighbour, full_mean, preferred_element_type=jnp.float32)
     hidden = jnp.maximum(pre_act, 0.0).astype(jnp.bfloat16)
@@ -233,7 +266,8 @@
     offset = lax.axis_index("feat") * width
     self_cols = lax.dynamic_slice_in_dim(outer_self, offset, width, 1)
     neigh_cols = lax.dynamic_slice_in_dim(outer_neighbour, offset, width, 1)
-    full_hidden, full_two = widen(hidden, mean_two)
+    full_hidden = lax.all_gather(hidden, "feat", axis=0, tiled=True)
+    full_two = feat_gather(mean_two, "feat")
     logits = jnp.dot(outer_self, full_hidden, preferred_element_type=jnp.float32)
     logits = logits + jnp.dot(outer_neighbour, full_two, preferred_element_type=jnp.float32)
     logit_grad = class_gradient(logits, labels, nodes_all)
@@ -246,22 +280,21 @@
     band = send_rows.shape[1]
     span = rows + hub_count + send_rows.shape[0] * band
     back_rows = back_mean.T.astype(jnp.float32)
-    spread = scatter_mean(back_rows, neighbours, span)
-    grad_rows = direct.T + spread[:rows]
+    own_grad, hub_grad, band_grad = scatter_mean(
+        back_rows, neighbours, rows, hub_count, send_rows.shape[0] * band
+    )
+    grad_rows = direct.T + own_grad
     owners = lax.axis_size("dom")
-    hub_parts = spread[rows : rows + hub_count].reshape(owners, hub_count // owners, width)
+    hub_parts = hub_grad.reshape(owners, hub_count // owners, width)
     hub_back = jnp.sum(
-        lax.all_to_all(
-            hub_parts.astype(jnp.bfloat16), "dom", split_axis=0, concat_axis=0, tiled=True
-        ).astype(jnp.float32),
+        lax.all_to_all(hub_parts, "dom", split_axis=0, concat_axis=0, tiled=True).astype(
+            jnp.float32
+        ),
         axis=0,
     )
-    base = rows + hub_count
     landed = [hub_back]
     for bit_index in range(send_rows.shape[0]):
-        outgoing = spread[base + bit_index * band : base + (bit_index + 1) * band].astype(
-            jnp.bfloat16
-        )
+        outgoing = band_grad[bit_index * band : (bit_index + 1) * band]
         landed.append(trade(outgoing, bit_index).astype(jnp.float32))
     targets = jnp.concatenate([hub_rows, send_rows.reshape(-1)])
     grad_rows = land_rows(grad_rows, targets, jnp.concatenate(landed, axis=0))

time: 571 us -> 575 us (level)
  local copies, waits for them, and re-layouts: 60.8 us -> 83.1 us
  waiting for transfers between devices: 174 us -> 159 us
    all_gather x3 -> x1, waiting for transfers between devices: 51.9 us -> 0.01 us  [body(): full_hidden = lax.all_gather(hidden, 'feat', axis=0, tiled=True)]
    ppermute x0 -> x6, waiting for transfers between devices: none -> 33.7 us  [feat_gather(): lax.ppermute(value, axis, [(source, (source + shift) % count) for source...]
    unnamed x38 -> x65, local copies, waits for them, and re-layouts: 18.9 us -> 29.2 us
    dynamic_slice x0 -> x3, local copies, waits for them, and re-layouts: none -> 9.42 us  [feat_gather(): lax.dynamic_slice_in_dim(stacked, (count - 1 - index) % count, count, axi...]
    ppermute x0 -> x6, starting transfers between devices: none -> 6.87 us  [feat_gather(): lax.ppermute(value, axis, [(source, (source + shift) % count) for source...]
    convert_element_type x1 -> x0, local copies, waits for them, and re-layouts: 6.14 us -> none  [body(): hub_parts.astype(jnp.bfloat16)]
    reshape x0 -> x1, local copies, waits for them, and re-layouts: none -> 6.12 us  [body(): hub_parts = hub_grad.reshape(owners, hub_count // owners, width)]
  transfers between devices with their start and end apart: 21 -> 25, of which waited for: 12 -> 15; matrix products, arithmetic and copies ran while one was open for 13% -> 13% of each run, Pallas kernels for 11% -> 11%
where the time goes in v8:
time: 575 us; the launch traced here: 570 us
  Pallas kernels  227 us (39%)
  waiting for transfers between devices  159 us (28%)
  local copies, waits for them, and re-layouts  83.1 us (14%)
  other arithmetic  39.1 us (7%)
  starting transfers between devices  33.7 us (6%)
  matrix products  15.2 us (3%)
  between operations  14.3 us (2%)
    pallas_call x2, Pallas kernels, gather_mean(): pl.pallas_call(kernel, grid_spec=pltpu.PrefetchScalarGridSpec(num_scalar_...  123 us
    pallas_call x1, Pallas kernels, scatter_mean(): pl.pallas_call(kernel, in_specs=[pl.BlockSpec(memory_space=pltpu.SMEM), p...  91.7 us
    all_gather x2, waiting for transfers between devices, source_table(): hub_all = lax.all_gather(hub_local, 'dom', axis=0, tiled=True)  68.9 us
    ppermute x6, waiting for transfers between devices, feat_gather(): lax.ppermute(value, axis, [(source, (source + shift) % count) for source...  33.7 us
    ppermute x9, waiting for transfers between devices, partner(): return lax.ppermute(value, axis, pairs)  31.4 us
    unnamed x65, local copies, waits for them, and re-layouts  29.2 us
    gather x6, local copies, waits for them, and re-layouts, source_table(): jnp.take(local_rows, send_rows[bit_index], axis=0)  19.2 us
    ppermute x5, waiting for transfers between devices, tree_sum(): value = value + lax.ppermute(value, axis, pairs)  18.1 us
  transfers between devices with their start and end apart: 25, of which 15 were waited for; matrix products, arithmetic and copies ran while one was open for 13% of the time, Pallas kernels for 11%

profile of v8, /device:TPU:1, one launch (start us, length us, event | category | flops | bytes accessed | tf_op | source)
XLA Modules:
  0.0 570.4 jit_solution(1248250242277264586)
XLA Ops:
  10.9 2.0 gather_fusion
  13.8 3.2 gather_fusion.2
  18.7 3.2 gather_fusion.3
  24.0 3.2 gather_fusion.4
  27.4 3.4 collective-permute-start.2
  31.9 35.3 %all-gather.7.cloned.1.call-done = bf16[20480,32]{1,0:T(8,128)(2,1)} async-done(((bf16[640,32]{1,0:T(8,128)(2,1)}), bf16[20480,32]{1,0:T(8,128)(2,1)}) %all-gather.7.cloned.1.call-update) | async-done | bytes 1310736 | tf_op jit(solution)/shard_map/all_gather | solution.py:217
  67.2 5.3 constant_dynamic-update-slice_fusion.3
  74.7 8.6 %convert_element_type.51.tab_ref = f32[27648,32]{1,0:T(8,128)} convert(bf16[27648,32]{1,0:T(8,128)(2,1)} %constant_dynamic-update-slice_fusion) | non-fusion elementwise | flops 884736 | bytes 5308416 | tf_op jit(solution)/shard_map/convert_element_type | solution.py:210
  83.3 6.4 %all-gather.5.cloned.1.call-done.after_ref = bf16[128,4096]{1,0:T(8,128)(2,1)} async-done(((bf16[32,4096]{1,0:T(8,128)(2,1)}), bf16[128,4096]{1,0:T(8,128)(2,1)}) %all-gather.5.cloned.1.call-update) | async-done | bytes 1048592 | tf_op jit(solution)/shard_map/all_gather | solution.py:258
  89.7 61.3 %shard_map.120 = f32[4096,32]{1,0:T(8,128)} custom-call(s32[8,4096]{1,0:T(8,128)} %nb_ref.5, f32[27648,32]{1,0:T(8,128)} %convert_element_type.51.tab_ref, bf16[128,4096]{1,0:T(8,128)(2,1)} %all-gather.5.cloned.1.call-done.after_ref), custom_call_target="tpu_custom_call" | custom-call | tf_op jit(solution)/shard_map/pallas_call | solution.py:33
  156.8 2.8 collective-permute-done.3
  159.6 2.2 collective-permute-done.4
  161.8 8.1 %collective-permute-done.5 = bf16[32,4096]{1,0:T(8,128)(2,1)S(1)} collective-permute-done((bf16[32,4096]{1,0:T(8,128)(2,1)S(1)}, bf16[32,4096]{1,0:T(8,128)(2,1)S(1)}, u32[]{:S(2)}, u32[]{:S(2)}) %collective-permute-start.5) | collective-permute-done | bytes 262176 | tf_op jit(solution)/shard_map/ppermute | solution.py:106
  176.6 3.2 gather_fusion.5
  179.8 3.2 gather_fusion.6
  183.0 3.2 gather_fusion.7
  189.2 2.7 collective-permute-start.8
  193.0 33.6 %all-gather.11.cloned.1.call-done = bf16[20480,64]{1,0:T(8,128)(2,1)} async-done(((bf16[640,64]{1,0:T(8,128)(2,1)}), bf16[20480,64]{1,0:T(8,128)(2,1)}) %all-gather.11.cloned.1.call-update) | async-done | bytes 2621456 | tf_op jit(solution)/shard_map/all_gather | solution.py:217
  226.6 5.3 constant_dynamic-update-slice_fusion.10
  234.1 8.6 %convert_element_type.56.tab_ref = f32[27648,64]{1,0:T(8,128)} convert(bf16[27648,64]{1,0:T(8,128)(2,1)} %constant_dynamic-update-slice_fusion.7) | non-fusion elementwise | flops 1769472 | bytes 10616832 | tf_op jit(solution)/shard_map/convert_element_type | solution.py:210
  242.7 61.4 %shard_map.121 = f32[4096,64]{1,0:T(8,128)} custom-call(s32[8,4096]{1,0:T(8,128)} %nb_ref.5, f32[27648,64]{1,0:T(8,128)} %convert_element_type.56.tab_ref, bf16[64,4096]{1,0:T(8,128)(2,1)} %copy.135.after_ref), custom_call_target="tpu_custom_call" | custom-call | tf_op jit(solution)/shard_map/pallas_call | solution.py:33
  307.0 2.5 collective-permute-start.9
  309.5 3.7 fusion.24
  314.3 17.6 %collective-permute-done.9 = bf16[64,4096]{1,0:T(8,128)(2,1)S(1)} collective-permute-done((bf16[64,4096]{1,0:T(8,128)(2,1)}, bf16[64,4096]{1,0:T(8,128)(2,1)S(1)}, u32[]{:S(2)}, u32[]{:S(2)}) %collective-permute-start.9) | collective-permute-done | bytes 524320 | tf_op jit(solution)/shard_map/ppermute | solution.py:106
  337.1 3.0 collective-permute-done.11
  340.1 2.4 copy.144
  342.4 2.3 bitcast_dynamic-update-slice_fusion.2
  350.7 4.5 constant_dynamic-slice_fusion
  355.2 4.8 copy.145
  360.0 3.2 fusion.22
  366.2 2.4 copy.146
  368.6 2.7 convert_element_type.62.rows_ref
  371.3 91.7 %shard_map.122 = (f32[4096,64]{1,0:T(8,128)}, bf16[20480,64]{1,0:T(8,128)(2,1)}, bf16[3072,64]{1,0:T(8,128)(2,1)}) custom-call(s32[8,4096]{1,0:T(8,128)} %nb_ref.5, f32[4096,64]{1,0:T(8,128)} %convert_element_type.62.rows_ref), custom_call_target="tpu_custom_call" | custom-call | tf_op jit(solution)/shard_map/pallas_call | solution.py:79
  463.0 6.1 %copy.148 = bf16[32,640,64]{1,2,0:T(8,128)(2,1)} copy(bf16[32,640,64]{2,1,0:T(8,128)(2,1)} %bitcast.93) | data formatting | bytes 5242880 | tf_op jit(solution)/shard_map/reshape | solution.py:288
  469.1 5.5 all-to-all-start
  475.3 2.0 fusion.19
  479.0 2.4 collective-permute-start.14
  482.0 2.2 convolution_add_fusion.1.base_ref
  485.8 25.3 %collective-permute-done.13 = bf16[1024,64]{1,0:T(8,128)(2,1)} collective-permute-done((bf16[1024,64]{1,0:T(8,128)(2,1)}, bf16[1024,64]{1,0:T(8,128)(2,1)}, u32[]{:S(2)}, u32[]{:S(2)}) %collective-permute-start.13) | collective-permute-done | bytes 131104 | tf_op jit(solution)/shard_map/ppermute | solution.py:195
  512.1 6.1 %collective-permute-done.14 = bf16[1024,64]{1,0:T(8,128)(2,1)} collective-permute-done((bf16[1024,64]{1,0:T(8,128)(2,1)}, bf16[1024,64]{1,0:T(8,128)(2,1)}, u32[]{:S(2)}, u32[]{:S(2)}) %collective-permute-start.14) | collective-permute-done | bytes 131104 | tf_op jit(solution)/shard_map/ppermute | solution.py:195
  519.2 2.1 convert_reduce_fusion
  522.9 12.1 %shard_map.123 = f32[4096,64]{1,0:T(8,128)} custom-call(s32[3712]{0:T(1024)} %pad_add_fusion.t_ref, f32[4096,64]{1,0:T(8,128)} %convolution_add_fusion.1.base_ref, f32[3712,64]{1,0:T(8,128)} %pad_maximum_fusion.upd_ref), custom_call_target="tpu_custom_call" | custom-call | tf_op jit(solution)/shard_map/pallas_call | solution.py:135
  535.0 2.3 convolution_bitcast_fusion
  540.2 5.2 collective-permute-done.16
  546.5 4.6 collective-permute-done.17
  552.0 3.3 collective-permute-done.18
  555.3 2.4 collective-permute-start.19
  557.7 4.0 collective-permute-done.19
  (154 shorter events, 63.8 us)
Async XLA Ops:
  7.2 352.8 %copy-start = (bf16[172,256]{1,0:T(8,128)(2,1)S(1)}, bf16[172,256]{1,0:T(8,128)(2,1)}, u32[]{:S(2)}) copy-start(bf16[172,256]{1,0:T(8,128)(2,1)} %param.21) | copy-start | bytes 264196
  7.2 60.1 %all-gather.7.cloned.1.call-start = ((), (), s32[]{:S(2)}) async-start(), calls=%async_computation.2 | async-start | bytes 5406720 | tf_op jit(solution)/shard_map/all_gather | solution.py:217
  13.8 75.9 %all-gather.5.cloned.1.call-start = ((), (), s32[]{:S(2)}) async-start(), calls=%async_computation.1 | async-start | bytes 1310720 | tf_op jit(solution)/shard_map/all_gather | solution.py:258
  17.2 55.3 %collective-permute-start = (bf16[1024,32]{1,0:T(8,128)(2,1)S(1)}, bf16[1024,32]{1,0:T(8,128)(2,1)S(1)}, u32[]{:S(2)}, u32[]{:S(2)}) collective-permute-start(bf16[1024,32]{1,0:T(8,128)(2,1)S(1)} %broadcast_select_fusion.5), channel_id=1, source_target_pairs={{0,4},{4,0},{8,12},{12,8},{16,20},{20,16},{24,28},{28,24},{32,36},... | collective-permute-start | bytes 196616 | tf_op jit(solution)/shard_map/ppermute | solution.py:195
  22.1 51.1 %collective-permute-start.1 = (bf16[1024,32]{1,0:T(8,128)(2,1)S(1)}, bf16[1024,32]{1,0:T(8,128)(2,1)S(1)}, u32[]{:S(2)}, u32[]{:S(2)}) collective-permute-start(bf16[1024,32]{1,0:T(8,128)(2,1)S(1)} %broadcast_select_fusion.4), channel_id=1, source_target_pairs={{0,8},{4,12},{8,0},{12,4},{16,24},{20,28},{24,16},{28,20},{32,40},... | collective-permute-start | bytes 196616 | tf_op jit(solution)/shard_map/ppermute | solution.py:195
  27.4 46.6 %collective-permute-start.2 = (bf16[1024,32]{1,0:T(8,128)(2,1)S(1)}, bf16[1024,32]{1,0:T(8,128)(2,1)S(1)}, u32[]{:S(2)}, u32[]{:S(2)}) collective-permute-start(bf16[1024,32]{1,0:T(8,128)(2,1)S(1)} %broadcast_select_fusion.3), channel_id=1, source_target_pairs={{0,16},{4,20},{8,24},{12,28},{16,0},{20,4},{24,8},{28,12},{32,48},... | collective-permute-start | bytes 196616 | tf_op jit(solution)/shard_map/ppermute | solution.py:195
  30.8 195.8 %all-gather.11.cloned.1.call-start = ((), (), s32[]{:S(2)}) async-start(), calls=%async_computation.4 | async-start | bytes 5406720 | tf_op jit(solution)/shard_map/all_gather | solution.py:217
  153.2 6.4 %collective-permute-start.3 = (bf16[32,4096]{1,0:T(8,128)(2,1)S(1)}, bf16[32,4096]{1,0:T(8,128)(2,1)S(1)}, u32[]{:S(2)}, u32[]{:S(2)}) collective-permute-start(bf16[32,4096]{1,0:T(8,128)(2,1)S(1)} %copy.128), channel_id=1, source_target_pairs={{0,3},{1,0},{2,1},{3,2},{4,7},{5,4},{6,5},{7,6},{8,11},{9,8},{10,9... | collective-permute-start | bytes 786440 | tf_op jit(solution)/shard_map/ppermute | solution.py:106
  154.9 6.8 %collective-permute-start.4 = (bf16[32,4096]{1,0:T(8,128)(2,1)S(1)}, bf16[32,4096]{1,0:T(8,128)(2,1)S(1)}, u32[]{:S(2)}, u32[]{:S(2)}) collective-permute-start(bf16[32,4096]{1,0:T(8,128)(2,1)S(1)} %copy.128), channel_id=1, source_target_pairs={{0,2},{1,3},{2,0},{3,1},{4,6},{5,7},{6,4},{7,5},{8,10},{9,11},{10,... | collective-permute-start | bytes 786440 | tf_op jit(solution)/shard_map/ppermute | solution.py:106
  155.7 14.2 %collective-permute-start.5 = (bf16[32,4096]{1,0:T(8,128)(2,1)S(1)}, bf16[32,4096]{1,0:T(8,128)(2,1)S(1)}, u32[]{:S(2)}, u32[]{:S(2)}) collective-permute-start(bf16[32,4096]{1,0:T(8,128)(2,1)S(1)} %copy.128), channel_id=1, source_target_pairs={{0,1},{1,2},{2,3},{3,0},{4,5},{5,6},{6,7},{7,4},{8,9},{9,10},{10,1... | collective-permute-start | bytes 786440 | tf_op jit(solution)/shard_map/ppermute | solution.py:106
  169.9 1.3 copy-start.18
  170.2 1.1 copy-start.5
  170.2 1.6 copy-start.12
  170.2 1.6 copy-start.19
  176.5 133.0 %all-gather.9.cloned.1.call-start = ((), (), s32[]{:S(2)}) async-start(), calls=%async_computation.3 | async-start | bytes 2621440 | tf_op jit(solution)/shard_map/all_gather | solution.py:269
  186.4 45.5 %collective-permute-start.6 = (bf16[1024,64]{1,0:T(8,128)(2,1)S(1)}, bf16[1024,64]{1,0:T(8,128)(2,1)S(1)}, u32[]{:S(2)}, u32[]{:S(2)}) collective-permute-start(bf16[1024,64]{1,0:T(8,128)(2,1)S(1)} %broadcast_select_fusion.2), channel_id=1, source_target_pairs={{0,4},{4,0},{8,12},{12,8},{16,20},{20,16},{24,28},{28,24},{32,36},... | collective-permute-start | bytes 393224 | tf_op jit(solution)/shard_map/ppermute | solution.py:195
  187.6 45.0 %collective-permute-start.7 = (bf16[1024,64]{1,0:T(8,128)(2,1)S(1)}, bf16[1024,64]{1,0:T(8,128)(2,1)S(1)}, u32[]{:S(2)}, u32[]{:S(2)}) collective-permute-start(bf16[1024,64]{1,0:T(8,128)(2,1)S(1)} %broadcast_select_fusion.1), channel_id=1, source_target_pairs={{0,8},{4,12},{8,0},{12,4},{16,24},{20,28},{24,16},{28,20},{32,40},... | collective-permute-start | bytes 393224 | tf_op jit(solution)/shard_map/ppermute | solution.py:195
  189.2 44.2 %collective-permute-start.8 = (bf16[1024,64]{1,0:T(8,128)(2,1)S(1)}, bf16[1024,64]{1,0:T(8,128)(2,1)S(1)}, u32[]{:S(2)}, u32[]{:S(2)}) collective-permute-start(bf16[1024,64]{1,0:T(8,128)(2,1)S(1)} %broadcast_select_fusion), channel_id=1, source_target_pairs={{0,16},{4,20},{8,24},{12,28},{16,0},{20,4},{24,8},{28,12},{32,48},... | collective-permute-start | bytes 393224 | tf_op jit(solution)/shard_map/ppermute | solution.py:195
  304.1 5.4 copy-start.15
  307.0 24.9 %collective-permute-start.9 = (bf16[64,4096]{1,0:T(8,128)(2,1)}, bf16[64,4096]{1,0:T(8,128)(2,1)S(1)}, u32[]{:S(2)}, u32[]{:S(2)}) collective-permute-start(bf16[64,4096]{1,0:T(8,128)(2,1)} %copy.139), channel_id=1, source_target_pairs={{0,3},{1,0},{2,1},{3,2},{4,7},{5,4},{6,5},{7,6},{8,11},{9,8},{10,9... | collective-permute-start | bytes 1572872 | tf_op jit(solution)/shard_map/ppermute | solution.py:106
  313.2 20.4 %collective-permute-start.10 = (bf16[64,4096]{1,0:T(8,128)(2,1)}, bf16[64,4096]{1,0:T(8,128)(2,1)}, u32[]{:S(2)}, u32[]{:S(2)}) collective-permute-start(bf16[64,4096]{1,0:T(8,128)(2,1)} %copy.139), channel_id=1, source_target_pairs={{0,2},{1,3},{2,0},{3,1},{4,6},{5,7},{6,4},{7,5},{8,10},{9,11},{10,... | collective-permute-start | bytes 1572872 | tf_op jit(solution)/shard_map/ppermute | solution.py:106
  313.7 26.4 %collective-permute-start.11 = (bf16[64,4096]{1,0:T(8,128)(2,1)}, bf16[64,4096]{1,0:T(8,128)(2,1)}, u32[]{:S(2)}, u32[]{:S(2)}) collective-permute-start(bf16[64,4096]{1,0:T(8,128)(2,1)} %copy.139), channel_id=1, source_target_pairs={{0,1},{1,2},{2,3},{3,0},{4,5},{5,6},{6,7},{7,4},{8,9},{9,10},{10,1... | collective-permute-start | bytes 1572872 | tf_op jit(solution)/shard_map/ppermute | solution.py:106
  332.4 2.7 copy-start.7
  335.1 1.0 copy-start.9
  337.1 7.6 %copy-start.1 = (f32[4096,64]{1,0:T(8,128)S(1)}, f32[4096,64]{1,0:T(8,128)}, u32[]{:S(2)}) copy-start(f32[4096,64]{1,0:T(8,128)} %shard_map.121) | copy-start | bytes 3145732
  344.7 1.6 copy-start.8
  344.7 2.7 copy-start.10
  346.3 2.2 copy-start.11
  360.0 3.2 copy-start.20
  363.8 1.1 copy-start.2
  469.1 5.5 copy-start.16
  469.1 5.5 copy-start.17
  469.1 50.1 %all-to-all-start = ((bf16[32,640,64]{1,2,0:T(8,128)(2,1)}), bf16[32,640,64]{1,2,0:T(8,128)(2,1)}, u32[]{:S(2)}, u32[]{:S(2)}) async-start(bf16[32,640,64]{1,2,0:T(8,128)(2,1)} %copy.148), calls=%async_computation | async-start | bytes 5242880 | tf_op jit(solution)/shard_map/all_to_all | solution.py:290
  474.6 6.8 %copy-start.3 = (bf16[172,4096]{1,0:T(8,128)(2,1)S(1)}, bf16[172,4096]{1,0:T(8,128)(2,1)}, u32[]{:S(2)}) copy-start(bf16[172,4096]{1,0:T(8,128)(2,1)} %copy-done.2) | copy-start | bytes 4227076
  477.3 4.7 copy-start.14
  477.3 7.6 %collective-permute-start.12 = (bf16[1024,64]{1,0:T(8,128)(2,1)}, bf16[1024,64]{1,0:T(8,128)(2,1)}, u32[]{:S(2)}, u32[]{:S(2)}) collective-permute-start(bf16[1024,64]{1,0:T(8,128)(2,1)} %get-tuple-element.36), channel_id=1, source_target_pairs={{0,4},{4,0},{8,12},{12,8},{16,20},{20,16},{24,28},{28,24},{32,36},... | collective-permute-start | bytes 393224 | tf_op jit(solution)/shard_map/ppermute | solution.py:195
  477.6 33.6 %collective-permute-start.13 = (bf16[1024,64]{1,0:T(8,128)(2,1)}, bf16[1024,64]{1,0:T(8,128)(2,1)}, u32[]{:S(2)}, u32[]{:S(2)}) collective-permute-start(bf16[1024,64]{1,0:T(8,128)(2,1)} %get-tuple-element.38), channel_id=1, source_target_pairs={{0,8},{4,12},{8,0},{12,4},{16,24},{20,28},{24,16},{28,20},{32,40},... | collective-permute-start | bytes 393224 | tf_op jit(solution)/shard_map/ppermute | solution.py:195
  479.0 39.2 %collective-permute-start.14 = (bf16[1024,64]{1,0:T(8,128)(2,1)}, bf16[1024,64]{1,0:T(8,128)(2,1)}, u32[]{:S(2)}, u32[]{:S(2)}) collective-permute-start(bf16[1024,64]{1,0:T(8,128)(2,1)} %get-tuple-element.37), channel_id=1, source_target_pairs={{0,16},{4,20},{8,24},{12,28},{16,0},{20,4},{24,8},{28,12},{32,48},... | collective-permute-start | bytes 393224 | tf_op jit(solution)/shard_map/ppermute | solution.py:195
  522.9 12.1 %copy-start.6 = (bf16[4,32,4096]{2,1,0:T(8,128)(2,1)S(1)}, bf16[4,32,4096]{2,1,0:T(8,128)(2,1)}, u32[]{:S(2)}) copy-start(bf16[4,32,4096]{2,1,0:T(8,128)(2,1)} %copy-done.5) | copy-start | bytes 3145732
  535.0 2.3 copy-start.4
  535.0 2.5 copy-start.13
  538.0 2.1 collective-permute-start.15
  540.1 5.3 collective-permute-start.16
  545.4 5.7 collective-permute-start.17
  551.1 4.2 collective-permute-start.18
  555.3 6.3 %collective-permute-start.19 = (f32[38400]{0:T(1024)S(1)}, f32[38400]{0:T(1024)S(1)}, u32[]{:S(2)}, u32[]{:S(2)}) collective-permute-start(f32[38400]{0:T(1024)S(1)} %add.77), channel_id=1, source_target_pairs={{0,64},{4,68},{8,72},{12,76},{16,80},{20,84},{24,88},{28,92},{32,9... | collective-permute-start | bytes 460808 | tf_op jit(solution)/shard_map/ppermute | solution.py:169
Sparse Core Ops, SparseCore 0:
  13.9 53.3 all-gather.6
  68.9 20.7 all-gather.4
  176.6 49.8 all-gather.10
  228.1 29.2 all-gather.8

commit v9 on v7

--- a/solution.py
+++ b/solution.py
@@ -45,26 +45,29 @@
     )(neighbours, table, after)
 
 
-def scatter_mean(rows, neighbours, size):
+def scatter_mean(rows, neighbours, size, chains=4):
     nodes, width = rows.shape
     degree = neighbours.shape[0]
-    half = degree // 2
-
-    def kernel(nb_ref, rows_ref, first_ref, second_ref):
-        first_ref[...] = jnp.zeros_like(first_ref)
-        second_ref[...] = jnp.zeros_like(second_ref)
+    per_chain = degree // chains
+
+    def kernel(nb_ref, rows_ref, out_ref, *extra_refs):
+        accumulators = (out_ref,) + extra_refs
+        for acc_ref in accumulators:
+            acc_ref[...] = jnp.zeros_like(acc_ref)
 
         def step(n, carry):
             x = rows_ref[pl.ds(n, 1), :]
-            for k in range(half):
-                s = nb_ref[k, n]
-                t = nb_ref[k + half, n]
-                first_ref[pl.ds(s, 1), :] = first_ref[pl.ds(s, 1), :] + x
-                second_ref[pl.ds(t, 1), :] = second_ref[pl.ds(t, 1), :] + x
+            for k in range(per_chain):
+                for chain, acc_ref in enumerate(accumulators):
+                    s = nb_ref[chain * per_chain + k, n]
+                    acc_ref[pl.ds(s, 1), :] = acc_ref[pl.ds(s, 1), :] + x
             return carry
 
-        lax.fori_loop(0, nodes, step, 0, unroll=4)
-        first_ref[...] = (first_ref[...] + second_ref[...]) * (1.0 / degree)
+        lax.fori_loop(0, nodes, step, 0, unroll=2)
+        total = out_ref[...]
+        for acc_ref in extra_refs:
+            total = total + acc_ref[...]
+        out_ref[...] = total * (1.0 / degree)
 
     return pl.pallas_call(
         kernel,
@@ -74,7 +77,8 @@
         ],
         out_specs=pl.BlockSpec(memory_space=pltpu.VMEM),
         out_shape=jax.ShapeDtypeStruct((size, width), jnp.float32),
-        scratch_shapes=[pltpu.VMEM((size, width), jnp.float32)],
+        scratch_shapes=[pltpu.VMEM((size, width), jnp.float32) for _ in range(chains - 1)],
+        compiler_params=pltpu.CompilerParams(vmem_limit_bytes=63 * 1024 * 1024),
     )(neighbours, rows)
 
 

time: 571 us -> 544 us (0.953)
  Pallas kernels: 228 us -> 200 us
    pallas_call x1, Pallas kernels: 93 us -> 65.7 us  [scatter_mean(): pl.pallas_call(kernel, in_specs=[pl.BlockSpec(memory_space=pltpu.SMEM), p...]
    unnamed x38 -> x42, local copies, waits for them, and re-layouts: 18.9 us -> 20 us
where the time goes in v9:
time: 544 us; the launch traced here: 540 us
  Pallas kernels  200 us (37%)
  waiting for transfers between devices  174 us (32%)
  local copies, waits for them, and re-layouts  62 us (11%)
  other arithmetic  39.3 us (7%)
  starting transfers between devices  32.8 us (6%)
  matrix products  16.6 us (3%)
  between operations  14.6 us (3%)
    pallas_call x2, Pallas kernels, gather_mean(): pl.pallas_call(kernel, grid_spec=pltpu.PrefetchScalarGridSpec(num_scalar_...  123 us
    all_gather x2, waiting for transfers between devices, source_table(): hub_all = lax.all_gather(hub_local, 'dom', axis=0, tiled=True)  71.9 us
    pallas_call x1, Pallas kernels, scatter_mean(): pl.pallas_call(kernel, in_specs=[pl.BlockSpec(memory_space=pltpu.SMEM), p...  65.7 us
    ppermute x9, waiting for transfers between devices, partner(): return lax.ppermute(value, axis, pairs)  27.6 us
    all_gather x1, waiting for transfers between devices, widen(): lax.all_gather(second_rows, 'feat', axis=0, tiled=True)  27.3 us
    all_gather x1, waiting for transfers between devices, body(): full_mean = lax.all_gather(mean_one, 'feat', axis=0, tiled=True)  24.6 us
    unnamed x42, local copies, waits for them, and re-layouts  20 us
    gather x6, local copies, waits for them, and re-layouts, source_table(): jnp.take(local_rows, send_rows[bit_index], axis=0)  19.2 us
  transfers between devices with their start and end apart: 21, of which 12 were waited for; matrix products, arithmetic and copies ran while one was open for 13% of the time, Pallas kernels for 11%

profile of v9, /device:TPU:1, one launch (start us, length us, event | category | flops | bytes accessed | tf_op | source)
XLA Modules:
  0.0 540.0 jit_solution(10057788994514015041)
XLA Ops:
  10.9 2.0 gather_fusion
  13.8 3.2 gather_fusion.2
  18.7 3.2 gather_fusion.3
  22.1 1.8 collective-permute-start.1
  24.0 3.2 gather_fusion.4
  27.4 3.4 collective-permute-start.2
  31.9 35.3 %all-gather.9.cloned.1.call-done = bf16[20480,32]{1,0:T(8,128)(2,1)} async-done(((bf16[640,32]{1,0:T(8,128)(2,1)}), bf16[20480,32]{1,0:T(8,128)(2,1)}) %all-gather.9.cloned.1.call-update) | async-done | bytes 1310736 | tf_op jit(solution)/shard_map/all_gather | solution.py:188
  67.2 5.3 constant_dynamic-update-slice_fusion.3
  74.7 8.6 %convert_element_type.58.tab_ref = f32[27648,32]{1,0:T(8,128)} convert(bf16[27648,32]{1,0:T(8,128)(2,1)} %constant_dynamic-update-slice_fusion) | non-fusion elementwise | flops 884736 | bytes 5308416 | tf_op jit(solution)/shard_map/convert_element_type | solution.py:181
  83.3 6.4 %all-gather.7.cloned.1.call-done.after_ref = bf16[128,4096]{1,0:T(8,128)(2,1)} async-done(((bf16[32,4096]{1,0:T(8,128)(2,1)}), bf16[128,4096]{1,0:T(8,128)(2,1)}) %all-gather.7.cloned.1.call-update) | async-done | bytes 1048592 | tf_op jit(solution)/shard_map/all_gather | solution.py:229
  89.7 61.3 %shard_map.120 = f32[4096,32]{1,0:T(8,128)} custom-call(s32[8,4096]{1,0:T(8,128)} %nb_ref.5, f32[27648,32]{1,0:T(8,128)} %convert_element_type.58.tab_ref, bf16[128,4096]{1,0:T(8,128)(2,1)} %all-gather.7.cloned.1.call-done.after_ref), custom_call_target="tpu_custom_call" | custom-call | tf_op jit(solution)/shard_map/pallas_call | solution.py:33
  150.9 1.7 convert_bitcast_fusion
  153.8 24.6 %all-gather.11.cloned.1.call-done = bf16[128,4096]{1,0:T(8,128)(2,1)} async-done(((bf16[32,4096]{1,0:T(8,128)(2,1)}), bf16[128,4096]{1,0:T(8,128)(2,1)}) %all-gather.11.cloned.1.call-update) | async-done | bytes 1048592 | tf_op jit(solution)/shard_map/all_gather | solution.py:231
  178.4 1.7 fusion.25
  182.0 2.0 gather_fusion.1
  184.9 3.2 gather_fusion.5
  188.1 3.2 gather_fusion.6
  191.3 3.2 gather_fusion.7
  195.9 2.8 collective-permute-start.3
  200.5 2.7 collective-permute-start.5
  203.4 36.6 %all-gather.15.cloned.1.call-done = bf16[20480,64]{1,0:T(8,128)(2,1)} async-done(((bf16[640,64]{1,0:T(8,128)(2,1)}), bf16[20480,64]{1,0:T(8,128)(2,1)}) %all-gather.15.cloned.1.call-update) | async-done | bytes 2621456 | tf_op jit(solution)/shard_map/all_gather | solution.py:188
  240.0 5.3 constant_dynamic-update-slice_fusion.8
  247.5 8.6 %convert_element_type.63.tab_ref = f32[27648,64]{1,0:T(8,128)} convert(bf16[27648,64]{1,0:T(8,128)(2,1)} %constant_dynamic-update-slice_fusion.5) | non-fusion elementwise | flops 1769472 | bytes 10616832 | tf_op jit(solution)/shard_map/convert_element_type | solution.py:181
  256.1 61.4 %shard_map.121 = f32[4096,64]{1,0:T(8,128)} custom-call(s32[8,4096]{1,0:T(8,128)} %nb_ref.5, f32[27648,64]{1,0:T(8,128)} %convert_element_type.63.tab_ref, bf16[64,4096]{1,0:T(8,128)(2,1)} %copy.99.after_ref), custom_call_target="tpu_custom_call" | custom-call | tf_op jit(solution)/shard_map/pallas_call | solution.py:33
  317.5 1.7 convert_bitcast_fusion.1
  320.5 2.1 fusion.26
  322.6 27.3 %all-gather.17.cloned.1.call-done = bf16[256,4096]{1,0:T(8,128)(2,1)} async-done(((bf16[64,4096]{1,0:T(8,128)(2,1)}), bf16[256,4096]{1,0:T(8,128)(2,1)}) %all-gather.17.cloned.1.call-update) | async-done | bytes 2097168 | tf_op jit(solution)/shard_map/all_gather | solution.py:176
  349.9 2.3 fusion.24
  356.5 65.7 %shard_map.122 = f32[27648,64]{1,0:T(8,128)} custom-call(s32[8,4096]{1,0:T(8,128)} %nb_ref.5, f32[4096,64]{1,0:T(8,128)} %convert_element_type.69.rows_ref), custom_call_target="tpu_custom_call" | custom-call | tf_op jit(solution)/shard_map/pallas_call | solution.py:72
  422.2 5.7 %convert.6 = bf16[27648,64]{1,0:T(8,128)(2,1)S(1)} convert(f32[27648,64]{1,0:T(8,128)} %shard_map.122) | non-fusion elementwise | flops 1769472 | bytes 10616832 | tf_op jit(solution)/shard_map/convert.3
  427.8 3.3 slice.116
  432.3 6.1 %copy.106 = bf16[32,640,64]{1,2,0:T(8,128)(2,1)} copy(bf16[32,640,64]{2,1,0:T(8,128)(2,1)} %bitcast.62) | data formatting | bytes 5242880 | tf_op jit(solution)/shard_map/convert_element_type | solution.py:259
  438.5 8.0 %all-to-all-start = ((bf16[32,640,64]{1,2,0:T(8,128)(2,1)}), bf16[32,640,64]{1,2,0:T(8,128)(2,1)}, u32[]{:S(2)}, u32[]{:S(2)}) async-start(bf16[32,640,64]{1,2,0:T(8,128)(2,1)} %copy.106), calls=%async_computation | async-start | bytes 5242880 | tf_op jit(solution)/shard_map/all_to_all | solution.py:258
  447.2 2.0 fusion.21
  449.2 2.9 collective-permute-start.8
  453.3 2.2 fusion.8
  455.4 3.9 convolution_add_fusion.1.base_ref
  460.0 25.2 %collective-permute-done.8 = bf16[1024,64]{1,0:T(8,128)(2,1)} collective-permute-done((bf16[1024,64]{1,0:T(8,128)(2,1)}, bf16[1024,64]{1,0:T(8,128)(2,1)}, u32[]{:S(2)}, u32[]{:S(2)}) %collective-permute-start.8) | collective-permute-done | bytes 131104 | tf_op jit(solution)/shard_map/ppermute | solution.py:166
  486.2 2.3 collective-permute-done.7
  488.7 2.1 convert_reduce_fusion
  492.4 12.1 %shard_map.123 = f32[4096,64]{1,0:T(8,128)} custom-call(s32[3712]{0:T(1024)} %pad_add_fusion.t_ref, f32[4096,64]{1,0:T(8,128)} %convolution_add_fusion.1.base_ref, f32[3712,64]{1,0:T(8,128)} %pad_maximum_fusion.upd_ref), custom_call_target="tpu_custom_call" | custom-call | tf_op jit(solution)/shard_map/pallas_call | solution.py:106
  504.5 2.3 convolution_bitcast_fusion
  509.7 5.2 collective-permute-done.10
  514.9 2.6 collective-permute-start.11
  517.5 3.1 collective-permute-done.11
  521.3 3.5 collective-permute-done.12
  524.8 2.4 collective-permute-start.13
  527.1 3.7 collective-permute-done.13
  (117 shorter events, 37.1 us)
Async XLA Ops:
  7.2 342.8 %copy-start = (bf16[172,256]{1,0:T(8,128)(2,1)S(1)}, bf16[172,256]{1,0:T(8,128)(2,1)}, u32[]{:S(2)}) copy-start(bf16[172,256]{1,0:T(8,128)(2,1)} %param.21) | copy-start | bytes 264196
  7.2 60.1 %all-gather.9.cloned.1.call-start = ((), (), s32[]{:S(2)}) async-start(), calls=%async_computation.2 | async-start | bytes 5406720 | tf_op jit(solution)/shard_map/all_gather | solution.py:188
  13.8 75.9 %all-gather.7.cloned.1.call-start = ((), (), s32[]{:S(2)}) async-start(), calls=%async_computation.1 | async-start | bytes 1310720 | tf_op jit(solution)/shard_map/all_gather | solution.py:229
  17.2 55.3 %collective-permute-start = (bf16[1024,32]{1,0:T(8,128)(2,1)S(1)}, bf16[1024,32]{1,0:T(8,128)(2,1)S(1)}, u32[]{:S(2)}, u32[]{:S(2)}) collective-permute-start(bf16[1024,32]{1,0:T(8,128)(2,1)S(1)} %broadcast_select_fusion.5), channel_id=1, source_target_pairs={{0,4},{4,0},{8,12},{12,8},{16,20},{20,16},{24,28},{28,24},{32,36},... | collective-permute-start | bytes 196616 | tf_op jit(solution)/shard_map/ppermute | solution.py:166
  22.1 51.1 %collective-permute-start.1 = (bf16[1024,32]{1,0:T(8,128)(2,1)S(1)}, bf16[1024,32]{1,0:T(8,128)(2,1)S(1)}, u32[]{:S(2)}, u32[]{:S(2)}) collective-permute-start(bf16[1024,32]{1,0:T(8,128)(2,1)S(1)} %broadcast_select_fusion.4), channel_id=1, source_target_pairs={{0,8},{4,12},{8,0},{12,4},{16,24},{20,28},{24,16},{28,20},{32,40},... | collective-permute-start | bytes 196616 | tf_op jit(solution)/shard_map/ppermute | solution.py:166
  27.4 46.6 %collective-permute-start.2 = (bf16[1024,32]{1,0:T(8,128)(2,1)S(1)}, bf16[1024,32]{1,0:T(8,128)(2,1)S(1)}, u32[]{:S(2)}, u32[]{:S(2)}) collective-permute-start(bf16[1024,32]{1,0:T(8,128)(2,1)S(1)} %broadcast_select_fusion.3), channel_id=1, source_target_pairs={{0,16},{4,20},{8,24},{12,28},{16,0},{20,4},{24,8},{28,12},{32,48},... | collective-permute-start | bytes 196616 | tf_op jit(solution)/shard_map/ppermute | solution.py:166
  30.8 147.5 %all-gather.11.cloned.1.call-start = ((), (), s32[]{:S(2)}) async-start(), calls=%async_computation.3 | async-start | bytes 1310720 | tf_op jit(solution)/shard_map/all_gather | solution.py:231
  150.9 27.4 %copy-start.13 = (bf16[64,128]{1,0:T(8,128)(2,1)S(1)}, bf16[64,128]{1,0:T(8,128)(2,1)}, u32[]{:S(2)}) copy-start(bf16[64,128]{1,0:T(8,128)(2,1)} %param.19) | copy-start | bytes 49156
  152.7 27.4 %copy-start.7 = (bf16[128,4096]{1,0:T(8,128)(2,1)S(1)}, bf16[128,4096]{1,0:T(8,128)(2,1)}, u32[]{:S(2)}) copy-start(bf16[128,4096]{1,0:T(8,128)(2,1)} %all-gather.7.cloned.1.call-done.after_ref) | copy-start | bytes 3145732
  152.7 27.4 %copy-start.14 = (bf16[64,128]{1,0:T(8,128)(2,1)S(1)}, bf16[64,128]{1,0:T(8,128)(2,1)}, u32[]{:S(2)}) copy-start(bf16[64,128]{1,0:T(8,128)(2,1)} %param.18) | copy-start | bytes 49156
  153.8 86.2 %all-gather.15.cloned.1.call-start = ((), (), s32[]{:S(2)}) async-start(), calls=%async_computation.5 | async-start | bytes 5406720 | tf_op jit(solution)/shard_map/all_gather | solution.py:188
  180.7 13.9 %copy-start.3 = (bf16[64,4096]{0,1:T(8,128)(2,1)}, bf16[64,4096]{0,1:T(8,128)(2,1)S(1)}, u32[]{:S(2)}) copy-start(bf16[64,4096]{0,1:T(8,128)(2,1)S(1)} %get-tuple-element.38) | copy-start | bytes 1572868
  184.8 135.7 %all-gather.13.cloned.1.call-start = ((), (), s32[]{:S(2)}) async-start(), calls=%async_computation.4 | async-start | bytes 2621440 | tf_op jit(solution)/shard_map/all_gather | solution.py:175
  195.9 49.4 %collective-permute-start.3 = (bf16[1024,64]{1,0:T(8,128)(2,1)S(1)}, bf16[1024,64]{1,0:T(8,128)(2,1)S(1)}, u32[]{:S(2)}, u32[]{:S(2)}) collective-permute-start(bf16[1024,64]{1,0:T(8,128)(2,1)S(1)} %broadcast_select_fusion.2), channel_id=1, source_target_pairs={{0,4},{4,0},{8,12},{12,8},{16,20},{20,16},{24,28},{28,24},{32,36},... | collective-permute-start | bytes 393224 | tf_op jit(solution)/shard_map/ppermute | solution.py:166
  199.0 47.1 %collective-permute-start.4 = (bf16[1024,64]{1,0:T(8,128)(2,1)S(1)}, bf16[1024,64]{1,0:T(8,128)(2,1)S(1)}, u32[]{:S(2)}, u32[]{:S(2)}) collective-permute-start(bf16[1024,64]{1,0:T(8,128)(2,1)S(1)} %broadcast_select_fusion.1), channel_id=1, source_target_pairs={{0,8},{4,12},{8,0},{12,4},{16,24},{20,28},{24,16},{28,20},{32,40},... | collective-permute-start | bytes 393224 | tf_op jit(solution)/shard_map/ppermute | solution.py:166
  200.5 46.2 %collective-permute-start.5 = (bf16[1024,64]{1,0:T(8,128)(2,1)S(1)}, bf16[1024,64]{1,0:T(8,128)(2,1)S(1)}, u32[]{:S(2)}, u32[]{:S(2)}) collective-permute-start(bf16[1024,64]{1,0:T(8,128)(2,1)S(1)} %broadcast_select_fusion), channel_id=1, source_target_pairs={{0,16},{4,20},{8,24},{12,28},{16,0},{20,4},{24,8},{28,12},{32,48},... | collective-permute-start | bytes 393224 | tf_op jit(solution)/shard_map/ppermute | solution.py:166
  203.2 146.7 %all-gather.17.cloned.1.call-start = ((), (), s32[]{:S(2)}) async-start(), calls=%async_computation.6 | async-start | bytes 2621440 | tf_op jit(solution)/shard_map/all_gather | solution.py:176
  317.5 2.9 copy-start.10
  322.6 29.7 %copy-start.15 = (s32[4096]{0:T(1024)S(1)}, s32[4096]{0:T(1024)}, u32[]{:S(2)}) copy-start(s32[4096]{0:T(1024)} %param.17) | copy-start | bytes 49156
  352.9 1.1 copy-start.1
  427.8 4.5 copy-start.5
  438.5 8.0 %copy-start.11 = (s32[3,1024]{1,0:T(4,128)S(1)}, s32[3,1024]{1,0:T(4,128)}, u32[]{:S(2)}) copy-start(s32[3,1024]{1,0:T(4,128)} %param.16) | copy-start | bytes 36868
  438.5 8.1 %copy-start.12 = (s32[640]{0:T(1024)S(1)}, s32[640]{0:T(1024)}, u32[]{:S(2)}) copy-start(s32[640]{0:T(1024)} %param.15) | copy-start | bytes 7684
  438.5 50.2 %all-to-all-start = ((bf16[32,640,64]{1,2,0:T(8,128)(2,1)}), bf16[32,640,64]{1,2,0:T(8,128)(2,1)}, u32[]{:S(2)}, u32[]{:S(2)}) async-start(bf16[32,640,64]{1,2,0:T(8,128)(2,1)} %copy.106), calls=%async_computation | async-start | bytes 5242880 | tf_op jit(solution)/shard_map/all_to_all | solution.py:258
  446.5 6.7 %copy-start.2 = (bf16[172,4096]{1,0:T(8,128)(2,1)S(1)}, bf16[172,4096]{1,0:T(8,128)(2,1)}, u32[]{:S(2)}) copy-start(bf16[172,4096]{1,0:T(8,128)(2,1)} %copy-done.1) | copy-start | bytes 4227076
  449.2 36.1 %collective-permute-start.8 = (bf16[1024,64]{1,0:T(8,128)(2,1)}, bf16[1024,64]{1,0:T(8,128)(2,1)}, u32[]{:S(2)}, u32[]{:S(2)}) collective-permute-start(bf16[1024,64]{1,0:T(8,128)(2,1)} %get-tuple-element.29), channel_id=1, source_target_pairs={{0,16},{4,20},{8,24},{12,28},{16,0},{20,4},{24,8},{28,12},{32,48},... | collective-permute-start | bytes 393224 | tf_op jit(solution)/shard_map/ppermute | solution.py:166
  452.0 36.5 %collective-permute-start.7 = (bf16[1024,64]{1,0:T(8,128)(2,1)}, bf16[1024,64]{1,0:T(8,128)(2,1)S(1)}, u32[]{:S(2)}, u32[]{:S(2)}) collective-permute-start(bf16[1024,64]{1,0:T(8,128)(2,1)} %get-tuple-element.30), channel_id=1, source_target_pairs={{0,8},{4,12},{8,0},{12,4},{16,24},{20,28},{24,16},{28,20},{32,40},... | collective-permute-start | bytes 393224 | tf_op jit(solution)/shard_map/ppermute | solution.py:166
  452.3 36.3 %collective-permute-start.6 = (bf16[1024,64]{1,0:T(8,128)(2,1)}, bf16[1024,64]{1,0:T(8,128)(2,1)S(1)}, u32[]{:S(2)}, u32[]{:S(2)}) collective-permute-start(bf16[1024,64]{1,0:T(8,128)(2,1)} %get-tuple-element.28), channel_id=1, source_target_pairs={{0,4},{4,0},{8,12},{12,8},{16,20},{20,16},{24,28},{28,24},{32,36},... | collective-permute-start | bytes 393224 | tf_op jit(solution)/shard_map/ppermute | solution.py:166
  455.4 3.9 copy-start.4
  492.4 12.1 %copy-start.9 = (bf16[128,4096]{1,0:T(8,128)(2,1)S(1)}, bf16[128,4096]{1,0:T(8,128)(2,1)}, u32[]{:S(2)}) copy-start(bf16[128,4096]{1,0:T(8,128)(2,1)} %all-gather.11.cloned.1.call-done) | copy-start | bytes 3145732
  504.5 2.3 copy-start.6
  504.5 2.5 copy-start.8
  507.5 2.1 collective-permute-start.9
  509.6 5.3 collective-permute-start.10
  514.9 5.7 %collective-permute-start.11 = (f32[38400]{0:T(1024)S(1)}, f32[38400]{0:T(1024)S(1)}, u32[]{:S(2)}, u32[]{:S(2)}) collective-permute-start(f32[38400]{0:T(1024)S(1)} %add.64), channel_id=1, source_target_pairs={{0,16},{4,20},{8,24},{12,28},{16,0},{20,4},{24,8},{28,12},{32,48},... | collective-permute-start | bytes 460808 | tf_op jit(solution)/shard_map/ppermute | solution.py:140
  520.6 4.2 collective-permute-start.12
  524.8 6.1 %collective-permute-start.13 = (f32[38400]{0:T(1024)S(1)}, f32[38400]{0:T(1024)S(1)}, u32[]{:S(2)}, u32[]{:S(2)}) collective-permute-start(f32[38400]{0:T(1024)S(1)} %add.66), channel_id=1, source_target_pairs={{0,64},{4,68},{8,72},{12,76},{16,80},{20,84},{24,88},{28,92},{32,9... | collective-permute-start | bytes 460808 | tf_op jit(solution)/shard_map/ppermute | solution.py:140
Sparse Core Ops, SparseCore 0:
  13.9 53.3 all-gather.8
  68.9 20.7 all-gather.6
  153.9 24.4 all-gather.10
  184.9 55.0 all-gather.14
  241.5 29.2 all-gather.12
  320.6 29.3 all-gather.16

commit v10 on v9

--- a/solution.py
+++ b/solution.py
@@ -1,3 +1,5 @@
+import math
+
 import jax
 import jax.numpy as jnp
 from jax import lax
@@ -9,40 +11,47 @@
 loss_scale = 4096.0
 
 
-def gather_mean(table, neighbours, after, block=512):
-    size, width = table.shape
+def gather_mean(pieces, neighbours, after):
+    width = pieces[0].shape[1]
     degree, nodes = neighbours.shape
-
-    def kernel(nb_ref, tab_ref, after_ref, out_ref):
-        base = pl.program_id(0) * block
-
-        def group(g, carry):
-            picked = []
-            for r in range(8):
-                n = base + g * 8 + r
-                acc = tab_ref[pl.ds(nb_ref[0, n], 1), :]
-                for k in range(1, degree):
-                    acc = acc + tab_ref[pl.ds(nb_ref[k, n], 1), :]
-                picked.append(acc)
-            start = pl.multiple_of(g * 8, 8)
-            out_ref[pl.ds(start, 8), :] = jnp.concatenate(picked, axis=0) / degree
+    size = sum(piece.shape[0] for piece in pieces)
+    chunk = 512
+    for piece in pieces:
+        chunk = math.gcd(chunk, piece.shape[0])
+
+    def kernel(nb_ref, *refs):
+        piece_refs = refs[: len(pieces)]
+        out_ref = refs[len(pieces) + 1]
+        tab_ref = refs[len(pieces) + 2]
+        start = 0
+        for piece_ref, piece in zip(piece_refs, pieces):
+
+            def fill(c, carry, piece_ref=piece_ref, start=start):
+                r = pl.multiple_of(c * chunk, chunk)
+                tab_ref[pl.ds(start + r, chunk), :] = piece_ref[pl.ds(r, chunk), :].astype(jnp.float32)
+                return carry
+
+            lax.fori_loop(0, piece.shape[0] // chunk, fill, 0)
+            start += piece.shape[0]
+
+        def body(n, carry):
+            acc = tab_ref[pl.ds(nb_ref[0, n], 1), :]
+            for k in range(1, degree):
+                acc = acc + tab_ref[pl.ds(nb_ref[k, n], 1), :]
+            out_ref[pl.ds(n, 1), :] = acc / degree
             return carry
 
-        lax.fori_loop(0, block // 8, group, 0)
+        lax.fori_loop(0, nodes, body, 0, unroll=8)
 
     return pl.pallas_call(
         kernel,
-        grid_spec=pltpu.PrefetchScalarGridSpec(
-            num_scalar_prefetch=1,
-            grid=(nodes // block,),
-            in_specs=[
-                pl.BlockSpec((size, width), lambda j, nb: (0, 0)),
-                pl.BlockSpec(memory_space=pl.ANY),
-            ],
-            out_specs=pl.BlockSpec((block, width), lambda j, nb: (j, 0)),
-        ),
+        in_specs=[pl.BlockSpec(memory_space=pltpu.SMEM)]
+        + [pl.BlockSpec(memory_space=pltpu.VMEM) for _ in pieces]
+        + [pl.BlockSpec(memory_space=pl.ANY)],
+        out_specs=pl.BlockSpec(memory_space=pltpu.VMEM),
         out_shape=jax.ShapeDtypeStruct((nodes, width), jnp.float32),
-    )(neighbours, table, after)
+        scratch_shapes=[pltpu.VMEM((size, width), jnp.float32)],
+    )(neighbours, *pieces, after)
 
 
 def scatter_mean(rows, neighbours, size, chains=4):
@@ -177,8 +186,8 @@
     )
 
 
-def average(table_rows, neighbours, after):
-    summed = gather_mean(table_rows.astype(jnp.float32), neighbours, after)
+def average(pieces, neighbours, after):
+    summed = gather_mean(pieces, neighbours, after)
     return summed.T.astype(jnp.bfloat16)
 
 
@@ -190,7 +199,7 @@
         trade(jnp.take(local_rows, send_rows[bit_index], axis=0), bit_index)
         for bit_index in range(send_rows.shape[0])
     ]
-    return jnp.concatenate([local_rows, hub_all] + received, axis=0)
+    return [local_rows, hub_all] + received
 
 
 def contract(left, right):

time: 544 us -> 489 us (0.90)
  Pallas kernels: 200 us -> 171 us
  other arithmetic: 39.3 us -> 20.3 us
  local copies, waits for them, and re-layouts: 62 us -> 45.2 us
  waiting for transfers between devices: 174 us -> 186 us
    pallas_call x2, Pallas kernels: 123 us -> 93 us  [gather_mean(): pl.pallas_call(kernel, in_specs=[pl.BlockSpec(memory_space=pltpu.SMEM)] +...]
    ppermute x9, waiting for transfers between devices: 27.6 us -> 50.2 us  [partner(): return lax.ppermute(value, axis, pairs)]
    convert_element_type x2 -> x1, other arithmetic: 17.2 us -> 0.24 us  [body(): hidden = jnp.maximum(pre_act, 0.0).astype(jnp.bfloat16)]
    unnamed x42 -> x53, local copies, waits for them, and re-layouts: 20 us -> 5.46 us
    all_gather x1, waiting for transfers between devices: 6.35 us -> 0.01 us  [body(): full_input = lax.all_gather(features, 'feat', axis=0, tiled=True)]
  transfers between devices with their start and end apart: 21 -> 21, of which waited for: 12 -> 14; matrix products, arithmetic and copies ran while one was open for 13% -> 9% of each run, Pallas kernels for 11% -> 10%
where the time goes in v10:
time: 489 us; the launch traced here: 485 us
  waiting for transfers between devices  186 us (38%)
  Pallas kernels  171 us (35%)
  local copies, waits for them, and re-layouts  45.2 us (9%)
  starting transfers between devices  31.7 us (6%)
  other arithmetic  20.3 us (4%)
  matrix products  16.5 us (3%)
  between operations  14.7 us (3%)
    pallas_call x2, Pallas kernels, gather_mean(): pl.pallas_call(kernel, in_specs=[pl.BlockSpec(memory_space=pltpu.SMEM)] +...  93 us
    all_gather x2, waiting for transfers between devices, source_table(): hub_all = lax.all_gather(hub_local, 'dom', axis=0, tiled=True)  70.6 us
    pallas_call x1, Pallas kernels, scatter_mean(): pl.pallas_call(kernel, in_specs=[pl.BlockSpec(memory_space=pltpu.SMEM), p...  65.7 us
    ppermute x9, waiting for transfers between devices, partner(): return lax.ppermute(value, axis, pairs)  50.2 us
    all_gather x1, waiting for transfers between devices, widen(): lax.all_gather(second_rows, 'feat', axis=0, tiled=True)  27.3 us
    all_gather x1, waiting for transfers between devices, body(): full_mean = lax.all_gather(mean_one, 'feat', axis=0, tiled=True)  20.8 us
    gather x6, local copies, waits for them, and re-layouts, source_table(): jnp.take(local_rows, send_rows[bit_index], axis=0)  19.2 us
    ppermute x9, starting transfers between devices, partner(): return lax.ppermute(value, axis, pairs)  16.9 us
  transfers between devices with their start and end apart: 21, of which 14 were waited for; matrix products, arithmetic and copies ran while one was open for 9% of the time, Pallas kernels for 10%

profile of v10, /device:TPU:1, one launch (start us, length us, event | category | flops | bytes accessed | tf_op | source)
XLA Modules:
  0.0 485.4 jit_solution(11729571460542988548)
XLA Ops:
  10.2 2.0 gather_fusion
  13.1 3.2 gather_fusion.2
  16.5 1.5 collective-permute-start
  18.0 3.2 gather_fusion.3
  21.4 1.8 collective-permute-start.1
  23.3 3.2 gather_fusion.4
  26.7 3.4 collective-permute-start.2
  30.1 8.4 %collective-permute-done.2.refs_4_ = bf16[1024,32]{1,0:T(8,128)(2,1)S(1)} collective-permute-done((bf16[1024,32]{1,0:T(8,128)(2,1)S(1)}, bf16[1024,32]{1,0:T(8,128)(2,1)S(1)}, u32[]{:S(2)}, u32[]{:S(2)}) %collective-permute-start.2) | collective-permute-done | bytes 65568 | tf_op jit(solution)/shard_map/ppermute | solution.py:175
  38.6 48.8 %all-gather.9.cloned.1.call-done.refs_1_ = bf16[20480,32]{1,0:T(8,128)(2,1)} async-done(((bf16[640,32]{1,0:T(8,128)(2,1)}), bf16[20480,32]{1,0:T(8,128)(2,1)}) %all-gather.9.cloned.1.call-update) | async-done | bytes 1310736 | tf_op jit(solution)/shard_map/all_gather | solution.py:197
  87.4 46.5 %shard_map.120 = f32[4096,32]{1,0:T(8,128)} custom-call(s32[8,4096]{1,0:T(8,128)} %nb_ref.5, bf16[4096,32]{1,0:T(8,128)(2,1)} %bitcast.60, bf16[20480,32]{1,0:T(8,128)(2,1)} %all-gather.9.cloned.1.call-done.refs_1_, bf16[1024,32]{1,0:T(8,128)(2,1)} %copy-done.13, bf16[1024,32]{1,0:T(8,128)(2,1)} %copy-done.14, bf16[1024,32]{1,0:T(8,128)(2,1)} %copy-done.16, ...), custom_call_target="tpu_custom_call" | custom-call | tf_op jit(solution)/shard_map/pallas_call | solution.py:46
  133.8 1.7 convert_bitcast_fusion
  136.7 20.8 %all-gather.11.cloned.1.call-done = bf16[128,4096]{1,0:T(8,128)(2,1)} async-done(((bf16[32,4096]{1,0:T(8,128)(2,1)}), bf16[128,4096]{1,0:T(8,128)(2,1)}) %all-gather.11.cloned.1.call-update) | async-done | bytes 1048592 | tf_op jit(solution)/shard_map/all_gather | solution.py:240
  157.5 1.7 fusion.24
  160.1 2.0 gather_fusion.1
  164.3 3.2 gather_fusion.7
  167.5 3.2 gather_fusion.6
  170.7 3.2 gather_fusion.5
  174.6 2.8 collective-permute-start.3
  178.7 2.6 collective-permute-start.5
  181.3 5.2 %collective-permute-done.4.refs_3_ = bf16[1024,64]{1,0:T(8,128)(2,1)S(1)} collective-permute-done((bf16[1024,64]{1,0:T(8,128)(2,1)S(1)}, bf16[1024,64]{1,0:T(8,128)(2,1)S(1)}, u32[]{:S(2)}, u32[]{:S(2)}) %collective-permute-start.4) | collective-permute-done | bytes 131104 | tf_op jit(solution)/shard_map/ppermute | solution.py:175
  186.5 8.4 %collective-permute-done.5.refs_4_ = bf16[1024,64]{1,0:T(8,128)(2,1)S(1)} collective-permute-done((bf16[1024,64]{1,0:T(8,128)(2,1)S(1)}, bf16[1024,64]{1,0:T(8,128)(2,1)S(1)}, u32[]{:S(2)}, u32[]{:S(2)}) %collective-permute-start.5) | collective-permute-done | bytes 131104 | tf_op jit(solution)/shard_map/ppermute | solution.py:175
  194.9 21.8 %all-gather.15.cloned.1.call-done.refs_1_ = bf16[20480,64]{1,0:T(8,128)(2,1)} async-done(((bf16[640,64]{1,0:T(8,128)(2,1)}), bf16[20480,64]{1,0:T(8,128)(2,1)}) %all-gather.15.cloned.1.call-update) | async-done | bytes 2621456 | tf_op jit(solution)/shard_map/all_gather | solution.py:197
  216.7 46.5 %shard_map.121 = f32[4096,64]{1,0:T(8,128)} custom-call(s32[8,4096]{1,0:T(8,128)} %nb_ref.5, bf16[4096,64]{1,0:T(8,128)(2,1)} %copy-done.2, bf16[20480,64]{1,0:T(8,128)(2,1)} %all-gather.15.cloned.1.call-done.refs_1_, bf16[1024,64]{1,0:T(8,128)(2,1)} %copy-done.15, bf16[1024,64]{1,0:T(8,128)(2,1)} %copy-done.17, bf16[1024,64]{1,0:T(8,128)(2,1)} %copy-done.18, ...), custom_call_target="tpu_custom_call" | custom-call | tf_op jit(solution)/shard_map/pallas_call | solution.py:46
  263.2 1.7 convert_bitcast_fusion.1
  266.2 2.1 fusion.25
  268.3 27.3 %all-gather.17.cloned.1.call-done = bf16[256,4096]{1,0:T(8,128)(2,1)} async-done(((bf16[64,4096]{1,0:T(8,128)(2,1)}), bf16[256,4096]{1,0:T(8,128)(2,1)}) %all-gather.17.cloned.1.call-update) | async-done | bytes 2097168 | tf_op jit(solution)/shard_map/all_gather | solution.py:185
  295.6 2.3 fusion.23
  300.6 1.5 convert_element_type.61.rows_ref
  302.1 65.7 %shard_map.122 = f32[27648,64]{1,0:T(8,128)} custom-call(s32[8,4096]{1,0:T(8,128)} %nb_ref.5, f32[4096,64]{1,0:T(8,128)} %convert_element_type.61.rows_ref), custom_call_target="tpu_custom_call" | custom-call | tf_op jit(solution)/shard_map/pallas_call | solution.py:81
  367.8 5.7 %convert.6 = bf16[27648,64]{1,0:T(8,128)(2,1)S(1)} convert(f32[27648,64]{1,0:T(8,128)} %shard_map.122) | non-fusion elementwise | flops 1769472 | bytes 10616832 | tf_op jit(solution)/shard_map/convert.3
  373.5 3.3 slice.116
  378.0 6.1 %copy.77 = bf16[32,640,64]{1,2,0:T(8,128)(2,1)} copy(bf16[32,640,64]{2,1,0:T(8,128)(2,1)} %bitcast.61) | data formatting | bytes 5242880 | tf_op jit(solution)/shard_map/convert_element_type | solution.py:268
  384.1 7.9 %all-to-all-start = ((bf16[32,640,64]{1,2,0:T(8,128)(2,1)}), bf16[32,640,64]{1,2,0:T(8,128)(2,1)}, u32[]{:S(2)}, u32[]{:S(2)}) async-start(bf16[32,640,64]{1,2,0:T(8,128)(2,1)} %copy.77), calls=%async_computation | async-start | bytes 5242880 | tf_op jit(solution)/shard_map/all_to_all | solution.py:267
  392.6 2.0 fusion.20
  394.9 3.0 collective-permute-start.8
  398.2 2.2 fusion.8
  400.4 3.9 convolution_add_fusion.1.base_ref
  405.9 24.7 %collective-permute-done.8 = bf16[1024,64]{1,0:T(8,128)(2,1)S(1)} collective-permute-done((bf16[1024,64]{1,0:T(8,128)(2,1)}, bf16[1024,64]{1,0:T(8,128)(2,1)S(1)}, u32[]{:S(2)}, u32[]{:S(2)}) %collective-permute-start.8) | collective-permute-done | bytes 131104 | tf_op jit(solution)/shard_map/ppermute | solution.py:175
  430.7 3.4 collective-permute-done.7
  434.1 2.1 convert_reduce_fusion
  437.8 12.1 %shard_map.123 = f32[4096,64]{1,0:T(8,128)} custom-call(s32[3712]{0:T(1024)} %pad_add_fusion.t_ref, f32[4096,64]{1,0:T(8,128)} %convolution_add_fusion.1.base_ref, f32[3712,64]{1,0:T(8,128)} %pad_maximum_fusion.upd_ref), custom_call_target="tpu_custom_call" | custom-call | tf_op jit(solution)/shard_map/pallas_call | solution.py:115
  450.0 2.3 convolution_bitcast_fusion
  455.2 5.2 %collective-permute-done.10 = f32[38400]{0:T(1024)S(1)} collective-permute-done((f32[38400]{0:T(1024)S(1)}, f32[38400]{0:T(1024)S(1)}, u32[]{:S(2)}, u32[]{:S(2)}) %collective-permute-start.10) | collective-permute-done | bytes 153632 | tf_op jit(solution)/shard_map/ppermute | solution.py:149
  460.4 2.6 collective-permute-start.11
  462.9 3.1 collective-permute-done.11
  466.7 3.5 collective-permute-done.12
  470.3 2.4 collective-permute-start.13
  472.6 3.7 collective-permute-done.13
  (126 shorter events, 25.9 us)
Async XLA Ops:
  7.2 288.4 %copy-start = (bf16[172,256]{1,0:T(8,128)(2,1)S(1)}, bf16[172,256]{1,0:T(8,128)(2,1)}, u32[]{:S(2)}) copy-start(bf16[172,256]{1,0:T(8,128)(2,1)} %param.21) | copy-start | bytes 264196
  7.2 5.0 %copy-start.21 = (s32[640]{0:T(1024)S(1)}, s32[640]{0:T(1024)}, u32[]{:S(2)}) copy-start(s32[640]{0:T(1024)} %param.15) | copy-start | bytes 7684
  7.2 5.8 %copy-start.20 = (s32[3,1024]{1,0:T(4,128)S(1)}, s32[3,1024]{1,0:T(4,128)}, u32[]{:S(2)}) copy-start(s32[3,1024]{1,0:T(4,128)} %param.16) | copy-start | bytes 36868
  7.2 31.3 %all-gather.7.cloned.1.call-start = ((), (), s32[]{:S(2)}) async-start(), calls=%async_computation.1 | async-start | bytes 1310720 | tf_op jit(solution)/shard_map/all_gather | solution.py:238
  7.9 79.4 %all-gather.9.cloned.1.call-start = ((), (), s32[]{:S(2)}) async-start(), calls=%async_computation.2 | async-start | bytes 5406720 | tf_op jit(solution)/shard_map/all_gather | solution.py:197
  9.4 13.8 %copy-start.3 = (bf16[32,4096]{0,1:T(8,128)(2,1)}, bf16[32,4096]{0,1:T(8,128)(2,1)S(1)}, u32[]{:S(2)}) copy-start(bf16[32,4096]{0,1:T(8,128)(2,1)S(1)} %copy.66) | copy-start | bytes 786436
  13.0 144.5 %all-gather.11.cloned.1.call-start = ((), (), s32[]{:S(2)}) async-start(), calls=%async_computation.3 | async-start | bytes 1310720 | tf_op jit(solution)/shard_map/all_gather | solution.py:240
  16.5 13.6 %collective-permute-start = (bf16[1024,32]{1,0:T(8,128)(2,1)S(1)}, bf16[1024,32]{1,0:T(8,128)(2,1)S(1)}, u32[]{:S(2)}, u32[]{:S(2)}) collective-permute-start(bf16[1024,32]{1,0:T(8,128)(2,1)S(1)} %broadcast_select_fusion.5), channel_id=1, source_target_pairs={{0,4},{4,0},{8,12},{12,8},{16,20},{20,16},{24,28},{28,24},{32,36},... | collective-permute-start | bytes 196616 | tf_op jit(solution)/shard_map/ppermute | solution.py:175
  21.4 8.7 %collective-permute-start.1 = (bf16[1024,32]{1,0:T(8,128)(2,1)S(1)}, bf16[1024,32]{1,0:T(8,128)(2,1)S(1)}, u32[]{:S(2)}, u32[]{:S(2)}) collective-permute-start(bf16[1024,32]{1,0:T(8,128)(2,1)S(1)} %broadcast_select_fusion.4), channel_id=1, source_target_pairs={{0,8},{4,12},{8,0},{12,4},{16,24},{20,28},{24,16},{28,20},{32,40},... | collective-permute-start | bytes 196616 | tf_op jit(solution)/shard_map/ppermute | solution.py:175
  26.7 11.9 %collective-permute-start.2 = (bf16[1024,32]{1,0:T(8,128)(2,1)S(1)}, bf16[1024,32]{1,0:T(8,128)(2,1)S(1)}, u32[]{:S(2)}, u32[]{:S(2)}) collective-permute-start(bf16[1024,32]{1,0:T(8,128)(2,1)S(1)} %broadcast_select_fusion.3), channel_id=1, source_target_pairs={{0,16},{4,20},{8,24},{12,28},{16,0},{20,4},{24,8},{28,12},{32,48},... | collective-permute-start | bytes 196616 | tf_op jit(solution)/shard_map/ppermute | solution.py:175
  30.1 57.3 %copy-start.13 = (bf16[1024,32]{1,0:T(8,128)(2,1)}, bf16[1024,32]{1,0:T(8,128)(2,1)S(1)}, u32[]{:S(2)}) copy-start(bf16[1024,32]{1,0:T(8,128)(2,1)S(1)} %collective-permute-done.refs_2_) | copy-start | bytes 196612
  30.1 57.3 %copy-start.14 = (bf16[1024,32]{1,0:T(8,128)(2,1)}, bf16[1024,32]{1,0:T(8,128)(2,1)S(1)}, u32[]{:S(2)}) copy-start(bf16[1024,32]{1,0:T(8,128)(2,1)S(1)} %collective-permute-done.1.refs_3_) | copy-start | bytes 196612
  38.5 48.8 %copy-start.16 = (bf16[1024,32]{1,0:T(8,128)(2,1)}, bf16[1024,32]{1,0:T(8,128)(2,1)S(1)}, u32[]{:S(2)}) copy-start(bf16[1024,32]{1,0:T(8,128)(2,1)S(1)} %collective-permute-done.2.refs_4_) | copy-start | bytes 196612
  133.8 23.7 %copy-start.22 = (bf16[64,128]{1,0:T(8,128)(2,1)S(1)}, bf16[64,128]{1,0:T(8,128)(2,1)}, u32[]{:S(2)}) copy-start(bf16[64,128]{1,0:T(8,128)(2,1)} %param.19) | copy-start | bytes 49156
  135.6 23.7 %copy-start.10 = (bf16[128,4096]{1,0:T(8,128)(2,1)S(1)}, bf16[128,4096]{1,0:T(8,128)(2,1)}, u32[]{:S(2)}) copy-start(bf16[128,4096]{1,0:T(8,128)(2,1)} %all-gather.7.cloned.1.call-done.refs_5_) | copy-start | bytes 3145732
  135.6 23.7 %copy-start.23 = (bf16[64,128]{1,0:T(8,128)(2,1)S(1)}, bf16[64,128]{1,0:T(8,128)(2,1)}, u32[]{:S(2)}) copy-start(bf16[64,128]{1,0:T(8,128)(2,1)} %param.18) | copy-start | bytes 49156
  136.7 80.0 %all-gather.15.cloned.1.call-start = ((), (), s32[]{:S(2)}) async-start(), calls=%async_computation.5 | async-start | bytes 5406720 | tf_op jit(solution)/shard_map/all_gather | solution.py:197
  159.8 3.2 copy-start.6
  160.1 10.6 %copy-start.2 = (bf16[4096,64]{1,0:T(8,128)(2,1)}, bf16[4096,64]{1,0:T(8,128)(2,1)S(1)}, u32[]{:S(2)}) copy-start(bf16[4096,64]{1,0:T(8,128)(2,1)S(1)} %fusion.5.refs_0_) | copy-start | bytes 1572868
  162.9 103.2 %all-gather.13.cloned.1.call-start = ((), (), s32[]{:S(2)}) async-start(), calls=%async_computation.4 | async-start | bytes 2621440 | tf_op jit(solution)/shard_map/all_gather | solution.py:184
  164.2 131.3 %all-gather.17.cloned.1.call-start = ((), (), s32[]{:S(2)}) async-start(), calls=%async_computation.6 | async-start | bytes 2621440 | tf_op jit(solution)/shard_map/all_gather | solution.py:185
  174.6 6.7 %collective-permute-start.3 = (bf16[1024,64]{1,0:T(8,128)(2,1)S(1)}, bf16[1024,64]{1,0:T(8,128)(2,1)S(1)}, u32[]{:S(2)}, u32[]{:S(2)}) collective-permute-start(bf16[1024,64]{1,0:T(8,128)(2,1)S(1)} %broadcast_select_fusion.2), channel_id=1, source_target_pairs={{0,4},{4,0},{8,12},{12,8},{16,20},{20,16},{24,28},{28,24},{32,36},... | collective-permute-start | bytes 393224 | tf_op jit(solution)/shard_map/ppermute | solution.py:175
  177.4 9.1 %collective-permute-start.4 = (bf16[1024,64]{1,0:T(8,128)(2,1)S(1)}, bf16[1024,64]{1,0:T(8,128)(2,1)S(1)}, u32[]{:S(2)}, u32[]{:S(2)}) collective-permute-start(bf16[1024,64]{1,0:T(8,128)(2,1)S(1)} %broadcast_select_fusion.1), channel_id=1, source_target_pairs={{0,8},{4,12},{8,0},{12,4},{16,24},{20,28},{24,16},{28,20},{32,40},... | collective-permute-start | bytes 393224 | tf_op jit(solution)/shard_map/ppermute | solution.py:175
  178.7 16.3 %collective-permute-start.5 = (bf16[1024,64]{1,0:T(8,128)(2,1)S(1)}, bf16[1024,64]{1,0:T(8,128)(2,1)S(1)}, u32[]{:S(2)}, u32[]{:S(2)}) collective-permute-start(bf16[1024,64]{1,0:T(8,128)(2,1)S(1)} %broadcast_select_fusion), channel_id=1, source_target_pairs={{0,16},{4,20},{8,24},{12,28},{16,0},{20,4},{24,8},{28,12},{32,48},... | collective-permute-start | bytes 393224 | tf_op jit(solution)/shard_map/ppermute | solution.py:175
  181.3 35.4 %copy-start.15 = (bf16[1024,64]{1,0:T(8,128)(2,1)}, bf16[1024,64]{1,0:T(8,128)(2,1)S(1)}, u32[]{:S(2)}) copy-start(bf16[1024,64]{1,0:T(8,128)(2,1)S(1)} %collective-permute-done.3.refs_2_) | copy-start | bytes 393220
  186.5 30.2 %copy-start.17 = (bf16[1024,64]{1,0:T(8,128)(2,1)}, bf16[1024,64]{1,0:T(8,128)(2,1)S(1)}, u32[]{:S(2)}) copy-start(bf16[1024,64]{1,0:T(8,128)(2,1)S(1)} %collective-permute-done.4.refs_3_) | copy-start | bytes 393220
  194.9 21.8 %copy-start.18 = (bf16[1024,64]{1,0:T(8,128)(2,1)}, bf16[1024,64]{1,0:T(8,128)(2,1)S(1)}, u32[]{:S(2)}) copy-start(bf16[1024,64]{1,0:T(8,128)(2,1)S(1)} %collective-permute-done.5.refs_4_) | copy-start | bytes 393220
  263.2 3.0 copy-start.19
  268.3 29.6 %copy-start.24 = (s32[4096]{0:T(1024)S(1)}, s32[4096]{0:T(1024)}, u32[]{:S(2)}) copy-start(s32[4096]{0:T(1024)} %param.17) | copy-start | bytes 49156
  298.5 1.1 copy-start.4
  373.4 4.5 copy-start.8
  384.1 50.0 %all-to-all-start = ((bf16[32,640,64]{1,2,0:T(8,128)(2,1)}), bf16[32,640,64]{1,2,0:T(8,128)(2,1)}, u32[]{:S(2)}, u32[]{:S(2)}) async-start(bf16[32,640,64]{1,2,0:T(8,128)(2,1)} %copy.77), calls=%async_computation | async-start | bytes 5242880 | tf_op jit(solution)/shard_map/all_to_all | solution.py:267
  392.0 6.2 %copy-start.5 = (bf16[172,4096]{1,0:T(8,128)(2,1)S(1)}, bf16[172,4096]{1,0:T(8,128)(2,1)}, u32[]{:S(2)}) copy-start(bf16[172,4096]{1,0:T(8,128)(2,1)} %copy-done.4) | copy-start | bytes 4227076
  394.6 10.3 %collective-permute-start.6 = (bf16[1024,64]{1,0:T(8,128)(2,1)}, bf16[1024,64]{1,0:T(8,128)(2,1)}, u32[]{:S(2)}, u32[]{:S(2)}) collective-permute-start(bf16[1024,64]{1,0:T(8,128)(2,1)} %get-tuple-element.22), channel_id=1, source_target_pairs={{0,4},{4,0},{8,12},{12,8},{16,20},{20,16},{24,28},{28,24},{32,36},... | collective-permute-start | bytes 393224 | tf_op jit(solution)/shard_map/ppermute | solution.py:175
  394.9 35.7 %collective-permute-start.8 = (bf16[1024,64]{1,0:T(8,128)(2,1)}, bf16[1024,64]{1,0:T(8,128)(2,1)S(1)}, u32[]{:S(2)}, u32[]{:S(2)}) collective-permute-start(bf16[1024,64]{1,0:T(8,128)(2,1)} %get-tuple-element.23), channel_id=1, source_target_pairs={{0,16},{4,20},{8,24},{12,28},{16,0},{20,4},{24,8},{28,12},{32,48},... | collective-permute-start | bytes 393224 | tf_op jit(solution)/shard_map/ppermute | solution.py:175
  397.9 36.2 %collective-permute-start.7 = (bf16[1024,64]{1,0:T(8,128)(2,1)}, bf16[1024,64]{1,0:T(8,128)(2,1)S(1)}, u32[]{:S(2)}, u32[]{:S(2)}) collective-permute-start(bf16[1024,64]{1,0:T(8,128)(2,1)} %get-tuple-element.24), channel_id=1, source_target_pairs={{0,8},{4,12},{8,0},{12,4},{16,24},{20,28},{24,16},{28,20},{32,40},... | collective-permute-start | bytes 393224 | tf_op jit(solution)/shard_map/ppermute | solution.py:175
  400.3 3.9 copy-start.7
  437.8 12.1 %copy-start.12 = (bf16[128,4096]{1,0:T(8,128)(2,1)S(1)}, bf16[128,4096]{1,0:T(8,128)(2,1)}, u32[]{:S(2)}) copy-start(bf16[128,4096]{1,0:T(8,128)(2,1)} %all-gather.11.cloned.1.call-done) | copy-start | bytes 3145732
  450.0 2.3 copy-start.9
  450.0 2.5 copy-start.11
  452.4 26.2 %copy-start.1 = (bf16[172,256]{1,0:T(8,128)(2,1)S(1)}, bf16[172,256]{1,0:T(8,128)(2,1)}, u32[]{:S(2)}) copy-start(bf16[172,256]{1,0:T(8,128)(2,1)} %param.21) | copy-start | bytes 264196
  453.0 2.1 collective-permute-start.9
  455.1 5.3 %collective-permute-start.10 = (f32[38400]{0:T(1024)S(1)}, f32[38400]{0:T(1024)S(1)}, u32[]{:S(2)}, u32[]{:S(2)}) collective-permute-start(f32[38400]{0:T(1024)S(1)} %fusion.17), channel_id=1, source_target_pairs={{0,8},{4,12},{8,0},{12,4},{16,24},{20,28},{24,16},{28,20},{32,40},... | collective-permute-start | bytes 460808 | tf_op jit(solution)/shard_map/ppermute | solution.py:149
  460.4 5.7 %collective-permute-start.11 = (f32[38400]{0:T(1024)S(1)}, f32[38400]{0:T(1024)S(1)}, u32[]{:S(2)}, u32[]{:S(2)}) collective-permute-start(f32[38400]{0:T(1024)S(1)} %add.64), channel_id=1, source_target_pairs={{0,16},{4,20},{8,24},{12,28},{16,0},{20,4},{24,8},{28,12},{32,48},... | collective-permute-start | bytes 460808 | tf_op jit(solution)/shard_map/ppermute | solution.py:149
  466.1 4.2 collective-permute-start.12
  470.3 6.1 %collective-permute-start.13 = (f32[38400]{0:T(1024)S(1)}, f32[38400]{0:T(1024)S(1)}, u32[]{:S(2)}, u32[]{:S(2)}) collective-permute-start(f32[38400]{0:T(1024)S(1)} %add.66), channel_id=1, source_target_pairs={{0,64},{4,68},{8,72},{12,76},{16,80},{20,84},{24,88},{28,92},{32,9... | collective-permute-start | bytes 460808 | tf_op jit(solution)/shard_map/ppermute | solution.py:149
Sparse Core Ops, SparseCore 0:
  9.7 25.4 all-gather.6
  37.4 49.9 all-gather.8
  136.8 20.7 all-gather.10
  163.0 53.5 all-gather.14
  218.2 29.2 all-gather.12
  266.2 29.2 all-gather.16

commit v11 on v10

--- a/solution.py
+++ b/solution.py
@@ -89,6 +89,18 @@
         scratch_shapes=[pltpu.VMEM((size, width), jnp.float32) for _ in range(chains - 1)],
         compiler_params=pltpu.CompilerParams(vmem_limit_bytes=63 * 1024 * 1024),
     )(neighbours, rows)
+
+
+def feat_gather(value, axis):
+    count = lax.axis_size(axis)
+    index = lax.axis_index(axis)
+    got = [value] + [
+        lax.ppermute(value, axis, [(source, (source + shift) % count) for source in range(count)])
+        for shift in range(1, count)
+    ]
+    stacked = jnp.stack(got[::-1] * 2)
+    full = lax.dynamic_slice_in_dim(stacked, (count - 1 - index) % count, count, axis=0)
+    return full.reshape(count * value.shape[0], value.shape[1])
 
 
 def land_rows(base, targets, updates):
@@ -235,7 +247,7 @@
 ):
     rows = features.shape[1]
     nodes_all = rows * lax.axis_size("dom")
-    full_input = lax.all_gather(features, "feat", axis=0, tiled=True)
+    full_input = feat_gather(features, "feat")
     mean_one = average(source_table(features, hub_rows, send_rows), neighbours, full_input)
     full_mean = lax.all_gather(mean_one, "feat", axis=0, tiled=True)
     pre_act = jnp.dot(inner_self, full_input, preferred_element_type=jnp.float32)

time: 489 us -> 472 us (0.965)
  waiting for transfers between devices: 186 us -> 160 us
  starting transfers between devices: 31.7 us -> 37.7 us
    all_gather x2, waiting for transfers between devices: 70.6 us -> 44.7 us  [source_table(): hub_all = lax.all_gather(hub_local, 'dom', axis=0, tiled=True)]
    ppermute x0 -> x3, starting transfers between devices: none -> 5.87 us  [feat_gather(): lax.ppermute(value, axis, [(source, (source + shift) % count) for source...]
  transfers between devices with their start and end apart: 21 -> 23, of which waited for: 14 -> 14; matrix products, arithmetic and copies ran while one was open for 9% -> 10% of each run, Pallas kernels for 10% -> 10%
where the time goes in v11:
time: 472 us; the launch traced here: 468 us
  Pallas kernels  171 us (36%)
  waiting for transfers between devices  160 us (34%)
  local copies, waits for them, and re-layouts  47.3 us (10%)
  starting transfers between devices  37.7 us (8%)
  other arithmetic  20.8 us (4%)
  matrix products  16.5 us (3%)
  between operations  14.4 us (3%)
    pallas_call x2, Pallas kernels, gather_mean(): pl.pallas_call(kernel, in_specs=[pl.BlockSpec(memory_space=pltpu.SMEM)] +...  92.8 us
    pallas_call x1, Pallas kernels, scatter_mean(): pl.pallas_call(kernel, in_specs=[pl.BlockSpec(memory_space=pltpu.SMEM), p...  65.7 us
    ppermute x9, waiting for transfers between devices, partner(): return lax.ppermute(value, axis, pairs)  51.5 us
    all_gather x2, waiting for transfers between devices, source_table(): hub_all = lax.all_gather(hub_local, 'dom', axis=0, tiled=True)  44.7 us
    all_gather x1, waiting for transfers between devices, widen(): lax.all_gather(second_rows, 'feat', axis=0, tiled=True)  27.3 us
    all_gather x1, waiting for transfers between devices, body(): full_mean = lax.all_gather(mean_one, 'feat', axis=0, tiled=True)  20.3 us
    gather x6, local copies, waits for them, and re-layouts, source_table(): jnp.take(local_rows, send_rows[bit_index], axis=0)  19.2 us
    ppermute x9, starting transfers between devices, partner(): return lax.ppermute(value, axis, pairs)  16.9 us
  transfers between devices with their start and end apart: 23, of which 14 were waited for; matrix products, arithmetic and copies ran while one was open for 10% of the time, Pallas kernels for 10%

profile of v11, /device:TPU:1, one launch (start us, length us, event | category | flops | bytes accessed | tf_op | source)
XLA Modules:
  0.0 467.8 jit_solution(8844976420706112687)
XLA Ops:
  7.2 2.2 collective-permute-start.2
  9.4 2.6 collective-permute-start.1
  16.8 2.0 gather_fusion
  19.7 3.2 gather_fusion.2
  24.7 3.2 gather_fusion.3
  28.2 1.7 collective-permute-start.4
  29.9 3.2 gather_fusion.4
  33.3 3.4 collective-permute-start.5
  38.0 9.8 %collective-permute-done.5.refs_4_ = bf16[1024,32]{1,0:T(8,128)(2,1)S(1)} collective-permute-done((bf16[1024,32]{1,0:T(8,128)(2,1)S(1)}, bf16[1024,32]{1,0:T(8,128)(2,1)S(1)}, u32[]{:S(2)}, u32[]{:S(2)}) %collective-permute-start.5) | collective-permute-done | bytes 65568 | tf_op jit(solution)/shard_map/ppermute | solution.py:187
  47.8 22.9 %all-gather.6.cloned.1.call-done.refs_1_ = bf16[20480,32]{1,0:T(8,128)(2,1)} async-done(((bf16[640,32]{1,0:T(8,128)(2,1)}), bf16[20480,32]{1,0:T(8,128)(2,1)}) %all-gather.6.cloned.1.call-update) | async-done | bytes 1310736 | tf_op jit(solution)/shard_map/all_gather | solution.py:209
  70.7 46.5 %shard_map.120 = f32[4096,32]{1,0:T(8,128)} custom-call(s32[8,4096]{1,0:T(8,128)} %nb_ref.5, bf16[4096,32]{1,0:T(8,128)(2,1)} %bitcast.66, bf16[20480,32]{1,0:T(8,128)(2,1)} %all-gather.6.cloned.1.call-done.refs_1_, bf16[1024,32]{1,0:T(8,128)(2,1)} %copy-done.13, bf16[1024,32]{1,0:T(8,128)(2,1)} %copy-done.14, bf16[1024,32]{1,0:T(8,128)(2,1)} %copy-done.15, ...), custom_call_target="tpu_custom_call" | custom-call | tf_op jit(solution)/shard_map/pallas_call | solution.py:46
  117.2 1.8 convert_bitcast_fusion
  120.6 20.3 %all-gather.8.cloned.1.call-done = bf16[128,4096]{1,0:T(8,128)(2,1)} async-done(((bf16[32,4096]{1,0:T(8,128)(2,1)}), bf16[128,4096]{1,0:T(8,128)(2,1)}) %all-gather.8.cloned.1.call-update) | async-done | bytes 1048592 | tf_op jit(solution)/shard_map/all_gather | solution.py:252
  140.9 1.7 fusion.2.refs_0_
  142.7 2.0 gather_fusion.1
  146.8 3.2 gather_fusion.7
  150.1 3.2 gather_fusion.6
  153.3 3.2 gather_fusion.5
  157.1 2.8 collective-permute-start.6
  161.2 2.6 collective-permute-start.8
  163.8 5.2 %collective-permute-done.7.refs_3_ = bf16[1024,64]{1,0:T(8,128)(2,1)S(1)} collective-permute-done((bf16[1024,64]{1,0:T(8,128)(2,1)S(1)}, bf16[1024,64]{1,0:T(8,128)(2,1)S(1)}, u32[]{:S(2)}, u32[]{:S(2)}) %collective-permute-start.7) | collective-permute-done | bytes 131104 | tf_op jit(solution)/shard_map/ppermute | solution.py:187
  169.0 8.4 %collective-permute-done.8.refs_4_ = bf16[1024,64]{1,0:T(8,128)(2,1)S(1)} collective-permute-done((bf16[1024,64]{1,0:T(8,128)(2,1)S(1)}, bf16[1024,64]{1,0:T(8,128)(2,1)S(1)}, u32[]{:S(2)}, u32[]{:S(2)}) %collective-permute-start.8) | collective-permute-done | bytes 131104 | tf_op jit(solution)/shard_map/ppermute | solution.py:187
  177.5 21.8 %all-gather.12.cloned.1.call-done.refs_1_ = bf16[20480,64]{1,0:T(8,128)(2,1)} async-done(((bf16[640,64]{1,0:T(8,128)(2,1)}), bf16[20480,64]{1,0:T(8,128)(2,1)}) %all-gather.12.cloned.1.call-update) | async-done | bytes 2621456 | tf_op jit(solution)/shard_map/all_gather | solution.py:209
  199.3 46.4 %shard_map.121 = f32[4096,64]{1,0:T(8,128)} custom-call(s32[8,4096]{1,0:T(8,128)} %nb_ref.5, bf16[4096,64]{1,0:T(8,128)(2,1)} %copy-done.2, bf16[20480,64]{1,0:T(8,128)(2,1)} %all-gather.12.cloned.1.call-done.refs_1_, bf16[1024,64]{1,0:T(8,128)(2,1)} %copy-done.16, bf16[1024,64]{1,0:T(8,128)(2,1)} %copy-done.17, bf16[1024,64]{1,0:T(8,128)(2,1)} %copy-done.18, ...), custom_call_target="tpu_custom_call" | custom-call | tf_op jit(solution)/shard_map/pallas_call | solution.py:46
  245.7 1.7 convert_bitcast_fusion.1
  248.7 2.1 fusion.23
  250.8 27.3 %all-gather.14.cloned.1.call-done = bf16[256,4096]{1,0:T(8,128)(2,1)} async-done(((bf16[64,4096]{1,0:T(8,128)(2,1)}), bf16[256,4096]{1,0:T(8,128)(2,1)}) %all-gather.14.cloned.1.call-update) | async-done | bytes 2097168 | tf_op jit(solution)/shard_map/all_gather | solution.py:197
  278.1 2.3 fusion.21
  284.6 65.7 %shard_map.122 = f32[27648,64]{1,0:T(8,128)} custom-call(s32[8,4096]{1,0:T(8,128)} %nb_ref.5, f32[4096,64]{1,0:T(8,128)} %convert_element_type.61.rows_ref), custom_call_target="tpu_custom_call" | custom-call | tf_op jit(solution)/shard_map/pallas_call | solution.py:81
  350.3 5.7 %convert.6 = bf16[27648,64]{1,0:T(8,128)(2,1)S(1)} convert(f32[27648,64]{1,0:T(8,128)} %shard_map.122) | non-fusion elementwise | flops 1769472 | bytes 10616832 | tf_op jit(solution)/shard_map/convert.3
  356.0 3.3 slice.116
  360.5 6.2 %copy.67 = bf16[32,640,64]{1,2,0:T(8,128)(2,1)} copy(bf16[32,640,64]{2,1,0:T(8,128)(2,1)} %bitcast.67) | data formatting | bytes 5242880 | tf_op jit(solution)/shard_map/convert_element_type | solution.py:280
  366.7 8.0 %all-to-all-start = ((bf16[32,640,64]{1,2,0:T(8,128)(2,1)}), bf16[32,640,64]{1,2,0:T(8,128)(2,1)}, u32[]{:S(2)}, u32[]{:S(2)}) async-start(bf16[32,640,64]{1,2,0:T(8,128)(2,1)} %copy.67), calls=%async_computation | async-start | bytes 5242880 | tf_op jit(solution)/shard_map/all_to_all | solution.py:279
  375.3 2.0 fusion.18
  377.7 3.0 collective-permute-start.11
  380.9 2.2 fusion.6
  383.1 3.9 convolution_add_fusion.1.base_ref
  388.6 24.7 %collective-permute-done.11 = bf16[1024,64]{1,0:T(8,128)(2,1)S(1)} collective-permute-done((bf16[1024,64]{1,0:T(8,128)(2,1)}, bf16[1024,64]{1,0:T(8,128)(2,1)S(1)}, u32[]{:S(2)}, u32[]{:S(2)}) %collective-permute-start.11) | collective-permute-done | bytes 131104 | tf_op jit(solution)/shard_map/ppermute | solution.py:187
  413.3 3.4 collective-permute-done.10
  416.8 2.1 convert_reduce_fusion
  420.5 12.1 %shard_map.123 = f32[4096,64]{1,0:T(8,128)} custom-call(s32[3712]{0:T(1024)} %pad_add_fusion.t_ref, f32[4096,64]{1,0:T(8,128)} %convolution_add_fusion.1.base_ref, f32[3712,64]{1,0:T(8,128)} %pad_maximum_fusion.upd_ref), custom_call_target="tpu_custom_call" | custom-call | tf_op jit(solution)/shard_map/pallas_call | solution.py:127
  432.6 2.3 convolution_bitcast_fusion.1
  437.8 5.2 %collective-permute-done.13 = f32[38400]{0:T(1024)S(1)} collective-permute-done((f32[38400]{0:T(1024)S(1)}, f32[38400]{0:T(1024)S(1)}, u32[]{:S(2)}, u32[]{:S(2)}) %collective-permute-start.13) | collective-permute-done | bytes 153632 | tf_op jit(solution)/shard_map/ppermute | solution.py:161
  443.1 2.6 collective-permute-start.14
  445.6 3.1 collective-permute-done.14
  449.4 3.5 collective-permute-done.15
  452.9 2.4 collective-permute-start.16
  455.3 3.7 collective-permute-done.16
  (135 shorter events, 31.8 us)
Async XLA Ops:
  7.2 270.9 %copy-start = (bf16[172,256]{1,0:T(8,128)(2,1)S(1)}, bf16[172,256]{1,0:T(8,128)(2,1)}, u32[]{:S(2)}) copy-start(bf16[172,256]{1,0:T(8,128)(2,1)} %param.21) | copy-start | bytes 264196
  7.2 63.5 %all-gather.6.cloned.1.call-start = ((), (), s32[]{:S(2)}) async-start(), calls=%async_computation.1 | async-start | bytes 5406720 | tf_op jit(solution)/shard_map/all_gather | solution.py:209
  7.2 29.6 %collective-permute-start.2 = (bf16[32,4096]{1,0:T(8,128)(2,1)}, bf16[32,4096]{1,0:T(8,128)(2,1)S(1)}, u32[]{:S(2)}, u32[]{:S(2)}) collective-permute-start(bf16[32,4096]{1,0:T(8,128)(2,1)} %param.13), channel_id=1, source_target_pairs={{0,1},{1,2},{2,3},{3,0},{4,5},{5,6},{6,7},{7,4},{8,9},{9,10},{10,1... | collective-permute-start | bytes 786440 | tf_op jit(solution)/shard_map/ppermute | solution.py:98
  9.4 27.3 %collective-permute-start.1 = (bf16[32,4096]{1,0:T(8,128)(2,1)}, bf16[32,4096]{1,0:T(8,128)(2,1)S(1)}, u32[]{:S(2)}, u32[]{:S(2)}) collective-permute-start(bf16[32,4096]{1,0:T(8,128)(2,1)} %param.13), channel_id=1, source_target_pairs={{0,2},{1,3},{2,0},{3,1},{4,6},{5,7},{6,4},{7,5},{8,10},{9,11},{10,... | collective-permute-start | bytes 786440 | tf_op jit(solution)/shard_map/ppermute | solution.py:98
  12.0 21.3 %collective-permute-start = (bf16[32,4096]{1,0:T(8,128)(2,1)}, bf16[32,4096]{1,0:T(8,128)(2,1)S(1)}, u32[]{:S(2)}, u32[]{:S(2)}) collective-permute-start(bf16[32,4096]{1,0:T(8,128)(2,1)} %param.13), channel_id=1, source_target_pairs={{0,3},{1,0},{2,1},{3,2},{4,7},{5,4},{6,5},{7,6},{8,11},{9,8},{10,9... | collective-permute-start | bytes 786440 | tf_op jit(solution)/shard_map/ppermute | solution.py:98
  15.9 14.0 %copy-start.4 = (bf16[32,4096]{0,1:T(8,128)(2,1)}, bf16[32,4096]{0,1:T(8,128)(2,1)S(1)}, u32[]{:S(2)}) copy-start(bf16[32,4096]{0,1:T(8,128)(2,1)S(1)} %copy.58) | copy-start | bytes 786436
  19.6 121.3 %all-gather.8.cloned.1.call-start = ((), (), s32[]{:S(2)}) async-start(), calls=%async_computation.2 | async-start | bytes 1310720 | tf_op jit(solution)/shard_map/all_gather | solution.py:252
  23.1 14.9 %collective-permute-start.3 = (bf16[1024,32]{1,0:T(8,128)(2,1)S(1)}, bf16[1024,32]{1,0:T(8,128)(2,1)S(1)}, u32[]{:S(2)}, u32[]{:S(2)}) collective-permute-start(bf16[1024,32]{1,0:T(8,128)(2,1)S(1)} %broadcast_select_fusion.5), channel_id=1, source_target_pairs={{0,4},{4,0},{8,12},{12,8},{16,20},{20,16},{24,28},{28,24},{32,36},... | collective-permute-start | bytes 196616 | tf_op jit(solution)/shard_map/ppermute | solution.py:187
  28.2 9.9 %collective-permute-start.4 = (bf16[1024,32]{1,0:T(8,128)(2,1)S(1)}, bf16[1024,32]{1,0:T(8,128)(2,1)S(1)}, u32[]{:S(2)}, u32[]{:S(2)}) collective-permute-start(bf16[1024,32]{1,0:T(8,128)(2,1)S(1)} %broadcast_select_fusion.4), channel_id=1, source_target_pairs={{0,8},{4,12},{8,0},{12,4},{16,24},{20,28},{24,16},{28,20},{32,40},... | collective-permute-start | bytes 196616 | tf_op jit(solution)/shard_map/ppermute | solution.py:187
  29.9 6.9 %copy-start.12 = (bf16[32,4096]{1,0:T(8,128)(2,1)S(1)}, bf16[32,4096]{1,0:T(8,128)(2,1)}, u32[]{:S(2)}) copy-start(bf16[32,4096]{1,0:T(8,128)(2,1)} %param.13) | copy-start | bytes 786436
  33.3 14.5 %collective-permute-start.5 = (bf16[1024,32]{1,0:T(8,128)(2,1)S(1)}, bf16[1024,32]{1,0:T(8,128)(2,1)S(1)}, u32[]{:S(2)}, u32[]{:S(2)}) collective-permute-start(bf16[1024,32]{1,0:T(8,128)(2,1)S(1)} %broadcast_select_fusion.3), channel_id=1, source_target_pairs={{0,16},{4,20},{8,24},{12,28},{16,0},{20,4},{24,8},{28,12},{32,48},... | collective-permute-start | bytes 196616 | tf_op jit(solution)/shard_map/ppermute | solution.py:187
  38.0 32.7 %copy-start.13 = (bf16[1024,32]{1,0:T(8,128)(2,1)}, bf16[1024,32]{1,0:T(8,128)(2,1)S(1)}, u32[]{:S(2)}) copy-start(bf16[1024,32]{1,0:T(8,128)(2,1)S(1)} %collective-permute-done.3.refs_2_) | copy-start | bytes 196612
  38.0 32.7 %copy-start.14 = (bf16[1024,32]{1,0:T(8,128)(2,1)}, bf16[1024,32]{1,0:T(8,128)(2,1)S(1)}, u32[]{:S(2)}) copy-start(bf16[1024,32]{1,0:T(8,128)(2,1)S(1)} %collective-permute-done.4.refs_3_) | copy-start | bytes 196612
  47.8 22.9 %copy-start.15 = (bf16[1024,32]{1,0:T(8,128)(2,1)}, bf16[1024,32]{1,0:T(8,128)(2,1)S(1)}, u32[]{:S(2)}) copy-start(bf16[1024,32]{1,0:T(8,128)(2,1)S(1)} %collective-permute-done.5.refs_4_) | copy-start | bytes 196612
  117.2 2.9 copy-start.9
  117.2 3.0 copy-start.22
  118.9 22.0 %copy-start.23 = (bf16[64,128]{1,0:T(8,128)(2,1)S(1)}, bf16[64,128]{1,0:T(8,128)(2,1)}, u32[]{:S(2)}) copy-start(bf16[64,128]{1,0:T(8,128)(2,1)} %param.19) | copy-start | bytes 49156
  120.0 79.2 %all-gather.12.cloned.1.call-start = ((), (), s32[]{:S(2)}) async-start(), calls=%async_computation.4 | async-start | bytes 5406720 | tf_op jit(solution)/shard_map/all_gather | solution.py:209
  142.7 10.6 %copy-start.2 = (bf16[4096,64]{1,0:T(8,128)(2,1)}, bf16[4096,64]{1,0:T(8,128)(2,1)S(1)}, u32[]{:S(2)}) copy-start(bf16[4096,64]{1,0:T(8,128)(2,1)S(1)} %fusion.2.refs_0_) | copy-start | bytes 1572868
  145.5 103.1 %all-gather.10.cloned.1.call-start = ((), (), s32[]{:S(2)}) async-start(), calls=%async_computation.3 | async-start | bytes 2621440 | tf_op jit(solution)/shard_map/all_gather | solution.py:196
  146.8 131.3 %all-gather.14.cloned.1.call-start = ((), (), s32[]{:S(2)}) async-start(), calls=%async_computation.5 | async-start | bytes 2621440 | tf_op jit(solution)/shard_map/all_gather | solution.py:197
  157.1 6.7 %collective-permute-start.6 = (bf16[1024,64]{1,0:T(8,128)(2,1)S(1)}, bf16[1024,64]{1,0:T(8,128)(2,1)S(1)}, u32[]{:S(2)}, u32[]{:S(2)}) collective-permute-start(bf16[1024,64]{1,0:T(8,128)(2,1)S(1)} %broadcast_select_fusion.2), channel_id=1, source_target_pairs={{0,4},{4,0},{8,12},{12,8},{16,20},{20,16},{24,28},{28,24},{32,36},... | collective-permute-start | bytes 393224 | tf_op jit(solution)/shard_map/ppermute | solution.py:187
  160.0 9.1 %collective-permute-start.7 = (bf16[1024,64]{1,0:T(8,128)(2,1)S(1)}, bf16[1024,64]{1,0:T(8,128)(2,1)S(1)}, u32[]{:S(2)}, u32[]{:S(2)}) collective-permute-start(bf16[1024,64]{1,0:T(8,128)(2,1)S(1)} %broadcast_select_fusion.1), channel_id=1, source_target_pairs={{0,8},{4,12},{8,0},{12,4},{16,24},{20,28},{24,16},{28,20},{32,40},... | collective-permute-start | bytes 393224 | tf_op jit(solution)/shard_map/ppermute | solution.py:187
  161.2 16.3 %collective-permute-start.8 = (bf16[1024,64]{1,0:T(8,128)(2,1)S(1)}, bf16[1024,64]{1,0:T(8,128)(2,1)S(1)}, u32[]{:S(2)}, u32[]{:S(2)}) collective-permute-start(bf16[1024,64]{1,0:T(8,128)(2,1)S(1)} %broadcast_select_fusion), channel_id=1, source_target_pairs={{0,16},{4,20},{8,24},{12,28},{16,0},{20,4},{24,8},{28,12},{32,48},... | collective-permute-start | bytes 393224 | tf_op jit(solution)/shard_map/ppermute | solution.py:187
  163.8 35.5 %copy-start.16 = (bf16[1024,64]{1,0:T(8,128)(2,1)}, bf16[1024,64]{1,0:T(8,128)(2,1)S(1)}, u32[]{:S(2)}) copy-start(bf16[1024,64]{1,0:T(8,128)(2,1)S(1)} %collective-permute-done.6.refs_2_) | copy-start | bytes 393220
  169.0 30.3 %copy-start.17 = (bf16[1024,64]{1,0:T(8,128)(2,1)}, bf16[1024,64]{1,0:T(8,128)(2,1)S(1)}, u32[]{:S(2)}) copy-start(bf16[1024,64]{1,0:T(8,128)(2,1)S(1)} %collective-permute-done.7.refs_3_) | copy-start | bytes 393220
  177.5 21.8 %copy-start.18 = (bf16[1024,64]{1,0:T(8,128)(2,1)}, bf16[1024,64]{1,0:T(8,128)(2,1)S(1)}, u32[]{:S(2)}) copy-start(bf16[1024,64]{1,0:T(8,128)(2,1)S(1)} %collective-permute-done.8.refs_4_) | copy-start | bytes 393220
  245.7 3.0 copy-start.19
  250.8 29.6 %copy-start.24 = (s32[4096]{0:T(1024)S(1)}, s32[4096]{0:T(1024)}, u32[]{:S(2)}) copy-start(s32[4096]{0:T(1024)} %param.17) | copy-start | bytes 49156
  281.1 1.1 copy-start.5
  355.9 4.5 copy-start.7
  366.7 8.0 %copy-start.20 = (s32[3,1024]{1,0:T(4,128)S(1)}, s32[3,1024]{1,0:T(4,128)}, u32[]{:S(2)}) copy-start(s32[3,1024]{1,0:T(4,128)} %param.16) | copy-start | bytes 36868
  366.7 8.1 %copy-start.21 = (s32[640]{0:T(1024)S(1)}, s32[640]{0:T(1024)}, u32[]{:S(2)}) copy-start(s32[640]{0:T(1024)} %param.15) | copy-start | bytes 7684
  366.7 50.1 %all-to-all-start = ((bf16[32,640,64]{1,2,0:T(8,128)(2,1)}), bf16[32,640,64]{1,2,0:T(8,128)(2,1)}, u32[]{:S(2)}, u32[]{:S(2)}) async-start(bf16[32,640,64]{1,2,0:T(8,128)(2,1)} %copy.67), calls=%async_computation | async-start | bytes 5242880 | tf_op jit(solution)/shard_map/all_to_all | solution.py:279
  374.7 6.2 %copy-start.6 = (bf16[172,4096]{1,0:T(8,128)(2,1)S(1)}, bf16[172,4096]{1,0:T(8,128)(2,1)}, u32[]{:S(2)}) copy-start(bf16[172,4096]{1,0:T(8,128)(2,1)} %copy-done.5) | copy-start | bytes 4227076
  377.4 10.3 %collective-permute-start.9 = (bf16[1024,64]{1,0:T(8,128)(2,1)}, bf16[1024,64]{1,0:T(8,128)(2,1)}, u32[]{:S(2)}, u32[]{:S(2)}) collective-permute-start(bf16[1024,64]{1,0:T(8,128)(2,1)} %get-tuple-element.22), channel_id=1, source_target_pairs={{0,4},{4,0},{8,12},{12,8},{16,20},{20,16},{24,28},{28,24},{32,36},... | collective-permute-start | bytes 393224 | tf_op jit(solution)/shard_map/ppermute | solution.py:187
  377.7 35.6 %collective-permute-start.11 = (bf16[1024,64]{1,0:T(8,128)(2,1)}, bf16[1024,64]{1,0:T(8,128)(2,1)S(1)}, u32[]{:S(2)}, u32[]{:S(2)}) collective-permute-start(bf16[1024,64]{1,0:T(8,128)(2,1)} %get-tuple-element.23), channel_id=1, source_target_pairs={{0,16},{4,20},{8,24},{12,28},{16,0},{20,4},{24,8},{28,12},{32,48},... | collective-permute-start | bytes 393224 | tf_op jit(solution)/shard_map/ppermute | solution.py:187
  380.6 36.1 %collective-permute-start.10 = (bf16[1024,64]{1,0:T(8,128)(2,1)}, bf16[1024,64]{1,0:T(8,128)(2,1)S(1)}, u32[]{:S(2)}, u32[]{:S(2)}) collective-permute-start(bf16[1024,64]{1,0:T(8,128)(2,1)} %get-tuple-element.24), channel_id=1, source_target_pairs={{0,8},{4,12},{8,0},{12,4},{16,24},{20,28},{24,16},{28,20},{32,40},... | collective-permute-start | bytes 393224 | tf_op jit(solution)/shard_map/ppermute | solution.py:187
  383.1 3.9 copy-start.3
  420.5 12.1 %copy-start.10 = (bf16[4,32,4096]{2,1,0:T(8,128)(2,1)S(1)}, bf16[4,32,4096]{2,1,0:T(8,128)(2,1)}, u32[]{:S(2)}) copy-start(bf16[4,32,4096]{2,1,0:T(8,128)(2,1)} %constant_dynamic-slice_fusion) | copy-start | bytes 3145732
  432.6 2.3 copy-start.8
  432.6 2.5 copy-start.11
  435.1 26.2 %copy-start.1 = (bf16[172,256]{1,0:T(8,128)(2,1)S(1)}, bf16[172,256]{1,0:T(8,128)(2,1)}, u32[]{:S(2)}) copy-start(bf16[172,256]{1,0:T(8,128)(2,1)} %param.21) | copy-start | bytes 264196
  435.6 2.1 collective-permute-start.12
  437.7 5.3 %collective-permute-start.13 = (f32[38400]{0:T(1024)S(1)}, f32[38400]{0:T(1024)S(1)}, u32[]{:S(2)}, u32[]{:S(2)}) collective-permute-start(f32[38400]{0:T(1024)S(1)} %fusion.15), channel_id=1, source_target_pairs={{0,8},{4,12},{8,0},{12,4},{16,24},{20,28},{24,16},{28,20},{32,40},... | collective-permute-start | bytes 460808 | tf_op jit(solution)/shard_map/ppermute | solution.py:161
  443.1 5.7 %collective-permute-start.14 = (f32[38400]{0:T(1024)S(1)}, f32[38400]{0:T(1024)S(1)}, u32[]{:S(2)}, u32[]{:S(2)}) collective-permute-start(f32[38400]{0:T(1024)S(1)} %add.71), channel_id=1, source_target_pairs={{0,16},{4,20},{8,24},{12,28},{16,0},{20,4},{24,8},{28,12},{32,48},... | collective-permute-start | bytes 460808 | tf_op jit(solution)/shard_map/ppermute | solution.py:161
  448.7 4.2 collective-permute-start.15
  452.9 6.1 %collective-permute-start.16 = (f32[38400]{0:T(1024)S(1)}, f32[38400]{0:T(1024)S(1)}, u32[]{:S(2)}, u32[]{:S(2)}) collective-permute-start(f32[38400]{0:T(1024)S(1)} %add.73), channel_id=1, source_target_pairs={{0,64},{4,68},{8,72},{12,76},{16,80},{20,84},{24,88},{28,92},{32,9... | collective-permute-start | bytes 460808 | tf_op jit(solution)/shard_map/ppermute | solution.py:161
Sparse Core Ops, SparseCore 0:
  19.8 50.8 all-gather.5
  120.2 20.7 all-gather.7
  145.7 53.5 all-gather.11
  200.8 29.2 all-gather.9
  248.7 29.2 all-gather.13

commit v12 on v11

--- a/solution.py
+++ b/solution.py
@@ -151,6 +151,15 @@
         )
         stride *= 2
     return block
+
+
+def exchange_sum(flat, axis):
+    count = lax.axis_size(axis)
+    length = flat.shape[0]
+    padded = jnp.pad(flat, (0, (-length) % count)).reshape(count, -1)
+    reduced = jnp.sum(lax.all_to_all(padded, axis, 0, 0, tiled=True), axis=0)
+    spread = jnp.broadcast_to(reduced[None], (count, reduced.shape[0]))
+    return lax.all_to_all(spread, axis, 0, 0, tiled=True).reshape(-1)[:length]
 
 
 def tree_sum(value, axis):
@@ -295,7 +304,7 @@
     grad_inner_self = contract(grad_pre, full_input)
     grad_inner_neighbour = contract(grad_pre, full_mean)
     pieces = (grad_inner_self, grad_inner_neighbour, grad_outer_self, grad_outer_neighbour)
-    summed = tree_sum(jnp.concatenate([piece.reshape(-1) for piece in pieces]), "dom")
+    summed = exchange_sum(jnp.concatenate([piece.reshape(-1) for piece in pieces]), "dom")
     results = []
     offset = 0
     for piece in pieces:

time: 472 us -> 473 us (level)
  blocking collectives: 0 us -> 26.3 us
  waiting for transfers between devices: 160 us -> 144 us
  starting transfers between devices: 37.7 us -> 31 us
    all_to_all x0 -> x2, blocking collectives: none -> 26.3 us  [the longest x1 14.7 us: exchange_sum(): reduced = jnp.sum(lax.all_to_all(padded, axis, 0, 0, tiled=True), axis=0)]
    ppermute x5 -> x0, waiting for transfers between devices: 16.6 us -> none  [tree_sum(): value = value + lax.ppermute(value, axis, pairs)]
    ppermute x5 -> x0, starting transfers between devices: 6.71 us -> none  [tree_sum(): value = value + lax.ppermute(value, axis, pairs)]
  transfers between devices with their start and end apart: 23 -> 18, of which waited for: 14 -> 9; matrix products, arithmetic and copies ran while one was open for 10% -> 10% of each run, Pallas kernels for 10% -> 10%
where the time goes in v12:
time: 473 us; the launch traced here: 472 us
  Pallas kernels  171 us (36%)
  waiting for transfers between devices  144 us (30%)
  local copies, waits for them, and re-layouts  48.7 us (10%)
  starting transfers between devices  31 us (7%)
  blocking collectives  26.3 us (6%)
  other arithmetic  20.2 us (4%)
  matrix products  16.5 us (3%)
  between operations  14.4 us (3%)
    pallas_call x2, Pallas kernels, gather_mean(): pl.pallas_call(kernel, in_specs=[pl.BlockSpec(memory_space=pltpu.SMEM)] +...  92.8 us
    pallas_call x1, Pallas kernels, scatter_mean(): pl.pallas_call(kernel, in_specs=[pl.BlockSpec(memory_space=pltpu.SMEM), p...  65.7 us
    ppermute x9, waiting for transfers between devices, partner(): return lax.ppermute(value, axis, pairs)  51.8 us
    all_gather x2, waiting for transfers between devices, source_table(): hub_all = lax.all_gather(hub_local, 'dom', axis=0, tiled=True)  44.7 us
    all_gather x1, waiting for transfers between devices, widen(): lax.all_gather(second_rows, 'feat', axis=0, tiled=True)  27.3 us
    all_gather x1, waiting for transfers between devices, body(): full_mean = lax.all_gather(mean_one, 'feat', axis=0, tiled=True)  20.3 us
    gather x6, local copies, waits for them, and re-layouts, source_table(): jnp.take(local_rows, send_rows[bit_index], axis=0)  19.2 us
    ppermute x9, starting transfers between devices, partner(): return lax.ppermute(value, axis, pairs)  16.9 us
  transfers between devices with their start and end apart: 18, of which 9 were waited for; matrix products, arithmetic and copies ran while one was open for 10% of the time, Pallas kernels for 10%

profile of v12, /device:TPU:1, one launch (start us, length us, event | category | flops | bytes accessed | tf_op | source)
XLA Modules:
  0.0 471.9 jit_solution(13440848067813154212)
XLA Ops:
  7.2 2.2 collective-permute-start.2
  9.4 2.6 collective-permute-start.1
  14.5 1.4 copy.89
  16.8 2.0 gather_fusion
  19.7 3.2 gather_fusion.2
  23.1 1.6 collective-permute-start.3
  24.7 3.2 gather_fusion.3
  28.2 1.7 collective-permute-start.4
  29.9 3.2 gather_fusion.4
  33.4 3.4 collective-permute-start.5
  38.1 9.8 %collective-permute-done.5.refs_4_ = bf16[1024,32]{1,0:T(8,128)(2,1)S(1)} collective-permute-done((bf16[1024,32]{1,0:T(8,128)(2,1)S(1)}, bf16[1024,32]{1,0:T(8,128)(2,1)S(1)}, u32[]{:S(2)}, u32[]{:S(2)}) %collective-permute-start.5) | collective-permute-done | bytes 65568 | tf_op jit(solution)/shard_map/ppermute | solution.py:196
  47.8 22.9 %all-gather.6.cloned.1.call-done.refs_1_ = bf16[20480,32]{1,0:T(8,128)(2,1)} async-done(((bf16[640,32]{1,0:T(8,128)(2,1)}), bf16[20480,32]{1,0:T(8,128)(2,1)}) %all-gather.6.cloned.1.call-update) | async-done | bytes 1310736 | tf_op jit(solution)/shard_map/all_gather | solution.py:218
  70.7 46.4 %shard_map.120 = f32[4096,32]{1,0:T(8,128)} custom-call(s32[8,4096]{1,0:T(8,128)} %nb_ref.5, bf16[4096,32]{1,0:T(8,128)(2,1)} %bitcast.62, bf16[20480,32]{1,0:T(8,128)(2,1)} %all-gather.6.cloned.1.call-done.refs_1_, bf16[1024,32]{1,0:T(8,128)(2,1)} %copy-done.13, bf16[1024,32]{1,0:T(8,128)(2,1)} %copy-done.14, bf16[1024,32]{1,0:T(8,128)(2,1)} %copy-done.15, ...), custom_call_target="tpu_custom_call" | custom-call | tf_op jit(solution)/shard_map/pallas_call | solution.py:46
  117.1 1.8 convert_bitcast_fusion
  120.6 20.3 %all-gather.8.cloned.1.call-done = bf16[128,4096]{1,0:T(8,128)(2,1)} async-done(((bf16[32,4096]{1,0:T(8,128)(2,1)}), bf16[128,4096]{1,0:T(8,128)(2,1)}) %all-gather.8.cloned.1.call-update) | async-done | bytes 1048592 | tf_op jit(solution)/shard_map/all_gather | solution.py:261
  140.9 1.7 fusion.2.refs_0_
  142.6 2.0 gather_fusion.1
  146.8 3.2 gather_fusion.7
  150.0 3.2 gather_fusion.6
  153.2 3.2 gather_fusion.5
  157.1 2.8 collective-permute-start.6
  161.2 2.6 collective-permute-start.8
  163.8 5.2 %collective-permute-done.7.refs_3_ = bf16[1024,64]{1,0:T(8,128)(2,1)S(1)} collective-permute-done((bf16[1024,64]{1,0:T(8,128)(2,1)S(1)}, bf16[1024,64]{1,0:T(8,128)(2,1)S(1)}, u32[]{:S(2)}, u32[]{:S(2)}) %collective-permute-start.7) | collective-permute-done | bytes 131104 | tf_op jit(solution)/shard_map/ppermute | solution.py:196
  169.0 8.4 %collective-permute-done.8.refs_4_ = bf16[1024,64]{1,0:T(8,128)(2,1)S(1)} collective-permute-done((bf16[1024,64]{1,0:T(8,128)(2,1)S(1)}, bf16[1024,64]{1,0:T(8,128)(2,1)S(1)}, u32[]{:S(2)}, u32[]{:S(2)}) %collective-permute-start.8) | collective-permute-done | bytes 131104 | tf_op jit(solution)/shard_map/ppermute | solution.py:196
  177.4 21.8 %all-gather.12.cloned.1.call-done.refs_1_ = bf16[20480,64]{1,0:T(8,128)(2,1)} async-done(((bf16[640,64]{1,0:T(8,128)(2,1)}), bf16[20480,64]{1,0:T(8,128)(2,1)}) %all-gather.12.cloned.1.call-update) | async-done | bytes 2621456 | tf_op jit(solution)/shard_map/all_gather | solution.py:218
  199.2 46.4 %shard_map.121 = f32[4096,64]{1,0:T(8,128)} custom-call(s32[8,4096]{1,0:T(8,128)} %nb_ref.5, bf16[4096,64]{1,0:T(8,128)(2,1)} %copy-done.2, bf16[20480,64]{1,0:T(8,128)(2,1)} %all-gather.12.cloned.1.call-done.refs_1_, bf16[1024,64]{1,0:T(8,128)(2,1)} %copy-done.16, bf16[1024,64]{1,0:T(8,128)(2,1)} %copy-done.17, bf16[1024,64]{1,0:T(8,128)(2,1)} %copy-done.18, ...), custom_call_target="tpu_custom_call" | custom-call | tf_op jit(solution)/shard_map/pallas_call | solution.py:46
  245.6 1.7 convert_bitcast_fusion.1
  248.6 2.1 fusion.23
  250.7 27.3 %all-gather.14.cloned.1.call-done = bf16[256,4096]{1,0:T(8,128)(2,1)} async-done(((bf16[64,4096]{1,0:T(8,128)(2,1)}), bf16[256,4096]{1,0:T(8,128)(2,1)}) %all-gather.14.cloned.1.call-update) | async-done | bytes 2097168 | tf_op jit(solution)/shard_map/all_gather | solution.py:206
  278.0 2.3 fusion.21
  283.1 1.4 convert_element_type.61.rows_ref
  284.5 65.7 %shard_map.122 = f32[27648,64]{1,0:T(8,128)} custom-call(s32[8,4096]{1,0:T(8,128)} %nb_ref.5, f32[4096,64]{1,0:T(8,128)} %convert_element_type.61.rows_ref), custom_call_target="tpu_custom_call" | custom-call | tf_op jit(solution)/shard_map/pallas_call | solution.py:81
  350.2 5.7 %convert.6 = bf16[27648,64]{1,0:T(8,128)(2,1)S(1)} convert(f32[27648,64]{1,0:T(8,128)} %shard_map.122) | non-fusion elementwise | flops 1769472 | bytes 10616832 | tf_op jit(solution)/shard_map/convert.3
  355.9 3.3 slice.82
  360.4 6.1 %copy.98 = bf16[32,640,64]{1,2,0:T(8,128)(2,1)} copy(bf16[32,640,64]{2,1,0:T(8,128)(2,1)} %bitcast.63) | data formatting | bytes 5242880 | tf_op jit(solution)/shard_map/convert_element_type | solution.py:289
  366.5 8.0 %all-to-all-start = ((bf16[32,640,64]{1,2,0:T(8,128)(2,1)}), bf16[32,640,64]{1,2,0:T(8,128)(2,1)}, u32[]{:S(2)}, u32[]{:S(2)}) async-start(bf16[32,640,64]{1,2,0:T(8,128)(2,1)} %copy.98), calls=%async_computation | async-start | bytes 5242880 | tf_op jit(solution)/shard_map/all_to_all | solution.py:288
  375.2 2.0 fusion.17
  377.5 3.0 collective-permute-start.11
  380.8 2.1 fusion.6
  382.9 3.9 convolution_add_fusion.1.base_ref
  388.2 25.0 %collective-permute-done.11 = bf16[1024,64]{1,0:T(8,128)(2,1)S(1)} collective-permute-done((bf16[1024,64]{1,0:T(8,128)(2,1)}, bf16[1024,64]{1,0:T(8,128)(2,1)S(1)}, u32[]{:S(2)}, u32[]{:S(2)}) %collective-permute-start.11) | collective-permute-done | bytes 131104 | tf_op jit(solution)/shard_map/ppermute | solution.py:196
  413.2 3.4 collective-permute-done.10
  416.6 2.1 convert_reduce_fusion
  418.9 1.4 pad_maximum_fusion.upd_ref
  420.3 12.1 %shard_map.123 = f32[4096,64]{1,0:T(8,128)} custom-call(s32[3712]{0:T(1024)} %pad_add_fusion.t_ref, f32[4096,64]{1,0:T(8,128)} %convolution_add_fusion.1.base_ref, f32[3712,64]{1,0:T(8,128)} %pad_maximum_fusion.upd_ref), custom_call_target="tpu_custom_call" | custom-call | tf_op jit(solution)/shard_map/pallas_call | solution.py:127
  432.5 2.3 convolution_bitcast_fusion.1
  436.0 14.7 %all_to_all.20 = f32[32,1,1200]{2,1,0:T(1,128)S(1)} all-to-all(f32[32,1,1200]{2,1,0:T(1,128)S(1)} %all_to_all.14), channel_id=1, replica_groups=mesh['dom'=32,'feat'=4] {'dom'}, dimensions={0} | all-to-all | bytes 307200 | tf_op jit(solution)/shard_map/all_to_all | solution.py:160
  450.9 11.5 %all_to_all.21 = f32[32,1,1200]{2,1,0:T(1,128)S(1)} all-to-all(f32[32,1,1200]{2,1,0:T(1,128)S(1)} %broadcast_in_dim.55), channel_id=1, replica_groups=mesh['dom'=32,'feat'=4] {'dom'}, dimensions={0} | all-to-all | bytes 307200 | tf_op jit(solution)/shard_map/all_to_all | solution.py:162
  (130 shorter events, 23.9 us)
Async XLA Ops:
  7.2 270.8 %copy-start = (bf16[172,256]{1,0:T(8,128)(2,1)S(1)}, bf16[172,256]{1,0:T(8,128)(2,1)}, u32[]{:S(2)}) copy-start(bf16[172,256]{1,0:T(8,128)(2,1)} %param.21) | copy-start | bytes 264196
  7.2 63.5 %all-gather.6.cloned.1.call-start = ((), (), s32[]{:S(2)}) async-start(), calls=%async_computation.3 | async-start | bytes 5406720 | tf_op jit(solution)/shard_map/all_gather | solution.py:218
  7.2 29.6 %collective-permute-start.2 = (bf16[32,4096]{1,0:T(8,128)(2,1)}, bf16[32,4096]{1,0:T(8,128)(2,1)S(1)}, u32[]{:S(2)}, u32[]{:S(2)}) collective-permute-start(bf16[32,4096]{1,0:T(8,128)(2,1)} %param.13), channel_id=1, source_target_pairs={{0,1},{1,2},{2,3},{3,0},{4,5},{5,6},{6,7},{7,4},{8,9},{9,10},{10,1... | collective-permute-start | bytes 786440 | tf_op jit(solution)/shard_map/ppermute | solution.py:98
  9.4 27.4 %collective-permute-start.1 = (bf16[32,4096]{1,0:T(8,128)(2,1)}, bf16[32,4096]{1,0:T(8,128)(2,1)S(1)}, u32[]{:S(2)}, u32[]{:S(2)}) collective-permute-start(bf16[32,4096]{1,0:T(8,128)(2,1)} %param.13), channel_id=1, source_target_pairs={{0,2},{1,3},{2,0},{3,1},{4,6},{5,7},{6,4},{7,5},{8,10},{9,11},{10,... | collective-permute-start | bytes 786440 | tf_op jit(solution)/shard_map/ppermute | solution.py:98
  12.0 21.3 %collective-permute-start = (bf16[32,4096]{1,0:T(8,128)(2,1)}, bf16[32,4096]{1,0:T(8,128)(2,1)S(1)}, u32[]{:S(2)}, u32[]{:S(2)}) collective-permute-start(bf16[32,4096]{1,0:T(8,128)(2,1)} %param.13), channel_id=1, source_target_pairs={{0,3},{1,0},{2,1},{3,2},{4,7},{5,4},{6,5},{7,6},{8,11},{9,8},{10,9... | collective-permute-start | bytes 786440 | tf_op jit(solution)/shard_map/ppermute | solution.py:98
  15.9 14.0 %copy-start.4 = (bf16[32,4096]{0,1:T(8,128)(2,1)}, bf16[32,4096]{0,1:T(8,128)(2,1)S(1)}, u32[]{:S(2)}) copy-start(bf16[32,4096]{0,1:T(8,128)(2,1)S(1)} %copy.89) | copy-start | bytes 786436
  19.6 121.2 %all-gather.8.cloned.1.call-start = ((), (), s32[]{:S(2)}) async-start(), calls=%async_computation.4 | async-start | bytes 1310720 | tf_op jit(solution)/shard_map/all_gather | solution.py:261
  23.1 14.9 %collective-permute-start.3 = (bf16[1024,32]{1,0:T(8,128)(2,1)S(1)}, bf16[1024,32]{1,0:T(8,128)(2,1)S(1)}, u32[]{:S(2)}, u32[]{:S(2)}) collective-permute-start(bf16[1024,32]{1,0:T(8,128)(2,1)S(1)} %broadcast_select_fusion.5), channel_id=1, source_target_pairs={{0,4},{4,0},{8,12},{12,8},{16,20},{20,16},{24,28},{28,24},{32,36},... | collective-permute-start | bytes 196616 | tf_op jit(solution)/shard_map/ppermute | solution.py:196
  28.2 9.9 %collective-permute-start.4 = (bf16[1024,32]{1,0:T(8,128)(2,1)S(1)}, bf16[1024,32]{1,0:T(8,128)(2,1)S(1)}, u32[]{:S(2)}, u32[]{:S(2)}) collective-permute-start(bf16[1024,32]{1,0:T(8,128)(2,1)S(1)} %broadcast_select_fusion.4), channel_id=1, source_target_pairs={{0,8},{4,12},{8,0},{12,4},{16,24},{20,28},{24,16},{28,20},{32,40},... | collective-permute-start | bytes 196616 | tf_op jit(solution)/shard_map/ppermute | solution.py:196
  29.9 6.9 %copy-start.12 = (bf16[32,4096]{1,0:T(8,128)(2,1)S(1)}, bf16[32,4096]{1,0:T(8,128)(2,1)}, u32[]{:S(2)}) copy-start(bf16[32,4096]{1,0:T(8,128)(2,1)} %param.13) | copy-start | bytes 786436
  33.4 14.5 %collective-permute-start.5 = (bf16[1024,32]{1,0:T(8,128)(2,1)S(1)}, bf16[1024,32]{1,0:T(8,128)(2,1)S(1)}, u32[]{:S(2)}, u32[]{:S(2)}) collective-permute-start(bf16[1024,32]{1,0:T(8,128)(2,1)S(1)} %broadcast_select_fusion.3), channel_id=1, source_target_pairs={{0,16},{4,20},{8,24},{12,28},{16,0},{20,4},{24,8},{28,12},{32,48},... | collective-permute-start | bytes 196616 | tf_op jit(solution)/shard_map/ppermute | solution.py:196
  38.0 32.7 %copy-start.13 = (bf16[1024,32]{1,0:T(8,128)(2,1)}, bf16[1024,32]{1,0:T(8,128)(2,1)S(1)}, u32[]{:S(2)}) copy-start(bf16[1024,32]{1,0:T(8,128)(2,1)S(1)} %collective-permute-done.3.refs_2_) | copy-start | bytes 196612
  38.0 32.7 %copy-start.14 = (bf16[1024,32]{1,0:T(8,128)(2,1)}, bf16[1024,32]{1,0:T(8,128)(2,1)S(1)}, u32[]{:S(2)}) copy-start(bf16[1024,32]{1,0:T(8,128)(2,1)S(1)} %collective-permute-done.4.refs_3_) | copy-start | bytes 196612
  47.8 22.9 %copy-start.15 = (bf16[1024,32]{1,0:T(8,128)(2,1)}, bf16[1024,32]{1,0:T(8,128)(2,1)S(1)}, u32[]{:S(2)}) copy-start(bf16[1024,32]{1,0:T(8,128)(2,1)S(1)} %collective-permute-done.5.refs_4_) | copy-start | bytes 196612
  117.1 2.9 copy-start.9
  117.1 2.9 copy-start.24
  118.9 22.0 %copy-start.25 = (bf16[64,128]{1,0:T(8,128)(2,1)S(1)}, bf16[64,128]{1,0:T(8,128)(2,1)}, u32[]{:S(2)}) copy-start(bf16[64,128]{1,0:T(8,128)(2,1)} %param.19) | copy-start | bytes 49156
  120.0 79.2 %all-gather.12.cloned.1.call-start = ((), (), s32[]{:S(2)}) async-start(), calls=%async_computation.6 | async-start | bytes 5406720 | tf_op jit(solution)/shard_map/all_gather | solution.py:218
  142.6 10.6 %copy-start.2 = (bf16[4096,64]{1,0:T(8,128)(2,1)}, bf16[4096,64]{1,0:T(8,128)(2,1)S(1)}, u32[]{:S(2)}) copy-start(bf16[4096,64]{1,0:T(8,128)(2,1)S(1)} %fusion.2.refs_0_) | copy-start | bytes 1572868
  145.5 103.1 %all-gather.10.cloned.1.call-start = ((), (), s32[]{:S(2)}) async-start(), calls=%async_computation.5 | async-start | bytes 2621440 | tf_op jit(solution)/shard_map/all_gather | solution.py:205
  146.7 131.3 %all-gather.14.cloned.1.call-start = ((), (), s32[]{:S(2)}) async-start(), calls=%async_computation.7 | async-start | bytes 2621440 | tf_op jit(solution)/shard_map/all_gather | solution.py:206
  157.1 6.7 %collective-permute-start.6 = (bf16[1024,64]{1,0:T(8,128)(2,1)S(1)}, bf16[1024,64]{1,0:T(8,128)(2,1)S(1)}, u32[]{:S(2)}, u32[]{:S(2)}) collective-permute-start(bf16[1024,64]{1,0:T(8,128)(2,1)S(1)} %broadcast_select_fusion.2), channel_id=1, source_target_pairs={{0,4},{4,0},{8,12},{12,8},{16,20},{20,16},{24,28},{28,24},{32,36},... | collective-permute-start | bytes 393224 | tf_op jit(solution)/shard_map/ppermute | solution.py:196
  159.9 9.1 %collective-permute-start.7 = (bf16[1024,64]{1,0:T(8,128)(2,1)S(1)}, bf16[1024,64]{1,0:T(8,128)(2,1)S(1)}, u32[]{:S(2)}, u32[]{:S(2)}) collective-permute-start(bf16[1024,64]{1,0:T(8,128)(2,1)S(1)} %broadcast_select_fusion.1), channel_id=1, source_target_pairs={{0,8},{4,12},{8,0},{12,4},{16,24},{20,28},{24,16},{28,20},{32,40},... | collective-permute-start | bytes 393224 | tf_op jit(solution)/shard_map/ppermute | solution.py:196
  161.2 16.3 %collective-permute-start.8 = (bf16[1024,64]{1,0:T(8,128)(2,1)S(1)}, bf16[1024,64]{1,0:T(8,128)(2,1)S(1)}, u32[]{:S(2)}, u32[]{:S(2)}) collective-permute-start(bf16[1024,64]{1,0:T(8,128)(2,1)S(1)} %broadcast_select_fusion), channel_id=1, source_target_pairs={{0,16},{4,20},{8,24},{12,28},{16,0},{20,4},{24,8},{28,12},{32,48},... | collective-permute-start | bytes 393224 | tf_op jit(solution)/shard_map/ppermute | solution.py:196
  163.8 35.5 %copy-start.16 = (bf16[1024,64]{1,0:T(8,128)(2,1)}, bf16[1024,64]{1,0:T(8,128)(2,1)S(1)}, u32[]{:S(2)}) copy-start(bf16[1024,64]{1,0:T(8,128)(2,1)S(1)} %collective-permute-done.6.refs_2_) | copy-start | bytes 393220
  169.0 30.2 %copy-start.17 = (bf16[1024,64]{1,0:T(8,128)(2,1)}, bf16[1024,64]{1,0:T(8,128)(2,1)S(1)}, u32[]{:S(2)}) copy-start(bf16[1024,64]{1,0:T(8,128)(2,1)S(1)} %collective-permute-done.7.refs_3_) | copy-start | bytes 393220
  177.4 21.8 %copy-start.18 = (bf16[1024,64]{1,0:T(8,128)(2,1)}, bf16[1024,64]{1,0:T(8,128)(2,1)S(1)}, u32[]{:S(2)}) copy-start(bf16[1024,64]{1,0:T(8,128)(2,1)S(1)} %collective-permute-done.8.refs_4_) | copy-start | bytes 393220
  245.6 3.0 copy-start.19
  250.7 29.7 %copy-start.26 = (s32[4096]{0:T(1024)S(1)}, s32[4096]{0:T(1024)}, u32[]{:S(2)}) copy-start(s32[4096]{0:T(1024)} %param.17) | copy-start | bytes 49156
  281.0 1.1 copy-start.5
  355.8 4.5 copy-start.7
  366.5 8.0 %copy-start.22 = (s32[3,1024]{1,0:T(4,128)S(1)}, s32[3,1024]{1,0:T(4,128)}, u32[]{:S(2)}) copy-start(s32[3,1024]{1,0:T(4,128)} %param.16) | copy-start | bytes 36868
  366.5 8.1 %copy-start.23 = (s32[640]{0:T(1024)S(1)}, s32[640]{0:T(1024)}, u32[]{:S(2)}) copy-start(s32[640]{0:T(1024)} %param.15) | copy-start | bytes 7684
  366.5 50.1 %all-to-all-start = ((bf16[32,640,64]{1,2,0:T(8,128)(2,1)}), bf16[32,640,64]{1,2,0:T(8,128)(2,1)}, u32[]{:S(2)}, u32[]{:S(2)}) async-start(bf16[32,640,64]{1,2,0:T(8,128)(2,1)} %copy.98), calls=%async_computation | async-start | bytes 5242880 | tf_op jit(solution)/shard_map/all_to_all | solution.py:288
  374.6 6.2 %copy-start.6 = (bf16[172,4096]{1,0:T(8,128)(2,1)S(1)}, bf16[172,4096]{1,0:T(8,128)(2,1)}, u32[]{:S(2)}) copy-start(bf16[172,4096]{1,0:T(8,128)(2,1)} %copy-done.5) | copy-start | bytes 4227076
  377.2 5.7 %copy-start.20 = (bf16[172,256]{1,0:T(8,128)(2,1)S(1)}, bf16[172,256]{1,0:T(8,128)(2,1)}, u32[]{:S(2)}) copy-start(bf16[172,256]{1,0:T(8,128)(2,1)} %param.20) | copy-start | bytes 264196
  377.2 10.9 %collective-permute-start.9 = (bf16[1024,64]{1,0:T(8,128)(2,1)}, bf16[1024,64]{1,0:T(8,128)(2,1)S(1)}, u32[]{:S(2)}, u32[]{:S(2)}) collective-permute-start(bf16[1024,64]{1,0:T(8,128)(2,1)} %get-tuple-element.30), channel_id=1, source_target_pairs={{0,4},{4,0},{8,12},{12,8},{16,20},{20,16},{24,28},{28,24},{32,36},... | collective-permute-start | bytes 393224 | tf_op jit(solution)/shard_map/ppermute | solution.py:196
  377.5 35.7 %collective-permute-start.11 = (bf16[1024,64]{1,0:T(8,128)(2,1)}, bf16[1024,64]{1,0:T(8,128)(2,1)S(1)}, u32[]{:S(2)}, u32[]{:S(2)}) collective-permute-start(bf16[1024,64]{1,0:T(8,128)(2,1)} %get-tuple-element.31), channel_id=1, source_target_pairs={{0,16},{4,20},{8,24},{12,28},{16,0},{20,4},{24,8},{28,12},{32,48},... | collective-permute-start | bytes 393224 | tf_op jit(solution)/shard_map/ppermute | solution.py:196
  380.5 36.1 %collective-permute-start.10 = (bf16[1024,64]{1,0:T(8,128)(2,1)}, bf16[1024,64]{1,0:T(8,128)(2,1)S(1)}, u32[]{:S(2)}, u32[]{:S(2)}) collective-permute-start(bf16[1024,64]{1,0:T(8,128)(2,1)} %get-tuple-element.32), channel_id=1, source_target_pairs={{0,8},{4,12},{8,0},{12,4},{16,24},{20,28},{24,16},{28,20},{32,40},... | collective-permute-start | bytes 393224 | tf_op jit(solution)/shard_map/ppermute | solution.py:196
  382.9 3.9 copy-start.3
  420.3 12.1 %copy-start.10 = (bf16[4,32,4096]{2,1,0:T(8,128)(2,1)S(1)}, bf16[4,32,4096]{2,1,0:T(8,128)(2,1)}, u32[]{:S(2)}) copy-start(bf16[4,32,4096]{2,1,0:T(8,128)(2,1)} %constant_dynamic-slice_fusion) | copy-start | bytes 3145732
  432.5 2.3 copy-start.8
  432.5 2.5 copy-start.11
  435.0 0.8 copy-start.21
  435.0 30.4 %copy-start.1 = (bf16[172,256]{1,0:T(8,128)(2,1)S(1)}, bf16[172,256]{1,0:T(8,128)(2,1)}, u32[]{:S(2)}) copy-start(bf16[172,256]{1,0:T(8,128)(2,1)} %param.21) | copy-start | bytes 264196
Sparse Core Ops, SparseCore 0:
  19.8 50.8 all-gather.5
  120.1 20.7 all-gather.7
  145.6 53.5 all-gather.11
  200.7 29.2 all-gather.9
  248.6 29.2 all-gather.13

commit v13 on v12

--- a/solution.py
+++ b/solution.py
@@ -215,7 +215,10 @@
 def source_table(local, hub_rows, send_rows):
     local_rows = local.T
     hub_local = jnp.take(local_rows, hub_rows, axis=0)
-    hub_all = lax.all_gather(hub_local, "dom", axis=0, tiled=True)
+    owners = lax.axis_size("dom")
+    hub_all = lax.all_to_all(
+        jnp.broadcast_to(hub_local[None], (owners,) + hub_local.shape), "dom", 0, 0, tiled=True
+    ).reshape(owners * hub_local.shape[0], hub_local.shape[1])
     received = [
         trade(jnp.take(local_rows, send_rows[bit_index], axis=0), bit_index)
         for bit_index in range(send_rows.shape[0])
@@ -283,11 +286,11 @@
     spread = scatter_mean(back_rows, neighbours, span)
     grad_rows = direct.T + spread[:rows]
     owners = lax.axis_size("dom")
-    hub_parts = spread[rows : rows + hub_count].reshape(owners, hub_count // owners, width)
+    hub_flat = spread[rows : rows + hub_count].astype(jnp.bfloat16)
     hub_back = jnp.sum(
-        lax.all_to_all(
-            hub_parts.astype(jnp.bfloat16), "dom", split_axis=0, concat_axis=0, tiled=True
-        ).astype(jnp.float32),
+        lax.all_to_all(hub_flat, "dom", 0, 0, tiled=True)
+        .astype(jnp.float32)
+        .reshape(owners, hub_count // owners, width),
         axis=0,
     )
     base = rows + hub_count

time: 473 us -> 465 us (0.983)
  waiting for transfers between devices: 144 us -> 106 us
  local copies, waits for them, and re-layouts: 48.7 us -> 65.4 us
  starting transfers between devices: 31 us -> 45.4 us
    all_gather x2 -> x0, waiting for transfers between devices: 44.7 us -> none  [source_table(): hub_all = lax.all_gather(hub_local, 'dom', axis=0, tiled=True)]
    all_to_all x1 -> x3, waiting for transfers between devices: 0.01 us -> 28.3 us  [the longest x2 28.3 us: source_table(): lax.all_to_all(jnp.broadcast_to(hub_local[None], (owners,) + hub_local.sh...]
    ppermute x9, waiting for transfers between devices: 51.8 us -> 31.9 us  [partner(): return lax.ppermute(value, axis, pairs)]
    all_to_all x1 -> x3, starting transfers between devices: 8.01 us -> 25.6 us  [the longest x2 17.6 us: source_table(): lax.all_to_all(jnp.broadcast_to(hub_local[None], (owners,) + hub_local.sh...]
    all_to_all x0 -> x3, local copies, waits for them, and re-layouts: none -> 16.2 us  [the longest x2 10 us: source_table(): lax.all_to_all(jnp.broadcast_to(hub_local[None], (owners,) + hub_local.sh...]
    convert_element_type x1 -> x0, local copies, waits for them, and re-layouts: 6.14 us -> none  [body(): hub_parts.astype(jnp.bfloat16)]
  transfers between devices with their start and end apart: 18 -> 18, of which waited for: 9 -> 7; matrix products, arithmetic and copies ran while one was open for 10% -> 13% of each run, Pallas kernels for 10% -> 10%
where the time goes in v13:
time: 465 us; the launch traced here: 464 us
  Pallas kernels  171 us (37%)
  waiting for transfers between devices  106 us (23%)
  local copies, waits for them, and re-layouts  65.4 us (14%)
  starting transfers between devices  45.4 us (10%)
  blocking collectives  26.3 us (6%)
  other arithmetic  19.7 us (4%)
  matrix products  16.5 us (4%)
  between operations  14.4 us (3%)
    pallas_call x2, Pallas kernels, gather_mean(): pl.pallas_call(kernel, in_specs=[pl.BlockSpec(memory_space=pltpu.SMEM)] +...  92.7 us
    pallas_call x1, Pallas kernels, scatter_mean(): pl.pallas_call(kernel, in_specs=[pl.BlockSpec(memory_space=pltpu.SMEM), p...  65.7 us
    ppermute x9, waiting for transfers between devices, partner(): return lax.ppermute(value, axis, pairs)  31.9 us
    all_to_all x2, waiting for transfers between devices, source_table(): lax.all_to_all(jnp.broadcast_to(hub_local[None], (owners,) + hub_local.sh...  28.3 us
    all_gather x1, waiting for transfers between devices, widen(): lax.all_gather(second_rows, 'feat', axis=0, tiled=True)  26.9 us
    gather x6, local copies, waits for them, and re-layouts, source_table(): jnp.take(local_rows, send_rows[bit_index], axis=0)  19.2 us
    all_gather x1, waiting for transfers between devices, body(): full_mean = lax.all_gather(mean_one, 'feat', axis=0, tiled=True)  18.3 us
    all_to_all x2, starting transfers between devices, source_table(): lax.all_to_all(jnp.broadcast_to(hub_local[None], (owners,) + hub_local.sh...  17.6 us
  transfers between devices with their start and end apart: 18, of which 7 were waited for; matrix products, arithmetic and copies ran while one was open for 13% of the time, Pallas kernels for 10%

profile of v13, /device:TPU:1, one launch (start us, length us, event | category | flops | bytes accessed | tf_op | source)
XLA Modules:
  0.0 463.7 jit_solution(4514972079350699125)
XLA Ops:
  7.2 2.2 collective-permute-start.2
  9.4 2.6 collective-permute-start.1
  13.1 1.5 copy.105
  16.1 3.2 gather_fusion.2
  20.3 1.5 collective-permute-start.3
  21.8 3.2 gather_fusion.3
  25.9 1.6 collective-permute-start.4
  27.6 2.0 gather_fusion
  31.1 7.8 %all-to-all-start = ((bf16[32,640,32]{1,2,0:T(8,128)(2,1)}), bf16[32,640,32]{1,2,0:T(8,128)(2,1)S(1)}, u32[]{:S(2)}, u32[]{:S(2)}) async-start(bf16[32,640,32]{1,2,0:T(8,128)(2,1)} %broadcast_in_dim.65), calls=%async_computation | async-start | bytes 2621440 | tf_op jit(solution)/shard_map/all_to_all | solution.py:219
  38.9 3.2 gather_fusion.4
  42.4 2.9 collective-permute-start.5
  48.5 10.1 %all-to-all-done = bf16[32,640,32]{1,2,0:T(8,128)(2,1)S(1)} async-done(((bf16[32,640,32]{1,2,0:T(8,128)(2,1)}), bf16[32,640,32]{1,2,0:T(8,128)(2,1)S(1)}, u32[]{:S(2)}, u32[]{:S(2)}) %all-to-all-start) | async-done | bytes 1310752 | tf_op jit(solution)/shard_map/all_to_all | solution.py:219
  58.6 4.1 copy.107
  63.5 46.4 %shard_map.120 = f32[4096,32]{1,0:T(8,128)} custom-call(s32[8,4096]{1,0:T(8,128)} %nb_ref.5, bf16[4096,32]{1,0:T(8,128)(2,1)} %bitcast.64, bf16[20480,32]{1,0:T(8,128)(2,1)} %bitcast.65, bf16[1024,32]{1,0:T(8,128)(2,1)} %collective-permute-done.3.refs_2_, bf16[1024,32]{1,0:T(8,128)(2,1)} %collective-permute-done.4.refs_3_, bf16[1024,32]{1,0:T(8,128)(2,1)} %copy-done.13, ...), custom_call_target="tpu_custom_call" | custom-call | tf_op jit(solution)/shard_map/pallas_call | solution.py:46
  109.8 1.8 convert_bitcast_fusion
  113.2 18.3 %all-gather.4.cloned.1.call-done = bf16[128,4096]{1,0:T(8,128)(2,1)} async-done(((bf16[32,4096]{1,0:T(8,128)(2,1)}), bf16[128,4096]{1,0:T(8,128)(2,1)}) %all-gather.4.cloned.1.call-update) | async-done | bytes 1048592 | tf_op jit(solution)/shard_map/all_gather | solution.py:264
  131.6 1.7 fusion.2.refs_0_
  133.3 2.0 gather_fusion.1
  135.6 1.8 broadcast_in_dim.68
  137.4 9.8 %all-to-all-start.1 = ((bf16[32,640,64]{1,2,0:T(8,128)(2,1)}), bf16[32,640,64]{1,2,0:T(8,128)(2,1)}, u32[]{:S(2)}, u32[]{:S(2)}) async-start(bf16[32,640,64]{1,2,0:T(8,128)(2,1)} %broadcast_in_dim.68), calls=%async_computation.1 | async-start | bytes 5242880 | tf_op jit(solution)/shard_map/all_to_all | solution.py:219
  148.5 3.2 gather_fusion.7
  151.7 3.2 gather_fusion.6
  155.0 3.2 gather_fusion.5
  160.6 2.4 collective-permute-start.8
  163.0 18.2 %all-to-all-done.1 = bf16[32,640,64]{1,2,0:T(8,128)(2,1)} async-done(((bf16[32,640,64]{1,2,0:T(8,128)(2,1)}), bf16[32,640,64]{1,2,0:T(8,128)(2,1)}, u32[]{:S(2)}, u32[]{:S(2)}) %all-to-all-start.1) | async-done | bytes 2621472 | tf_op jit(solution)/shard_map/all_to_all | solution.py:219
  181.2 6.0 %copy.113 = bf16[32,640,64]{2,1,0:T(8,128)(2,1)} copy(bf16[32,640,64]{1,2,0:T(8,128)(2,1)} %all-to-all-done.1) | data formatting | bytes 5242880 | tf_op jit(solution)/shard_map/all_to_all | solution.py:219
  187.2 3.5 collective-permute-done.8.refs_4_
  191.4 46.4 %shard_map.121 = f32[4096,64]{1,0:T(8,128)} custom-call(s32[8,4096]{1,0:T(8,128)} %nb_ref.5, bf16[4096,64]{1,0:T(8,128)(2,1)} %copy-done.2, bf16[20480,64]{1,0:T(8,128)(2,1)} %bitcast.66, bf16[1024,64]{1,0:T(8,128)(2,1)} %copy-done.14, bf16[1024,64]{1,0:T(8,128)(2,1)} %copy-done.15, bf16[1024,64]{1,0:T(8,128)(2,1)} %copy-done.16, bf16[64,4096]{1,0:T(8,128)(2,1)} %copy.111.refs_5_), custom_call_target="tpu_custom_call" | custom-call | tf_op jit(solution)/shard_map/pallas_call | solution.py:46
  237.8 1.7 convert_bitcast_fusion.1
  240.7 2.1 fusion.23
  242.9 26.9 %all-gather.8.cloned.1.call-done = bf16[256,4096]{1,0:T(8,128)(2,1)} async-done(((bf16[64,4096]{1,0:T(8,128)(2,1)}), bf16[256,4096]{1,0:T(8,128)(2,1)}) %all-gather.8.cloned.1.call-update) | async-done | bytes 2097168 | tf_op jit(solution)/shard_map/all_gather | solution.py:206
  269.8 2.3 fusion.21
  276.3 65.7 %shard_map.122 = f32[27648,64]{1,0:T(8,128)} custom-call(s32[8,4096]{1,0:T(8,128)} %nb_ref.5, f32[4096,64]{1,0:T(8,128)} %convert_element_type.59.rows_ref), custom_call_target="tpu_custom_call" | custom-call | tf_op jit(solution)/shard_map/pallas_call | solution.py:81
  342.0 5.7 %convert.6 = bf16[27648,64]{1,0:T(8,128)(2,1)S(1)} convert(f32[27648,64]{1,0:T(8,128)} %shard_map.122) | non-fusion elementwise | flops 1769472 | bytes 10616832 | tf_op jit(solution)/shard_map/convert.3
  347.6 3.3 slice.82
  352.2 6.1 %copy.118 = bf16[32,640,64]{1,2,0:T(8,128)(2,1)} copy(bf16[32,640,64]{2,1,0:T(8,128)(2,1)} %bitcast.67) | data formatting | bytes 5242880 | tf_op jit(solution)/shard_map/all_to_all | solution.py:291
  358.3 8.0 %all-to-all-start.2 = ((bf16[32,640,64]{1,2,0:T(8,128)(2,1)}), bf16[32,640,64]{1,2,0:T(8,128)(2,1)}, u32[]{:S(2)}, u32[]{:S(2)}) async-start(bf16[32,640,64]{1,2,0:T(8,128)(2,1)} %copy.118), calls=%async_computation.2 | async-start | bytes 5242880 | tf_op jit(solution)/shard_map/all_to_all | solution.py:291
  367.0 2.0 fusion.17
  369.3 3.0 collective-permute-start.11
  372.6 2.1 fusion.6
  374.7 3.9 convolution_add_fusion.1.base_ref
  380.0 25.0 %collective-permute-done.11 = bf16[1024,64]{1,0:T(8,128)(2,1)S(1)} collective-permute-done((bf16[1024,64]{1,0:T(8,128)(2,1)}, bf16[1024,64]{1,0:T(8,128)(2,1)S(1)}, u32[]{:S(2)}, u32[]{:S(2)}) %collective-permute-start.11) | collective-permute-done | bytes 131104 | tf_op jit(solution)/shard_map/ppermute | solution.py:196
  405.0 3.4 collective-permute-done.10
  408.5 2.1 convert_reduce_fusion
  412.2 12.1 %shard_map.123 = f32[4096,64]{1,0:T(8,128)} custom-call(s32[3712]{0:T(1024)} %pad_add_fusion.t_ref, f32[4096,64]{1,0:T(8,128)} %convolution_add_fusion.1.base_ref, f32[3712,64]{1,0:T(8,128)} %pad_maximum_fusion.upd_ref), custom_call_target="tpu_custom_call" | custom-call | tf_op jit(solution)/shard_map/pallas_call | solution.py:127
  424.3 2.3 convolution_bitcast_fusion.1
  427.8 14.7 %all_to_all.34 = f32[32,1,1200]{2,1,0:T(1,128)S(1)} all-to-all(f32[32,1,1200]{2,1,0:T(1,128)S(1)} %all_to_all.26), channel_id=1, replica_groups=mesh['dom'=32,'feat'=4] {'dom'}, dimensions={0} | all-to-all | bytes 307200 | tf_op jit(solution)/shard_map/all_to_all | solution.py:160
  442.8 11.5 %all_to_all.35 = f32[32,1,1200]{2,1,0:T(1,128)S(1)} all-to-all(f32[32,1,1200]{2,1,0:T(1,128)S(1)} %broadcast_in_dim.69), channel_id=1, replica_groups=mesh['dom'=32,'feat'=4] {'dom'}, dimensions={0} | all-to-all | bytes 307200 | tf_op jit(solution)/shard_map/all_to_all | solution.py:162
  (130 shorter events, 31.4 us)
Async XLA Ops:
  7.2 262.6 %copy-start = (bf16[172,256]{1,0:T(8,128)(2,1)S(1)}, bf16[172,256]{1,0:T(8,128)(2,1)}, u32[]{:S(2)}) copy-start(bf16[172,256]{1,0:T(8,128)(2,1)} %param.21) | copy-start | bytes 264196
  7.2 39.2 %collective-permute-start.2 = (bf16[32,4096]{1,0:T(8,128)(2,1)}, bf16[32,4096]{1,0:T(8,128)(2,1)S(1)}, u32[]{:S(2)}, u32[]{:S(2)}) collective-permute-start(bf16[32,4096]{1,0:T(8,128)(2,1)} %param.13), channel_id=1, source_target_pairs={{0,1},{1,2},{2,3},{3,0},{4,5},{5,6},{6,7},{7,4},{8,9},{9,10},{10,1... | collective-permute-start | bytes 786440 | tf_op jit(solution)/shard_map/ppermute | solution.py:98
  9.4 36.9 %collective-permute-start.1 = (bf16[32,4096]{1,0:T(8,128)(2,1)}, bf16[32,4096]{1,0:T(8,128)(2,1)S(1)}, u32[]{:S(2)}, u32[]{:S(2)}) collective-permute-start(bf16[32,4096]{1,0:T(8,128)(2,1)} %param.13), channel_id=1, source_target_pairs={{0,2},{1,3},{2,0},{3,1},{4,6},{5,7},{6,4},{7,5},{8,10},{9,11},{10,... | collective-permute-start | bytes 786440 | tf_op jit(solution)/shard_map/ppermute | solution.py:98
  12.0 30.4 %collective-permute-start = (bf16[32,4096]{1,0:T(8,128)(2,1)}, bf16[32,4096]{1,0:T(8,128)(2,1)}, u32[]{:S(2)}, u32[]{:S(2)}) collective-permute-start(bf16[32,4096]{1,0:T(8,128)(2,1)} %param.13), channel_id=1, source_target_pairs={{0,3},{1,0},{2,1},{3,2},{4,7},{5,4},{6,5},{7,6},{8,11},{9,8},{10,9... | collective-permute-start | bytes 786440 | tf_op jit(solution)/shard_map/ppermute | solution.py:98
  14.5 24.4 %copy-start.4 = (bf16[32,4096]{0,1:T(8,128)(2,1)}, bf16[32,4096]{0,1:T(8,128)(2,1)S(1)}, u32[]{:S(2)}) copy-start(bf16[32,4096]{0,1:T(8,128)(2,1)S(1)} %copy.105) | copy-start | bytes 786436
  19.3 8.2 %copy-start.21 = (s32[640]{0:T(1024)S(1)}, s32[640]{0:T(1024)}, u32[]{:S(2)}) copy-start(s32[640]{0:T(1024)} %param.15) | copy-start | bytes 7684
  20.3 42.5 %collective-permute-start.3 = (bf16[1024,32]{1,0:T(8,128)(2,1)}, bf16[1024,32]{1,0:T(8,128)(2,1)}, u32[]{:S(2)}, u32[]{:S(2)}) collective-permute-start(bf16[1024,32]{1,0:T(8,128)(2,1)} %broadcast_select_fusion.5), channel_id=1, source_target_pairs={{0,4},{4,0},{8,12},{12,8},{16,20},{20,16},{24,28},{28,24},{32,36},... | collective-permute-start | bytes 196616 | tf_op jit(solution)/shard_map/ppermute | solution.py:196
  25.9 36.8 %collective-permute-start.4 = (bf16[1024,32]{1,0:T(8,128)(2,1)}, bf16[1024,32]{1,0:T(8,128)(2,1)}, u32[]{:S(2)}, u32[]{:S(2)}) collective-permute-start(bf16[1024,32]{1,0:T(8,128)(2,1)} %broadcast_select_fusion.4), channel_id=1, source_target_pairs={{0,8},{4,12},{8,0},{12,4},{16,24},{20,28},{24,16},{28,20},{32,40},... | collective-permute-start | bytes 196616 | tf_op jit(solution)/shard_map/ppermute | solution.py:196
  31.1 27.6 %all-to-all-start = ((bf16[32,640,32]{1,2,0:T(8,128)(2,1)}), bf16[32,640,32]{1,2,0:T(8,128)(2,1)S(1)}, u32[]{:S(2)}, u32[]{:S(2)}) async-start(bf16[32,640,32]{1,2,0:T(8,128)(2,1)} %broadcast_in_dim.65), calls=%async_computation | async-start | bytes 2621440 | tf_op jit(solution)/shard_map/all_to_all | solution.py:219
  38.8 92.7 %all-gather.4.cloned.1.call-start = ((), (), s32[]{:S(2)}) async-start(), calls=%async_computation.5 | async-start | bytes 1310720 | tf_op jit(solution)/shard_map/all_gather | solution.py:264
  38.9 7.4 %copy-start.12 = (bf16[32,4096]{1,0:T(8,128)(2,1)S(1)}, bf16[32,4096]{1,0:T(8,128)(2,1)}, u32[]{:S(2)}) copy-start(bf16[32,4096]{1,0:T(8,128)(2,1)} %param.13) | copy-start | bytes 786436
  42.4 20.3 %collective-permute-start.5 = (bf16[1024,32]{1,0:T(8,128)(2,1)S(1)}, bf16[1024,32]{1,0:T(8,128)(2,1)S(1)}, u32[]{:S(2)}, u32[]{:S(2)}) collective-permute-start(bf16[1024,32]{1,0:T(8,128)(2,1)S(1)} %broadcast_select_fusion.3), channel_id=1, source_target_pairs={{0,16},{4,20},{8,24},{12,28},{16,0},{20,4},{24,8},{28,12},{32,48},... | collective-permute-start | bytes 196616 | tf_op jit(solution)/shard_map/ppermute | solution.py:196
  62.7 0.7 copy-start.13
  109.8 2.9 copy-start.9
  109.8 2.9 copy-start.22
  111.6 19.9 %copy-start.23 = (bf16[64,128]{1,0:T(8,128)(2,1)S(1)}, bf16[64,128]{1,0:T(8,128)(2,1)}, u32[]{:S(2)}) copy-start(bf16[64,128]{1,0:T(8,128)(2,1)} %param.19) | copy-start | bytes 49156
  133.3 21.7 %copy-start.2 = (bf16[4096,64]{1,0:T(8,128)(2,1)}, bf16[4096,64]{1,0:T(8,128)(2,1)S(1)}, u32[]{:S(2)}) copy-start(bf16[4096,64]{1,0:T(8,128)(2,1)S(1)} %fusion.2.refs_0_) | copy-start | bytes 1572868
  137.4 43.8 %all-to-all-start.1 = ((bf16[32,640,64]{1,2,0:T(8,128)(2,1)}), bf16[32,640,64]{1,2,0:T(8,128)(2,1)}, u32[]{:S(2)}, u32[]{:S(2)}) async-start(bf16[32,640,64]{1,2,0:T(8,128)(2,1)} %broadcast_in_dim.68), calls=%async_computation.1 | async-start | bytes 5242880 | tf_op jit(solution)/shard_map/all_to_all | solution.py:219
  147.2 93.5 %all-gather.6.cloned.1.call-start = ((), (), s32[]{:S(2)}) async-start(), calls=%async_computation.6 | async-start | bytes 2621440 | tf_op jit(solution)/shard_map/all_gather | solution.py:205
  148.5 121.3 %all-gather.8.cloned.1.call-start = ((), (), s32[]{:S(2)}) async-start(), calls=%async_computation.7 | async-start | bytes 2621440 | tf_op jit(solution)/shard_map/all_gather | solution.py:206
  158.8 28.4 %collective-permute-start.6 = (bf16[1024,64]{1,0:T(8,128)(2,1)S(1)}, bf16[1024,64]{1,0:T(8,128)(2,1)S(1)}, u32[]{:S(2)}, u32[]{:S(2)}) collective-permute-start(bf16[1024,64]{1,0:T(8,128)(2,1)S(1)} %broadcast_select_fusion.2), channel_id=1, source_target_pairs={{0,4},{4,0},{8,12},{12,8},{16,20},{20,16},{24,28},{28,24},{32,36},... | collective-permute-start | bytes 393224 | tf_op jit(solution)/shard_map/ppermute | solution.py:196
  159.2 28.0 %collective-permute-start.7 = (bf16[1024,64]{1,0:T(8,128)(2,1)S(1)}, bf16[1024,64]{1,0:T(8,128)(2,1)S(1)}, u32[]{:S(2)}, u32[]{:S(2)}) collective-permute-start(bf16[1024,64]{1,0:T(8,128)(2,1)S(1)} %broadcast_select_fusion.1), channel_id=1, source_target_pairs={{0,8},{4,12},{8,0},{12,4},{16,24},{20,28},{24,16},{28,20},{32,40},... | collective-permute-start | bytes 393224 | tf_op jit(solution)/shard_map/ppermute | solution.py:196
  160.6 30.1 %collective-permute-start.8 = (bf16[1024,64]{1,0:T(8,128)(2,1)S(1)}, bf16[1024,64]{1,0:T(8,128)(2,1)S(1)}, u32[]{:S(2)}, u32[]{:S(2)}) collective-permute-start(bf16[1024,64]{1,0:T(8,128)(2,1)S(1)} %broadcast_select_fusion), channel_id=1, source_target_pairs={{0,16},{4,20},{8,24},{12,28},{16,0},{20,4},{24,8},{28,12},{32,48},... | collective-permute-start | bytes 393224 | tf_op jit(solution)/shard_map/ppermute | solution.py:196
  187.2 3.6 copy-start.14
  187.2 3.6 copy-start.15
  190.7 0.7 copy-start.16
  237.8 2.9 copy-start.17
  242.9 29.3 %copy-start.24 = (s32[4096]{0:T(1024)S(1)}, s32[4096]{0:T(1024)}, u32[]{:S(2)}) copy-start(s32[4096]{0:T(1024)} %param.17) | copy-start | bytes 49156
  272.8 1.1 copy-start.5
  347.6 4.6 copy-start.7
  358.3 8.0 %copy-start.20 = (s32[3,1024]{1,0:T(4,128)S(1)}, s32[3,1024]{1,0:T(4,128)}, u32[]{:S(2)}) copy-start(s32[3,1024]{1,0:T(4,128)} %param.16) | copy-start | bytes 36868
  358.3 50.1 %all-to-all-start.2 = ((bf16[32,640,64]{1,2,0:T(8,128)(2,1)}), bf16[32,640,64]{1,2,0:T(8,128)(2,1)}, u32[]{:S(2)}, u32[]{:S(2)}) async-start(bf16[32,640,64]{1,2,0:T(8,128)(2,1)} %copy.118), calls=%async_computation.2 | async-start | bytes 5242880 | tf_op jit(solution)/shard_map/all_to_all | solution.py:291
  366.4 6.2 %copy-start.6 = (bf16[172,4096]{1,0:T(8,128)(2,1)S(1)}, bf16[172,4096]{1,0:T(8,128)(2,1)}, u32[]{:S(2)}) copy-start(bf16[172,4096]{1,0:T(8,128)(2,1)} %copy-done.5) | copy-start | bytes 4227076
  369.0 5.7 %copy-start.18 = (bf16[172,256]{1,0:T(8,128)(2,1)S(1)}, bf16[172,256]{1,0:T(8,128)(2,1)}, u32[]{:S(2)}) copy-start(bf16[172,256]{1,0:T(8,128)(2,1)} %param.20) | copy-start | bytes 264196
  369.0 10.9 %collective-permute-start.9 = (bf16[1024,64]{1,0:T(8,128)(2,1)}, bf16[1024,64]{1,0:T(8,128)(2,1)S(1)}, u32[]{:S(2)}, u32[]{:S(2)}) collective-permute-start(bf16[1024,64]{1,0:T(8,128)(2,1)} %get-tuple-element.30), channel_id=1, source_target_pairs={{0,4},{4,0},{8,12},{12,8},{16,20},{20,16},{24,28},{28,24},{32,36},... | collective-permute-start | bytes 393224 | tf_op jit(solution)/shard_map/ppermute | solution.py:196
  369.3 35.7 %collective-permute-start.11 = (bf16[1024,64]{1,0:T(8,128)(2,1)}, bf16[1024,64]{1,0:T(8,128)(2,1)S(1)}, u32[]{:S(2)}, u32[]{:S(2)}) collective-permute-start(bf16[1024,64]{1,0:T(8,128)(2,1)} %get-tuple-element.31), channel_id=1, source_target_pairs={{0,16},{4,20},{8,24},{12,28},{16,0},{20,4},{24,8},{28,12},{32,48},... | collective-permute-start | bytes 393224 | tf_op jit(solution)/shard_map/ppermute | solution.py:196
  372.3 36.2 %collective-permute-start.10 = (bf16[1024,64]{1,0:T(8,128)(2,1)}, bf16[1024,64]{1,0:T(8,128)(2,1)S(1)}, u32[]{:S(2)}, u32[]{:S(2)}) collective-permute-start(bf16[1024,64]{1,0:T(8,128)(2,1)} %get-tuple-element.32), channel_id=1, source_target_pairs={{0,8},{4,12},{8,0},{12,4},{16,24},{20,28},{24,16},{28,20},{32,40},... | collective-permute-start | bytes 393224 | tf_op jit(solution)/shard_map/ppermute | solution.py:196
  374.7 3.9 copy-start.3
  412.1 12.1 %copy-start.10 = (bf16[4,32,4096]{2,1,0:T(8,128)(2,1)S(1)}, bf16[4,32,4096]{2,1,0:T(8,128)(2,1)}, u32[]{:S(2)}) copy-start(bf16[4,32,4096]{2,1,0:T(8,128)(2,1)} %constant_dynamic-slice_fusion) | copy-start | bytes 3145732
  424.3 2.3 copy-start.8
  424.3 2.5 copy-start.11
  426.8 0.8 copy-start.19
  426.8 30.4 %copy-start.1 = (bf16[172,256]{1,0:T(8,128)(2,1)S(1)}, bf16[172,256]{1,0:T(8,128)(2,1)}, u32[]{:S(2)}) copy-start(bf16[172,256]{1,0:T(8,128)(2,1)} %param.21) | copy-start | bytes 264196
Sparse Core Ops, SparseCore 0:
  112.8 18.6 all-gather.3
  149.7 30.6 all-gather.5
  240.8 28.9 all-gather.7

commit v14 on v13

--- a/solution.py
+++ b/solution.py
@@ -89,6 +89,13 @@
         scratch_shapes=[pltpu.VMEM((size, width), jnp.float32) for _ in range(chains - 1)],
         compiler_params=pltpu.CompilerParams(vmem_limit_bytes=63 * 1024 * 1024),
     )(neighbours, rows)
+
+
+def spread_gather(value, axis):
+    count = lax.axis_size(axis)
+    copies = jnp.broadcast_to(value[None], (count,) + value.shape)
+    gathered = lax.all_to_all(copies, axis, 0, 0, tiled=True)
+    return gathered.reshape(count * value.shape[0], value.shape[1])
 
 
 def feat_gather(value, axis):
@@ -261,7 +268,7 @@
     nodes_all = rows * lax.axis_size("dom")
     full_input = feat_gather(features, "feat")
     mean_one = average(source_table(features, hub_rows, send_rows), neighbours, full_input)
-    full_mean = lax.all_gather(mean_one, "feat", axis=0, tiled=True)
+    full_mean = spread_gather(mean_one, "feat")
     pre_act = jnp.dot(inner_self, full_input, preferred_element_type=jnp.float32)
     pre_act = pre_act + jnp.dot(inner_neighbour, full_mean, preferred_element_type=jnp.float32)
     hidden = jnp.maximum(pre_act, 0.0).astype(jnp.bfloat16)
@@ -270,7 +277,8 @@
     offset = lax.axis_index("feat") * width
     self_cols = lax.dynamic_slice_in_dim(outer_self, offset, width, 1)
     neigh_cols = lax.dynamic_slice_in_dim(outer_neighbour, offset, width, 1)
-    full_hidden, full_two = widen(hidden, mean_two)
+    full_hidden = lax.all_gather(hidden, "feat", axis=0, tiled=True)
+    full_two = spread_gather(mean_two, "feat")
     logits = jnp.dot(outer_self, full_hidden, preferred_element_type=jnp.float32)
     logits = logits + jnp.dot(outer_neighbour, full_two, preferred_element_type=jnp.float32)
     logit_grad = class_gradient(logits, labels, nodes_all)

time: 465 us -> 463 us (level)
  waiting for transfers between devices: 106 us -> 96.4 us
    all_gather x3 -> x1, waiting for transfers between devices: 45.2 us -> 0.02 us  [body(): full_hidden = lax.all_gather(hidden, 'feat', axis=0, tiled=True)]
    all_to_all x0 -> x2, waiting for transfers between devices: none -> 36.2 us  [spread_gather(): gathered = lax.all_to_all(copies, axis, 0, 0, tiled=True)]
    all_to_all x0 -> x2, starting transfers between devices: none -> 8.1 us  [spread_gather(): gathered = lax.all_to_all(copies, axis, 0, 0, tiled=True)]
where the time goes in v14:
time: 463 us; the launch traced here: 462 us
  Pallas kernels  171 us (37%)
  waiting for transfers between devices  96.4 us (21%)
  local copies, waits for them, and re-layouts  66.7 us (14%)
  starting transfers between devices  49 us (11%)
  blocking collectives  26.3 us (6%)
  other arithmetic  19.6 us (4%)
  matrix products  18.6 us (4%)
  between operations  14.7 us (3%)
    pallas_call x2, Pallas kernels, gather_mean(): pl.pallas_call(kernel, in_specs=[pl.BlockSpec(memory_space=pltpu.SMEM)] +...  92.8 us
    pallas_call x1, Pallas kernels, scatter_mean(): pl.pallas_call(kernel, in_specs=[pl.BlockSpec(memory_space=pltpu.SMEM), p...  65.7 us
    all_to_all x2, waiting for transfers between devices, spread_gather(): gathered = lax.all_to_all(copies, axis, 0, 0, tiled=True)  36.2 us
    ppermute x9, waiting for transfers between devices, partner(): return lax.ppermute(value, axis, pairs)  31.8 us
    all_to_all x2, waiting for transfers between devices, source_table(): lax.all_to_all(jnp.broadcast_to(hub_local[None], (owners,) + hub_local.sh...  28.4 us
    gather x6, local copies, waits for them, and re-layouts, source_table(): jnp.take(local_rows, send_rows[bit_index], axis=0)  19.2 us
    all_to_all x1, blocking collectives, exchange_sum(): reduced = jnp.sum(lax.all_to_all(padded, axis, 0, 0, tiled=True), axis=0)  14.7 us
    all_to_all x2, starting transfers between devices, source_table(): lax.all_to_all(jnp.broadcast_to(hub_local[None], (owners,) + hub_local.sh...  13.9 us
  transfers between devices with their start and end apart: 18, of which 7 were waited for; matrix products, arithmetic and copies ran while one was open for 13% of the time, Pallas kernels for 10%

profile of v14, /device:TPU:1, one launch (start us, length us, event | category | flops | bytes accessed | tf_op | source)
XLA Modules:
  0.0 461.8 jit_solution(14668741717438056178)
XLA Ops:
  7.2 2.2 collective-permute-start.2
  9.4 2.6 collective-permute-start.1
  16.1 3.2 gather_fusion.2
  21.8 3.2 gather_fusion.3
  27.6 2.0 gather_fusion
  31.1 7.8 %all-to-all-start = ((bf16[32,640,32]{1,2,0:T(8,128)(2,1)}), bf16[32,640,32]{1,2,0:T(8,128)(2,1)S(1)}, u32[]{:S(2)}, u32[]{:S(2)}) async-start(bf16[32,640,32]{1,2,0:T(8,128)(2,1)} %broadcast_in_dim.77), calls=%async_computation | async-start | bytes 2621440 | tf_op jit(solution)/shard_map/all_to_all | solution.py:226
  38.9 3.2 gather_fusion.4
  42.4 2.9 collective-permute-start.5
  48.5 10.2 %all-to-all-done = bf16[32,640,32]{1,2,0:T(8,128)(2,1)S(1)} async-done(((bf16[32,640,32]{1,2,0:T(8,128)(2,1)}), bf16[32,640,32]{1,2,0:T(8,128)(2,1)S(1)}, u32[]{:S(2)}, u32[]{:S(2)}) %all-to-all-start) | async-done | bytes 1310752 | tf_op jit(solution)/shard_map/all_to_all | solution.py:226
  58.7 4.3 copy.111
  63.6 46.4 %shard_map.120 = f32[4096,32]{1,0:T(8,128)} custom-call(s32[8,4096]{1,0:T(8,128)} %nb_ref.5, bf16[4096,32]{1,0:T(8,128)(2,1)} %bitcast.66, bf16[20480,32]{1,0:T(8,128)(2,1)} %bitcast.67, bf16[1024,32]{1,0:T(8,128)(2,1)} %collective-permute-done.3.refs_2_, bf16[1024,32]{1,0:T(8,128)(2,1)} %collective-permute-done.4.refs_3_, bf16[1024,32]{1,0:T(8,128)(2,1)} %copy-done.14, ...), custom_call_target="tpu_custom_call" | custom-call | tf_op jit(solution)/shard_map/pallas_call | solution.py:46
  110.0 1.7 convert_bitcast_fusion
  113.2 3.5 all-to-all-start.1
  116.7 1.8 fusion.22
  118.5 12.8 %all-to-all-done.1 = bf16[4,32,4096]{2,1,0:T(8,128)(2,1)S(1)} async-done(((bf16[4,32,4096]{2,1,0:T(8,128)(2,1)}), bf16[4,32,4096]{2,1,0:T(8,128)(2,1)S(1)}, u32[]{:S(2)}, u32[]{:S(2)}) %all-to-all-start.1) | async-done | bytes 1048608 | tf_op jit(solution)/shard_map/all_to_all | solution.py:97
  131.4 2.5 fusion.2.refs_0_
  133.9 2.0 gather_fusion.1
  136.2 1.8 broadcast_in_dim.81
  138.0 6.1 %all-to-all-start.2 = ((bf16[32,640,64]{1,2,0:T(8,128)(2,1)}), bf16[32,640,64]{1,2,0:T(8,128)(2,1)}, u32[]{:S(2)}, u32[]{:S(2)}) async-start(bf16[32,640,64]{1,2,0:T(8,128)(2,1)} %broadcast_in_dim.81), calls=%async_computation.2 | async-start | bytes 5242880 | tf_op jit(solution)/shard_map/all_to_all | solution.py:226
  145.4 3.2 gather_fusion.7
  148.6 3.2 gather_fusion.6
  151.8 3.2 gather_fusion.5
  157.5 2.4 collective-permute-start.8
  159.9 18.2 %all-to-all-done.2 = bf16[32,640,64]{1,2,0:T(8,128)(2,1)} async-done(((bf16[32,640,64]{1,2,0:T(8,128)(2,1)}), bf16[32,640,64]{1,2,0:T(8,128)(2,1)}, u32[]{:S(2)}, u32[]{:S(2)}) %all-to-all-start.2) | async-done | bytes 2621472 | tf_op jit(solution)/shard_map/all_to_all | solution.py:226
  178.1 6.0 %copy.117 = bf16[32,640,64]{2,1,0:T(8,128)(2,1)} copy(bf16[32,640,64]{1,2,0:T(8,128)(2,1)} %all-to-all-done.2) | data formatting | bytes 5242880 | tf_op jit(solution)/shard_map/all_to_all | solution.py:226
  184.2 3.5 collective-permute-done.8.refs_4_
  188.3 46.4 %shard_map.121 = f32[4096,64]{1,0:T(8,128)} custom-call(s32[8,4096]{1,0:T(8,128)} %nb_ref.5, bf16[4096,64]{1,0:T(8,128)(2,1)} %copy-done.2, bf16[20480,64]{1,0:T(8,128)(2,1)} %bitcast.68, bf16[1024,64]{1,0:T(8,128)(2,1)} %copy-done.15, bf16[1024,64]{1,0:T(8,128)(2,1)} %copy-done.16, bf16[1024,64]{1,0:T(8,128)(2,1)} %copy-done.17, bf16[64,4096]{1,0:T(8,128)(2,1)} %copy.115.refs_5_), custom_call_target="tpu_custom_call" | custom-call | tf_op jit(solution)/shard_map/pallas_call | solution.py:46
  234.7 1.7 convert_bitcast_fusion.1
  238.3 4.6 all-to-all-start.3
  243.0 2.1 fusion.23
  245.1 23.3 %all-to-all-done.3 = bf16[4,64,4096]{2,1,0:T(8,128)(2,1)} async-done(((bf16[4,64,4096]{2,1,0:T(8,128)(2,1)}), bf16[4,64,4096]{2,1,0:T(8,128)(2,1)}, u32[]{:S(2)}, u32[]{:S(2)}) %all-to-all-start.3) | async-done | bytes 2097184 | tf_op jit(solution)/shard_map/all_to_all | solution.py:97
  268.5 2.4 fusion.21
  275.0 65.7 %shard_map.122 = f32[27648,64]{1,0:T(8,128)} custom-call(s32[8,4096]{1,0:T(8,128)} %nb_ref.5, f32[4096,64]{1,0:T(8,128)} %convert_element_type.59.rows_ref), custom_call_target="tpu_custom_call" | custom-call | tf_op jit(solution)/shard_map/pallas_call | solution.py:81
  340.6 5.7 %convert.6 = bf16[27648,64]{1,0:T(8,128)(2,1)S(1)} convert(f32[27648,64]{1,0:T(8,128)} %shard_map.122) | non-fusion elementwise | flops 1769472 | bytes 10616832 | tf_op jit(solution)/shard_map/convert.3
  346.3 3.4 slice.82
  350.8 6.1 %copy.122 = bf16[32,640,64]{1,2,0:T(8,128)(2,1)} copy(bf16[32,640,64]{2,1,0:T(8,128)(2,1)} %bitcast.69) | data formatting | bytes 5242880 | tf_op jit(solution)/shard_map/all_to_all | solution.py:299
  357.0 7.2 %all-to-all-start.4 = ((bf16[32,640,64]{1,2,0:T(8,128)(2,1)}), bf16[32,640,64]{1,2,0:T(8,128)(2,1)}, u32[]{:S(2)}, u32[]{:S(2)}) async-start(bf16[32,640,64]{1,2,0:T(8,128)(2,1)} %copy.122), calls=%async_computation.4 | async-start | bytes 5242880 | tf_op jit(solution)/shard_map/all_to_all | solution.py:299
  364.8 2.0 fusion.17
  367.1 3.0 collective-permute-start.11
  370.4 2.2 fusion.6
  372.6 3.9 convolution_add_fusion.1.base_ref
  377.8 25.0 %collective-permute-done.11 = bf16[1024,64]{1,0:T(8,128)(2,1)S(1)} collective-permute-done((bf16[1024,64]{1,0:T(8,128)(2,1)}, bf16[1024,64]{1,0:T(8,128)(2,1)S(1)}, u32[]{:S(2)}, u32[]{:S(2)}) %collective-permute-start.11) | collective-permute-done | bytes 131104 | tf_op jit(solution)/shard_map/ppermute | solution.py:203
  402.8 3.4 collective-permute-done.10
  406.3 2.1 convert_reduce_fusion
  410.0 12.1 %shard_map.123 = f32[4096,64]{1,0:T(8,128)} custom-call(s32[3712]{0:T(1024)} %pad_add_fusion.t_ref, f32[4096,64]{1,0:T(8,128)} %convolution_add_fusion.1.base_ref, f32[3712,64]{1,0:T(8,128)} %pad_maximum_fusion.upd_ref), custom_call_target="tpu_custom_call" | custom-call | tf_op jit(solution)/shard_map/pallas_call | solution.py:134
  422.1 2.3 convolution_bitcast_fusion
  425.6 14.7 %all_to_all.44 = f32[32,1,1200]{2,1,0:T(1,128)S(1)} all-to-all(f32[32,1,1200]{2,1,0:T(1,128)S(1)} %all_to_all.34), channel_id=1, replica_groups=mesh['dom'=32,'feat'=4] {'dom'}, dimensions={0} | all-to-all | bytes 307200 | tf_op jit(solution)/shard_map/all_to_all | solution.py:167
  440.6 11.5 %all_to_all.45 = f32[32,1,1200]{2,1,0:T(1,128)S(1)} all-to-all(f32[32,1,1200]{2,1,0:T(1,128)S(1)} %broadcast_in_dim.83), channel_id=1, replica_groups=mesh['dom'=32,'feat'=4] {'dom'}, dimensions={0} | all-to-all | bytes 307200 | tf_op jit(solution)/shard_map/all_to_all | solution.py:169
  (132 shorter events, 36.5 us)
Async XLA Ops:
  7.2 261.3 %copy-start = (bf16[172,256]{1,0:T(8,128)(2,1)S(1)}, bf16[172,256]{1,0:T(8,128)(2,1)}, u32[]{:S(2)}) copy-start(bf16[172,256]{1,0:T(8,128)(2,1)} %param.21) | copy-start | bytes 264196
  7.2 39.1 %collective-permute-start.2 = (bf16[32,4096]{1,0:T(8,128)(2,1)}, bf16[32,4096]{1,0:T(8,128)(2,1)S(1)}, u32[]{:S(2)}, u32[]{:S(2)}) collective-permute-start(bf16[32,4096]{1,0:T(8,128)(2,1)} %param.13), channel_id=1, source_target_pairs={{0,1},{1,2},{2,3},{3,0},{4,5},{5,6},{6,7},{7,4},{8,9},{9,10},{10,1... | collective-permute-start | bytes 786440 | tf_op jit(solution)/shard_map/ppermute | solution.py:105
  9.4 36.9 %collective-permute-start.1 = (bf16[32,4096]{1,0:T(8,128)(2,1)}, bf16[32,4096]{1,0:T(8,128)(2,1)S(1)}, u32[]{:S(2)}, u32[]{:S(2)}) collective-permute-start(bf16[32,4096]{1,0:T(8,128)(2,1)} %param.13), channel_id=1, source_target_pairs={{0,2},{1,3},{2,0},{3,1},{4,6},{5,7},{6,4},{7,5},{8,10},{9,11},{10,... | collective-permute-start | bytes 786440 | tf_op jit(solution)/shard_map/ppermute | solution.py:105
  12.0 30.4 %collective-permute-start = (bf16[32,4096]{1,0:T(8,128)(2,1)}, bf16[32,4096]{1,0:T(8,128)(2,1)}, u32[]{:S(2)}, u32[]{:S(2)}) collective-permute-start(bf16[32,4096]{1,0:T(8,128)(2,1)} %param.13), channel_id=1, source_target_pairs={{0,3},{1,0},{2,1},{3,2},{4,7},{5,4},{6,5},{7,6},{8,11},{9,8},{10,9... | collective-permute-start | bytes 786440 | tf_op jit(solution)/shard_map/ppermute | solution.py:105
  14.5 24.4 %copy-start.4 = (bf16[32,4096]{0,1:T(8,128)(2,1)}, bf16[32,4096]{0,1:T(8,128)(2,1)S(1)}, u32[]{:S(2)}) copy-start(bf16[32,4096]{0,1:T(8,128)(2,1)S(1)} %copy.109) | copy-start | bytes 786436
  19.3 8.2 %copy-start.22 = (s32[640]{0:T(1024)S(1)}, s32[640]{0:T(1024)}, u32[]{:S(2)}) copy-start(s32[640]{0:T(1024)} %param.15) | copy-start | bytes 7684
  20.3 42.7 %collective-permute-start.3 = (bf16[1024,32]{1,0:T(8,128)(2,1)}, bf16[1024,32]{1,0:T(8,128)(2,1)}, u32[]{:S(2)}, u32[]{:S(2)}) collective-permute-start(bf16[1024,32]{1,0:T(8,128)(2,1)} %broadcast_select_fusion.5), channel_id=1, source_target_pairs={{0,4},{4,0},{8,12},{12,8},{16,20},{20,16},{24,28},{28,24},{32,36},... | collective-permute-start | bytes 196616 | tf_op jit(solution)/shard_map/ppermute | solution.py:203
  25.9 37.0 %collective-permute-start.4 = (bf16[1024,32]{1,0:T(8,128)(2,1)}, bf16[1024,32]{1,0:T(8,128)(2,1)}, u32[]{:S(2)}, u32[]{:S(2)}) collective-permute-start(bf16[1024,32]{1,0:T(8,128)(2,1)} %broadcast_select_fusion.4), channel_id=1, source_target_pairs={{0,8},{4,12},{8,0},{12,4},{16,24},{20,28},{24,16},{28,20},{32,40},... | collective-permute-start | bytes 196616 | tf_op jit(solution)/shard_map/ppermute | solution.py:203
  31.1 27.6 %all-to-all-start = ((bf16[32,640,32]{1,2,0:T(8,128)(2,1)}), bf16[32,640,32]{1,2,0:T(8,128)(2,1)S(1)}, u32[]{:S(2)}, u32[]{:S(2)}) async-start(bf16[32,640,32]{1,2,0:T(8,128)(2,1)} %broadcast_in_dim.77), calls=%async_computation | async-start | bytes 2621440 | tf_op jit(solution)/shard_map/all_to_all | solution.py:226
  38.9 7.4 %copy-start.13 = (bf16[32,4096]{1,0:T(8,128)(2,1)S(1)}, bf16[32,4096]{1,0:T(8,128)(2,1)}, u32[]{:S(2)}) copy-start(bf16[32,4096]{1,0:T(8,128)(2,1)} %param.13) | copy-start | bytes 786436
  42.4 20.6 %collective-permute-start.5 = (bf16[1024,32]{1,0:T(8,128)(2,1)S(1)}, bf16[1024,32]{1,0:T(8,128)(2,1)S(1)}, u32[]{:S(2)}, u32[]{:S(2)}) collective-permute-start(bf16[1024,32]{1,0:T(8,128)(2,1)S(1)} %broadcast_select_fusion.3), channel_id=1, source_target_pairs={{0,16},{4,20},{8,24},{12,28},{16,0},{20,4},{24,8},{28,12},{32,48},... | collective-permute-start | bytes 196616 | tf_op jit(solution)/shard_map/ppermute | solution.py:203
  62.9 0.7 copy-start.14
  111.7 5.0 %copy-start.9 = (bf16[4,32,4096]{2,1,0:T(8,128)(2,1)S(1)}, bf16[4,32,4096]{2,1,0:T(8,128)(2,1)}, u32[]{:S(2)}) copy-start(bf16[4,32,4096]{2,1,0:T(8,128)(2,1)} %constant_dynamic-slice_fusion) | copy-start | bytes 3145732
  111.7 5.0 %copy-start.23 = (bf16[64,128]{1,0:T(8,128)(2,1)S(1)}, bf16[64,128]{1,0:T(8,128)(2,1)}, u32[]{:S(2)}) copy-start(bf16[64,128]{1,0:T(8,128)(2,1)} %param.18) | copy-start | bytes 49156
  113.2 18.2 %all-to-all-start.1 = ((bf16[4,32,4096]{2,1,0:T(8,128)(2,1)}), bf16[4,32,4096]{2,1,0:T(8,128)(2,1)S(1)}, u32[]{:S(2)}, u32[]{:S(2)}) async-start(bf16[4,32,4096]{2,1,0:T(8,128)(2,1)} %broadcast_in_dim.78), calls=%async_computation.1 | async-start | bytes 2097152 | tf_op jit(solution)/shard_map/all_to_all | solution.py:97
  116.7 14.7 %copy-start.24 = (bf16[64,128]{1,0:T(8,128)(2,1)S(1)}, bf16[64,128]{1,0:T(8,128)(2,1)}, u32[]{:S(2)}) copy-start(bf16[64,128]{1,0:T(8,128)(2,1)} %param.19) | copy-start | bytes 49156
  131.4 2.5 copy-start.11
  133.9 18.0 %copy-start.2 = (bf16[4096,64]{1,0:T(8,128)(2,1)}, bf16[4096,64]{1,0:T(8,128)(2,1)S(1)}, u32[]{:S(2)}) copy-start(bf16[4096,64]{1,0:T(8,128)(2,1)S(1)} %fusion.2.refs_0_) | copy-start | bytes 1572868
  138.0 40.1 %all-to-all-start.2 = ((bf16[32,640,64]{1,2,0:T(8,128)(2,1)}), bf16[32,640,64]{1,2,0:T(8,128)(2,1)}, u32[]{:S(2)}, u32[]{:S(2)}) async-start(bf16[32,640,64]{1,2,0:T(8,128)(2,1)} %broadcast_in_dim.81), calls=%async_computation.2 | async-start | bytes 5242880 | tf_op jit(solution)/shard_map/all_to_all | solution.py:226
  144.1 98.8 %all-gather.2.cloned.1.call-start = ((), (), s32[]{:S(2)}) async-start(), calls=%async_computation.7 | async-start | bytes 2621440 | tf_op jit(solution)/shard_map/all_gather | solution.py:280
  155.7 28.5 %collective-permute-start.6 = (bf16[1024,64]{1,0:T(8,128)(2,1)S(1)}, bf16[1024,64]{1,0:T(8,128)(2,1)S(1)}, u32[]{:S(2)}, u32[]{:S(2)}) collective-permute-start(bf16[1024,64]{1,0:T(8,128)(2,1)S(1)} %broadcast_select_fusion.2), channel_id=1, source_target_pairs={{0,4},{4,0},{8,12},{12,8},{16,20},{20,16},{24,28},{28,24},{32,36},... | collective-permute-start | bytes 393224 | tf_op jit(solution)/shard_map/ppermute | solution.py:203
  156.1 28.1 %collective-permute-start.7 = (bf16[1024,64]{1,0:T(8,128)(2,1)S(1)}, bf16[1024,64]{1,0:T(8,128)(2,1)S(1)}, u32[]{:S(2)}, u32[]{:S(2)}) collective-permute-start(bf16[1024,64]{1,0:T(8,128)(2,1)S(1)} %broadcast_select_fusion.1), channel_id=1, source_target_pairs={{0,8},{4,12},{8,0},{12,4},{16,24},{20,28},{24,16},{28,20},{32,40},... | collective-permute-start | bytes 393224 | tf_op jit(solution)/shard_map/ppermute | solution.py:203
  157.5 30.1 %collective-permute-start.8 = (bf16[1024,64]{1,0:T(8,128)(2,1)S(1)}, bf16[1024,64]{1,0:T(8,128)(2,1)S(1)}, u32[]{:S(2)}, u32[]{:S(2)}) collective-permute-start(bf16[1024,64]{1,0:T(8,128)(2,1)S(1)} %broadcast_select_fusion), channel_id=1, source_target_pairs={{0,16},{4,20},{8,24},{12,28},{16,0},{20,4},{24,8},{28,12},{32,48},... | collective-permute-start | bytes 393224 | tf_op jit(solution)/shard_map/ppermute | solution.py:203
  184.1 3.5 copy-start.15
  184.1 3.5 copy-start.16
  187.6 0.7 copy-start.17
  238.3 4.6 %copy-start.18 = (bf16[172,256]{1,0:T(8,128)(2,1)S(1)}, bf16[172,256]{1,0:T(8,128)(2,1)}, u32[]{:S(2)}) copy-start(bf16[172,256]{1,0:T(8,128)(2,1)} %param.20) | copy-start | bytes 264196
  238.3 30.1 %all-to-all-start.3 = ((bf16[4,64,4096]{2,1,0:T(8,128)(2,1)}), bf16[4,64,4096]{2,1,0:T(8,128)(2,1)}, u32[]{:S(2)}, u32[]{:S(2)}) async-start(bf16[4,64,4096]{2,1,0:T(8,128)(2,1)} %broadcast_in_dim.82), calls=%async_computation.3 | async-start | bytes 4194304 | tf_op jit(solution)/shard_map/all_to_all | solution.py:97
  268.5 2.4 copy-start.25
  271.4 1.1 copy-start.5
  346.3 4.5 copy-start.7
  356.9 7.2 %copy-start.21 = (s32[3,1024]{1,0:T(4,128)S(1)}, s32[3,1024]{1,0:T(4,128)}, u32[]{:S(2)}) copy-start(s32[3,1024]{1,0:T(4,128)} %param.16) | copy-start | bytes 36868
  357.0 49.3 %all-to-all-start.4 = ((bf16[32,640,64]{1,2,0:T(8,128)(2,1)}), bf16[32,640,64]{1,2,0:T(8,128)(2,1)}, u32[]{:S(2)}, u32[]{:S(2)}) async-start(bf16[32,640,64]{1,2,0:T(8,128)(2,1)} %copy.122), calls=%async_computation.4 | async-start | bytes 5242880 | tf_op jit(solution)/shard_map/all_to_all | solution.py:299
  364.2 6.2 %copy-start.6 = (bf16[172,4096]{1,0:T(8,128)(2,1)S(1)}, bf16[172,4096]{1,0:T(8,128)(2,1)}, u32[]{:S(2)}) copy-start(bf16[172,4096]{1,0:T(8,128)(2,1)} %copy-done.5) | copy-start | bytes 4227076
  366.8 5.7 %copy-start.19 = (bf16[172,256]{1,0:T(8,128)(2,1)S(1)}, bf16[172,256]{1,0:T(8,128)(2,1)}, u32[]{:S(2)}) copy-start(bf16[172,256]{1,0:T(8,128)(2,1)} %param.20) | copy-start | bytes 264196
  366.8 10.9 %collective-permute-start.9 = (bf16[1024,64]{1,0:T(8,128)(2,1)}, bf16[1024,64]{1,0:T(8,128)(2,1)S(1)}, u32[]{:S(2)}, u32[]{:S(2)}) collective-permute-start(bf16[1024,64]{1,0:T(8,128)(2,1)} %get-tuple-element.30), channel_id=1, source_target_pairs={{0,4},{4,0},{8,12},{12,8},{16,20},{20,16},{24,28},{28,24},{32,36},... | collective-permute-start | bytes 393224 | tf_op jit(solution)/shard_map/ppermute | solution.py:203
  367.1 35.6 %collective-permute-start.11 = (bf16[1024,64]{1,0:T(8,128)(2,1)}, bf16[1024,64]{1,0:T(8,128)(2,1)S(1)}, u32[]{:S(2)}, u32[]{:S(2)}) collective-permute-start(bf16[1024,64]{1,0:T(8,128)(2,1)} %get-tuple-element.31), channel_id=1, source_target_pairs={{0,16},{4,20},{8,24},{12,28},{16,0},{20,4},{24,8},{28,12},{32,48},... | collective-permute-start | bytes 393224 | tf_op jit(solution)/shard_map/ppermute | solution.py:203
  370.1 36.1 %collective-permute-start.10 = (bf16[1024,64]{1,0:T(8,128)(2,1)}, bf16[1024,64]{1,0:T(8,128)(2,1)S(1)}, u32[]{:S(2)}, u32[]{:S(2)}) collective-permute-start(bf16[1024,64]{1,0:T(8,128)(2,1)} %get-tuple-element.32), channel_id=1, source_target_pairs={{0,8},{4,12},{8,0},{12,4},{16,24},{20,28},{24,16},{28,20},{32,40},... | collective-permute-start | bytes 393224 | tf_op jit(solution)/shard_map/ppermute | solution.py:203
  372.6 3.9 copy-start.3
  409.9 12.1 %copy-start.12 = (bf16[4,32,4096]{2,1,0:T(8,128)(2,1)S(1)}, bf16[4,32,4096]{2,1,0:T(8,128)(2,1)}, u32[]{:S(2)}) copy-start(bf16[4,32,4096]{2,1,0:T(8,128)(2,1)} %copy-done.11) | copy-start | bytes 3145732
  422.1 2.3 copy-start.8
  422.1 2.5 copy-start.10
  424.6 0.8 copy-start.20
  424.6 30.4 %copy-start.1 = (bf16[172,256]{1,0:T(8,128)(2,1)S(1)}, bf16[172,256]{1,0:T(8,128)(2,1)}, u32[]{:S(2)}) copy-start(bf16[172,256]{1,0:T(8,128)(2,1)} %param.21) | copy-start | bytes 264196
Sparse Core Ops, SparseCore 0:
  146.6 29.7 all-gather.1

commit v15 on v14

--- a/solution.py
+++ b/solution.py
@@ -221,13 +221,16 @@
 
 def source_table(local, hub_rows, send_rows):
     local_rows = local.T
-    hub_local = jnp.take(local_rows, hub_rows, axis=0)
+    hub_count = hub_rows.shape[0]
+    band = send_rows.shape[1]
+    picked = jnp.take(local_rows, jnp.concatenate([hub_rows, send_rows.reshape(-1)]), axis=0)
+    hub_local = picked[:hub_count]
     owners = lax.axis_size("dom")
     hub_all = lax.all_to_all(
         jnp.broadcast_to(hub_local[None], (owners,) + hub_local.shape), "dom", 0, 0, tiled=True
     ).reshape(owners * hub_local.shape[0], hub_local.shape[1])
     received = [
-        trade(jnp.take(local_rows, send_rows[bit_index], axis=0), bit_index)
+        trade(picked[hub_count + bit_index * band : hub_count + (bit_index + 1) * band], bit_index)
         for bit_index in range(send_rows.shape[0])
     ]
     return [local_rows, hub_all] + received

time: 463 us -> 473 us (1.022)
  waiting for transfers between devices: 96.4 us -> 115 us
  local copies, waits for them, and re-layouts: 66.7 us -> 60.3 us
    all_to_all x2, waiting for transfers between devices: 28.4 us -> 46.7 us  [source_table(): lax.all_to_all(jnp.broadcast_to(hub_local[None], (owners,) + hub_local.sh...]
    gather x8 -> x2, local copies, waits for them, and re-layouts: 23.2 us -> 15.3 us  [source_table(): jnp.take(local_rows, jnp.concatenate([hub_rows, send_rows.reshape(-1)]),...]
    unnamed x62 -> x69, local copies, waits for them, and re-layouts: 9.16 us -> 9.66 us
  transfers between devices with their start and end apart: 18 -> 18, of which waited for: 7 -> 7; matrix products, arithmetic and copies ran while one was open for 13% -> 9% of each run, Pallas kernels for 10% -> 10%
where the time goes in v15:
time: 473 us; the launch traced here: 471 us
  Pallas kernels  171 us (36%)
  waiting for transfers between devices  115 us (24%)
  local copies, waits for them, and re-layouts  60.3 us (13%)
  starting transfers between devices  47.9 us (10%)
  blocking collectives  26.3 us (6%)
  other arithmetic  19.2 us (4%)
  matrix products  17 us (4%)
  between operations  14.7 us (3%)
    pallas_call x2, Pallas kernels, gather_mean(): pl.pallas_call(kernel, in_specs=[pl.BlockSpec(memory_space=pltpu.SMEM)] +...  92.8 us
    pallas_call x1, Pallas kernels, scatter_mean(): pl.pallas_call(kernel, in_specs=[pl.BlockSpec(memory_space=pltpu.SMEM), p...  65.7 us
    all_to_all x2, waiting for transfers between devices, source_table(): lax.all_to_all(jnp.broadcast_to(hub_local[None], (owners,) + hub_local.sh...  46.7 us
    all_to_all x2, waiting for transfers between devices, spread_gather(): gathered = lax.all_to_all(copies, axis, 0, 0, tiled=True)  36.2 us
    ppermute x9, waiting for transfers between devices, partner(): return lax.ppermute(value, axis, pairs)  32.5 us
    gather x2, local copies, waits for them, and re-layouts, source_table(): jnp.take(local_rows, jnp.concatenate([hub_rows, send_rows.reshape(-1)]),...  15.3 us
    all_to_all x1, blocking collectives, exchange_sum(): reduced = jnp.sum(lax.all_to_all(padded, axis, 0, 0, tiled=True), axis=0)  14.7 us
    all_to_all x2, starting transfers between devices, source_table(): lax.all_to_all(jnp.broadcast_to(hub_local[None], (owners,) + hub_local.sh...  12.7 us
  transfers between devices with their start and end apart: 18, of which 7 were waited for; matrix products, arithmetic and copies ran while one was open for 9% of the time, Pallas kernels for 10%

profile of v15, /device:TPU:1, one launch (start us, length us, event | category | flops | bytes accessed | tf_op | source)
XLA Modules:
  0.0 471.4 jit_solution(10604566670567287907)
XLA Ops:
  7.2 2.2 collective-permute-start.2
  9.4 2.6 collective-permute-start.1
  13.1 1.5 copy.109
  17.5 7.7 %gather_fusion = bf16[3712,32]{1,0:T(8,128)(2,1)S(1)} fusion(bf16[4096,32]{1,0:T(8,128)(2,1)S(1)} %bitcast.63, s32[4096]{0:T(1024)S(1)} %pad_clamp_fusion), kind=kCustom, calls=%fused_computation | custom fusion | bytes 489984 | tf_op jit(solution)/shard_map/jit(_take)/gather | solution.py:226
  25.2 2.0 broadcast_select_fusion.1
  28.1 3.6 collective-permute-start.5
  32.6 1.2 broadcast_in_dim.34
  33.8 7.3 %all-to-all-start = ((bf16[32,640,32]{1,2,0:T(8,128)(2,1)}), bf16[32,640,32]{1,2,0:T(8,128)(2,1)S(1)}, u32[]{:S(2)}, u32[]{:S(2)}) async-start(bf16[32,640,32]{1,2,0:T(8,128)(2,1)} %broadcast_in_dim.34), calls=%async_computation | async-start | bytes 2621440 | tf_op jit(solution)/shard_map/all_to_all | solution.py:229
  42.7 18.1 %all-to-all-done = bf16[32,640,32]{1,2,0:T(8,128)(2,1)S(1)} async-done(((bf16[32,640,32]{1,2,0:T(8,128)(2,1)}), bf16[32,640,32]{1,2,0:T(8,128)(2,1)S(1)}, u32[]{:S(2)}, u32[]{:S(2)}) %all-to-all-start) | async-done | bytes 1310752 | tf_op jit(solution)/shard_map/all_to_all | solution.py:229
  60.9 4.3 copy.111
  66.0 46.4 %shard_map.120 = f32[4096,32]{1,0:T(8,128)} custom-call(s32[8,4096]{1,0:T(8,128)} %nb_ref.5, bf16[4096,32]{1,0:T(8,128)(2,1)} %bitcast.64, bf16[20480,32]{1,0:T(8,128)(2,1)} %bitcast.65, bf16[1024,32]{1,0:T(8,128)(2,1)} %copy-done.17, bf16[1024,32]{1,0:T(8,128)(2,1)} %copy-done.16, bf16[1024,32]{1,0:T(8,128)(2,1)} %copy-done.15, bf16[128,4096]{1,0:T(8,128)(2,1)} %bitcast.68), custom_call_target="tpu_custom_call" | custom-call | tf_op jit(solution)/shard_map/pallas_call | solution.py:46
  112.5 1.7 convert_bitcast_fusion
  115.6 3.5 all-to-all-start.1
  119.2 1.8 fusion.21
  121.0 13.1 %all-to-all-done.1 = bf16[4,32,4096]{2,1,0:T(8,128)(2,1)S(1)} async-done(((bf16[4,32,4096]{2,1,0:T(8,128)(2,1)}), bf16[4,32,4096]{2,1,0:T(8,128)(2,1)S(1)}, u32[]{:S(2)}, u32[]{:S(2)}) %all-to-all-start.1) | async-done | bytes 1048608 | tf_op jit(solution)/shard_map/all_to_all | solution.py:97
  134.1 2.5 fusion.2.refs_0_
  136.6 7.7 %gather_fusion.1 = bf16[3712,64]{1,0:T(8,128)(2,1)S(1)} fusion(bf16[4096,64]{1,0:T(8,128)(2,1)S(1)} %fusion.2.refs_0_, s32[4096]{0:T(1024)S(1)} %pad_clamp_fusion), kind=kCustom, calls=%fused_computation.1 | custom fusion | bytes 965120 | tf_op jit(solution)/shard_map/jit(_take)/gather | solution.py:226
  144.3 2.0 broadcast_select_fusion
  146.4 1.8 broadcast_in_dim.60
  148.2 5.5 %all-to-all-start.2 = ((bf16[32,640,64]{1,2,0:T(8,128)(2,1)}), bf16[32,640,64]{1,2,0:T(8,128)(2,1)}, u32[]{:S(2)}, u32[]{:S(2)}) async-start(bf16[32,640,64]{1,2,0:T(8,128)(2,1)} %broadcast_in_dim.60), calls=%async_computation.2 | async-start | bytes 5242880 | tf_op jit(solution)/shard_map/all_to_all | solution.py:229
  155.0 3.0 collective-permute-start.8
  159.2 28.5 %all-to-all-done.2 = bf16[32,640,64]{1,2,0:T(8,128)(2,1)} async-done(((bf16[32,640,64]{1,2,0:T(8,128)(2,1)}), bf16[32,640,64]{1,2,0:T(8,128)(2,1)}, u32[]{:S(2)}, u32[]{:S(2)}) %all-to-all-start.2) | async-done | bytes 2621472 | tf_op jit(solution)/shard_map/all_to_all | solution.py:229
  187.8 6.0 %copy.117 = bf16[32,640,64]{2,1,0:T(8,128)(2,1)} copy(bf16[32,640,64]{1,2,0:T(8,128)(2,1)} %all-to-all-done.2) | data formatting | bytes 5242880 | tf_op jit(solution)/shard_map/all_to_all | solution.py:229
  193.8 1.9 collective-permute-done.7.refs_3_
  196.5 46.4 %shard_map.121 = f32[4096,64]{1,0:T(8,128)} custom-call(s32[8,4096]{1,0:T(8,128)} %nb_ref.5, bf16[4096,64]{1,0:T(8,128)(2,1)} %copy-done.2, bf16[20480,64]{1,0:T(8,128)(2,1)} %bitcast.66, bf16[1024,64]{1,0:T(8,128)(2,1)} %copy-done.20, bf16[1024,64]{1,0:T(8,128)(2,1)} %copy-done.19, bf16[1024,64]{1,0:T(8,128)(2,1)} %copy-done.18, bf16[64,4096]{1,0:T(8,128)(2,1)} %copy.115.refs_5_), custom_call_target="tpu_custom_call" | custom-call | tf_op jit(solution)/shard_map/pallas_call | solution.py:46
  242.9 1.7 convert_bitcast_fusion.1
  245.0 1.6 broadcast_in_dim.61
  246.5 4.8 %all-to-all-start.3 = ((bf16[4,64,4096]{2,1,0:T(8,128)(2,1)}), bf16[4,64,4096]{2,1,0:T(8,128)(2,1)}, u32[]{:S(2)}, u32[]{:S(2)}) async-start(bf16[4,64,4096]{2,1,0:T(8,128)(2,1)} %broadcast_in_dim.61), calls=%async_computation.3 | async-start | bytes 4194304 | tf_op jit(solution)/shard_map/all_to_all | solution.py:97
  251.3 2.1 fusion.22
  253.5 23.2 %all-to-all-done.3 = bf16[4,64,4096]{2,1,0:T(8,128)(2,1)} async-done(((bf16[4,64,4096]{2,1,0:T(8,128)(2,1)}), bf16[4,64,4096]{2,1,0:T(8,128)(2,1)}, u32[]{:S(2)}, u32[]{:S(2)}) %all-to-all-start.3) | async-done | bytes 2097184 | tf_op jit(solution)/shard_map/all_to_all | solution.py:97
  276.6 2.4 fusion.20
  281.7 1.4 convert_element_type.59.rows_ref
  283.1 65.7 %shard_map.122 = f32[27648,64]{1,0:T(8,128)} custom-call(s32[8,4096]{1,0:T(8,128)} %nb_ref.5, f32[4096,64]{1,0:T(8,128)} %convert_element_type.59.rows_ref), custom_call_target="tpu_custom_call" | custom-call | tf_op jit(solution)/shard_map/pallas_call | solution.py:81
  348.8 5.7 %convert.6 = bf16[27648,64]{1,0:T(8,128)(2,1)S(1)} convert(f32[27648,64]{1,0:T(8,128)} %shard_map.122) | non-fusion elementwise | flops 1769472 | bytes 10616832 | tf_op jit(solution)/shard_map/convert.3
  354.5 3.4 slice.95
  359.0 6.2 %copy.122 = bf16[32,640,64]{1,2,0:T(8,128)(2,1)} copy(bf16[32,640,64]{2,1,0:T(8,128)(2,1)} %bitcast.67) | data formatting | bytes 5242880 | tf_op jit(solution)/shard_map/all_to_all | solution.py:302
  365.2 8.5 %all-to-all-start.4 = ((bf16[32,640,64]{1,2,0:T(8,128)(2,1)}), bf16[32,640,64]{1,2,0:T(8,128)(2,1)}, u32[]{:S(2)}, u32[]{:S(2)}) async-start(bf16[32,640,64]{1,2,0:T(8,128)(2,1)} %copy.122), calls=%async_computation.4 | async-start | bytes 5242880 | tf_op jit(solution)/shard_map/all_to_all | solution.py:302
  373.7 2.1 fusion.15
  376.1 3.0 collective-permute-start.11
  379.9 3.9 convolution_add_fusion.1.base_ref
  385.2 27.2 %collective-permute-done.11 = bf16[1024,64]{1,0:T(8,128)(2,1)S(1)} collective-permute-done((bf16[1024,64]{1,0:T(8,128)(2,1)}, bf16[1024,64]{1,0:T(8,128)(2,1)S(1)}, u32[]{:S(2)}, u32[]{:S(2)}) %collective-permute-start.11) | collective-permute-done | bytes 131104 | tf_op jit(solution)/shard_map/ppermute | solution.py:203
  412.4 3.4 collective-permute-done.10
  415.8 2.1 convert_reduce_fusion
  418.1 1.4 pad_maximum_fusion.upd_ref
  419.5 12.1 %shard_map.123 = f32[4096,64]{1,0:T(8,128)} custom-call(s32[3712]{0:T(1024)} %copy-done.24, f32[4096,64]{1,0:T(8,128)} %convolution_add_fusion.1.base_ref, f32[3712,64]{1,0:T(8,128)} %pad_maximum_fusion.upd_ref), custom_call_target="tpu_custom_call" | custom-call | tf_op jit(solution)/shard_map/pallas_call | solution.py:134
  431.7 2.3 convolution_bitcast_fusion
  435.2 14.7 %all_to_all.44 = f32[32,1,1200]{2,1,0:T(1,128)S(1)} all-to-all(f32[32,1,1200]{2,1,0:T(1,128)S(1)} %all_to_all.34), channel_id=1, replica_groups=mesh['dom'=32,'feat'=4] {'dom'}, dimensions={0} | all-to-all | bytes 307200 | tf_op jit(solution)/shard_map/all_to_all | solution.py:167
  450.1 11.5 %all_to_all.45 = f32[32,1,1200]{2,1,0:T(1,128)S(1)} all-to-all(f32[32,1,1200]{2,1,0:T(1,128)S(1)} %broadcast_in_dim.62), channel_id=1, replica_groups=mesh['dom'=32,'feat'=4] {'dom'}, dimensions={0} | all-to-all | bytes 307200 | tf_op jit(solution)/shard_map/all_to_all | solution.py:169
  (128 shorter events, 24.4 us)
Async XLA Ops:
  7.2 269.5 %copy-start = (bf16[172,256]{1,0:T(8,128)(2,1)S(1)}, bf16[172,256]{1,0:T(8,128)(2,1)}, u32[]{:S(2)}) copy-start(bf16[172,256]{1,0:T(8,128)(2,1)} %param.17) | copy-start | bytes 264196
  7.2 34.3 %collective-permute-start.2 = (bf16[32,4096]{1,0:T(8,128)(2,1)}, bf16[32,4096]{1,0:T(8,128)(2,1)S(1)}, u32[]{:S(2)}, u32[]{:S(2)}) collective-permute-start(bf16[32,4096]{1,0:T(8,128)(2,1)} %param.9), channel_id=1, source_target_pairs={{0,1},{1,2},{2,3},{3,0},{4,5},{5,6},{6,7},{7,4},{8,9},{9,10},{10,1... | collective-permute-start | bytes 786440 | tf_op jit(solution)/shard_map/ppermute | solution.py:105
  9.4 32.1 %collective-permute-start.1 = (bf16[32,4096]{1,0:T(8,128)(2,1)}, bf16[32,4096]{1,0:T(8,128)(2,1)S(1)}, u32[]{:S(2)}, u32[]{:S(2)}) collective-permute-start(bf16[32,4096]{1,0:T(8,128)(2,1)} %param.9), channel_id=1, source_target_pairs={{0,2},{1,3},{2,0},{3,1},{4,6},{5,7},{6,4},{7,5},{8,10},{9,11},{10,... | collective-permute-start | bytes 786440 | tf_op jit(solution)/shard_map/ppermute | solution.py:105
  12.0 29.1 %collective-permute-start = (bf16[32,4096]{1,0:T(8,128)(2,1)}, bf16[32,4096]{1,0:T(8,128)(2,1)S(1)}, u32[]{:S(2)}, u32[]{:S(2)}) collective-permute-start(bf16[32,4096]{1,0:T(8,128)(2,1)} %param.9), channel_id=1, source_target_pairs={{0,3},{1,0},{2,1},{3,2},{4,7},{5,4},{6,5},{7,6},{8,11},{9,8},{10,9... | collective-permute-start | bytes 786440 | tf_op jit(solution)/shard_map/ppermute | solution.py:105
  14.5 10.7 %copy-start.4 = (bf16[32,4096]{0,1:T(8,128)(2,1)}, bf16[32,4096]{0,1:T(8,128)(2,1)S(1)}, u32[]{:S(2)}) copy-start(bf16[32,4096]{0,1:T(8,128)(2,1)S(1)} %copy.109) | copy-start | bytes 786436
  17.5 7.7 %copy-start.24 = (s32[3712]{0:T(1024)}, s32[3712]{0:T(1024)S(1)}, u32[]{:S(2)}) copy-start(s32[3712]{0:T(1024)S(1)} %constant_dynamic-update-slice_fusion.3.t_ref) | copy-start | bytes 44548
  28.1 37.0 %collective-permute-start.5 = (bf16[1024,32]{1,0:T(8,128)(2,1)}, bf16[1024,32]{1,0:T(8,128)(2,1)S(1)}, u32[]{:S(2)}, u32[]{:S(2)}) collective-permute-start(bf16[1024,32]{1,0:T(8,128)(2,1)} %get-tuple-element.34), channel_id=1, source_target_pairs={{0,16},{4,20},{8,24},{12,28},{16,0},{20,4},{24,8},{28,12},{32,48},... | collective-permute-start | bytes 196616 | tf_op jit(solution)/shard_map/ppermute | solution.py:203
  31.7 33.4 %collective-permute-start.4 = (bf16[1024,32]{1,0:T(8,128)(2,1)}, bf16[1024,32]{1,0:T(8,128)(2,1)S(1)}, u32[]{:S(2)}, u32[]{:S(2)}) collective-permute-start(bf16[1024,32]{1,0:T(8,128)(2,1)} %get-tuple-element.35), channel_id=1, source_target_pairs={{0,8},{4,12},{8,0},{12,4},{16,24},{20,28},{24,16},{28,20},{32,40},... | collective-permute-start | bytes 196616 | tf_op jit(solution)/shard_map/ppermute | solution.py:203
  33.8 7.7 %copy-start.14 = (bf16[32,4096]{1,0:T(8,128)(2,1)S(1)}, bf16[32,4096]{1,0:T(8,128)(2,1)}, u32[]{:S(2)}) copy-start(bf16[32,4096]{1,0:T(8,128)(2,1)} %param.9) | copy-start | bytes 786436
  33.8 27.1 %all-to-all-start = ((bf16[32,640,32]{1,2,0:T(8,128)(2,1)}), bf16[32,640,32]{1,2,0:T(8,128)(2,1)S(1)}, u32[]{:S(2)}, u32[]{:S(2)}) async-start(bf16[32,640,32]{1,2,0:T(8,128)(2,1)} %broadcast_in_dim.34), calls=%async_computation | async-start | bytes 2621440 | tf_op jit(solution)/shard_map/all_to_all | solution.py:229
  41.1 24.1 %collective-permute-start.3 = (bf16[1024,32]{1,0:T(8,128)(2,1)}, bf16[1024,32]{1,0:T(8,128)(2,1)S(1)}, u32[]{:S(2)}, u32[]{:S(2)}) collective-permute-start(bf16[1024,32]{1,0:T(8,128)(2,1)} %get-tuple-element.36), channel_id=1, source_target_pairs={{0,4},{4,0},{8,12},{12,8},{16,20},{20,16},{24,28},{28,24},{32,36},... | collective-permute-start | bytes 196616 | tf_op jit(solution)/shard_map/ppermute | solution.py:203
  65.1 0.7 copy-start.15
  65.1 0.8 copy-start.16
  65.2 0.9 copy-start.17
  114.2 5.0 %copy-start.10 = (bf16[4,32,4096]{2,1,0:T(8,128)(2,1)S(1)}, bf16[4,32,4096]{2,1,0:T(8,128)(2,1)}, u32[]{:S(2)}) copy-start(bf16[4,32,4096]{2,1,0:T(8,128)(2,1)} %constant_dynamic-slice_fusion) | copy-start | bytes 3145732
  114.2 5.0 %copy-start.25 = (bf16[64,128]{1,0:T(8,128)(2,1)S(1)}, bf16[64,128]{1,0:T(8,128)(2,1)}, u32[]{:S(2)}) copy-start(bf16[64,128]{1,0:T(8,128)(2,1)} %param.14) | copy-start | bytes 49156
  115.6 18.5 %all-to-all-start.1 = ((bf16[4,32,4096]{2,1,0:T(8,128)(2,1)}), bf16[4,32,4096]{2,1,0:T(8,128)(2,1)S(1)}, u32[]{:S(2)}, u32[]{:S(2)}) async-start(bf16[4,32,4096]{2,1,0:T(8,128)(2,1)} %broadcast_in_dim.35), calls=%async_computation.1 | async-start | bytes 2097152 | tf_op jit(solution)/shard_map/all_to_all | solution.py:97
  119.2 14.9 %copy-start.26 = (bf16[64,128]{1,0:T(8,128)(2,1)S(1)}, bf16[64,128]{1,0:T(8,128)(2,1)}, u32[]{:S(2)}) copy-start(bf16[64,128]{1,0:T(8,128)(2,1)} %param.15) | copy-start | bytes 49156
  134.1 2.5 copy-start.12
  136.6 17.2 %copy-start.2 = (bf16[4096,64]{1,0:T(8,128)(2,1)}, bf16[4096,64]{1,0:T(8,128)(2,1)S(1)}, u32[]{:S(2)}) copy-start(bf16[4096,64]{1,0:T(8,128)(2,1)S(1)} %fusion.2.refs_0_) | copy-start | bytes 1572868
  148.2 39.6 %all-to-all-start.2 = ((bf16[32,640,64]{1,2,0:T(8,128)(2,1)}), bf16[32,640,64]{1,2,0:T(8,128)(2,1)}, u32[]{:S(2)}, u32[]{:S(2)}) async-start(bf16[32,640,64]{1,2,0:T(8,128)(2,1)} %broadcast_in_dim.60), calls=%async_computation.2 | async-start | bytes 5242880 | tf_op jit(solution)/shard_map/all_to_all | solution.py:229
  153.7 97.6 %all-gather.2.cloned.1.call-start = ((), (), s32[]{:S(2)}) async-start(), calls=%async_computation.7 | async-start | bytes 2621440 | tf_op jit(solution)/shard_map/all_gather | solution.py:283
  155.0 38.8 %collective-permute-start.8 = (bf16[1024,64]{1,0:T(8,128)(2,1)S(1)}, bf16[1024,64]{1,0:T(8,128)(2,1)S(1)}, u32[]{:S(2)}, u32[]{:S(2)}) collective-permute-start(bf16[1024,64]{1,0:T(8,128)(2,1)S(1)} %get-tuple-element.31), channel_id=1, source_target_pairs={{0,16},{4,20},{8,24},{12,28},{16,0},{20,4},{24,8},{28,12},{32,48},... | collective-permute-start | bytes 393224 | tf_op jit(solution)/shard_map/ppermute | solution.py:203
  158.0 37.7 %collective-permute-start.7 = (bf16[1024,64]{1,0:T(8,128)(2,1)S(1)}, bf16[1024,64]{1,0:T(8,128)(2,1)S(1)}, u32[]{:S(2)}, u32[]{:S(2)}) collective-permute-start(bf16[1024,64]{1,0:T(8,128)(2,1)S(1)} %get-tuple-element.32), channel_id=1, source_target_pairs={{0,8},{4,12},{8,0},{12,4},{16,24},{20,28},{24,16},{28,20},{32,40},... | collective-permute-start | bytes 393224 | tf_op jit(solution)/shard_map/ppermute | solution.py:203
  158.3 37.4 %collective-permute-start.6 = (bf16[1024,64]{1,0:T(8,128)(2,1)S(1)}, bf16[1024,64]{1,0:T(8,128)(2,1)S(1)}, u32[]{:S(2)}, u32[]{:S(2)}) collective-permute-start(bf16[1024,64]{1,0:T(8,128)(2,1)S(1)} %get-tuple-element.33), channel_id=1, source_target_pairs={{0,4},{4,0},{8,12},{12,8},{16,20},{20,16},{24,28},{28,24},{32,36},... | collective-permute-start | bytes 393224 | tf_op jit(solution)/shard_map/ppermute | solution.py:203
  193.8 1.9 copy-start.18
  195.7 0.7 copy-start.19
  195.7 0.8 copy-start.20
  246.5 4.8 %copy-start.21 = (bf16[172,256]{1,0:T(8,128)(2,1)S(1)}, bf16[172,256]{1,0:T(8,128)(2,1)}, u32[]{:S(2)}) copy-start(bf16[172,256]{1,0:T(8,128)(2,1)} %param.16) | copy-start | bytes 264196
  246.5 30.1 %all-to-all-start.3 = ((bf16[4,64,4096]{2,1,0:T(8,128)(2,1)}), bf16[4,64,4096]{2,1,0:T(8,128)(2,1)}, u32[]{:S(2)}, u32[]{:S(2)}) async-start(bf16[4,64,4096]{2,1,0:T(8,128)(2,1)} %broadcast_in_dim.61), calls=%async_computation.3 | async-start | bytes 4194304 | tf_op jit(solution)/shard_map/all_to_all | solution.py:97
  276.6 2.4 copy-start.27
  279.6 1.1 copy-start.5
  354.4 4.6 copy-start.7
  365.2 14.2 %copy-start.8 = (f32[4096,64]{1,0:T(8,128)S(1)}, f32[4096,64]{1,0:T(8,128)}, u32[]{:S(2)}) copy-start(f32[4096,64]{1,0:T(8,128)} %shard_map.121) | copy-start | bytes 3145732
  365.2 50.6 %all-to-all-start.4 = ((bf16[32,640,64]{1,2,0:T(8,128)(2,1)}), bf16[32,640,64]{1,2,0:T(8,128)(2,1)}, u32[]{:S(2)}, u32[]{:S(2)}) async-start(bf16[32,640,64]{1,2,0:T(8,128)(2,1)} %copy.122), calls=%async_computation.4 | async-start | bytes 5242880 | tf_op jit(solution)/shard_map/all_to_all | solution.py:302
  373.7 5.6 %copy-start.6 = (bf16[172,4096]{1,0:T(8,128)(2,1)S(1)}, bf16[172,4096]{1,0:T(8,128)(2,1)}, u32[]{:S(2)}) copy-start(bf16[172,4096]{1,0:T(8,128)(2,1)} %copy-done.5) | copy-start | bytes 4227076
  375.8 4.1 copy-start.22
  375.8 9.3 %collective-permute-start.9 = (bf16[1024,64]{1,0:T(8,128)(2,1)}, bf16[1024,64]{1,0:T(8,128)(2,1)S(1)}, u32[]{:S(2)}, u32[]{:S(2)}) collective-permute-start(bf16[1024,64]{1,0:T(8,128)(2,1)} %get-tuple-element.28), channel_id=1, source_target_pairs={{0,4},{4,0},{8,12},{12,8},{16,20},{20,16},{24,28},{28,24},{32,36},... | collective-permute-start | bytes 393224 | tf_op jit(solution)/shard_map/ppermute | solution.py:203
  376.1 36.2 %collective-permute-start.11 = (bf16[1024,64]{1,0:T(8,128)(2,1)}, bf16[1024,64]{1,0:T(8,128)(2,1)S(1)}, u32[]{:S(2)}, u32[]{:S(2)}) collective-permute-start(bf16[1024,64]{1,0:T(8,128)(2,1)} %get-tuple-element.29), channel_id=1, source_target_pairs={{0,16},{4,20},{8,24},{12,28},{16,0},{20,4},{24,8},{28,12},{32,48},... | collective-permute-start | bytes 393224 | tf_op jit(solution)/shard_map/ppermute | solution.py:203
  379.0 36.7 %collective-permute-start.10 = (bf16[1024,64]{1,0:T(8,128)(2,1)S(1)}, bf16[1024,64]{1,0:T(8,128)(2,1)S(1)}, u32[]{:S(2)}, u32[]{:S(2)}) collective-permute-start(bf16[1024,64]{1,0:T(8,128)(2,1)S(1)} %get-tuple-element.30), channel_id=1, source_target_pairs={{0,8},{4,12},{8,0},{12,4},{16,24},{20,28},{24,16},{28,20},{32,40},... | collective-permute-start | bytes 393224 | tf_op jit(solution)/shard_map/ppermute | solution.py:203
  379.9 3.9 copy-start.3
  419.5 12.2 %copy-start.13 = (bf16[4,32,4096]{2,1,0:T(8,128)(2,1)S(1)}, bf16[4,32,4096]{2,1,0:T(8,128)(2,1)}, u32[]{:S(2)}) copy-start(bf16[4,32,4096]{2,1,0:T(8,128)(2,1)} %copy-done.12) | copy-start | bytes 3145732
  431.6 2.3 copy-start.9
  431.6 2.5 copy-start.11
  434.1 0.8 copy-start.23
  434.1 30.4 %copy-start.1 = (bf16[172,256]{1,0:T(8,128)(2,1)S(1)}, bf16[172,256]{1,0:T(8,128)(2,1)}, u32[]{:S(2)}) copy-start(bf16[172,256]{1,0:T(8,128)(2,1)} %param.17) | copy-start | bytes 264196
Sparse Core Ops, SparseCore 0:
  156.2 29.8 all-gather.1

commit v16 on v14

--- a/solution.py
+++ b/solution.py
@@ -54,22 +54,26 @@
     )(neighbours, *pieces, after)
 
 
-def scatter_mean(rows, neighbours, size, chains=4):
+def scatter_mean(rows, neighbours, size):
     nodes, width = rows.shape
     degree = neighbours.shape[0]
-    per_chain = degree // chains
+    pack = 128 // width
+    lanes = pack * width
+    doubled = jnp.concatenate([rows] * pack, axis=1)
 
     def kernel(nb_ref, rows_ref, out_ref, *extra_refs):
         accumulators = (out_ref,) + extra_refs
         for acc_ref in accumulators:
             acc_ref[...] = jnp.zeros_like(acc_ref)
+        part = lax.broadcasted_iota(jnp.int32, (1, lanes), 1) // width
 
         def step(n, carry):
             x = rows_ref[pl.ds(n, 1), :]
-            for k in range(per_chain):
-                for chain, acc_ref in enumerate(accumulators):
-                    s = nb_ref[chain * per_chain + k, n]
-                    acc_ref[pl.ds(s, 1), :] = acc_ref[pl.ds(s, 1), :] + x
+            for k, acc_ref in enumerate(accumulators):
+                s = nb_ref[k, n]
+                row = s // pack
+                placed = jnp.where(part == s % pack, x, 0.0)
+                acc_ref[pl.ds(row, 1), :] = acc_ref[pl.ds(row, 1), :] + placed
             return carry
 
         lax.fori_loop(0, nodes, step, 0, unroll=2)
@@ -78,17 +82,18 @@
             total = total + acc_ref[...]
         out_ref[...] = total * (1.0 / degree)
 
-    return pl.pallas_call(
+    packed = pl.pallas_call(
         kernel,
         in_specs=[
             pl.BlockSpec(memory_space=pltpu.SMEM),
             pl.BlockSpec(memory_space=pltpu.VMEM),
         ],
         out_specs=pl.BlockSpec(memory_space=pltpu.VMEM),
-        out_shape=jax.ShapeDtypeStruct((size, width), jnp.float32),
-        scratch_shapes=[pltpu.VMEM((size, width), jnp.float32) for _ in range(chains - 1)],
+        out_shape=jax.ShapeDtypeStruct((size // pack, lanes), jnp.float32),
+        scratch_shapes=[pltpu.VMEM((size // pack, lanes), jnp.float32) for _ in range(degree - 1)],
         compiler_params=pltpu.CompilerParams(vmem_limit_bytes=63 * 1024 * 1024),
-    )(neighbours, rows)
+    )(neighbours, doubled)
+    return packed.reshape(size, width)
 
 
 def spread_gather(value, axis):

time: 463 us -> 617 us (1.33)
  Pallas kernels: 171 us -> 329 us
  waiting for transfers between devices: 96.4 us -> 88 us
    pallas_call x1, Pallas kernels: 65.7 us -> 224 us  [scatter_mean(): pl.pallas_call(kernel, in_specs=[pl.BlockSpec(memory_space=pltpu.SMEM), p...]
    convert_element_type x0 -> x5, local copies, waits for them, and re-layouts: none -> 13.1 us  [the longest x2 10.5 us: body(): hub_flat = spread[rows:rows + hub_count].astype(jnp.bfloat16)]
    all_to_all x2, waiting for transfers between devices: 28.4 us -> 18.5 us  [source_table(): lax.all_to_all(jnp.broadcast_to(hub_local[None], (owners,) + hub_local.sh...]
  transfers between devices with their start and end apart: 18 -> 18, of which waited for: 7 -> 8; matrix products, arithmetic and copies ran while one was open for 13% -> 10% of each run, Pallas kernels for 10% -> 8%
where the time goes in v16:
time: 617 us; the launch traced here: 615 us
  Pallas kernels  329 us (53%)
  waiting for transfers between devices  88 us (14%)
  local copies, waits for them, and re-layouts  71.5 us (12%)
  starting transfers between devices  48.9 us (8%)
  blocking collectives  26.3 us (4%)
  matrix products  18.5 us (3%)
  other arithmetic  18.3 us (3%)
  between operations  14.7 us (2%)
    pallas_call x1, Pallas kernels, scatter_mean(): pl.pallas_call(kernel, in_specs=[pl.BlockSpec(memory_space=pltpu.SMEM), p...  224 us
    pallas_call x2, Pallas kernels, gather_mean(): pl.pallas_call(kernel, in_specs=[pl.BlockSpec(memory_space=pltpu.SMEM)] +...  92.7 us
    all_to_all x2, waiting for transfers between devices, spread_gather(): gathered = lax.all_to_all(copies, axis, 0, 0, tiled=True)  36 us
    ppermute x9, waiting for transfers between devices, partner(): return lax.ppermute(value, axis, pairs)  33.5 us
    gather x6, local copies, waits for them, and re-layouts, source_table(): jnp.take(local_rows, send_rows[bit_index], axis=0)  19.3 us
    all_to_all x2, waiting for transfers between devices, source_table(): lax.all_to_all(jnp.broadcast_to(hub_local[None], (owners,) + hub_local.sh...  18.5 us
    all_to_all x2, starting transfers between devices, source_table(): lax.all_to_all(jnp.broadcast_to(hub_local[None], (owners,) + hub_local.sh...  16.1 us
    all_to_all x1, blocking collectives, exchange_sum(): reduced = jnp.sum(lax.all_to_all(padded, axis, 0, 0, tiled=True), axis=0)  14.7 us
  transfers between devices with their start and end apart: 18, of which 8 were waited for; matrix products, arithmetic and copies ran while one was open for 10% of the time, Pallas kernels for 8%

profile of v16, /device:TPU:1, one launch (start us, length us, event | category | flops | bytes accessed | tf_op | source)
XLA Modules:
  0.0 615.2 jit_solution(15486222898500709638)
XLA Ops:
  7.2 3.6 collective-permute-start
  15.6 2.0 gather_fusion
  19.1 9.4 %all-to-all-start = ((bf16[32,640,32]{1,2,0:T(8,128)(2,1)}), bf16[32,640,32]{1,2,0:T(8,128)(2,1)S(1)}, u32[]{:S(2)}, u32[]{:S(2)}) async-start(bf16[32,640,32]{1,2,0:T(8,128)(2,1)} %broadcast_in_dim.77), calls=%async_computation | async-start | bytes 2621440 | tf_op jit(solution)/shard_map/all_to_all | solution.py:231
  28.6 3.2 gather_fusion.2
  32.9 3.2 gather_fusion.3
  38.6 3.2 gather_fusion.4
  42.0 2.5 collective-permute-start.5
  48.3 4.3 copy.111
  52.6 5.3 collective-permute-done.5.refs_4_
  58.6 46.4 %shard_map.120 = f32[4096,32]{1,0:T(8,128)} custom-call(s32[8,4096]{1,0:T(8,128)} %nb_ref.5, bf16[4096,32]{1,0:T(8,128)(2,1)} %bitcast.65, bf16[20480,32]{1,0:T(8,128)(2,1)} %bitcast.66, bf16[1024,32]{1,0:T(8,128)(2,1)} %collective-permute-done.3.refs_2_, bf16[1024,32]{1,0:T(8,128)(2,1)} %collective-permute-done.4.refs_3_, bf16[1024,32]{1,0:T(8,128)(2,1)} %copy-done.14, ...), custom_call_target="tpu_custom_call" | custom-call | tf_op jit(solution)/shard_map/pallas_call | solution.py:46
  104.9 1.7 convert_bitcast_fusion
  108.1 3.5 all-to-all-start.1
  111.6 1.8 fusion.22
  113.5 12.7 %all-to-all-done.1 = bf16[4,32,4096]{2,1,0:T(8,128)(2,1)S(1)} async-done(((bf16[4,32,4096]{2,1,0:T(8,128)(2,1)}), bf16[4,32,4096]{2,1,0:T(8,128)(2,1)S(1)}, u32[]{:S(2)}, u32[]{:S(2)}) %all-to-all-start.1) | async-done | bytes 1048608 | tf_op jit(solution)/shard_map/all_to_all | solution.py:102
  126.2 2.5 fusion.2.refs_0_
  128.7 2.0 gather_fusion.1
  131.0 1.8 broadcast_in_dim.81
  132.8 6.6 %all-to-all-start.2 = ((bf16[32,640,64]{1,2,0:T(8,128)(2,1)}), bf16[32,640,64]{1,2,0:T(8,128)(2,1)}, u32[]{:S(2)}, u32[]{:S(2)}) async-start(bf16[32,640,64]{1,2,0:T(8,128)(2,1)} %broadcast_in_dim.81), calls=%async_computation.2 | async-start | bytes 5242880 | tf_op jit(solution)/shard_map/all_to_all | solution.py:231
  140.7 3.2 gather_fusion.5
  143.9 3.2 gather_fusion.6
  147.1 3.2 gather_fusion.7
  152.9 2.7 collective-permute-start.8
  155.5 17.9 %all-to-all-done.2 = bf16[32,640,64]{1,2,0:T(8,128)(2,1)} async-done(((bf16[32,640,64]{1,2,0:T(8,128)(2,1)}), bf16[32,640,64]{1,2,0:T(8,128)(2,1)}, u32[]{:S(2)}, u32[]{:S(2)}) %all-to-all-start.2) | async-done | bytes 2621472 | tf_op jit(solution)/shard_map/all_to_all | solution.py:231
  173.4 6.0 copy.117
  179.5 3.5 collective-permute-done.8.refs_4_
  183.6 46.4 %shard_map.121 = f32[4096,64]{1,0:T(8,128)} custom-call(s32[8,4096]{1,0:T(8,128)} %nb_ref.5, bf16[4096,64]{1,0:T(8,128)(2,1)} %copy-done.2, bf16[20480,64]{1,0:T(8,128)(2,1)} %bitcast.67, bf16[1024,64]{1,0:T(8,128)(2,1)} %copy-done.15, bf16[1024,64]{1,0:T(8,128)(2,1)} %copy-done.16, bf16[1024,64]{1,0:T(8,128)(2,1)} %copy-done.17, bf16[64,4096]{1,0:T(8,128)(2,1)} %copy.115.refs_5_), custom_call_target="tpu_custom_call" | custom-call | tf_op jit(solution)/shard_map/pallas_call | solution.py:46
  230.0 1.7 convert_bitcast_fusion.1
  233.6 4.6 all-to-all-start.3
  238.3 2.1 fusion.23
  240.4 23.3 %all-to-all-done.3 = bf16[4,64,4096]{2,1,0:T(8,128)(2,1)} async-done(((bf16[4,64,4096]{2,1,0:T(8,128)(2,1)}), bf16[4,64,4096]{2,1,0:T(8,128)(2,1)}, u32[]{:S(2)}, u32[]{:S(2)}) %all-to-all-start.3) | async-done | bytes 2097184 | tf_op jit(solution)/shard_map/all_to_all | solution.py:102
  263.7 2.4 fusion.21
  268.9 1.9 maximum_convert_fusion.rows_ref
  270.8 224.1 %shard_map.122 = f32[13824,128]{1,0:T(8,128)} custom-call(s32[8,4096]{1,0:T(8,128)} %nb_ref.5, f32[4096,128]{1,0:T(8,128)} %maximum_convert_fusion.rows_ref), custom_call_target="tpu_custom_call" | custom-call | tf_op jit(solution)/shard_map/pallas_call | solution.py:85
  494.8 3.3 convert.7
  498.1 1.7 copy-done.10
  500.1 4.4 convert_element_type.70
  504.4 6.1 copy.123
  510.6 7.2 %all-to-all-start.4 = ((bf16[32,640,64]{1,2,0:T(8,128)(2,1)}), bf16[32,640,64]{1,2,0:T(8,128)(2,1)}, u32[]{:S(2)}, u32[]{:S(2)}) async-start(bf16[32,640,64]{1,2,0:T(8,128)(2,1)} %copy.123), calls=%async_computation.4 | async-start | bytes 5242880 | tf_op jit(solution)/shard_map/all_to_all | solution.py:304
  522.6 2.9 collective-permute-start.11
  528.4 2.1 fusion.6
  530.6 3.8 convolution_add_fusion.1.base_ref
  535.1 21.3 %collective-permute-done.11 = bf16[1024,64]{1,0:T(8,128)(2,1)S(1)} collective-permute-done((bf16[1024,64]{1,0:T(8,128)(2,1)}, bf16[1024,64]{1,0:T(8,128)(2,1)S(1)}, u32[]{:S(2)}, u32[]{:S(2)}) %collective-permute-start.11) | collective-permute-done | bytes 131104 | tf_op jit(solution)/shard_map/ppermute | solution.py:208
  556.4 3.4 collective-permute-done.10
  559.9 2.1 convert_reduce_fusion
  563.6 12.1 %shard_map.123 = f32[4096,64]{1,0:T(8,128)} custom-call(s32[3712]{0:T(1024)} %pad_add_fusion.t_ref, f32[4096,64]{1,0:T(8,128)} %convolution_add_fusion.1.base_ref, f32[3712,64]{1,0:T(8,128)} %pad_maximum_fusion.upd_ref), custom_call_target="tpu_custom_call" | custom-call | tf_op jit(solution)/shard_map/pallas_call | solution.py:139
  575.8 2.3 convolution_bitcast_fusion
  579.0 14.7 %all_to_all.41 = f32[32,1,1200]{2,1,0:T(1,128)S(1)} all-to-all(f32[32,1,1200]{2,1,0:T(1,128)S(1)} %all_to_all.31), channel_id=1, replica_groups=mesh['dom'=32,'feat'=4] {'dom'}, dimensions={0} | all-to-all | bytes 307200 | tf_op jit(solution)/shard_map/all_to_all | solution.py:172
  593.9 11.5 %all_to_all.42 = f32[32,1,1200]{2,1,0:T(1,128)S(1)} all-to-all(f32[32,1,1200]{2,1,0:T(1,128)S(1)} %broadcast_in_dim.83), channel_id=1, replica_groups=mesh['dom'=32,'feat'=4] {'dom'}, dimensions={0} | all-to-all | bytes 307200 | tf_op jit(solution)/shard_map/all_to_all | solution.py:174
  (135 shorter events, 39.7 us)
Async XLA Ops:
  7.2 256.6 %copy-start = (bf16[172,256]{1,0:T(8,128)(2,1)S(1)}, bf16[172,256]{1,0:T(8,128)(2,1)}, u32[]{:S(2)}) copy-start(bf16[172,256]{1,0:T(8,128)(2,1)} %param.21) | copy-start | bytes 264196
  7.2 34.9 %collective-permute-start = (bf16[32,4096]{1,0:T(8,128)(2,1)}, bf16[32,4096]{1,0:T(8,128)(2,1)S(1)}, u32[]{:S(2)}, u32[]{:S(2)}) collective-permute-start(bf16[32,4096]{1,0:T(8,128)(2,1)} %param.13), channel_id=1, source_target_pairs={{0,3},{1,0},{2,1},{3,2},{4,7},{5,4},{6,5},{7,6},{8,11},{9,8},{10,9... | collective-permute-start | bytes 786440 | tf_op jit(solution)/shard_map/ppermute | solution.py:110
  10.8 33.7 %collective-permute-start.1 = (bf16[32,4096]{1,0:T(8,128)(2,1)}, bf16[32,4096]{1,0:T(8,128)(2,1)S(1)}, u32[]{:S(2)}, u32[]{:S(2)}) collective-permute-start(bf16[32,4096]{1,0:T(8,128)(2,1)} %param.13), channel_id=1, source_target_pairs={{0,2},{1,3},{2,0},{3,1},{4,6},{5,7},{6,4},{7,5},{8,10},{9,11},{10,... | collective-permute-start | bytes 786440 | tf_op jit(solution)/shard_map/ppermute | solution.py:110
  11.2 33.4 %collective-permute-start.2 = (bf16[32,4096]{1,0:T(8,128)(2,1)}, bf16[32,4096]{1,0:T(8,128)(2,1)}, u32[]{:S(2)}, u32[]{:S(2)}) collective-permute-start(bf16[32,4096]{1,0:T(8,128)(2,1)} %param.13), channel_id=1, source_target_pairs={{0,1},{1,2},{2,3},{3,0},{4,5},{5,6},{6,7},{7,4},{8,9},{9,10},{10,1... | collective-permute-start | bytes 786440 | tf_op jit(solution)/shard_map/ppermute | solution.py:110
  13.3 25.3 %copy-start.4 = (bf16[32,4096]{0,1:T(8,128)(2,1)}, bf16[32,4096]{0,1:T(8,128)(2,1)S(1)}, u32[]{:S(2)}) copy-start(bf16[32,4096]{0,1:T(8,128)(2,1)S(1)} %copy.109) | copy-start | bytes 786436
  19.1 29.2 %all-to-all-start = ((bf16[32,640,32]{1,2,0:T(8,128)(2,1)}), bf16[32,640,32]{1,2,0:T(8,128)(2,1)S(1)}, u32[]{:S(2)}, u32[]{:S(2)}) async-start(bf16[32,640,32]{1,2,0:T(8,128)(2,1)} %broadcast_in_dim.77), calls=%async_computation | async-start | bytes 2621440 | tf_op jit(solution)/shard_map/all_to_all | solution.py:231
  32.7 19.9 %collective-permute-start.3 = (bf16[1024,32]{1,0:T(8,128)(2,1)}, bf16[1024,32]{1,0:T(8,128)(2,1)}, u32[]{:S(2)}, u32[]{:S(2)}) collective-permute-start(bf16[1024,32]{1,0:T(8,128)(2,1)} %broadcast_select_fusion.5), channel_id=1, source_target_pairs={{0,4},{4,0},{8,12},{12,8},{16,20},{20,16},{24,28},{28,24},{32,36},... | collective-permute-start | bytes 196616 | tf_op jit(solution)/shard_map/ppermute | solution.py:208
  37.1 15.5 %collective-permute-start.4 = (bf16[1024,32]{1,0:T(8,128)(2,1)}, bf16[1024,32]{1,0:T(8,128)(2,1)}, u32[]{:S(2)}, u32[]{:S(2)}) collective-permute-start(bf16[1024,32]{1,0:T(8,128)(2,1)} %broadcast_select_fusion.4), channel_id=1, source_target_pairs={{0,8},{4,12},{8,0},{12,4},{16,24},{20,28},{24,16},{28,20},{32,40},... | collective-permute-start | bytes 196616 | tf_op jit(solution)/shard_map/ppermute | solution.py:208
  38.6 7.0 %copy-start.13 = (bf16[32,4096]{1,0:T(8,128)(2,1)S(1)}, bf16[32,4096]{1,0:T(8,128)(2,1)}, u32[]{:S(2)}) copy-start(bf16[32,4096]{1,0:T(8,128)(2,1)} %param.13) | copy-start | bytes 786436
  42.0 15.8 %collective-permute-start.5 = (bf16[1024,32]{1,0:T(8,128)(2,1)S(1)}, bf16[1024,32]{1,0:T(8,128)(2,1)S(1)}, u32[]{:S(2)}, u32[]{:S(2)}) collective-permute-start(bf16[1024,32]{1,0:T(8,128)(2,1)S(1)} %broadcast_select_fusion.3), channel_id=1, source_target_pairs={{0,16},{4,20},{8,24},{12,28},{16,0},{20,4},{24,8},{28,12},{32,48},... | collective-permute-start | bytes 196616 | tf_op jit(solution)/shard_map/ppermute | solution.py:208
  57.9 0.7 copy-start.14
  106.6 5.0 copy-start.8
  106.7 5.0 copy-start.21
  108.1 18.1 %all-to-all-start.1 = ((bf16[4,32,4096]{2,1,0:T(8,128)(2,1)}), bf16[4,32,4096]{2,1,0:T(8,128)(2,1)S(1)}, u32[]{:S(2)}, u32[]{:S(2)}) async-start(bf16[4,32,4096]{2,1,0:T(8,128)(2,1)} %broadcast_in_dim.78), calls=%async_computation.1 | async-start | bytes 2097152 | tf_op jit(solution)/shard_map/all_to_all | solution.py:102
  111.6 14.5 %copy-start.22 = (bf16[64,128]{1,0:T(8,128)(2,1)S(1)}, bf16[64,128]{1,0:T(8,128)(2,1)}, u32[]{:S(2)}) copy-start(bf16[64,128]{1,0:T(8,128)(2,1)} %param.19) | copy-start | bytes 49156
  126.2 2.5 copy-start.11
  128.7 18.5 %copy-start.2 = (bf16[4096,64]{1,0:T(8,128)(2,1)}, bf16[4096,64]{1,0:T(8,128)(2,1)S(1)}, u32[]{:S(2)}) copy-start(bf16[4096,64]{1,0:T(8,128)(2,1)S(1)} %fusion.2.refs_0_) | copy-start | bytes 1572868
  132.8 40.6 %all-to-all-start.2 = ((bf16[32,640,64]{1,2,0:T(8,128)(2,1)}), bf16[32,640,64]{1,2,0:T(8,128)(2,1)}, u32[]{:S(2)}, u32[]{:S(2)}) async-start(bf16[32,640,64]{1,2,0:T(8,128)(2,1)} %broadcast_in_dim.81), calls=%async_computation.2 | async-start | bytes 5242880 | tf_op jit(solution)/shard_map/all_to_all | solution.py:231
  139.4 98.8 %all-gather.2.cloned.1.call-start = ((), (), s32[]{:S(2)}) async-start(), calls=%async_computation.7 | async-start | bytes 2621440 | tf_op jit(solution)/shard_map/all_gather | solution.py:285
  150.6 28.9 %collective-permute-start.6 = (bf16[1024,64]{1,0:T(8,128)(2,1)S(1)}, bf16[1024,64]{1,0:T(8,128)(2,1)S(1)}, u32[]{:S(2)}, u32[]{:S(2)}) collective-permute-start(bf16[1024,64]{1,0:T(8,128)(2,1)S(1)} %broadcast_select_fusion.2), channel_id=1, source_target_pairs={{0,4},{4,0},{8,12},{12,8},{16,20},{20,16},{24,28},{28,24},{32,36},... | collective-permute-start | bytes 393224 | tf_op jit(solution)/shard_map/ppermute | solution.py:208
  151.1 28.3 %collective-permute-start.7 = (bf16[1024,64]{1,0:T(8,128)(2,1)S(1)}, bf16[1024,64]{1,0:T(8,128)(2,1)S(1)}, u32[]{:S(2)}, u32[]{:S(2)}) collective-permute-start(bf16[1024,64]{1,0:T(8,128)(2,1)S(1)} %broadcast_select_fusion.1), channel_id=1, source_target_pairs={{0,8},{4,12},{8,0},{12,4},{16,24},{20,28},{24,16},{28,20},{32,40},... | collective-permute-start | bytes 393224 | tf_op jit(solution)/shard_map/ppermute | solution.py:208
  152.9 30.1 %collective-permute-start.8 = (bf16[1024,64]{1,0:T(8,128)(2,1)S(1)}, bf16[1024,64]{1,0:T(8,128)(2,1)S(1)}, u32[]{:S(2)}, u32[]{:S(2)}) collective-permute-start(bf16[1024,64]{1,0:T(8,128)(2,1)S(1)} %broadcast_select_fusion), channel_id=1, source_target_pairs={{0,16},{4,20},{8,24},{12,28},{16,0},{20,4},{24,8},{28,12},{32,48},... | collective-permute-start | bytes 393224 | tf_op jit(solution)/shard_map/ppermute | solution.py:208
  179.4 3.5 copy-start.15
  179.4 3.5 copy-start.16
  182.9 0.7 copy-start.17
  233.6 4.6 copy-start.18
  233.6 30.1 %all-to-all-start.3 = ((bf16[4,64,4096]{2,1,0:T(8,128)(2,1)}), bf16[4,64,4096]{2,1,0:T(8,128)(2,1)}, u32[]{:S(2)}, u32[]{:S(2)}) async-start(bf16[4,64,4096]{2,1,0:T(8,128)(2,1)} %broadcast_in_dim.82), calls=%async_computation.3 | async-start | bytes 4194304 | tf_op jit(solution)/shard_map/all_to_all | solution.py:102
  263.7 2.4 copy-start.23
  266.7 1.2 copy-start.5
  498.1 1.7 copy-start.10
  510.6 7.2 %copy-start.19 = (s32[3,1024]{1,0:T(4,128)S(1)}, s32[3,1024]{1,0:T(4,128)}, u32[]{:S(2)}) copy-start(s32[3,1024]{1,0:T(4,128)} %param.16) | copy-start | bytes 36868
  510.6 7.2 %copy-start.20 = (s32[640]{0:T(1024)S(1)}, s32[640]{0:T(1024)}, u32[]{:S(2)}) copy-start(s32[640]{0:T(1024)} %param.15) | copy-start | bytes 7684
  510.6 49.4 %all-to-all-start.4 = ((bf16[32,640,64]{1,2,0:T(8,128)(2,1)}), bf16[32,640,64]{1,2,0:T(8,128)(2,1)}, u32[]{:S(2)}, u32[]{:S(2)}) async-start(bf16[32,640,64]{1,2,0:T(8,128)(2,1)} %copy.123), calls=%async_computation.4 | async-start | bytes 5242880 | tf_op jit(solution)/shard_map/all_to_all | solution.py:304
  517.8 1.2 slice-start
  519.0 9.4 %copy-start.6 = (bf16[172,4096]{1,0:T(8,128)(2,1)S(1)}, bf16[172,4096]{1,0:T(8,128)(2,1)}, u32[]{:S(2)}) copy-start(bf16[172,4096]{1,0:T(8,128)(2,1)} %copy-done.5) | copy-start | bytes 4227076
  522.6 33.8 %collective-permute-start.11 = (bf16[1024,64]{1,0:T(8,128)(2,1)}, bf16[1024,64]{1,0:T(8,128)(2,1)S(1)}, u32[]{:S(2)}, u32[]{:S(2)}) collective-permute-start(bf16[1024,64]{1,0:T(8,128)(2,1)} %convert_element_type.76), channel_id=1, source_target_pairs={{0,16},{4,20},{8,24},{12,28},{16,0},{20,4},{24,8},{28,12},{32,48},... | collective-permute-start | bytes 393224 | tf_op jit(solution)/shard_map/ppermute | solution.py:208
  526.3 33.5 %collective-permute-start.10 = (bf16[1024,64]{1,0:T(8,128)(2,1)}, bf16[1024,64]{1,0:T(8,128)(2,1)S(1)}, u32[]{:S(2)}, u32[]{:S(2)}) collective-permute-start(bf16[1024,64]{1,0:T(8,128)(2,1)} %convert_element_type.74), channel_id=1, source_target_pairs={{0,8},{4,12},{8,0},{12,4},{16,24},{20,28},{24,16},{28,20},{32,40},... | collective-permute-start | bytes 393224 | tf_op jit(solution)/shard_map/ppermute | solution.py:208
  527.4 32.4 %collective-permute-start.9 = (bf16[1024,64]{1,0:T(8,128)(2,1)}, bf16[1024,64]{1,0:T(8,128)(2,1)S(1)}, u32[]{:S(2)}, u32[]{:S(2)}) collective-permute-start(bf16[1024,64]{1,0:T(8,128)(2,1)} %convert_element_type.72), channel_id=1, source_target_pairs={{0,4},{4,0},{8,12},{12,8},{16,20},{20,16},{24,28},{28,24},{32,36},... | collective-permute-start | bytes 393224 | tf_op jit(solution)/shard_map/ppermute | solution.py:208
  530.5 3.8 copy-start.3
  563.6 12.1 %copy-start.12 = (bf16[4,32,4096]{2,1,0:T(8,128)(2,1)S(1)}, bf16[4,32,4096]{2,1,0:T(8,128)(2,1)}, u32[]{:S(2)}) copy-start(bf16[4,32,4096]{2,1,0:T(8,128)(2,1)} %copy-done.11) | copy-start | bytes 3145732
  575.8 2.3 copy-start.7
  575.8 2.5 copy-start.9
  578.2 30.1 %copy-start.1 = (bf16[172,256]{1,0:T(8,128)(2,1)S(1)}, bf16[172,256]{1,0:T(8,128)(2,1)}, u32[]{:S(2)}) copy-start(bf16[172,256]{1,0:T(8,128)(2,1)} %param.21) | copy-start | bytes 264196
Sparse Core Ops, SparseCore 0:
  141.9 29.8 all-gather.1

commit v17 on v14

--- a/solution.py
+++ b/solution.py
@@ -41,7 +41,7 @@
             out_ref[pl.ds(n, 1), :] = acc / degree
             return carry
 
-        lax.fori_loop(0, nodes, body, 0, unroll=8)
+        lax.fori_loop(0, nodes, body, 0, unroll=16)
 
     return pl.pallas_call(
         kernel,

time: 463 us -> 460 us (level)
  no operation moved by 1% of the time
where the time goes in v17:
time: 460 us; the launch traced here: 459 us
  Pallas kernels  167 us (36%)
  waiting for transfers between devices  96.4 us (21%)
  local copies, waits for them, and re-layouts  66.7 us (14%)
  starting transfers between devices  48.9 us (11%)
  blocking collectives  26.3 us (6%)
  other arithmetic  19.6 us (4%)
  matrix products  18.6 us (4%)
  between operations  14.7 us (3%)
    pallas_call x2, Pallas kernels, gather_mean(): pl.pallas_call(kernel, in_specs=[pl.BlockSpec(memory_space=pltpu.SMEM)] +...  89.5 us
    pallas_call x1, Pallas kernels, scatter_mean(): pl.pallas_call(kernel, in_specs=[pl.BlockSpec(memory_space=pltpu.SMEM), p...  65.7 us
    all_to_all x2, waiting for transfers between devices, spread_gather(): gathered = lax.all_to_all(copies, axis, 0, 0, tiled=True)  36.2 us
    ppermute x9, waiting for transfers between devices, partner(): return lax.ppermute(value, axis, pairs)  31.8 us
    all_to_all x2, waiting for transfers between devices, source_table(): lax.all_to_all(jnp.broadcast_to(hub_local[None], (owners,) + hub_local.sh...  28.4 us
    gather x6, local copies, waits for them, and re-layouts, source_table(): jnp.take(local_rows, send_rows[bit_index], axis=0)  19.2 us
    all_to_all x1, blocking collectives, exchange_sum(): reduced = jnp.sum(lax.all_to_all(padded, axis, 0, 0, tiled=True), axis=0)  14.7 us
    all_to_all x2, starting transfers between devices, source_table(): lax.all_to_all(jnp.broadcast_to(hub_local[None], (owners,) + hub_local.sh...  13.9 us
  transfers between devices with their start and end apart: 18, of which 7 were waited for; matrix products, arithmetic and copies ran while one was open for 13% of the time, Pallas kernels for 10%

profile of v17, /device:TPU:1, one launch (start us, length us, event | category | flops | bytes accessed | tf_op | source)
XLA Modules:
  0.0 458.6 jit_solution(15415361083630852901)
XLA Ops:
  7.2 2.2 collective-permute-start.2
  9.4 2.6 collective-permute-start.1
  16.1 3.2 gather_fusion.2
  21.8 3.2 gather_fusion.3
  27.6 2.0 gather_fusion
  31.1 7.8 %all-to-all-start = ((bf16[32,640,32]{1,2,0:T(8,128)(2,1)}), bf16[32,640,32]{1,2,0:T(8,128)(2,1)S(1)}, u32[]{:S(2)}, u32[]{:S(2)}) async-start(bf16[32,640,32]{1,2,0:T(8,128)(2,1)} %broadcast_in_dim.77), calls=%async_computation | async-start | bytes 2621440 | tf_op jit(solution)/shard_map/all_to_all | solution.py:226
  38.9 3.2 gather_fusion.4
  42.4 2.9 collective-permute-start.5
  48.5 10.2 %all-to-all-done = bf16[32,640,32]{1,2,0:T(8,128)(2,1)S(1)} async-done(((bf16[32,640,32]{1,2,0:T(8,128)(2,1)}), bf16[32,640,32]{1,2,0:T(8,128)(2,1)S(1)}, u32[]{:S(2)}, u32[]{:S(2)}) %all-to-all-start) | async-done | bytes 1310752 | tf_op jit(solution)/shard_map/all_to_all | solution.py:226
  58.7 4.3 copy.111
  63.6 44.8 %shard_map.120 = f32[4096,32]{1,0:T(8,128)} custom-call(s32[8,4096]{1,0:T(8,128)} %nb_ref.5, bf16[4096,32]{1,0:T(8,128)(2,1)} %bitcast.66, bf16[20480,32]{1,0:T(8,128)(2,1)} %bitcast.67, bf16[1024,32]{1,0:T(8,128)(2,1)} %collective-permute-done.3.refs_2_, bf16[1024,32]{1,0:T(8,128)(2,1)} %collective-permute-done.4.refs_3_, bf16[1024,32]{1,0:T(8,128)(2,1)} %copy-done.14, ...), custom_call_target="tpu_custom_call" | custom-call | tf_op jit(solution)/shard_map/pallas_call | solution.py:46
  108.4 1.7 convert_bitcast_fusion
  111.5 3.5 all-to-all-start.1
  115.1 1.8 fusion.22
  116.9 12.8 %all-to-all-done.1 = bf16[4,32,4096]{2,1,0:T(8,128)(2,1)S(1)} async-done(((bf16[4,32,4096]{2,1,0:T(8,128)(2,1)}), bf16[4,32,4096]{2,1,0:T(8,128)(2,1)S(1)}, u32[]{:S(2)}, u32[]{:S(2)}) %all-to-all-start.1) | async-done | bytes 1048608 | tf_op jit(solution)/shard_map/all_to_all | solution.py:97
  129.7 2.5 fusion.2.refs_0_
  132.2 2.0 gather_fusion.1
  134.5 1.8 broadcast_in_dim.81
  136.4 6.1 %all-to-all-start.2 = ((bf16[32,640,64]{1,2,0:T(8,128)(2,1)}), bf16[32,640,64]{1,2,0:T(8,128)(2,1)}, u32[]{:S(2)}, u32[]{:S(2)}) async-start(bf16[32,640,64]{1,2,0:T(8,128)(2,1)} %broadcast_in_dim.81), calls=%async_computation.2 | async-start | bytes 5242880 | tf_op jit(solution)/shard_map/all_to_all | solution.py:226
  143.8 3.2 gather_fusion.7
  147.0 3.2 gather_fusion.6
  150.2 3.2 gather_fusion.5
  155.9 2.4 collective-permute-start.8
  158.3 18.2 %all-to-all-done.2 = bf16[32,640,64]{1,2,0:T(8,128)(2,1)} async-done(((bf16[32,640,64]{1,2,0:T(8,128)(2,1)}), bf16[32,640,64]{1,2,0:T(8,128)(2,1)}, u32[]{:S(2)}, u32[]{:S(2)}) %all-to-all-start.2) | async-done | bytes 2621472 | tf_op jit(solution)/shard_map/all_to_all | solution.py:226
  176.5 6.0 %copy.117 = bf16[32,640,64]{2,1,0:T(8,128)(2,1)} copy(bf16[32,640,64]{1,2,0:T(8,128)(2,1)} %all-to-all-done.2) | data formatting | bytes 5242880 | tf_op jit(solution)/shard_map/all_to_all | solution.py:226
  182.5 3.5 collective-permute-done.8.refs_4_
  186.7 44.8 %shard_map.121 = f32[4096,64]{1,0:T(8,128)} custom-call(s32[8,4096]{1,0:T(8,128)} %nb_ref.5, bf16[4096,64]{1,0:T(8,128)(2,1)} %copy-done.2, bf16[20480,64]{1,0:T(8,128)(2,1)} %bitcast.68, bf16[1024,64]{1,0:T(8,128)(2,1)} %copy-done.15, bf16[1024,64]{1,0:T(8,128)(2,1)} %copy-done.16, bf16[1024,64]{1,0:T(8,128)(2,1)} %copy-done.17, bf16[64,4096]{1,0:T(8,128)(2,1)} %copy.115.refs_5_), custom_call_target="tpu_custom_call" | custom-call | tf_op jit(solution)/shard_map/pallas_call | solution.py:46
  231.5 1.7 convert_bitcast_fusion.1
  235.1 4.6 all-to-all-start.3
  239.7 2.1 fusion.23
  241.9 23.3 %all-to-all-done.3 = bf16[4,64,4096]{2,1,0:T(8,128)(2,1)} async-done(((bf16[4,64,4096]{2,1,0:T(8,128)(2,1)}), bf16[4,64,4096]{2,1,0:T(8,128)(2,1)}, u32[]{:S(2)}, u32[]{:S(2)}) %all-to-all-start.3) | async-done | bytes 2097184 | tf_op jit(solution)/shard_map/all_to_all | solution.py:97
  265.2 2.4 fusion.21
  271.7 65.7 %shard_map.122 = f32[27648,64]{1,0:T(8,128)} custom-call(s32[8,4096]{1,0:T(8,128)} %nb_ref.5, f32[4096,64]{1,0:T(8,128)} %convert_element_type.59.rows_ref), custom_call_target="tpu_custom_call" | custom-call | tf_op jit(solution)/shard_map/pallas_call | solution.py:81
  337.4 5.7 %convert.6 = bf16[27648,64]{1,0:T(8,128)(2,1)S(1)} convert(f32[27648,64]{1,0:T(8,128)} %shard_map.122) | non-fusion elementwise | flops 1769472 | bytes 10616832 | tf_op jit(solution)/shard_map/convert.3
  343.1 3.4 slice.82
  347.6 6.1 %copy.122 = bf16[32,640,64]{1,2,0:T(8,128)(2,1)} copy(bf16[32,640,64]{2,1,0:T(8,128)(2,1)} %bitcast.69) | data formatting | bytes 5242880 | tf_op jit(solution)/shard_map/all_to_all | solution.py:299
  353.7 7.2 %all-to-all-start.4 = ((bf16[32,640,64]{1,2,0:T(8,128)(2,1)}), bf16[32,640,64]{1,2,0:T(8,128)(2,1)}, u32[]{:S(2)}, u32[]{:S(2)}) async-start(bf16[32,640,64]{1,2,0:T(8,128)(2,1)} %copy.122), calls=%async_computation.4 | async-start | bytes 5242880 | tf_op jit(solution)/shard_map/all_to_all | solution.py:299
  361.6 2.0 fusion.17
  363.9 3.0 collective-permute-start.11
  367.1 2.1 fusion.6
  369.3 3.9 convolution_add_fusion.1.base_ref
  374.6 25.0 %collective-permute-done.11 = bf16[1024,64]{1,0:T(8,128)(2,1)S(1)} collective-permute-done((bf16[1024,64]{1,0:T(8,128)(2,1)}, bf16[1024,64]{1,0:T(8,128)(2,1)S(1)}, u32[]{:S(2)}, u32[]{:S(2)}) %collective-permute-start.11) | collective-permute-done | bytes 131104 | tf_op jit(solution)/shard_map/ppermute | solution.py:203
  399.6 3.4 collective-permute-done.10
  403.0 2.1 convert_reduce_fusion
  406.7 12.1 %shard_map.123 = f32[4096,64]{1,0:T(8,128)} custom-call(s32[3712]{0:T(1024)} %pad_add_fusion.t_ref, f32[4096,64]{1,0:T(8,128)} %convolution_add_fusion.1.base_ref, f32[3712,64]{1,0:T(8,128)} %pad_maximum_fusion.upd_ref), custom_call_target="tpu_custom_call" | custom-call | tf_op jit(solution)/shard_map/pallas_call | solution.py:134
  418.9 2.3 convolution_bitcast_fusion
  422.4 14.7 %all_to_all.44 = f32[32,1,1200]{2,1,0:T(1,128)S(1)} all-to-all(f32[32,1,1200]{2,1,0:T(1,128)S(1)} %all_to_all.34), channel_id=1, replica_groups=mesh['dom'=32,'feat'=4] {'dom'}, dimensions={0} | all-to-all | bytes 307200 | tf_op jit(solution)/shard_map/all_to_all | solution.py:167
  437.3 11.5 %all_to_all.45 = f32[32,1,1200]{2,1,0:T(1,128)S(1)} all-to-all(f32[32,1,1200]{2,1,0:T(1,128)S(1)} %broadcast_in_dim.83), channel_id=1, replica_groups=mesh['dom'=32,'feat'=4] {'dom'}, dimensions={0} | all-to-all | bytes 307200 | tf_op jit(solution)/shard_map/all_to_all | solution.py:169
  (132 shorter events, 36.5 us)
Async XLA Ops:
  7.2 258.1 %copy-start = (bf16[172,256]{1,0:T(8,128)(2,1)S(1)}, bf16[172,256]{1,0:T(8,128)(2,1)}, u32[]{:S(2)}) copy-start(bf16[172,256]{1,0:T(8,128)(2,1)} %param.21) | copy-start | bytes 264196
  7.2 39.1 %collective-permute-start.2 = (bf16[32,4096]{1,0:T(8,128)(2,1)}, bf16[32,4096]{1,0:T(8,128)(2,1)S(1)}, u32[]{:S(2)}, u32[]{:S(2)}) collective-permute-start(bf16[32,4096]{1,0:T(8,128)(2,1)} %param.13), channel_id=1, source_target_pairs={{0,1},{1,2},{2,3},{3,0},{4,5},{5,6},{6,7},{7,4},{8,9},{9,10},{10,1... | collective-permute-start | bytes 786440 | tf_op jit(solution)/shard_map/ppermute | solution.py:105
  9.4 36.9 %collective-permute-start.1 = (bf16[32,4096]{1,0:T(8,128)(2,1)}, bf16[32,4096]{1,0:T(8,128)(2,1)S(1)}, u32[]{:S(2)}, u32[]{:S(2)}) collective-permute-start(bf16[32,4096]{1,0:T(8,128)(2,1)} %param.13), channel_id=1, source_target_pairs={{0,2},{1,3},{2,0},{3,1},{4,6},{5,7},{6,4},{7,5},{8,10},{9,11},{10,... | collective-permute-start | bytes 786440 | tf_op jit(solution)/shard_map/ppermute | solution.py:105
  12.0 30.4 %collective-permute-start = (bf16[32,4096]{1,0:T(8,128)(2,1)}, bf16[32,4096]{1,0:T(8,128)(2,1)}, u32[]{:S(2)}, u32[]{:S(2)}) collective-permute-start(bf16[32,4096]{1,0:T(8,128)(2,1)} %param.13), channel_id=1, source_target_pairs={{0,3},{1,0},{2,1},{3,2},{4,7},{5,4},{6,5},{7,6},{8,11},{9,8},{10,9... | collective-permute-start | bytes 786440 | tf_op jit(solution)/shard_map/ppermute | solution.py:105
  14.5 24.4 %copy-start.4 = (bf16[32,4096]{0,1:T(8,128)(2,1)}, bf16[32,4096]{0,1:T(8,128)(2,1)S(1)}, u32[]{:S(2)}) copy-start(bf16[32,4096]{0,1:T(8,128)(2,1)S(1)} %copy.109) | copy-start | bytes 786436
  19.3 8.2 %copy-start.22 = (s32[640]{0:T(1024)S(1)}, s32[640]{0:T(1024)}, u32[]{:S(2)}) copy-start(s32[640]{0:T(1024)} %param.15) | copy-start | bytes 7684
  20.3 42.7 %collective-permute-start.3 = (bf16[1024,32]{1,0:T(8,128)(2,1)}, bf16[1024,32]{1,0:T(8,128)(2,1)}, u32[]{:S(2)}, u32[]{:S(2)}) collective-permute-start(bf16[1024,32]{1,0:T(8,128)(2,1)} %broadcast_select_fusion.5), channel_id=1, source_target_pairs={{0,4},{4,0},{8,12},{12,8},{16,20},{20,16},{24,28},{28,24},{32,36},... | collective-permute-start | bytes 196616 | tf_op jit(solution)/shard_map/ppermute | solution.py:203
  25.9 37.0 %collective-permute-start.4 = (bf16[1024,32]{1,0:T(8,128)(2,1)}, bf16[1024,32]{1,0:T(8,128)(2,1)}, u32[]{:S(2)}, u32[]{:S(2)}) collective-permute-start(bf16[1024,32]{1,0:T(8,128)(2,1)} %broadcast_select_fusion.4), channel_id=1, source_target_pairs={{0,8},{4,12},{8,0},{12,4},{16,24},{20,28},{24,16},{28,20},{32,40},... | collective-permute-start | bytes 196616 | tf_op jit(solution)/shard_map/ppermute | solution.py:203
  31.1 27.6 %all-to-all-start = ((bf16[32,640,32]{1,2,0:T(8,128)(2,1)}), bf16[32,640,32]{1,2,0:T(8,128)(2,1)S(1)}, u32[]{:S(2)}, u32[]{:S(2)}) async-start(bf16[32,640,32]{1,2,0:T(8,128)(2,1)} %broadcast_in_dim.77), calls=%async_computation | async-start | bytes 2621440 | tf_op jit(solution)/shard_map/all_to_all | solution.py:226
  38.9 7.4 %copy-start.13 = (bf16[32,4096]{1,0:T(8,128)(2,1)S(1)}, bf16[32,4096]{1,0:T(8,128)(2,1)}, u32[]{:S(2)}) copy-start(bf16[32,4096]{1,0:T(8,128)(2,1)} %param.13) | copy-start | bytes 786436
  42.4 20.6 %collective-permute-start.5 = (bf16[1024,32]{1,0:T(8,128)(2,1)S(1)}, bf16[1024,32]{1,0:T(8,128)(2,1)S(1)}, u32[]{:S(2)}, u32[]{:S(2)}) collective-permute-start(bf16[1024,32]{1,0:T(8,128)(2,1)S(1)} %broadcast_select_fusion.3), channel_id=1, source_target_pairs={{0,16},{4,20},{8,24},{12,28},{16,0},{20,4},{24,8},{28,12},{32,48},... | collective-permute-start | bytes 196616 | tf_op jit(solution)/shard_map/ppermute | solution.py:203
  62.9 0.7 copy-start.14
  110.1 5.0 %copy-start.9 = (bf16[4,32,4096]{2,1,0:T(8,128)(2,1)S(1)}, bf16[4,32,4096]{2,1,0:T(8,128)(2,1)}, u32[]{:S(2)}) copy-start(bf16[4,32,4096]{2,1,0:T(8,128)(2,1)} %constant_dynamic-slice_fusion) | copy-start | bytes 3145732
  110.1 5.0 %copy-start.23 = (bf16[64,128]{1,0:T(8,128)(2,1)S(1)}, bf16[64,128]{1,0:T(8,128)(2,1)}, u32[]{:S(2)}) copy-start(bf16[64,128]{1,0:T(8,128)(2,1)} %param.18) | copy-start | bytes 49156
  111.5 18.2 %all-to-all-start.1 = ((bf16[4,32,4096]{2,1,0:T(8,128)(2,1)}), bf16[4,32,4096]{2,1,0:T(8,128)(2,1)S(1)}, u32[]{:S(2)}, u32[]{:S(2)}) async-start(bf16[4,32,4096]{2,1,0:T(8,128)(2,1)} %broadcast_in_dim.78), calls=%async_computation.1 | async-start | bytes 2097152 | tf_op jit(solution)/shard_map/all_to_all | solution.py:97
  115.1 14.7 %copy-start.24 = (bf16[64,128]{1,0:T(8,128)(2,1)S(1)}, bf16[64,128]{1,0:T(8,128)(2,1)}, u32[]{:S(2)}) copy-start(bf16[64,128]{1,0:T(8,128)(2,1)} %param.19) | copy-start | bytes 49156
  129.7 2.5 copy-start.11
  132.2 18.0 %copy-start.2 = (bf16[4096,64]{1,0:T(8,128)(2,1)}, bf16[4096,64]{1,0:T(8,128)(2,1)S(1)}, u32[]{:S(2)}) copy-start(bf16[4096,64]{1,0:T(8,128)(2,1)S(1)} %fusion.2.refs_0_) | copy-start | bytes 1572868
  136.4 40.1 %all-to-all-start.2 = ((bf16[32,640,64]{1,2,0:T(8,128)(2,1)}), bf16[32,640,64]{1,2,0:T(8,128)(2,1)}, u32[]{:S(2)}, u32[]{:S(2)}) async-start(bf16[32,640,64]{1,2,0:T(8,128)(2,1)} %broadcast_in_dim.81), calls=%async_computation.2 | async-start | bytes 5242880 | tf_op jit(solution)/shard_map/all_to_all | solution.py:226
  142.5 97.2 %all-gather.2.cloned.1.call-start = ((), (), s32[]{:S(2)}) async-start(), calls=%async_computation.7 | async-start | bytes 2621440 | tf_op jit(solution)/shard_map/all_gather | solution.py:280
  154.1 28.5 %collective-permute-start.6 = (bf16[1024,64]{1,0:T(8,128)(2,1)S(1)}, bf16[1024,64]{1,0:T(8,128)(2,1)S(1)}, u32[]{:S(2)}, u32[]{:S(2)}) collective-permute-start(bf16[1024,64]{1,0:T(8,128)(2,1)S(1)} %broadcast_select_fusion.2), channel_id=1, source_target_pairs={{0,4},{4,0},{8,12},{12,8},{16,20},{20,16},{24,28},{28,24},{32,36},... | collective-permute-start | bytes 393224 | tf_op jit(solution)/shard_map/ppermute | solution.py:203
  154.4 28.1 %collective-permute-start.7 = (bf16[1024,64]{1,0:T(8,128)(2,1)S(1)}, bf16[1024,64]{1,0:T(8,128)(2,1)S(1)}, u32[]{:S(2)}, u32[]{:S(2)}) collective-permute-start(bf16[1024,64]{1,0:T(8,128)(2,1)S(1)} %broadcast_select_fusion.1), channel_id=1, source_target_pairs={{0,8},{4,12},{8,0},{12,4},{16,24},{20,28},{24,16},{28,20},{32,40},... | collective-permute-start | bytes 393224 | tf_op jit(solution)/shard_map/ppermute | solution.py:203
  155.9 30.1 %collective-permute-start.8 = (bf16[1024,64]{1,0:T(8,128)(2,1)S(1)}, bf16[1024,64]{1,0:T(8,128)(2,1)S(1)}, u32[]{:S(2)}, u32[]{:S(2)}) collective-permute-start(bf16[1024,64]{1,0:T(8,128)(2,1)S(1)} %broadcast_select_fusion), channel_id=1, source_target_pairs={{0,16},{4,20},{8,24},{12,28},{16,0},{20,4},{24,8},{28,12},{32,48},... | collective-permute-start | bytes 393224 | tf_op jit(solution)/shard_map/ppermute | solution.py:203
  182.5 3.5 copy-start.15
  182.5 3.5 copy-start.16
  186.0 0.7 copy-start.17
  235.1 4.6 %copy-start.18 = (bf16[172,256]{1,0:T(8,128)(2,1)S(1)}, bf16[172,256]{1,0:T(8,128)(2,1)}, u32[]{:S(2)}) copy-start(bf16[172,256]{1,0:T(8,128)(2,1)} %param.20) | copy-start | bytes 264196
  235.1 30.1 %all-to-all-start.3 = ((bf16[4,64,4096]{2,1,0:T(8,128)(2,1)}), bf16[4,64,4096]{2,1,0:T(8,128)(2,1)}, u32[]{:S(2)}, u32[]{:S(2)}) async-start(bf16[4,64,4096]{2,1,0:T(8,128)(2,1)} %broadcast_in_dim.82), calls=%async_computation.3 | async-start | bytes 4194304 | tf_op jit(solution)/shard_map/all_to_all | solution.py:97
  265.2 2.4 copy-start.25
  268.2 1.1 copy-start.5
  343.0 4.5 copy-start.7
  353.7 7.2 %copy-start.21 = (s32[3,1024]{1,0:T(4,128)S(1)}, s32[3,1024]{1,0:T(4,128)}, u32[]{:S(2)}) copy-start(s32[3,1024]{1,0:T(4,128)} %param.16) | copy-start | bytes 36868
  353.7 49.3 %all-to-all-start.4 = ((bf16[32,640,64]{1,2,0:T(8,128)(2,1)}), bf16[32,640,64]{1,2,0:T(8,128)(2,1)}, u32[]{:S(2)}, u32[]{:S(2)}) async-start(bf16[32,640,64]{1,2,0:T(8,128)(2,1)} %copy.122), calls=%async_computation.4 | async-start | bytes 5242880 | tf_op jit(solution)/shard_map/all_to_all | solution.py:299
  360.9 6.2 %copy-start.6 = (bf16[172,4096]{1,0:T(8,128)(2,1)S(1)}, bf16[172,4096]{1,0:T(8,128)(2,1)}, u32[]{:S(2)}) copy-start(bf16[172,4096]{1,0:T(8,128)(2,1)} %copy-done.5) | copy-start | bytes 4227076
  363.6 5.7 %copy-start.19 = (bf16[172,256]{1,0:T(8,128)(2,1)S(1)}, bf16[172,256]{1,0:T(8,128)(2,1)}, u32[]{:S(2)}) copy-start(bf16[172,256]{1,0:T(8,128)(2,1)} %param.20) | copy-start | bytes 264196
  363.6 10.9 %collective-permute-start.9 = (bf16[1024,64]{1,0:T(8,128)(2,1)}, bf16[1024,64]{1,0:T(8,128)(2,1)S(1)}, u32[]{:S(2)}, u32[]{:S(2)}) collective-permute-start(bf16[1024,64]{1,0:T(8,128)(2,1)} %get-tuple-element.30), channel_id=1, source_target_pairs={{0,4},{4,0},{8,12},{12,8},{16,20},{20,16},{24,28},{28,24},{32,36},... | collective-permute-start | bytes 393224 | tf_op jit(solution)/shard_map/ppermute | solution.py:203
  363.9 35.6 %collective-permute-start.11 = (bf16[1024,64]{1,0:T(8,128)(2,1)}, bf16[1024,64]{1,0:T(8,128)(2,1)S(1)}, u32[]{:S(2)}, u32[]{:S(2)}) collective-permute-start(bf16[1024,64]{1,0:T(8,128)(2,1)} %get-tuple-element.31), channel_id=1, source_target_pairs={{0,16},{4,20},{8,24},{12,28},{16,0},{20,4},{24,8},{28,12},{32,48},... | collective-permute-start | bytes 393224 | tf_op jit(solution)/shard_map/ppermute | solution.py:203
  366.9 36.1 %collective-permute-start.10 = (bf16[1024,64]{1,0:T(8,128)(2,1)}, bf16[1024,64]{1,0:T(8,128)(2,1)S(1)}, u32[]{:S(2)}, u32[]{:S(2)}) collective-permute-start(bf16[1024,64]{1,0:T(8,128)(2,1)} %get-tuple-element.32), channel_id=1, source_target_pairs={{0,8},{4,12},{8,0},{12,4},{16,24},{20,28},{24,16},{28,20},{32,40},... | collective-permute-start | bytes 393224 | tf_op jit(solution)/shard_map/ppermute | solution.py:203
  369.3 3.9 copy-start.3
  406.7 12.1 %copy-start.12 = (bf16[4,32,4096]{2,1,0:T(8,128)(2,1)S(1)}, bf16[4,32,4096]{2,1,0:T(8,128)(2,1)}, u32[]{:S(2)}) copy-start(bf16[4,32,4096]{2,1,0:T(8,128)(2,1)} %copy-done.11) | copy-start | bytes 3145732
  418.9 2.3 copy-start.8
  418.9 2.5 copy-start.10
  421.3 0.8 copy-start.20
  421.3 30.4 %copy-start.1 = (bf16[172,256]{1,0:T(8,128)(2,1)S(1)}, bf16[172,256]{1,0:T(8,128)(2,1)}, u32[]{:S(2)}) copy-start(bf16[172,256]{1,0:T(8,128)(2,1)} %param.21) | copy-start | bytes 264196
Sparse Core Ops, SparseCore 0:
  145.0 29.7 all-gather.1

commit v18 on v17

--- a/solution.py
+++ b/solution.py
@@ -72,7 +72,7 @@
                     acc_ref[pl.ds(s, 1), :] = acc_ref[pl.ds(s, 1), :] + x
             return carry
 
-        lax.fori_loop(0, nodes, step, 0, unroll=2)
+        lax.fori_loop(0, nodes, step, 0, unroll=4)
         total = out_ref[...]
         for acc_ref in extra_refs:
             total = total + acc_ref[...]

time: 460 us -> 455 us (0.989)
  Pallas kernels: 167 us -> 162 us
    pallas_call x1, Pallas kernels: 65.7 us -> 60.8 us  [scatter_mean(): pl.pallas_call(kernel, in_specs=[pl.BlockSpec(memory_space=pltpu.SMEM), p...]
where the time goes in v18:
time: 455 us; the launch traced here: 454 us
  Pallas kernels  162 us (36%)
  waiting for transfers between devices  96.4 us (21%)
  local copies, waits for them, and re-layouts  66.7 us (15%)
  starting transfers between devices  48.9 us (11%)
  blocking collectives  26.3 us (6%)
  other arithmetic  19.6 us (4%)
  matrix products  18.6 us (4%)
  between operations  14.7 us (3%)
    pallas_call x2, Pallas kernels, gather_mean(): pl.pallas_call(kernel, in_specs=[pl.BlockSpec(memory_space=pltpu.SMEM)] +...  89.5 us
    pallas_call x1, Pallas kernels, scatter_mean(): pl.pallas_call(kernel, in_specs=[pl.BlockSpec(memory_space=pltpu.SMEM), p...  60.8 us
    all_to_all x2, waiting for transfers between devices, spread_gather(): gathered = lax.all_to_all(copies, axis, 0, 0, tiled=True)  36.2 us
    ppermute x9, waiting for transfers between devices, partner(): return lax.ppermute(value, axis, pairs)  31.8 us
    all_to_all x2, waiting for transfers between devices, source_table(): lax.all_to_all(jnp.broadcast_to(hub_local[None], (owners,) + hub_local.sh...  28.4 us
    gather x6, local copies, waits for them, and re-layouts, source_table(): jnp.take(local_rows, send_rows[bit_index], axis=0)  19.2 us
    all_to_all x1, blocking collectives, exchange_sum(): reduced = jnp.sum(lax.all_to_all(padded, axis, 0, 0, tiled=True), axis=0)  14.7 us
    all_to_all x2, starting transfers between devices, source_table(): lax.all_to_all(jnp.broadcast_to(hub_local[None], (owners,) + hub_local.sh...  13.9 us
  transfers between devices with their start and end apart: 18, of which 7 were waited for; matrix products, arithmetic and copies ran while one was open for 13% of the time, Pallas kernels for 10%

profile of v18, /device:TPU:1, one launch (start us, length us, event | category | flops | bytes accessed | tf_op | source)
XLA Modules:
  0.0 453.7 jit_solution(1033080494271510383)
XLA Ops:
  7.2 2.2 collective-permute-start.2
  9.4 2.6 collective-permute-start.1
  16.1 3.2 gather_fusion.2
  21.8 3.2 gather_fusion.3
  27.6 2.0 gather_fusion
  31.1 7.8 %all-to-all-start = ((bf16[32,640,32]{1,2,0:T(8,128)(2,1)}), bf16[32,640,32]{1,2,0:T(8,128)(2,1)S(1)}, u32[]{:S(2)}, u32[]{:S(2)}) async-start(bf16[32,640,32]{1,2,0:T(8,128)(2,1)} %broadcast_in_dim.77), calls=%async_computation | async-start | bytes 2621440 | tf_op jit(solution)/shard_map/all_to_all | solution.py:226
  38.9 3.2 gather_fusion.4
  42.4 2.9 collective-permute-start.5
  48.5 10.2 %all-to-all-done = bf16[32,640,32]{1,2,0:T(8,128)(2,1)S(1)} async-done(((bf16[32,640,32]{1,2,0:T(8,128)(2,1)}), bf16[32,640,32]{1,2,0:T(8,128)(2,1)S(1)}, u32[]{:S(2)}, u32[]{:S(2)}) %all-to-all-start) | async-done | bytes 1310752 | tf_op jit(solution)/shard_map/all_to_all | solution.py:226
  58.7 4.3 copy.111
  63.6 44.8 %shard_map.120 = f32[4096,32]{1,0:T(8,128)} custom-call(s32[8,4096]{1,0:T(8,128)} %nb_ref.5, bf16[4096,32]{1,0:T(8,128)(2,1)} %bitcast.66, bf16[20480,32]{1,0:T(8,128)(2,1)} %bitcast.67, bf16[1024,32]{1,0:T(8,128)(2,1)} %collective-permute-done.3.refs_2_, bf16[1024,32]{1,0:T(8,128)(2,1)} %collective-permute-done.4.refs_3_, bf16[1024,32]{1,0:T(8,128)(2,1)} %copy-done.14, ...), custom_call_target="tpu_custom_call" | custom-call | tf_op jit(solution)/shard_map/pallas_call | solution.py:46
  108.4 1.7 convert_bitcast_fusion
  111.5 3.5 all-to-all-start.1
  115.1 1.8 fusion.22
  116.9 12.8 %all-to-all-done.1 = bf16[4,32,4096]{2,1,0:T(8,128)(2,1)S(1)} async-done(((bf16[4,32,4096]{2,1,0:T(8,128)(2,1)}), bf16[4,32,4096]{2,1,0:T(8,128)(2,1)S(1)}, u32[]{:S(2)}, u32[]{:S(2)}) %all-to-all-start.1) | async-done | bytes 1048608 | tf_op jit(solution)/shard_map/all_to_all | solution.py:97
  129.7 2.5 fusion.2.refs_0_
  132.2 2.0 gather_fusion.1
  134.5 1.8 broadcast_in_dim.81
  136.4 6.1 %all-to-all-start.2 = ((bf16[32,640,64]{1,2,0:T(8,128)(2,1)}), bf16[32,640,64]{1,2,0:T(8,128)(2,1)}, u32[]{:S(2)}, u32[]{:S(2)}) async-start(bf16[32,640,64]{1,2,0:T(8,128)(2,1)} %broadcast_in_dim.81), calls=%async_computation.2 | async-start | bytes 5242880 | tf_op jit(solution)/shard_map/all_to_all | solution.py:226
  143.8 3.2 gather_fusion.7
  147.0 3.2 gather_fusion.6
  150.2 3.2 gather_fusion.5
  155.9 2.4 collective-permute-start.8
  158.3 18.2 %all-to-all-done.2 = bf16[32,640,64]{1,2,0:T(8,128)(2,1)} async-done(((bf16[32,640,64]{1,2,0:T(8,128)(2,1)}), bf16[32,640,64]{1,2,0:T(8,128)(2,1)}, u32[]{:S(2)}, u32[]{:S(2)}) %all-to-all-start.2) | async-done | bytes 2621472 | tf_op jit(solution)/shard_map/all_to_all | solution.py:226
  176.5 6.0 %copy.117 = bf16[32,640,64]{2,1,0:T(8,128)(2,1)} copy(bf16[32,640,64]{1,2,0:T(8,128)(2,1)} %all-to-all-done.2) | data formatting | bytes 5242880 | tf_op jit(solution)/shard_map/all_to_all | solution.py:226
  182.5 3.5 collective-permute-done.8.refs_4_
  186.7 44.8 %shard_map.121 = f32[4096,64]{1,0:T(8,128)} custom-call(s32[8,4096]{1,0:T(8,128)} %nb_ref.5, bf16[4096,64]{1,0:T(8,128)(2,1)} %copy-done.2, bf16[20480,64]{1,0:T(8,128)(2,1)} %bitcast.68, bf16[1024,64]{1,0:T(8,128)(2,1)} %copy-done.15, bf16[1024,64]{1,0:T(8,128)(2,1)} %copy-done.16, bf16[1024,64]{1,0:T(8,128)(2,1)} %copy-done.17, bf16[64,4096]{1,0:T(8,128)(2,1)} %copy.115.refs_5_), custom_call_target="tpu_custom_call" | custom-call | tf_op jit(solution)/shard_map/pallas_call | solution.py:46
  231.5 1.7 convert_bitcast_fusion.1
  235.1 4.6 %all-to-all-start.3 = ((bf16[4,64,4096]{2,1,0:T(8,128)(2,1)}), bf16[4,64,4096]{2,1,0:T(8,128)(2,1)}, u32[]{:S(2)}, u32[]{:S(2)}) async-start(bf16[4,64,4096]{2,1,0:T(8,128)(2,1)} %broadcast_in_dim.82), calls=%async_computation.3 | async-start | bytes 4194304 | tf_op jit(solution)/shard_map/all_to_all | solution.py:97
  239.7 2.1 fusion.23
  241.9 23.3 %all-to-all-done.3 = bf16[4,64,4096]{2,1,0:T(8,128)(2,1)} async-done(((bf16[4,64,4096]{2,1,0:T(8,128)(2,1)}), bf16[4,64,4096]{2,1,0:T(8,128)(2,1)}, u32[]{:S(2)}, u32[]{:S(2)}) %all-to-all-start.3) | async-done | bytes 2097184 | tf_op jit(solution)/shard_map/all_to_all | solution.py:97
  265.2 2.4 fusion.21
  271.7 60.8 %shard_map.122 = f32[27648,64]{1,0:T(8,128)} custom-call(s32[8,4096]{1,0:T(8,128)} %nb_ref.5, f32[4096,64]{1,0:T(8,128)} %convert_element_type.59.rows_ref), custom_call_target="tpu_custom_call" | custom-call | tf_op jit(solution)/shard_map/pallas_call | solution.py:81
  332.5 5.7 %convert.6 = bf16[27648,64]{1,0:T(8,128)(2,1)S(1)} convert(f32[27648,64]{1,0:T(8,128)} %shard_map.122) | non-fusion elementwise | flops 1769472 | bytes 10616832 | tf_op jit(solution)/shard_map/convert.3
  338.2 3.4 slice.82
  342.7 6.1 %copy.122 = bf16[32,640,64]{1,2,0:T(8,128)(2,1)} copy(bf16[32,640,64]{2,1,0:T(8,128)(2,1)} %bitcast.69) | data formatting | bytes 5242880 | tf_op jit(solution)/shard_map/all_to_all | solution.py:299
  348.9 7.2 %all-to-all-start.4 = ((bf16[32,640,64]{1,2,0:T(8,128)(2,1)}), bf16[32,640,64]{1,2,0:T(8,128)(2,1)}, u32[]{:S(2)}, u32[]{:S(2)}) async-start(bf16[32,640,64]{1,2,0:T(8,128)(2,1)} %copy.122), calls=%async_computation.4 | async-start | bytes 5242880 | tf_op jit(solution)/shard_map/all_to_all | solution.py:299
  356.7 2.0 fusion.17
  359.1 3.0 collective-permute-start.11
  362.3 2.1 fusion.6
  364.5 3.9 convolution_add_fusion.1.base_ref
  369.7 25.0 %collective-permute-done.11 = bf16[1024,64]{1,0:T(8,128)(2,1)S(1)} collective-permute-done((bf16[1024,64]{1,0:T(8,128)(2,1)}, bf16[1024,64]{1,0:T(8,128)(2,1)S(1)}, u32[]{:S(2)}, u32[]{:S(2)}) %collective-permute-start.11) | collective-permute-done | bytes 131104 | tf_op jit(solution)/shard_map/ppermute | solution.py:203
  394.7 3.4 collective-permute-done.10
  398.2 2.1 convert_reduce_fusion
  401.9 12.1 %shard_map.123 = f32[4096,64]{1,0:T(8,128)} custom-call(s32[3712]{0:T(1024)} %pad_add_fusion.t_ref, f32[4096,64]{1,0:T(8,128)} %convolution_add_fusion.1.base_ref, f32[3712,64]{1,0:T(8,128)} %pad_maximum_fusion.upd_ref), custom_call_target="tpu_custom_call" | custom-call | tf_op jit(solution)/shard_map/pallas_call | solution.py:134
  414.0 2.3 convolution_bitcast_fusion
  417.6 14.7 %all_to_all.44 = f32[32,1,1200]{2,1,0:T(1,128)S(1)} all-to-all(f32[32,1,1200]{2,1,0:T(1,128)S(1)} %all_to_all.34), channel_id=1, replica_groups=mesh['dom'=32,'feat'=4] {'dom'}, dimensions={0} | all-to-all | bytes 307200 | tf_op jit(solution)/shard_map/all_to_all | solution.py:167
  432.5 11.5 %all_to_all.45 = f32[32,1,1200]{2,1,0:T(1,128)S(1)} all-to-all(f32[32,1,1200]{2,1,0:T(1,128)S(1)} %broadcast_in_dim.83), channel_id=1, replica_groups=mesh['dom'=32,'feat'=4] {'dom'}, dimensions={0} | all-to-all | bytes 307200 | tf_op jit(solution)/shard_map/all_to_all | solution.py:169
  (132 shorter events, 36.5 us)
Async XLA Ops:
  7.2 258.1 %copy-start = (bf16[172,256]{1,0:T(8,128)(2,1)S(1)}, bf16[172,256]{1,0:T(8,128)(2,1)}, u32[]{:S(2)}) copy-start(bf16[172,256]{1,0:T(8,128)(2,1)} %param.21) | copy-start | bytes 264196
  7.2 39.1 %collective-permute-start.2 = (bf16[32,4096]{1,0:T(8,128)(2,1)}, bf16[32,4096]{1,0:T(8,128)(2,1)S(1)}, u32[]{:S(2)}, u32[]{:S(2)}) collective-permute-start(bf16[32,4096]{1,0:T(8,128)(2,1)} %param.13), channel_id=1, source_target_pairs={{0,1},{1,2},{2,3},{3,0},{4,5},{5,6},{6,7},{7,4},{8,9},{9,10},{10,1... | collective-permute-start | bytes 786440 | tf_op jit(solution)/shard_map/ppermute | solution.py:105
  9.4 36.9 %collective-permute-start.1 = (bf16[32,4096]{1,0:T(8,128)(2,1)}, bf16[32,4096]{1,0:T(8,128)(2,1)S(1)}, u32[]{:S(2)}, u32[]{:S(2)}) collective-permute-start(bf16[32,4096]{1,0:T(8,128)(2,1)} %param.13), channel_id=1, source_target_pairs={{0,2},{1,3},{2,0},{3,1},{4,6},{5,7},{6,4},{7,5},{8,10},{9,11},{10,... | collective-permute-start | bytes 786440 | tf_op jit(solution)/shard_map/ppermute | solution.py:105
  12.0 30.4 %collective-permute-start = (bf16[32,4096]{1,0:T(8,128)(2,1)}, bf16[32,4096]{1,0:T(8,128)(2,1)}, u32[]{:S(2)}, u32[]{:S(2)}) collective-permute-start(bf16[32,4096]{1,0:T(8,128)(2,1)} %param.13), channel_id=1, source_target_pairs={{0,3},{1,0},{2,1},{3,2},{4,7},{5,4},{6,5},{7,6},{8,11},{9,8},{10,9... | collective-permute-start | bytes 786440 | tf_op jit(solution)/shard_map/ppermute | solution.py:105
  14.5 24.4 %copy-start.4 = (bf16[32,4096]{0,1:T(8,128)(2,1)}, bf16[32,4096]{0,1:T(8,128)(2,1)S(1)}, u32[]{:S(2)}) copy-start(bf16[32,4096]{0,1:T(8,128)(2,1)S(1)} %copy.109) | copy-start | bytes 786436
  19.3 8.2 %copy-start.22 = (s32[640]{0:T(1024)S(1)}, s32[640]{0:T(1024)}, u32[]{:S(2)}) copy-start(s32[640]{0:T(1024)} %param.15) | copy-start | bytes 7684
  20.3 42.6 %collective-permute-start.3 = (bf16[1024,32]{1,0:T(8,128)(2,1)}, bf16[1024,32]{1,0:T(8,128)(2,1)}, u32[]{:S(2)}, u32[]{:S(2)}) collective-permute-start(bf16[1024,32]{1,0:T(8,128)(2,1)} %broadcast_select_fusion.5), channel_id=1, source_target_pairs={{0,4},{4,0},{8,12},{12,8},{16,20},{20,16},{24,28},{28,24},{32,36},... | collective-permute-start | bytes 196616 | tf_op jit(solution)/shard_map/ppermute | solution.py:203
  25.9 37.0 %collective-permute-start.4 = (bf16[1024,32]{1,0:T(8,128)(2,1)}, bf16[1024,32]{1,0:T(8,128)(2,1)}, u32[]{:S(2)}, u32[]{:S(2)}) collective-permute-start(bf16[1024,32]{1,0:T(8,128)(2,1)} %broadcast_select_fusion.4), channel_id=1, source_target_pairs={{0,8},{4,12},{8,0},{12,4},{16,24},{20,28},{24,16},{28,20},{32,40},... | collective-permute-start | bytes 196616 | tf_op jit(solution)/shard_map/ppermute | solution.py:203
  31.1 27.6 %all-to-all-start = ((bf16[32,640,32]{1,2,0:T(8,128)(2,1)}), bf16[32,640,32]{1,2,0:T(8,128)(2,1)S(1)}, u32[]{:S(2)}, u32[]{:S(2)}) async-start(bf16[32,640,32]{1,2,0:T(8,128)(2,1)} %broadcast_in_dim.77), calls=%async_computation | async-start | bytes 2621440 | tf_op jit(solution)/shard_map/all_to_all | solution.py:226
  38.9 7.4 %copy-start.13 = (bf16[32,4096]{1,0:T(8,128)(2,1)S(1)}, bf16[32,4096]{1,0:T(8,128)(2,1)}, u32[]{:S(2)}) copy-start(bf16[32,4096]{1,0:T(8,128)(2,1)} %param.13) | copy-start | bytes 786436
  42.4 20.6 %collective-permute-start.5 = (bf16[1024,32]{1,0:T(8,128)(2,1)S(1)}, bf16[1024,32]{1,0:T(8,128)(2,1)S(1)}, u32[]{:S(2)}, u32[]{:S(2)}) collective-permute-start(bf16[1024,32]{1,0:T(8,128)(2,1)S(1)} %broadcast_select_fusion.3), channel_id=1, source_target_pairs={{0,16},{4,20},{8,24},{12,28},{16,0},{20,4},{24,8},{28,12},{32,48},... | collective-permute-start | bytes 196616 | tf_op jit(solution)/shard_map/ppermute | solution.py:203
  62.9 0.7 copy-start.14
  110.1 5.0 %copy-start.9 = (bf16[4,32,4096]{2,1,0:T(8,128)(2,1)S(1)}, bf16[4,32,4096]{2,1,0:T(8,128)(2,1)}, u32[]{:S(2)}) copy-start(bf16[4,32,4096]{2,1,0:T(8,128)(2,1)} %constant_dynamic-slice_fusion) | copy-start | bytes 3145732
  110.1 5.0 %copy-start.23 = (bf16[64,128]{1,0:T(8,128)(2,1)S(1)}, bf16[64,128]{1,0:T(8,128)(2,1)}, u32[]{:S(2)}) copy-start(bf16[64,128]{1,0:T(8,128)(2,1)} %param.18) | copy-start | bytes 49156
  111.5 18.2 %all-to-all-start.1 = ((bf16[4,32,4096]{2,1,0:T(8,128)(2,1)}), bf16[4,32,4096]{2,1,0:T(8,128)(2,1)S(1)}, u32[]{:S(2)}, u32[]{:S(2)}) async-start(bf16[4,32,4096]{2,1,0:T(8,128)(2,1)} %broadcast_in_dim.78), calls=%async_computation.1 | async-start | bytes 2097152 | tf_op jit(solution)/shard_map/all_to_all | solution.py:97
  115.1 14.7 %copy-start.24 = (bf16[64,128]{1,0:T(8,128)(2,1)S(1)}, bf16[64,128]{1,0:T(8,128)(2,1)}, u32[]{:S(2)}) copy-start(bf16[64,128]{1,0:T(8,128)(2,1)} %param.19) | copy-start | bytes 49156
  129.7 2.5 copy-start.11
  132.2 18.0 %copy-start.2 = (bf16[4096,64]{1,0:T(8,128)(2,1)}, bf16[4096,64]{1,0:T(8,128)(2,1)S(1)}, u32[]{:S(2)}) copy-start(bf16[4096,64]{1,0:T(8,128)(2,1)S(1)} %fusion.2.refs_0_) | copy-start | bytes 1572868
  136.4 40.1 %all-to-all-start.2 = ((bf16[32,640,64]{1,2,0:T(8,128)(2,1)}), bf16[32,640,64]{1,2,0:T(8,128)(2,1)}, u32[]{:S(2)}, u32[]{:S(2)}) async-start(bf16[32,640,64]{1,2,0:T(8,128)(2,1)} %broadcast_in_dim.81), calls=%async_computation.2 | async-start | bytes 5242880 | tf_op jit(solution)/shard_map/all_to_all | solution.py:226
  142.5 97.2 %all-gather.2.cloned.1.call-start = ((), (), s32[]{:S(2)}) async-start(), calls=%async_computation.7 | async-start | bytes 2621440 | tf_op jit(solution)/shard_map/all_gather | solution.py:280
  154.1 28.5 %collective-permute-start.6 = (bf16[1024,64]{1,0:T(8,128)(2,1)S(1)}, bf16[1024,64]{1,0:T(8,128)(2,1)S(1)}, u32[]{:S(2)}, u32[]{:S(2)}) collective-permute-start(bf16[1024,64]{1,0:T(8,128)(2,1)S(1)} %broadcast_select_fusion.2), channel_id=1, source_target_pairs={{0,4},{4,0},{8,12},{12,8},{16,20},{20,16},{24,28},{28,24},{32,36},... | collective-permute-start | bytes 393224 | tf_op jit(solution)/shard_map/ppermute | solution.py:203
  154.4 28.1 %collective-permute-start.7 = (bf16[1024,64]{1,0:T(8,128)(2,1)S(1)}, bf16[1024,64]{1,0:T(8,128)(2,1)S(1)}, u32[]{:S(2)}, u32[]{:S(2)}) collective-permute-start(bf16[1024,64]{1,0:T(8,128)(2,1)S(1)} %broadcast_select_fusion.1), channel_id=1, source_target_pairs={{0,8},{4,12},{8,0},{12,4},{16,24},{20,28},{24,16},{28,20},{32,40},... | collective-permute-start | bytes 393224 | tf_op jit(solution)/shard_map/ppermute | solution.py:203
  155.9 30.1 %collective-permute-start.8 = (bf16[1024,64]{1,0:T(8,128)(2,1)S(1)}, bf16[1024,64]{1,0:T(8,128)(2,1)S(1)}, u32[]{:S(2)}, u32[]{:S(2)}) collective-permute-start(bf16[1024,64]{1,0:T(8,128)(2,1)S(1)} %broadcast_select_fusion), channel_id=1, source_target_pairs={{0,16},{4,20},{8,24},{12,28},{16,0},{20,4},{24,8},{28,12},{32,48},... | collective-permute-start | bytes 393224 | tf_op jit(solution)/shard_map/ppermute | solution.py:203
  182.5 3.5 copy-start.15
  182.5 3.5 copy-start.16
  186.0 0.7 copy-start.17
  235.1 4.6 %copy-start.18 = (bf16[172,256]{1,0:T(8,128)(2,1)S(1)}, bf16[172,256]{1,0:T(8,128)(2,1)}, u32[]{:S(2)}) copy-start(bf16[172,256]{1,0:T(8,128)(2,1)} %param.20) | copy-start | bytes 264196
  235.1 30.1 %all-to-all-start.3 = ((bf16[4,64,4096]{2,1,0:T(8,128)(2,1)}), bf16[4,64,4096]{2,1,0:T(8,128)(2,1)}, u32[]{:S(2)}, u32[]{:S(2)}) async-start(bf16[4,64,4096]{2,1,0:T(8,128)(2,1)} %broadcast_in_dim.82), calls=%async_computation.3 | async-start | bytes 4194304 | tf_op jit(solution)/shard_map/all_to_all | solution.py:97
  265.2 2.4 copy-start.25
  268.2 1.1 copy-start.5
  338.2 4.5 %copy-start.7 = (bf16[27648,64]{1,0:T(8,128)(2,1)}, bf16[27648,64]{1,0:T(8,128)(2,1)S(1)}, u32[]{:S(2)}) copy-start(bf16[27648,64]{1,0:T(8,128)(2,1)S(1)} %convert.6) | copy-start | bytes 10616836
  348.9 7.2 %copy-start.21 = (s32[3,1024]{1,0:T(4,128)S(1)}, s32[3,1024]{1,0:T(4,128)}, u32[]{:S(2)}) copy-start(s32[3,1024]{1,0:T(4,128)} %param.16) | copy-start | bytes 36868
  348.9 49.3 %all-to-all-start.4 = ((bf16[32,640,64]{1,2,0:T(8,128)(2,1)}), bf16[32,640,64]{1,2,0:T(8,128)(2,1)}, u32[]{:S(2)}, u32[]{:S(2)}) async-start(bf16[32,640,64]{1,2,0:T(8,128)(2,1)} %copy.122), calls=%async_computation.4 | async-start | bytes 5242880 | tf_op jit(solution)/shard_map/all_to_all | solution.py:299
  356.1 6.2 %copy-start.6 = (bf16[172,4096]{1,0:T(8,128)(2,1)S(1)}, bf16[172,4096]{1,0:T(8,128)(2,1)}, u32[]{:S(2)}) copy-start(bf16[172,4096]{1,0:T(8,128)(2,1)} %copy-done.5) | copy-start | bytes 4227076
  358.8 5.7 %copy-start.19 = (bf16[172,256]{1,0:T(8,128)(2,1)S(1)}, bf16[172,256]{1,0:T(8,128)(2,1)}, u32[]{:S(2)}) copy-start(bf16[172,256]{1,0:T(8,128)(2,1)} %param.20) | copy-start | bytes 264196
  358.8 10.9 %collective-permute-start.9 = (bf16[1024,64]{1,0:T(8,128)(2,1)}, bf16[1024,64]{1,0:T(8,128)(2,1)S(1)}, u32[]{:S(2)}, u32[]{:S(2)}) collective-permute-start(bf16[1024,64]{1,0:T(8,128)(2,1)} %get-tuple-element.30), channel_id=1, source_target_pairs={{0,4},{4,0},{8,12},{12,8},{16,20},{20,16},{24,28},{28,24},{32,36},... | collective-permute-start | bytes 393224 | tf_op jit(solution)/shard_map/ppermute | solution.py:203
  359.1 35.6 %collective-permute-start.11 = (bf16[1024,64]{1,0:T(8,128)(2,1)}, bf16[1024,64]{1,0:T(8,128)(2,1)S(1)}, u32[]{:S(2)}, u32[]{:S(2)}) collective-permute-start(bf16[1024,64]{1,0:T(8,128)(2,1)} %get-tuple-element.31), channel_id=1, source_target_pairs={{0,16},{4,20},{8,24},{12,28},{16,0},{20,4},{24,8},{28,12},{32,48},... | collective-permute-start | bytes 393224 | tf_op jit(solution)/shard_map/ppermute | solution.py:203
  362.0 36.1 %collective-permute-start.10 = (bf16[1024,64]{1,0:T(8,128)(2,1)}, bf16[1024,64]{1,0:T(8,128)(2,1)S(1)}, u32[]{:S(2)}, u32[]{:S(2)}) collective-permute-start(bf16[1024,64]{1,0:T(8,128)(2,1)} %get-tuple-element.32), channel_id=1, source_target_pairs={{0,8},{4,12},{8,0},{12,4},{16,24},{20,28},{24,16},{28,20},{32,40},... | collective-permute-start | bytes 393224 | tf_op jit(solution)/shard_map/ppermute | solution.py:203
  364.5 3.9 copy-start.3
  401.9 12.1 %copy-start.12 = (bf16[4,32,4096]{2,1,0:T(8,128)(2,1)S(1)}, bf16[4,32,4096]{2,1,0:T(8,128)(2,1)}, u32[]{:S(2)}) copy-start(bf16[4,32,4096]{2,1,0:T(8,128)(2,1)} %copy-done.11) | copy-start | bytes 3145732
  414.0 2.3 copy-start.8
  414.0 2.5 copy-start.10
  416.5 0.8 copy-start.20
  416.5 30.4 %copy-start.1 = (bf16[172,256]{1,0:T(8,128)(2,1)S(1)}, bf16[172,256]{1,0:T(8,128)(2,1)}, u32[]{:S(2)}) copy-start(bf16[172,256]{1,0:T(8,128)(2,1)} %param.21) | copy-start | bytes 264196
Sparse Core Ops, SparseCore 0:
  145.0 29.7 all-gather.1

commit v19 on v18

--- a/solution.py
+++ b/solution.py
@@ -72,7 +72,7 @@
                     acc_ref[pl.ds(s, 1), :] = acc_ref[pl.ds(s, 1), :] + x
             return carry
 
-        lax.fori_loop(0, nodes, step, 0, unroll=4)
+        lax.fori_loop(0, nodes, step, 0, unroll=8)
         total = out_ref[...]
         for acc_ref in extra_refs:
             total = total + acc_ref[...]

time: 455 us -> 453 us (level)
  no operation moved by 1% of the time
where the time goes in v19:
time: 453 us; the launch traced here: 451 us
  Pallas kernels  160 us (35%)
  waiting for transfers between devices  96.4 us (21%)
  local copies, waits for them, and re-layouts  66.7 us (15%)
  starting transfers between devices  48.9 us (11%)
  blocking collectives  26.3 us (6%)
  other arithmetic  19.6 us (4%)
  matrix products  18.6 us (4%)
  between operations  14.7 us (3%)
    pallas_call x2, Pallas kernels, gather_mean(): pl.pallas_call(kernel, in_specs=[pl.BlockSpec(memory_space=pltpu.SMEM)] +...  89.5 us
    pallas_call x1, Pallas kernels, scatter_mean(): pl.pallas_call(kernel, in_specs=[pl.BlockSpec(memory_space=pltpu.SMEM), p...  58.4 us
    all_to_all x2, waiting for transfers between devices, spread_gather(): gathered = lax.all_to_all(copies, axis, 0, 0, tiled=True)  36.2 us
    ppermute x9, waiting for transfers between devices, partner(): return lax.ppermute(value, axis, pairs)  31.8 us
    all_to_all x2, waiting for transfers between devices, source_table(): lax.all_to_all(jnp.broadcast_to(hub_local[None], (owners,) + hub_local.sh...  28.4 us
    gather x6, local copies, waits for them, and re-layouts, source_table(): jnp.take(local_rows, send_rows[bit_index], axis=0)  19.2 us
    all_to_all x1, blocking collectives, exchange_sum(): reduced = jnp.sum(lax.all_to_all(padded, axis, 0, 0, tiled=True), axis=0)  14.7 us
    all_to_all x2, starting transfers between devices, source_table(): lax.all_to_all(jnp.broadcast_to(hub_local[None], (owners,) + hub_local.sh...  13.9 us
  transfers between devices with their start and end apart: 18, of which 7 were waited for; matrix products, arithmetic and copies ran while one was open for 13% of the time, Pallas kernels for 10%

profile of v19, /device:TPU:1, one launch (start us, length us, event | category | flops | bytes accessed | tf_op | source)
XLA Modules:
  0.0 451.3 jit_solution(10175886359306939518)
XLA Ops:
  7.2 2.2 collective-permute-start.2
  9.4 2.6 collective-permute-start.1
  16.1 3.2 gather_fusion.2
  21.8 3.2 gather_fusion.3
  27.6 2.0 gather_fusion
  31.1 7.8 %all-to-all-start = ((bf16[32,640,32]{1,2,0:T(8,128)(2,1)}), bf16[32,640,32]{1,2,0:T(8,128)(2,1)S(1)}, u32[]{:S(2)}, u32[]{:S(2)}) async-start(bf16[32,640,32]{1,2,0:T(8,128)(2,1)} %broadcast_in_dim.77), calls=%async_computation | async-start | bytes 2621440 | tf_op jit(solution)/shard_map/all_to_all | solution.py:226
  38.9 3.2 gather_fusion.4
  42.4 2.9 collective-permute-start.5
  48.5 10.2 %all-to-all-done = bf16[32,640,32]{1,2,0:T(8,128)(2,1)S(1)} async-done(((bf16[32,640,32]{1,2,0:T(8,128)(2,1)}), bf16[32,640,32]{1,2,0:T(8,128)(2,1)S(1)}, u32[]{:S(2)}, u32[]{:S(2)}) %all-to-all-start) | async-done | bytes 1310752 | tf_op jit(solution)/shard_map/all_to_all | solution.py:226
  58.7 4.3 copy.111
  63.6 44.8 %shard_map.120 = f32[4096,32]{1,0:T(8,128)} custom-call(s32[8,4096]{1,0:T(8,128)} %nb_ref.5, bf16[4096,32]{1,0:T(8,128)(2,1)} %bitcast.66, bf16[20480,32]{1,0:T(8,128)(2,1)} %bitcast.67, bf16[1024,32]{1,0:T(8,128)(2,1)} %collective-permute-done.3.refs_2_, bf16[1024,32]{1,0:T(8,128)(2,1)} %collective-permute-done.4.refs_3_, bf16[1024,32]{1,0:T(8,128)(2,1)} %copy-done.14, ...), custom_call_target="tpu_custom_call" | custom-call | tf_op jit(solution)/shard_map/pallas_call | solution.py:46
  108.4 1.7 convert_bitcast_fusion
  111.5 3.5 all-to-all-start.1
  115.1 1.8 fusion.22
  116.9 12.8 %all-to-all-done.1 = bf16[4,32,4096]{2,1,0:T(8,128)(2,1)S(1)} async-done(((bf16[4,32,4096]{2,1,0:T(8,128)(2,1)}), bf16[4,32,4096]{2,1,0:T(8,128)(2,1)S(1)}, u32[]{:S(2)}, u32[]{:S(2)}) %all-to-all-start.1) | async-done | bytes 1048608 | tf_op jit(solution)/shard_map/all_to_all | solution.py:97
  129.7 2.5 fusion.2.refs_0_
  132.3 2.0 gather_fusion.1
  134.5 1.8 broadcast_in_dim.81
  136.4 6.1 %all-to-all-start.2 = ((bf16[32,640,64]{1,2,0:T(8,128)(2,1)}), bf16[32,640,64]{1,2,0:T(8,128)(2,1)}, u32[]{:S(2)}, u32[]{:S(2)}) async-start(bf16[32,640,64]{1,2,0:T(8,128)(2,1)} %broadcast_in_dim.81), calls=%async_computation.2 | async-start | bytes 5242880 | tf_op jit(solution)/shard_map/all_to_all | solution.py:226
  143.8 3.2 gather_fusion.7
  147.0 3.2 gather_fusion.6
  150.2 3.2 gather_fusion.5
  155.9 2.4 collective-permute-start.8
  158.3 18.2 %all-to-all-done.2 = bf16[32,640,64]{1,2,0:T(8,128)(2,1)} async-done(((bf16[32,640,64]{1,2,0:T(8,128)(2,1)}), bf16[32,640,64]{1,2,0:T(8,128)(2,1)}, u32[]{:S(2)}, u32[]{:S(2)}) %all-to-all-start.2) | async-done | bytes 2621472 | tf_op jit(solution)/shard_map/all_to_all | solution.py:226
  176.5 6.0 %copy.117 = bf16[32,640,64]{2,1,0:T(8,128)(2,1)} copy(bf16[32,640,64]{1,2,0:T(8,128)(2,1)} %all-to-all-done.2) | data formatting | bytes 5242880 | tf_op jit(solution)/shard_map/all_to_all | solution.py:226
  182.5 3.5 collective-permute-done.8.refs_4_
  186.7 44.8 %shard_map.121 = f32[4096,64]{1,0:T(8,128)} custom-call(s32[8,4096]{1,0:T(8,128)} %nb_ref.5, bf16[4096,64]{1,0:T(8,128)(2,1)} %copy-done.2, bf16[20480,64]{1,0:T(8,128)(2,1)} %bitcast.68, bf16[1024,64]{1,0:T(8,128)(2,1)} %copy-done.15, bf16[1024,64]{1,0:T(8,128)(2,1)} %copy-done.16, bf16[1024,64]{1,0:T(8,128)(2,1)} %copy-done.17, bf16[64,4096]{1,0:T(8,128)(2,1)} %copy.115.refs_5_), custom_call_target="tpu_custom_call" | custom-call | tf_op jit(solution)/shard_map/pallas_call | solution.py:46
  231.5 1.7 convert_bitcast_fusion.1
  235.1 4.6 %all-to-all-start.3 = ((bf16[4,64,4096]{2,1,0:T(8,128)(2,1)}), bf16[4,64,4096]{2,1,0:T(8,128)(2,1)}, u32[]{:S(2)}, u32[]{:S(2)}) async-start(bf16[4,64,4096]{2,1,0:T(8,128)(2,1)} %broadcast_in_dim.82), calls=%async_computation.3 | async-start | bytes 4194304 | tf_op jit(solution)/shard_map/all_to_all | solution.py:97
  239.7 2.1 fusion.23
  241.9 23.3 %all-to-all-done.3 = bf16[4,64,4096]{2,1,0:T(8,128)(2,1)} async-done(((bf16[4,64,4096]{2,1,0:T(8,128)(2,1)}), bf16[4,64,4096]{2,1,0:T(8,128)(2,1)}, u32[]{:S(2)}, u32[]{:S(2)}) %all-to-all-start.3) | async-done | bytes 2097184 | tf_op jit(solution)/shard_map/all_to_all | solution.py:97
  265.2 2.4 fusion.21
  271.7 58.4 %shard_map.122 = f32[27648,64]{1,0:T(8,128)} custom-call(s32[8,4096]{1,0:T(8,128)} %nb_ref.5, f32[4096,64]{1,0:T(8,128)} %convert_element_type.59.rows_ref), custom_call_target="tpu_custom_call" | custom-call | tf_op jit(solution)/shard_map/pallas_call | solution.py:81
  330.1 5.7 %convert.6 = bf16[27648,64]{1,0:T(8,128)(2,1)S(1)} convert(f32[27648,64]{1,0:T(8,128)} %shard_map.122) | non-fusion elementwise | flops 1769472 | bytes 10616832 | tf_op jit(solution)/shard_map/convert.3
  335.8 3.4 slice.82
  340.3 6.1 %copy.122 = bf16[32,640,64]{1,2,0:T(8,128)(2,1)} copy(bf16[32,640,64]{2,1,0:T(8,128)(2,1)} %bitcast.69) | data formatting | bytes 5242880 | tf_op jit(solution)/shard_map/all_to_all | solution.py:299
  346.4 7.2 %all-to-all-start.4 = ((bf16[32,640,64]{1,2,0:T(8,128)(2,1)}), bf16[32,640,64]{1,2,0:T(8,128)(2,1)}, u32[]{:S(2)}, u32[]{:S(2)}) async-start(bf16[32,640,64]{1,2,0:T(8,128)(2,1)} %copy.122), calls=%async_computation.4 | async-start | bytes 5242880 | tf_op jit(solution)/shard_map/all_to_all | solution.py:299
  354.3 2.0 fusion.17
  356.6 3.0 collective-permute-start.11
  359.9 2.1 fusion.6
  362.1 3.9 convolution_add_fusion.1.base_ref
  367.3 25.0 %collective-permute-done.11 = bf16[1024,64]{1,0:T(8,128)(2,1)S(1)} collective-permute-done((bf16[1024,64]{1,0:T(8,128)(2,1)}, bf16[1024,64]{1,0:T(8,128)(2,1)S(1)}, u32[]{:S(2)}, u32[]{:S(2)}) %collective-permute-start.11) | collective-permute-done | bytes 131104 | tf_op jit(solution)/shard_map/ppermute | solution.py:203
  392.3 3.4 collective-permute-done.10
  395.8 2.1 convert_reduce_fusion
  399.4 12.1 %shard_map.123 = f32[4096,64]{1,0:T(8,128)} custom-call(s32[3712]{0:T(1024)} %pad_add_fusion.t_ref, f32[4096,64]{1,0:T(8,128)} %convolution_add_fusion.1.base_ref, f32[3712,64]{1,0:T(8,128)} %pad_maximum_fusion.upd_ref), custom_call_target="tpu_custom_call" | custom-call | tf_op jit(solution)/shard_map/pallas_call | solution.py:134
  411.6 2.3 convolution_bitcast_fusion
  415.1 14.7 %all_to_all.44 = f32[32,1,1200]{2,1,0:T(1,128)S(1)} all-to-all(f32[32,1,1200]{2,1,0:T(1,128)S(1)} %all_to_all.34), channel_id=1, replica_groups=mesh['dom'=32,'feat'=4] {'dom'}, dimensions={0} | all-to-all | bytes 307200 | tf_op jit(solution)/shard_map/all_to_all | solution.py:167
  430.1 11.5 %all_to_all.45 = f32[32,1,1200]{2,1,0:T(1,128)S(1)} all-to-all(f32[32,1,1200]{2,1,0:T(1,128)S(1)} %broadcast_in_dim.83), channel_id=1, replica_groups=mesh['dom'=32,'feat'=4] {'dom'}, dimensions={0} | all-to-all | bytes 307200 | tf_op jit(solution)/shard_map/all_to_all | solution.py:169
  (132 shorter events, 36.5 us)
Async XLA Ops:
  7.2 258.1 %copy-start = (bf16[172,256]{1,0:T(8,128)(2,1)S(1)}, bf16[172,256]{1,0:T(8,128)(2,1)}, u32[]{:S(2)}) copy-start(bf16[172,256]{1,0:T(8,128)(2,1)} %param.21) | copy-start | bytes 264196
  7.2 39.1 %collective-permute-start.2 = (bf16[32,4096]{1,0:T(8,128)(2,1)}, bf16[32,4096]{1,0:T(8,128)(2,1)S(1)}, u32[]{:S(2)}, u32[]{:S(2)}) collective-permute-start(bf16[32,4096]{1,0:T(8,128)(2,1)} %param.13), channel_id=1, source_target_pairs={{0,1},{1,2},{2,3},{3,0},{4,5},{5,6},{6,7},{7,4},{8,9},{9,10},{10,1... | collective-permute-start | bytes 786440 | tf_op jit(solution)/shard_map/ppermute | solution.py:105
  9.4 36.9 %collective-permute-start.1 = (bf16[32,4096]{1,0:T(8,128)(2,1)}, bf16[32,4096]{1,0:T(8,128)(2,1)S(1)}, u32[]{:S(2)}, u32[]{:S(2)}) collective-permute-start(bf16[32,4096]{1,0:T(8,128)(2,1)} %param.13), channel_id=1, source_target_pairs={{0,2},{1,3},{2,0},{3,1},{4,6},{5,7},{6,4},{7,5},{8,10},{9,11},{10,... | collective-permute-start | bytes 786440 | tf_op jit(solution)/shard_map/ppermute | solution.py:105
  12.0 30.4 %collective-permute-start = (bf16[32,4096]{1,0:T(8,128)(2,1)}, bf16[32,4096]{1,0:T(8,128)(2,1)}, u32[]{:S(2)}, u32[]{:S(2)}) collective-permute-start(bf16[32,4096]{1,0:T(8,128)(2,1)} %param.13), channel_id=1, source_target_pairs={{0,3},{1,0},{2,1},{3,2},{4,7},{5,4},{6,5},{7,6},{8,11},{9,8},{10,9... | collective-permute-start | bytes 786440 | tf_op jit(solution)/shard_map/ppermute | solution.py:105
  14.5 24.4 %copy-start.4 = (bf16[32,4096]{0,1:T(8,128)(2,1)}, bf16[32,4096]{0,1:T(8,128)(2,1)S(1)}, u32[]{:S(2)}) copy-start(bf16[32,4096]{0,1:T(8,128)(2,1)S(1)} %copy.109) | copy-start | bytes 786436
  19.3 8.2 %copy-start.22 = (s32[640]{0:T(1024)S(1)}, s32[640]{0:T(1024)}, u32[]{:S(2)}) copy-start(s32[640]{0:T(1024)} %param.15) | copy-start | bytes 7684
  20.3 42.7 %collective-permute-start.3 = (bf16[1024,32]{1,0:T(8,128)(2,1)}, bf16[1024,32]{1,0:T(8,128)(2,1)}, u32[]{:S(2)}, u32[]{:S(2)}) collective-permute-start(bf16[1024,32]{1,0:T(8,128)(2,1)} %broadcast_select_fusion.5), channel_id=1, source_target_pairs={{0,4},{4,0},{8,12},{12,8},{16,20},{20,16},{24,28},{28,24},{32,36},... | collective-permute-start | bytes 196616 | tf_op jit(solution)/shard_map/ppermute | solution.py:203
  25.9 37.0 %collective-permute-start.4 = (bf16[1024,32]{1,0:T(8,128)(2,1)}, bf16[1024,32]{1,0:T(8,128)(2,1)}, u32[]{:S(2)}, u32[]{:S(2)}) collective-permute-start(bf16[1024,32]{1,0:T(8,128)(2,1)} %broadcast_select_fusion.4), channel_id=1, source_target_pairs={{0,8},{4,12},{8,0},{12,4},{16,24},{20,28},{24,16},{28,20},{32,40},... | collective-permute-start | bytes 196616 | tf_op jit(solution)/shard_map/ppermute | solution.py:203
  31.1 27.6 %all-to-all-start = ((bf16[32,640,32]{1,2,0:T(8,128)(2,1)}), bf16[32,640,32]{1,2,0:T(8,128)(2,1)S(1)}, u32[]{:S(2)}, u32[]{:S(2)}) async-start(bf16[32,640,32]{1,2,0:T(8,128)(2,1)} %broadcast_in_dim.77), calls=%async_computation | async-start | bytes 2621440 | tf_op jit(solution)/shard_map/all_to_all | solution.py:226
  38.9 7.4 %copy-start.13 = (bf16[32,4096]{1,0:T(8,128)(2,1)S(1)}, bf16[32,4096]{1,0:T(8,128)(2,1)}, u32[]{:S(2)}) copy-start(bf16[32,4096]{1,0:T(8,128)(2,1)} %param.13) | copy-start | bytes 786436
  42.4 20.6 %collective-permute-start.5 = (bf16[1024,32]{1,0:T(8,128)(2,1)S(1)}, bf16[1024,32]{1,0:T(8,128)(2,1)S(1)}, u32[]{:S(2)}, u32[]{:S(2)}) collective-permute-start(bf16[1024,32]{1,0:T(8,128)(2,1)S(1)} %broadcast_select_fusion.3), channel_id=1, source_target_pairs={{0,16},{4,20},{8,24},{12,28},{16,0},{20,4},{24,8},{28,12},{32,48},... | collective-permute-start | bytes 196616 | tf_op jit(solution)/shard_map/ppermute | solution.py:203
  62.9 0.7 copy-start.14
  110.1 5.0 %copy-start.9 = (bf16[4,32,4096]{2,1,0:T(8,128)(2,1)S(1)}, bf16[4,32,4096]{2,1,0:T(8,128)(2,1)}, u32[]{:S(2)}) copy-start(bf16[4,32,4096]{2,1,0:T(8,128)(2,1)} %constant_dynamic-slice_fusion) | copy-start | bytes 3145732
  110.1 5.0 %copy-start.23 = (bf16[64,128]{1,0:T(8,128)(2,1)S(1)}, bf16[64,128]{1,0:T(8,128)(2,1)}, u32[]{:S(2)}) copy-start(bf16[64,128]{1,0:T(8,128)(2,1)} %param.18) | copy-start | bytes 49156
  111.5 18.2 %all-to-all-start.1 = ((bf16[4,32,4096]{2,1,0:T(8,128)(2,1)}), bf16[4,32,4096]{2,1,0:T(8,128)(2,1)S(1)}, u32[]{:S(2)}, u32[]{:S(2)}) async-start(bf16[4,32,4096]{2,1,0:T(8,128)(2,1)} %broadcast_in_dim.78), calls=%async_computation.1 | async-start | bytes 2097152 | tf_op jit(solution)/shard_map/all_to_all | solution.py:97
  115.1 14.7 %copy-start.24 = (bf16[64,128]{1,0:T(8,128)(2,1)S(1)}, bf16[64,128]{1,0:T(8,128)(2,1)}, u32[]{:S(2)}) copy-start(bf16[64,128]{1,0:T(8,128)(2,1)} %param.19) | copy-start | bytes 49156
  129.7 2.5 copy-start.11
  132.2 18.0 %copy-start.2 = (bf16[4096,64]{1,0:T(8,128)(2,1)}, bf16[4096,64]{1,0:T(8,128)(2,1)S(1)}, u32[]{:S(2)}) copy-start(bf16[4096,64]{1,0:T(8,128)(2,1)S(1)} %fusion.2.refs_0_) | copy-start | bytes 1572868
  136.4 40.1 %all-to-all-start.2 = ((bf16[32,640,64]{1,2,0:T(8,128)(2,1)}), bf16[32,640,64]{1,2,0:T(8,128)(2,1)}, u32[]{:S(2)}, u32[]{:S(2)}) async-start(bf16[32,640,64]{1,2,0:T(8,128)(2,1)} %broadcast_in_dim.81), calls=%async_computation.2 | async-start | bytes 5242880 | tf_op jit(solution)/shard_map/all_to_all | solution.py:226
  142.5 97.2 %all-gather.2.cloned.1.call-start = ((), (), s32[]{:S(2)}) async-start(), calls=%async_computation.7 | async-start | bytes 2621440 | tf_op jit(solution)/shard_map/all_gather | solution.py:280
  154.1 28.5 %collective-permute-start.6 = (bf16[1024,64]{1,0:T(8,128)(2,1)S(1)}, bf16[1024,64]{1,0:T(8,128)(2,1)S(1)}, u32[]{:S(2)}, u32[]{:S(2)}) collective-permute-start(bf16[1024,64]{1,0:T(8,128)(2,1)S(1)} %broadcast_select_fusion.2), channel_id=1, source_target_pairs={{0,4},{4,0},{8,12},{12,8},{16,20},{20,16},{24,28},{28,24},{32,36},... | collective-permute-start | bytes 393224 | tf_op jit(solution)/shard_map/ppermute | solution.py:203
  154.4 28.1 %collective-permute-start.7 = (bf16[1024,64]{1,0:T(8,128)(2,1)S(1)}, bf16[1024,64]{1,0:T(8,128)(2,1)S(1)}, u32[]{:S(2)}, u32[]{:S(2)}) collective-permute-start(bf16[1024,64]{1,0:T(8,128)(2,1)S(1)} %broadcast_select_fusion.1), channel_id=1, source_target_pairs={{0,8},{4,12},{8,0},{12,4},{16,24},{20,28},{24,16},{28,20},{32,40},... | collective-permute-start | bytes 393224 | tf_op jit(solution)/shard_map/ppermute | solution.py:203
  155.9 30.1 %collective-permute-start.8 = (bf16[1024,64]{1,0:T(8,128)(2,1)S(1)}, bf16[1024,64]{1,0:T(8,128)(2,1)S(1)}, u32[]{:S(2)}, u32[]{:S(2)}) collective-permute-start(bf16[1024,64]{1,0:T(8,128)(2,1)S(1)} %broadcast_select_fusion), channel_id=1, source_target_pairs={{0,16},{4,20},{8,24},{12,28},{16,0},{20,4},{24,8},{28,12},{32,48},... | collective-permute-start | bytes 393224 | tf_op jit(solution)/shard_map/ppermute | solution.py:203
  182.5 3.5 copy-start.15
  182.5 3.5 copy-start.16
  186.0 0.7 copy-start.17
  235.1 4.6 %copy-start.18 = (bf16[172,256]{1,0:T(8,128)(2,1)S(1)}, bf16[172,256]{1,0:T(8,128)(2,1)}, u32[]{:S(2)}) copy-start(bf16[172,256]{1,0:T(8,128)(2,1)} %param.20) | copy-start | bytes 264196
  235.1 30.1 %all-to-all-start.3 = ((bf16[4,64,4096]{2,1,0:T(8,128)(2,1)}), bf16[4,64,4096]{2,1,0:T(8,128)(2,1)}, u32[]{:S(2)}, u32[]{:S(2)}) async-start(bf16[4,64,4096]{2,1,0:T(8,128)(2,1)} %broadcast_in_dim.82), calls=%async_computation.3 | async-start | bytes 4194304 | tf_op jit(solution)/shard_map/all_to_all | solution.py:97
  265.2 2.4 copy-start.25
  268.2 1.1 copy-start.5
  335.8 4.5 %copy-start.7 = (bf16[27648,64]{1,0:T(8,128)(2,1)}, bf16[27648,64]{1,0:T(8,128)(2,1)S(1)}, u32[]{:S(2)}) copy-start(bf16[27648,64]{1,0:T(8,128)(2,1)S(1)} %convert.6) | copy-start | bytes 10616836
  346.4 7.2 %copy-start.21 = (s32[3,1024]{1,0:T(4,128)S(1)}, s32[3,1024]{1,0:T(4,128)}, u32[]{:S(2)}) copy-start(s32[3,1024]{1,0:T(4,128)} %param.16) | copy-start | bytes 36868
  346.4 49.3 %all-to-all-start.4 = ((bf16[32,640,64]{1,2,0:T(8,128)(2,1)}), bf16[32,640,64]{1,2,0:T(8,128)(2,1)}, u32[]{:S(2)}, u32[]{:S(2)}) async-start(bf16[32,640,64]{1,2,0:T(8,128)(2,1)} %copy.122), calls=%async_computation.4 | async-start | bytes 5242880 | tf_op jit(solution)/shard_map/all_to_all | solution.py:299
  353.7 6.2 %copy-start.6 = (bf16[172,4096]{1,0:T(8,128)(2,1)S(1)}, bf16[172,4096]{1,0:T(8,128)(2,1)}, u32[]{:S(2)}) copy-start(bf16[172,4096]{1,0:T(8,128)(2,1)} %copy-done.5) | copy-start | bytes 4227076
  356.3 5.7 %copy-start.19 = (bf16[172,256]{1,0:T(8,128)(2,1)S(1)}, bf16[172,256]{1,0:T(8,128)(2,1)}, u32[]{:S(2)}) copy-start(bf16[172,256]{1,0:T(8,128)(2,1)} %param.20) | copy-start | bytes 264196
  356.3 10.9 %collective-permute-start.9 = (bf16[1024,64]{1,0:T(8,128)(2,1)}, bf16[1024,64]{1,0:T(8,128)(2,1)S(1)}, u32[]{:S(2)}, u32[]{:S(2)}) collective-permute-start(bf16[1024,64]{1,0:T(8,128)(2,1)} %get-tuple-element.30), channel_id=1, source_target_pairs={{0,4},{4,0},{8,12},{12,8},{16,20},{20,16},{24,28},{28,24},{32,36},... | collective-permute-start | bytes 393224 | tf_op jit(solution)/shard_map/ppermute | solution.py:203
  356.6 35.6 %collective-permute-start.11 = (bf16[1024,64]{1,0:T(8,128)(2,1)}, bf16[1024,64]{1,0:T(8,128)(2,1)S(1)}, u32[]{:S(2)}, u32[]{:S(2)}) collective-permute-start(bf16[1024,64]{1,0:T(8,128)(2,1)} %get-tuple-element.31), channel_id=1, source_target_pairs={{0,16},{4,20},{8,24},{12,28},{16,0},{20,4},{24,8},{28,12},{32,48},... | collective-permute-start | bytes 393224 | tf_op jit(solution)/shard_map/ppermute | solution.py:203
  359.6 36.1 %collective-permute-start.10 = (bf16[1024,64]{1,0:T(8,128)(2,1)}, bf16[1024,64]{1,0:T(8,128)(2,1)S(1)}, u32[]{:S(2)}, u32[]{:S(2)}) collective-permute-start(bf16[1024,64]{1,0:T(8,128)(2,1)} %get-tuple-element.32), channel_id=1, source_target_pairs={{0,8},{4,12},{8,0},{12,4},{16,24},{20,28},{24,16},{28,20},{32,40},... | collective-permute-start | bytes 393224 | tf_op jit(solution)/shard_map/ppermute | solution.py:203
  362.0 3.9 copy-start.3
  399.4 12.1 %copy-start.12 = (bf16[4,32,4096]{2,1,0:T(8,128)(2,1)S(1)}, bf16[4,32,4096]{2,1,0:T(8,128)(2,1)}, u32[]{:S(2)}) copy-start(bf16[4,32,4096]{2,1,0:T(8,128)(2,1)} %copy-done.11) | copy-start | bytes 3145732
  411.6 2.3 copy-start.8
  411.6 2.5 copy-start.10
  414.1 0.8 copy-start.20
  414.1 30.4 %copy-start.1 = (bf16[172,256]{1,0:T(8,128)(2,1)S(1)}, bf16[172,256]{1,0:T(8,128)(2,1)}, u32[]{:S(2)}) copy-start(bf16[172,256]{1,0:T(8,128)(2,1)} %param.21) | copy-start | bytes 264196
Sparse Core Ops, SparseCore 0:
  145.0 29.7 all-gather.1
